TPU v7x, 32 devices: a whole 2x2x4 slice. The times are simulated.
32 devices in a mesh: ctx: 4 (over y, x), dp: 4 (over z), tp: 2 (over core).
Axes of the slice: x: 2, y: 2, z: 4, core: 2. Of those that a mesh axis runs over, the one named last changes fastest.
Arguments:
- queries: bfloat16 [4, 512, 32, 128], P('dp', 'ctx', 'tp'), may hold values from -21 to 21
- keys: bfloat16 [4, 512, 4, 128], P('dp', 'ctx', 'tp'), may hold values from -6 to 6
- values: bfloat16 [4, 512, 4, 128], P('dp', 'ctx', 'tp'), may hold values from -6 to 6
- output_cotangent: bfloat16 [4, 512, 32, 128], P('dp', 'ctx', 'tp'), may hold values from -6 to 6
- features: bfloat16 [4, 512, 4096], P('dp', 'ctx'), may hold values from -60 to 60
- doc_lengths: int32 [4, 48], P('dp'), may hold values from 1 to 16, 512 in all within a row
- rope_num: int32 [64], replicated, may hold values from 1 to 40
- rope_den: int32 [64], replicated, may hold values from 1 to 8
- param: float32 [4096, 512], P('dp', 'tp'), may hold values from -0.4375 to 0.4375
- first_moment_state: float32 [4096, 512], P('dp', 'tp'), may hold values from -4 to 4
- second_moment_state: float32 [4096, 512], P('dp', 'tp'), may hold values from 0.05 to 1
Outputs:
- grad_queries: bfloat16 [4, 512, 32, 128], P('dp', 'ctx', 'tp')
- grad_keys: bfloat16 [4, 512, 4, 128], P('dp', 'ctx', 'tp')
- value_gradient: bfloat16 [4, 512, 4, 128], P('dp', 'ctx', 'tp')
- new_param: float32 [4096, 512], P('dp', 'tp')
- new_first: float32 [4096, 512], P('dp', 'tp')
- new_second: float32 [4096, 512], P('dp', 'tp')
Inputs may be any that keep to these rules, and one draw needn't show every extreme that they name: `doc_lengths`: each row's 48 lengths sum to 512, and the largest of each row is exactly 16.
All inputs are finite; a program needn't handle non-finite values.
Results may differ from a plain program's by a relative error of at most 0.0064.
Values may be sent and summed in bfloat16 or wider, within the bound.
No kernel may reach another device: no remote copies, remote signals or barrier semaphores. Data moves between devices by JAX's collectives and lax.ppermute only.
A program may use at most 64 MiB of HBM per device.

v0:
```python
from functools import reduce
import math

import jax
import jax.numpy as jnp
from jax import lax
from jax.sharding import PartitionSpec as P

ROPE_BASE = 500000.0
NEG_FILL = -1e30
CLIP_NORM = 1000.0
LEARN_RATE = 0.0001
DECAY_RATE = 0.1
BETA_ONE = 0.9
BETA_TWO = 0.95
ADAM_EPS = 1e-08
FIRST_FIX = 1.0 - 0.9**10
SECOND_FIX = 1.0 - 0.95**10


def shifted(array, axis, by):
    peers = lax.axis_size(axis)
    pairs = [(i, i + by) for i in range(peers) if 0 <= i + by < peers]
    return lax.ppermute(array, axis, pairs)


def doc_layout(lengths_row, token_index):
    doc_ends = jnp.cumsum(lengths_row)
    passed = doc_ends[None, :] <= token_index[:, None]
    doc_start = jnp.max(jnp.where(passed, doc_ends[None, :], 0), axis=1)
    doc_id = jnp.sum(passed.astype(jnp.int32), axis=1)
    return (doc_id, (token_index - doc_start).astype(jnp.float32))


def rope_tables(position, rope_num, rope_den, head_dim):
    expo = jnp.arange(head_dim // 2, dtype=jnp.float32) * (2.0 / head_dim)
    freq = (
        jnp.exp(-math.log(ROPE_BASE) * expo)
        * rope_den.astype(jnp.float32)
        / rope_num.astype(jnp.float32)
    )
    angle = position[:, None] * freq[None, :]
    cosine = jnp.concatenate([jnp.cos(angle), jnp.cos(angle)], axis=1)
    sine = jnp.concatenate([jnp.sin(angle), jnp.sin(angle)], axis=1)
    return (cosine[:, None, :], sine[:, None, :])


def rotate(vectors, cosine, sine):
    half = vectors.shape[-1] // 2
    turned = jnp.concatenate([-vectors[..., half:], vectors[..., :half]], axis=-1)
    return vectors * cosine + turned * sine


def unrotate(grads_in, cosine, sine):
    half = grads_in.shape[-1] // 2
    scaled = grads_in * sine
    turned = jnp.concatenate([scaled[..., half:], -scaled[..., :half]], axis=-1)
    return grads_in * cosine + turned


def adam_update(param, first_moment_state, second_moment_state, weight_gradient, grad_total):
    clip_factor = jnp.minimum(jnp.float32(1.0), CLIP_NORM / jnp.sqrt(grad_total))
    clipped = weight_gradient * clip_factor
    new_first = BETA_ONE * first_moment_state + (1.0 - BETA_ONE) * clipped
    new_second = BETA_TWO * second_moment_state + (1.0 - BETA_TWO) * clipped * clipped
    step_size = new_first / FIRST_FIX / (jnp.sqrt(new_second / SECOND_FIX) + ADAM_EPS)
    new_param = param - LEARN_RATE * (step_size + DECAY_RATE * param)
    return (new_param, new_first, new_second)


def local(
    queries,
    keys,
    values,
    output_cotangent,
    features,
    doc_lengths,
    rope_num,
    rope_den,
    param,
    first_moment_state,
    second_moment_state,
):
    tok_rows = queries.shape[1]
    head_count = queries.shape[2]
    head_dim = queries.shape[3]
    kv_count = keys.shape[2]
    group_size = head_count // kv_count
    n_ctx = lax.axis_size("ctx")
    place = lax.axis_index("ctx")
    seq_len = tok_rows * n_ctx
    doc_most = seq_len // 32
    reach = (doc_most + tok_rows - 2) // tok_rows
    scale = head_dim ** (-0.5)
    lengths_row = doc_lengths[0]
    own_index = place * tok_rows + jnp.arange(tok_rows, dtype=jnp.int32)
    own_doc, position = doc_layout(lengths_row, own_index)
    cosine, sine = rope_tables(position, rope_num, rope_den, head_dim)
    rotated_query_rows = rotate(queries[0].astype(jnp.float32), cosine, sine).astype(jnp.bfloat16)
    rotated_query_rows = rotated_query_rows.reshape(tok_rows, kv_count, group_size, head_dim)
    rotated_key_rows = rotate(keys[0].astype(jnp.float32), cosine, sine).astype(jnp.bfloat16)
    grad_out = output_cotangent[0].reshape(tok_rows, kv_count, group_size, head_dim)
    kv_pair = jnp.stack([rotated_key_rows, values[0]])
    pairs = [kv_pair]
    offset = 1
    kv_pair = shifted(kv_pair, "ctx", 1)
    pairs.append(kv_pair)
    masks = []
    for offset in range(reach + 1):
        key_index = (place - offset) * tok_rows + jnp.arange(tok_rows, dtype=jnp.int32)
        key_doc = doc_layout(lengths_row, key_index)[0]
        valid = (
            (key_index[None, :] >= 0)
            & (key_index[None, :] <= own_index[:, None])
            & (key_doc[None, :] == own_doc[:, None])
        )
        masks.append(valid)
    score_list = []
    for pair_in, valid_in in zip(pairs, masks):
        raw = (
            jnp.einsum(
                "qhgd,khd->hgqk", rotated_query_rows, pair_in[0], preferred_element_type=jnp.float32
            )
            * scale
        )
        score_list.append(jnp.where(valid_in, raw, NEG_FILL))
    row_top = reduce(
        jnp.maximum, [jnp.max(scores, axis=-1, keepdims=True) for scores in score_list]
    )
    weight_list = [
        jnp.where(valid_in, jnp.exp(scores - row_top), 0.0)
        for scores, valid_in in zip(score_list, masks)
    ]
    row_total = reduce(
        jnp.add, [jnp.sum(weights, axis=-1, keepdims=True) for weights in weight_list]
    )
    prob_list = [weights / row_total for weights in weight_list]
    low_list = [probs.astype(jnp.bfloat16) for probs in prob_list]
    attn_out = reduce(
        jnp.add,
        [
            jnp.einsum("hgqk,khd->qhgd", probs_low, pair_in[1], preferred_element_type=jnp.float32)
            for probs_low, pair_in in zip(low_list, pairs)
        ],
    )
    delta = jnp.einsum("qhgd,qhgd->hgq", grad_out.astype(jnp.float32), attn_out)[..., None]
    query_terms = []
    key_terms = []
    for pair_in, probs, probs_low, valid_in in zip(pairs, prob_list, low_list, masks):
        dprobs = jnp.einsum(
            "qhgd,khd->hgqk", grad_out, pair_in[1], preferred_element_type=jnp.float32
        )
        dscores = (probs * (dprobs - delta)).astype(jnp.bfloat16)
        q_part = (
            jnp.einsum("hgqk,khd->qhgd", dscores, pair_in[0], preferred_element_type=jnp.float32)
            * scale
        )
        k_part = (
            jnp.einsum(
                "hgqk,qhgd->khd", dscores, rotated_query_rows, preferred_element_type=jnp.float32
            )
            * scale
        )
        v_part = jnp.einsum(
            "hgqk,qhgd->khd", probs_low, grad_out, preferred_element_type=jnp.float32
        )
        q_part, kv_part = (q_part, jnp.stack([k_part, v_part]))
        query_terms.append(q_part)
        key_terms.append(kv_part)
    query_grad = reduce(jnp.add, query_terms)
    key_total = key_terms[reach]
    offset = 0
    key_total = (
        shifted(key_total.astype(jnp.bfloat16), "ctx", -1).astype(key_total.dtype)
        + key_terms[offset]
    )
    grad_q = unrotate(query_grad.reshape(tok_rows, head_count, head_dim), cosine, sine).astype(
        jnp.bfloat16
    )
    grad_k = unrotate(key_total[0], cosine, sine).astype(jnp.bfloat16)
    grad_v = key_total[1].astype(jnp.bfloat16)
    feats = features[0]
    width = feats.shape[1]
    value_flat = grad_v.reshape(tok_rows, kv_count * head_dim)
    own_rows = param.shape[0]
    n_dp = lax.axis_size("dp")
    piece_rows = own_rows // n_ctx
    permuted = (
        feats.reshape(tok_rows, n_dp, n_ctx, piece_rows)
        .transpose(0, 2, 1, 3)
        .reshape(tok_rows, width)
    )
    pieces = lax.psum_scatter(
        lax.dot_general(
            permuted, value_flat, (((0,), (0,)), ((), ())), preferred_element_type=jnp.float32
        ),
        ("ctx", "dp"),
        scatter_dimension=0,
        tiled=True,
    )
    weight_gradient = lax.all_gather(pieces, "ctx", axis=0, tiled=True)
    norm_part = jnp.sum(weight_gradient * weight_gradient)
    grad_total = lax.psum(norm_part, ("dp", "tp"))
    new_param, new_first, new_second = adam_update(
        param, first_moment_state, second_moment_state, weight_gradient, grad_total
    )
    return (grad_q[None], grad_k[None], grad_v[None], new_param, new_first, new_second)


def solution(mesh):
    placed = (
        P("dp", "ctx", "tp", None),
        P("dp", "ctx", "tp", None),
        P("dp", "ctx", "tp", None),
        P("dp", "ctx", "tp", None),
        P("dp", "ctx", None),
        P("dp", None),
        P(),
        P(),
        P("dp", "tp"),
        P("dp", "tp"),
        P("dp", "tp"),
    )
    return jax.shard_map(
        local,
        mesh=mesh,
        in_specs=placed,
        out_specs=(
            P("dp", "ctx", "tp", None),
            P("dp", "ctx", "tp", None),
            P("dp", "ctx", "tp", None),
            P("dp", "tp"),
            P("dp", "tp"),
            P("dp", "tp"),
        ),
        check_vma=False,
    )
```

profile of v0, /device:TPU:0, one launch (start us, length us, event | category | flops | bytes accessed | tf_op | source)
XLA Modules:
  0.0 216.5 jit_solution(16039566260402643105)
XLA Ops:
  7.2 0.7 copy.135
  8.3 0.7 convert_divide_fusion
  9.4 0.9 convert_bitcast_fusion.2
  10.3 0.7 fusion.45
  11.0 0.8 copy.142
  11.9 0.9 fusion.35
  12.8 0.7 pad_maximum_fusion
  13.5 5.5 %collective-permute-start = (bf16[2,128,2,128]{3,1,2,0:T(8,128)(2,1)}, bf16[2,128,2,128]{3,1,2,0:T(8,128)(2,1)}, u32[]{:S(2)}, u32[]{:S(2)}) collective-permute-start(bf16[2,128,2,128]{3,1,2,0:T(8,128)(2,1)} %pad_maximum_fusion), channel_id=1, source_target_pairs={{0,8},{8,16},{16,24},{1,9},{9,17},{17,25},{2,10},{10,18},{18,26},{... | collective-permute-start | bytes 393224 | tf_op jit(solution)/shard_map/ppermute | solution.py:24
  19.0 0.6 broadcast_compare_fusion
  19.7 0.7 copy.140
  20.4 1.2 convert_bitcast_fusion.1
  21.6 1.3 fusion.22
  22.9 2.4 %copy.138 = f32[128,2,8,64]{0,3,2,1:T(8,128)} copy(f32[128,2,8,64]{3,2,1,0:T(8,128)} %get-tuple-element.40) | data formatting | bytes 1048576 | tf_op jit(solution)/shard_map/concatenate | solution.py:50
  25.3 1.2 copy.139
  27.0 1.0 fusion.40
  28.0 0.8 compare_and_fusion
  28.8 1.4 fusion.24
  30.5 1.2 copy.164
  31.8 1.6 copy.168
  33.4 1.0 copy.169
  34.4 1.1 fusion.52
  36.0 1.0 fusion.18
  37.0 1.0 convolution_bitcast_fusion.5
  38.5 1.2 fusion.3
  39.7 0.8 multiply_reduce_fusion
  40.5 1.4 fusion.12
  42.0 1.6 fusion.11
  43.9 1.3 collective-permute-start.1
  45.6 5.2 %collective-permute-done.1 = bf16[2,128,2,128]{3,1,2,0:T(8,128)(2,1)S(1)} collective-permute-done((bf16[2,128,2,128]{3,1,2,0:T(8,128)(2,1)S(1)}, bf16[2,128,2,128]{3,1,2,0:T(8,128)(2,1)S(1)}, u32[]{:S(2)}, u32[]{:S(2)}) %collective-permute-start.1) | collective-permute-done | bytes 131104 | tf_op jit(solution)/shard_map/ppermute | solution.py:24
  51.5 2.6 %convolution_bitcast_fusion = f32[4096,256]{0,1:T(8,128)} fusion(bf16[128,256]{0,1:T(8,128)(2,1)S(1)} %bitcast.172, bf16[128,4096]{0,1:T(8,128)(2,1)S(1)} %bitcast.170), kind=kOutput, calls=%fused_computation | convolution fusion | flops 268435456 | bytes 5308416 | tf_op jit(solution)/shard_map/dot_general | solution.py:194
  54.4 1.0 copy-done.6
  55.4 1.3 copy.166
  56.7 1.3 copy.170
  58.0 2.5 %copy.172 = f32[1024,256]{0,1:T(8,128)} copy(f32[1024,256]{1,0:T(8,128)} %param.19) | data formatting | bytes 2097152 | tf_op args[8]
  60.5 1.2 fusion.53
  61.7 90.6 %reduce-scatter.2.cloned.1.call-done = f32[256,256]{0,1:T(8,128)} async-done(((f32[4096,256]{0,1:T(8,128)}), f32[256,256]{0,1:T(8,128)}) %reduce-scatter.2.cloned.1.call-update) | async-done | bytes 262160 | tf_op jit(solution)/shard_map/reduce_scatter | solution.py:193
  152.3 1.2 fusion.6
  153.5 0.5 copy.157
  155.0 1.2 fusion.25
  156.2 0.7 copy.174
  157.1 22.0 %all-gather.2.cloned.1.call-done = f32[1024,256]{0,1:T(8,128)} async-done(((f32[256,256]{0,1:T(8,128)}), f32[1024,256]{0,1:T(8,128)}) %all-gather.2.cloned.1.call-update) | async-done | bytes 1048592 | tf_op jit(solution)/shard_map/all_gather | solution.py:201
  179.1 2.2 %multiply_reduce_fusion.1 = f32[]{:T(128)} fusion(f32[1024,256]{0,1:T(8,128)} %all-gather.2.cloned.1.call-done), kind=kLoop, calls=%fused_computation.50 | loop fusion | flops 524287 | bytes 1048580 | tf_op jit(solution)/shard_map/reduce_sum | solution.py:202
  181.3 0.7 copy.173
  182.0 16.9 %psum.7 = f32[]{:T(128)} all-reduce(f32[]{:T(128)} %multiply_reduce_fusion.1), channel_id=1, replica_groups=mesh['ctx'=4,'dp'=4,'tp'=2] {'dp','tp'}, use_global_device_ids=true, to_apply=%region_10.11 | all-reduce | flops 1 | bytes 8 | tf_op jit(solution)/shard_map/psum | solution.py:203
  199.7 3.7 %multiply_subtract_fusion = (f32[1024,256]{0,1:T(8,128)}, f32[1024,256]{0,1:T(8,128)}, f32[1024,256]{0,1:T(8,128)S(1)}) fusion(f32[1024,256]{0,1:T(8,128)} %copy.172, f32[1024,256]{0,1:T(8,128)} %all-gather.2.cloned.1.call-done, f32[]{:T(128)S(6)} %min_shard_map.3, f32[1024,256]{0,1:T(8,128)S(1)} %copy-done.1, f32[1024,256]{0,1:T(8,128)S(1)} %copy-done.2), kind=kLoop, calls=%fused_computation.48 | loop fusion | flops 4194304 | bytes 7340036 | tf_op jit(solution)/shard_map/sub | solution.py:67
  203.3 2.5 %copy.175 = f32[1024,256]{1,0:T(8,128)} copy(f32[1024,256]{0,1:T(8,128)} %get-tuple-element.35) | data formatting | bytes 2097152
  205.9 2.5 %copy.176 = f32[1024,256]{1,0:T(8,128)} copy(f32[1024,256]{0,1:T(8,128)} %get-tuple-element.36) | data formatting | bytes 2097152
  208.4 1.3 copy.177
  (64 shorter events, 5.3 us)
Async XLA Ops:
  7.2 145.1 %reduce-scatter.2.cloned.1.call-start = ((), (), s32[]{:S(2)}) async-start(), calls=%async_computation.1 | async-start | bytes 4456448 | tf_op jit(solution)/shard_map/reduce_scatter | solution.py:193
  13.5 21.0 %collective-permute-start = (bf16[2,128,2,128]{3,1,2,0:T(8,128)(2,1)}, bf16[2,128,2,128]{3,1,2,0:T(8,128)(2,1)}, u32[]{:S(2)}, u32[]{:S(2)}) collective-permute-start(bf16[2,128,2,128]{3,1,2,0:T(8,128)(2,1)} %pad_maximum_fusion), channel_id=1, source_target_pairs={{0,8},{8,16},{16,24},{1,9},{9,17},{17,25},{2,10},{10,18},{18,26},{... | collective-permute-start | bytes 393224 | tf_op jit(solution)/shard_map/ppermute | solution.py:24
  21.6 5.4 %copy-start.11 = (bf16[1,128,2,128]{3,2,1,0:T(2,128)(2,1)S(1)}, bf16[1,128,2,128]{3,2,1,0:T(2,128)(2,1)}, u32[]{:S(2)}) copy-start(bf16[1,128,2,128]{3,2,1,0:T(2,128)(2,1)} %param.12) | copy-start | bytes 196612
  25.3 5.2 %copy-start.3 = (bf16[1,128,16,128]{3,2,1,0:T(8,128)(2,1)S(1)}, bf16[1,128,16,128]{3,2,1,0:T(8,128)(2,1)}, u32[]{:S(2)}) copy-start(bf16[1,128,16,128]{3,2,1,0:T(8,128)(2,1)} %param.14) | copy-start | bytes 1572868
  28.0 2.5 %copy-start.10 = (bf16[128,2,128,1]{2,0,3,1:T(8,128)(2,1)}, bf16[128,2,128,1]{2,0,3,1:T(8,128)(2,1)S(1)}, u32[]{:S(2)}) copy-start(bf16[128,2,128,1]{2,0,3,1:T(8,128)(2,1)S(1)} %fusion.40) | copy-start | bytes 196612
  33.4 2.6 %copy-start.12 = (bf16[128,2,8,128]{0,3,2,1:T(8,128)(2,1)S(1)}, bf16[128,2,8,128]{0,3,2,1:T(8,128)(2,1)}, u32[]{:S(2)}) copy-start(bf16[128,2,8,128]{0,3,2,1:T(8,128)(2,1)} %copy.164) | copy-start | bytes 1572868
  36.0 2.0 copy-start.14
  42.0 1.9 copy-start.15
  42.0 8.8 %copy-start.13 = (f32[1,128,2,128]{3,1,2,0:T(8,128)S(1)}, f32[1,128,2,128]{3,1,2,0:T(8,128)}, u32[]{:S(2)}) copy-start(f32[1,128,2,128]{3,1,2,0:T(8,128)} %convolution_bitcast_fusion.5) | copy-start | bytes 393220
  42.0 9.5 %copy-start = (bf16[128,4,4,256]{0,3,2,1:T(8,128)(2,1)S(1)}, bf16[128,4,4,256]{0,3,2,1:T(8,128)(2,1)}, u32[]{:S(2)}) copy-start(bf16[128,4,4,256]{0,3,2,1:T(8,128)(2,1)} %copy.169) | copy-start | bytes 3145732
  43.6 2.0 copy-start.4
  43.9 6.9 %collective-permute-start.1 = (bf16[2,128,2,128]{3,1,2,0:T(8,128)(2,1)S(1)}, bf16[2,128,2,128]{3,1,2,0:T(8,128)(2,1)S(1)}, u32[]{:S(2)}, u32[]{:S(2)}) collective-permute-start(bf16[2,128,2,128]{3,1,2,0:T(8,128)(2,1)S(1)} %pad_maximum_fusion.1), channel_id=1, source_target_pairs={{8,0},{16,8},{24,16},{9,1},{17,9},{25,17},{10,2},{18,10},{26,18},{... | collective-permute-start | bytes 393224 | tf_op jit(solution)/shard_map/ppermute | solution.py:24
  50.9 0.6 copy-start.8
  54.1 1.2 copy-start.6
  54.1 2.5 %copy-start.7 = (f32[1024,256]{1,0:T(8,128)S(1)}, f32[1024,256]{1,0:T(8,128)}, u32[]{:S(2)}) copy-start(f32[1024,256]{1,0:T(8,128)} %param.21) | copy-start | bytes 3145732
  54.2 98.2 %copy-start.5 = (bf16[2,8,128,128]{2,3,1,0:T(8,128)(2,1)S(1)}, bf16[2,8,128,128]{2,3,1,0:T(8,128)(2,1)}, u32[]{:S(2)}) copy-start(bf16[2,8,128,128]{2,3,1,0:T(8,128)(2,1)} %copy-done.4) | copy-start | bytes 1572868
  54.2 125.0 %all-gather.2.cloned.1.call-start = ((), (), s32[]{:S(2)}) async-start(), calls=%async_computation.2 | async-start | bytes 1310720 | tf_op jit(solution)/shard_map/all_gather | solution.py:201
  154.7 1.6 copy-start.9
  155.0 44.6 %copy-start.1 = (f32[1024,256]{0,1:T(8,128)S(1)}, f32[1024,256]{0,1:T(8,128)}, u32[]{:S(2)}) copy-start(f32[1024,256]{0,1:T(8,128)} %copy.166) | copy-start | bytes 3145732
  155.0 44.6 %copy-start.2 = (f32[1024,256]{0,1:T(8,128)S(1)}, f32[1024,256]{0,1:T(8,128)}, u32[]{:S(2)}) copy-start(f32[1024,256]{0,1:T(8,128)} %copy.170) | copy-start | bytes 3145732
Sparse Core Ops, SparseCore 0:
  54.3 97.9 reduce-scatter.1
  154.1 24.9 all-gather.1
where the time goes:
time: 218 us; the launch traced here: 217 us
  waiting for transfers between devices  118 us (54%)
  local copies, waits for them, and re-layouts  26 us (12%)
  other arithmetic  19.8 us (9%)
  blocking collectives  16.9 us (8%)
  between operations  15.2 us (7%)
  matrix products  13.7 us (6%)
  starting transfers between devices  7.07 us (3%)
    reduce_scatter x1, waiting for transfers between devices, local(): lax.psum_scatter(lax.dot_general(permuted, value_flat, (((0,), (0,)), (()...  90.6 us
    all_gather x1, waiting for transfers between devices, local(): weight_gradient = lax.all_gather(pieces, 'ctx', axis=0, tiled=True)  22 us
    unnamed x42, local copies, waits for them, and re-layouts  16.9 us
    psum x1, blocking collectives, local(): grad_total = lax.psum(norm_part, ('dp', 'tp'))  16.9 us
    ppermute x2, starting transfers between devices, shifted(): return lax.ppermute(array, axis, pairs)  6.81 us
    ppermute x2, waiting for transfers between devices, shifted(): return lax.ppermute(array, axis, pairs)  5.25 us
  transfers between devices with their start and end apart: 4, of which 3 were waited for; matrix products, arithmetic and copies ran while one was open for 12% of the time, Pallas kernels for 0%

commit v1 on v0

--- a/solution.py
+++ b/solution.py
@@ -185,22 +185,20 @@
     own_rows = param.shape[0]
     n_dp = lax.axis_size("dp")
     piece_rows = own_rows // n_ctx
-    permuted = (
-        feats.reshape(tok_rows, n_dp, n_ctx, piece_rows)
-        .transpose(0, 2, 1, 3)
-        .reshape(tok_rows, width)
-    )
-    pieces = lax.psum_scatter(
-        lax.dot_general(
-            permuted, value_flat, (((0,), (0,)), ((), ())), preferred_element_type=jnp.float32
-        ),
-        ("ctx", "dp"),
-        scatter_dimension=0,
-        tiled=True,
-    )
+    spread = ("dp", "ctx")
+    feat_cols = lax.all_to_all(
+        feats.reshape(tok_rows, n_dp * n_ctx, piece_rows), spread, 1, 0, tiled=False
+    )
+    value_rows = lax.all_gather(value_flat, spread, axis=0, tiled=False)
+    pieces = lax.dot_general(
+        feat_cols.reshape(-1, piece_rows),
+        value_rows.reshape(-1, kv_count * head_dim),
+        (((0,), (0,)), ((), ())),
+        preferred_element_type=jnp.float32,
+    )
+    norm_part = jnp.sum(pieces * pieces)
+    grad_total = lax.psum(norm_part, ("ctx", "dp", "tp"))
     weight_gradient = lax.all_gather(pieces, "ctx", axis=0, tiled=True)
-    norm_part = jnp.sum(weight_gradient * weight_gradient)
-    grad_total = lax.psum(norm_part, ("dp", "tp"))
     new_param, new_first, new_second = adam_update(
         param, first_moment_state, second_moment_state, weight_gradient, grad_total
     )

time: 218 us -> 177 us (0.81)
  waiting for transfers between devices: 118 us -> 55.5 us
  blocking collectives: 16.9 us -> 38.5 us
  other arithmetic: 19.8 us -> 13.5 us
  starting transfers between devices: 7.07 us -> 12.6 us
    reduce_scatter x1 -> x0, waiting for transfers between devices: 90.6 us -> none  [local(): lax.psum_scatter(lax.dot_general(permuted, value_flat, (((0,), (0,)), (()...]
    all_gather x0 -> x1, waiting for transfers between devices: none -> 50.1 us  [local(): value_rows = lax.all_gather(value_flat, spread, axis=0, tiled=False)]
    all_gather x1, waiting for transfers between devices: 22 us -> 0.02 us  [local(): weight_gradient = lax.all_gather(pieces, 'ctx', axis=0, tiled=True)]
    psum x1, blocking collectives: 16.9 us -> 38.5 us  [local(): grad_total = lax.psum(norm_part, ('ctx', 'dp', 'tp'))]
    all_to_all x0 -> x1, starting transfers between devices: none -> 5.44 us  [local(): lax.all_to_all(feats.reshape(tok_rows, n_dp * n_ctx, piece_rows), spread,...]
    unnamed x42 -> x68, local copies, waits for them, and re-layouts: 16.9 us -> 18.8 us
  transfers between devices with their start and end apart: 4 -> 5, of which waited for: 3 -> 2; matrix products, arithmetic and copies ran while one was open for 12% -> 19% of each run, Pallas kernels for 0% -> 0%
where the time goes in v1:
time: 177 us; the launch traced here: 176 us
  waiting for transfers between devices  55.5 us (31%)
  blocking collectives  38.5 us (22%)
  local copies, waits for them, and re-layouts  27.5 us (16%)
  between operations  15.2 us (9%)
  other arithmetic  13.5 us (8%)
  matrix products  13.1 us (7%)
  starting transfers between devices  12.6 us (7%)
    all_gather x1, waiting for transfers between devices, local(): value_rows = lax.all_gather(value_flat, spread, axis=0, tiled=False)  50.1 us
    psum x1, blocking collectives, local(): grad_total = lax.psum(norm_part, ('ctx', 'dp', 'tp'))  38.5 us
    unnamed x68, local copies, waits for them, and re-layouts  18.8 us
    ppermute x2, starting transfers between devices, shifted(): return lax.ppermute(array, axis, pairs)  6.94 us
    all_to_all x1, starting transfers between devices, local(): lax.all_to_all(feats.reshape(tok_rows, n_dp * n_ctx, piece_rows), spread,...  5.44 us
    ppermute x2, waiting for transfers between devices, shifted(): return lax.ppermute(array, axis, pairs)  5.26 us
    sub x1, other arithmetic, adam_update(): new_param = param - LEARN_RATE * (step_size + DECAY_RATE * param)  3.67 us
    concatenate x2, local copies, waits for them, and re-layouts, rotate(): jnp.concatenate([-vectors[..., half:], vectors[..., :half]], axis=-1)  3.63 us
  transfers between devices with their start and end apart: 5, of which 2 were waited for; matrix products, arithmetic and copies ran while one was open for 19% of the time, Pallas kernels for 0%

profile of v1, /device:TPU:0, one launch (start us, length us, event | category | flops | bytes accessed | tf_op | source)
XLA Modules:
  0.0 175.8 jit_solution(11911717144391699120)
XLA Ops:
  7.2 0.6 copy-done.26
  8.3 0.6 copy-done.27
  9.4 0.6 copy-done.16
  10.1 0.7 fusion.45
  11.0 0.7 pad_maximum_fusion
  11.7 5.5 %collective-permute-start = (bf16[2,128,2,128]{3,1,2,0:T(8,128)(2,1)}, bf16[2,128,2,128]{3,1,2,0:T(8,128)(2,1)}, u32[]{:S(2)}, u32[]{:S(2)}) collective-permute-start(bf16[2,128,2,128]{3,1,2,0:T(8,128)(2,1)} %pad_maximum_fusion), channel_id=1, source_target_pairs={{0,8},{8,16},{16,24},{1,9},{9,17},{17,25},{2,10},{10,18},{18,26},{... | collective-permute-start | bytes 393224 | tf_op jit(solution)/shard_map/ppermute | solution.py:24
  17.3 1.3 copy.216
  18.6 5.4 %all-to-all-start = ((bf16[1,128,16,256]{1,3,0,2:T(8,128)(2,1)}), bf16[1,128,16,256]{1,3,0,2:T(8,128)(2,1)S(1)}, u32[]{:S(2)}, u32[]{:S(2)}) async-start(bf16[1,128,16,256]{1,3,0,2:T(8,128)(2,1)} %bitcast.56), calls=%async_computation | async-start | bytes 2097152 | tf_op jit(solution)/shard_map/all_to_all | solution.py:189
  24.1 0.6 broadcast_compare_fusion
  24.7 0.7 copy.187
  25.6 1.3 fusion.22
  26.9 2.4 %copy.185 = f32[128,2,8,64]{0,3,2,1:T(8,128)} copy(f32[128,2,8,64]{3,2,1,0:T(8,128)} %get-tuple-element.46) | data formatting | bytes 1048576 | tf_op jit(solution)/shard_map/concatenate | solution.py:50
  29.3 1.2 copy.186
  31.0 1.1 fusion.40
  32.1 0.6 copy-done.24
  32.9 1.2 fusion.24
  34.4 0.7 copy-done.5
  35.1 1.2 copy.211
  36.4 1.1 fusion.52
  37.9 1.0 copy-done.18
  38.9 1.0 fusion.18
  39.9 1.0 convolution_bitcast_fusion.5
  41.4 1.2 fusion.3
  42.6 0.8 multiply_reduce_fusion
  43.5 1.6 fusion.12
  45.1 1.2 fusion.11
  46.6 0.5 copy-done.7
  47.3 1.4 collective-permute-start.1
  49.0 5.3 %collective-permute-done.1 = bf16[2,128,2,128]{3,1,2,0:T(8,128)(2,1)S(1)} collective-permute-done((bf16[2,128,2,128]{3,1,2,0:T(8,128)(2,1)S(1)}, bf16[2,128,2,128]{3,1,2,0:T(8,128)(2,1)S(1)}, u32[]{:S(2)}, u32[]{:S(2)}) %collective-permute-start.1) | collective-permute-done | bytes 131104 | tf_op jit(solution)/shard_map/ppermute | solution.py:24
  54.4 0.5 copy-done.12
  54.9 0.7 copy.215
  55.9 1.3 copy.213
  57.3 2.6 %copy.219 = f32[1024,256]{0,1:T(8,128)} copy(f32[1024,256]{1,0:T(8,128)} %param.21) | data formatting | bytes 2097152 | tf_op args[10]
  59.9 1.3 copy.221
  61.6 0.5 copy.218
  62.1 50.1 %all-gather.3.cloned.1.call-done = bf16[16,128,256]{2,1,0:T(8,128)(2,1)} async-done(((bf16[1,128,256]{2,1,0:T(8,128)(2,1)}), bf16[16,128,256]{2,1,0:T(8,128)(2,1)}) %all-gather.3.cloned.1.call-update) | async-done | bytes 1048592 | tf_op jit(solution)/shard_map/all_gather | solution.py:192
  112.2 3.1 %multiply_reduce_fusion.1 = (f32[]{:T(128)}, f32[256,256]{0,1:T(8,128)}) fusion(bf16[2048,256]{1,0:T(8,128)(2,1)} %bitcast.176, bf16[2048,256]{1,0:T(8,128)(2,1)S(1)} %bitcast.174), kind=kOutput, calls=%fused_computation.58 | convolution fusion | flops 268566528 | bytes 2359300 | tf_op jit(solution)/shard_map/dot_general | solution.py:193
  115.3 1.2 fusion.6
  116.5 0.5 copy.204
  117.1 0.5 copy.203
  118.1 1.2 fusion.25
  119.2 0.7 copy.223
  120.2 0.7 copy.222
  120.9 38.5 %psum.7 = f32[]{:T(128)} all-reduce(f32[]{:T(128)} %get-tuple-element.64), channel_id=1, replica_groups=mesh['ctx'=4,'dp'=4,'tp'=2] {'ctx','dp','tp'}, use_global_device_ids=true, to_apply=%region_9.10 | all-reduce | flops 1 | bytes 8 | tf_op jit(solution)/shard_map/psum | solution.py:200
  160.0 3.7 %multiply_subtract_fusion = (f32[1024,256]{0,1:T(8,128)}, f32[1024,256]{0,1:T(8,128)}, f32[1024,256]{0,1:T(8,128)S(1)}) fusion(f32[1024,256]{0,1:T(8,128)} %copy.221, f32[1024,256]{0,1:T(8,128)} %all-gather.5.cloned.1.call-done, f32[]{:T(128)S(6)} %min_shard_map.3, f32[1024,256]{0,1:T(8,128)S(1)} %copy-done.2, f32[1024,256]{0,1:T(8,128)S(1)} %copy-done.3), kind=kLoop, calls=%fused_computation.48 | loop fusion | flops 4194304 | bytes 7340036 | tf_op jit(solution)/shard_map/sub | solution.py:67
  163.7 2.6 %copy.224 = f32[1024,256]{1,0:T(8,128)} copy(f32[1024,256]{0,1:T(8,128)} %get-tuple-element.41) | data formatting | bytes 2097152
  166.3 1.3 copy.225
  167.6 1.3 copy.226
  (92 shorter events, 5.5 us)
Async XLA Ops:
  7.2 0.7 copy-start.26
  8.2 0.7 copy-start.27
  8.2 0.7 copy-start.28
  9.2 0.8 copy-start.16
  9.3 7.9 %copy-start.9 = (bf16[1,128,4096]{2,1,0:T(8,128)(2,1)S(1)}, bf16[1,128,4096]{2,1,0:T(8,128)(2,1)}, u32[]{:S(2)}) copy-start(bf16[1,128,4096]{2,1,0:T(8,128)(2,1)} %param.15) | copy-start | bytes 3145732
  10.1 0.8 copy-start.21
  11.7 24.6 %collective-permute-start = (bf16[2,128,2,128]{3,1,2,0:T(8,128)(2,1)}, bf16[2,128,2,128]{3,1,2,0:T(8,128)(2,1)}, u32[]{:S(2)}, u32[]{:S(2)}) collective-permute-start(bf16[2,128,2,128]{3,1,2,0:T(8,128)(2,1)} %pad_maximum_fusion), channel_id=1, source_target_pairs={{0,8},{8,16},{16,24},{1,9},{9,17},{17,25},{2,10},{10,18},{18,26},{... | collective-permute-start | bytes 393224 | tf_op jit(solution)/shard_map/ppermute | solution.py:24
  18.6 6.9 %copy-start.17 = (bf16[1,128,16,128]{3,2,1,0:T(8,128)(2,1)S(1)}, bf16[1,128,16,128]{3,2,1,0:T(8,128)(2,1)}, u32[]{:S(2)}) copy-start(bf16[1,128,16,128]{3,2,1,0:T(8,128)(2,1)} %param.11) | copy-start | bytes 1572868
  18.6 43.0 %all-to-all-start = ((bf16[1,128,16,256]{1,3,0,2:T(8,128)(2,1)}), bf16[1,128,16,256]{1,3,0,2:T(8,128)(2,1)S(1)}, u32[]{:S(2)}, u32[]{:S(2)}) async-start(bf16[1,128,16,256]{1,3,0,2:T(8,128)(2,1)} %bitcast.56), calls=%async_computation | async-start | bytes 2097152 | tf_op jit(solution)/shard_map/all_to_all | solution.py:189
  24.0 88.2 %all-gather.3.cloned.1.call-start = ((), (), s32[]{:S(2)}) async-start(), calls=%async_computation.1 | async-start | bytes 1114112 | tf_op jit(solution)/shard_map/all_gather | solution.py:192
  30.9 1.9 %copy-start.6 = (f32[128,2,8,64]{0,3,2,1:T(8,128)S(1)}, f32[128,2,8,64]{0,3,2,1:T(8,128)}, u32[]{:S(2)}) copy-start(f32[128,2,8,64]{0,3,2,1:T(8,128)} %copy.185) | copy-start | bytes 1572868
  32.0 2.0 %copy-start.14 = (bf16[128,2,128,1]{2,0,3,1:T(8,128)(2,1)}, bf16[128,2,128,1]{2,0,3,1:T(8,128)(2,1)S(1)}, u32[]{:S(2)}) copy-start(bf16[128,2,128,1]{2,0,3,1:T(8,128)(2,1)S(1)} %fusion.40) | copy-start | bytes 196612
  32.0 0.6 copy-start.24
  32.1 0.6 copy-start.25
  34.1 1.0 copy-start.5
  37.5 3.9 %copy-start = (f32[2,8,128,128]{2,3,1,0:T(8,128)}, f32[2,8,128,128]{2,3,1,0:T(8,128)S(1)}, u32[]{:S(2)}) copy-start(f32[2,8,128,128]{2,3,1,0:T(8,128)S(1)} %get-tuple-element.63) | copy-start | bytes 3145732
  37.5 1.4 copy-start.18
  39.9 1.0 copy-start.22
  43.5 1.6 copy-start.1
  43.5 1.6 copy-start.19
  46.3 0.8 copy-start.7
  46.3 0.9 copy-start.23
  47.2 7.0 %copy-start.20 = (f32[1,128,2,128]{3,1,2,0:T(8,128)S(1)}, f32[1,128,2,128]{3,1,2,0:T(8,128)}, u32[]{:S(2)}) copy-start(f32[1,128,2,128]{3,1,2,0:T(8,128)} %convolution_bitcast_fusion.5) | copy-start | bytes 393220
  47.2 8.7 %copy-start.10 = (f32[1024,256]{1,0:T(8,128)S(1)}, f32[1024,256]{1,0:T(8,128)}, u32[]{:S(2)}) copy-start(f32[1024,256]{1,0:T(8,128)} %param.20) | copy-start | bytes 3145732
  47.3 7.0 %collective-permute-start.1 = (bf16[2,128,2,128]{3,1,2,0:T(8,128)(2,1)S(1)}, bf16[2,128,2,128]{3,1,2,0:T(8,128)(2,1)S(1)}, u32[]{:S(2)}, u32[]{:S(2)}) collective-permute-start(bf16[2,128,2,128]{3,1,2,0:T(8,128)(2,1)S(1)} %pad_maximum_fusion.1), channel_id=1, source_target_pairs={{8,0},{16,8},{24,16},{9,1},{17,9},{25,17},{10,2},{18,10},{26,18},{... | collective-permute-start | bytes 393224 | tf_op jit(solution)/shard_map/ppermute | solution.py:24
  54.3 0.6 copy-start.12
  55.7 104.3 %all-gather.5.cloned.1.call-start = ((), (), s32[]{:S(2)}) async-start(), calls=%async_computation.2 | async-start | bytes 1310720 | tf_op jit(solution)/shard_map/all_gather | solution.py:201
  57.3 2.6 %copy-start.11 = (f32[1024,256]{1,0:T(8,128)S(1)}, f32[1024,256]{1,0:T(8,128)}, u32[]{:S(2)}) copy-start(f32[1024,256]{1,0:T(8,128)} %param.19) | copy-start | bytes 3145732
  59.9 1.3 copy-start.15
  112.2 3.1 %copy-start.8 = (bf16[2,8,128,128]{2,3,1,0:T(8,128)(2,1)S(1)}, bf16[2,8,128,128]{2,3,1,0:T(8,128)(2,1)}, u32[]{:S(2)}) copy-start(bf16[2,8,128,128]{2,3,1,0:T(8,128)(2,1)} %copy-done.7) | copy-start | bytes 1572868
  118.0 1.2 copy-start.13
  118.1 42.0 %copy-start.3 = (f32[1024,256]{0,1:T(8,128)S(1)}, f32[1024,256]{0,1:T(8,128)}, u32[]{:S(2)}) copy-start(f32[1024,256]{0,1:T(8,128)} %copy.219) | copy-start | bytes 3145732
  119.2 40.8 %copy-start.2 = (f32[1024,256]{0,1:T(8,128)S(1)}, f32[1024,256]{0,1:T(8,128)}, u32[]{:S(2)}) copy-start(f32[1024,256]{0,1:T(8,128)} %copy.213) | copy-start | bytes 3145732
  163.7 2.6 %copy-start.4 = (f32[1024,256]{0,1:T(8,128)S(1)}, f32[1024,256]{0,1:T(8,128)}, u32[]{:S(2)}) copy-start(f32[1024,256]{0,1:T(8,128)} %get-tuple-element.42) | copy-start | bytes 3145732
Sparse Core Ops, SparseCore 0:
  55.8 56.3 all-gather.2
  115.5 25.6 all-gather.4

commit v2 on v1

--- a/solution.py
+++ b/solution.py
@@ -22,6 +22,21 @@
     peers = lax.axis_size(axis)
     pairs = [(i, i + by) for i in range(peers) if 0 <= i + by < peers]
     return lax.ppermute(array, axis, pairs)
+
+
+def spread_copy(array, axes):
+    peers = lax.axis_size(axes)
+    if peers * array.size * array.dtype.itemsize > (4 << 20):
+        return lax.all_gather(array, axes, axis=0, tiled=False)
+    stacked = jnp.broadcast_to(array[None], (peers,) + array.shape)
+    return lax.all_to_all(stacked, axes, 0, 0, tiled=False)
+
+
+def spread_sum(value, axes):
+    peers = lax.axis_size(axes)
+    if peers > 64:
+        return lax.psum(value, axes)
+    return jnp.sum(spread_copy(jnp.full((8, 128), value), axes)[:, 0, 0])
 
 
 def doc_layout(lengths_row, token_index):
@@ -189,7 +204,7 @@
     feat_cols = lax.all_to_all(
         feats.reshape(tok_rows, n_dp * n_ctx, piece_rows), spread, 1, 0, tiled=False
     )
-    value_rows = lax.all_gather(value_flat, spread, axis=0, tiled=False)
+    value_rows = spread_copy(value_flat, spread)
     pieces = lax.dot_general(
         feat_cols.reshape(-1, piece_rows),
         value_rows.reshape(-1, kv_count * head_dim),
@@ -197,8 +212,9 @@
         preferred_element_type=jnp.float32,
     )
     norm_part = jnp.sum(pieces * pieces)
-    grad_total = lax.psum(norm_part, ("ctx", "dp", "tp"))
-    weight_gradient = lax.all_gather(pieces, "ctx", axis=0, tiled=True)
+    everyone = ("ctx", "dp", "tp")
+    grad_total = spread_sum(norm_part, everyone)
+    weight_gradient = spread_copy(pieces, "ctx").reshape(own_rows, pieces.shape[1])
     new_param, new_first, new_second = adam_update(
         param, first_moment_state, second_moment_state, weight_gradient, grad_total
     )

time: 177 us -> 119 us (0.67)
  blocking collectives: 38.5 us -> 0 us
  waiting for transfers between devices: 55.5 us -> 35.1 us
  starting transfers between devices: 12.6 us -> 27.6 us
  between operations: 15.2 us -> 1.89 us
  other arithmetic: 13.5 us -> 19.4 us
  local copies, waits for them, and re-layouts: 27.5 us -> 23.6 us
  matrix products: 13.1 us -> 9.94 us
    all_gather x2 -> x0, waiting for transfers between devices: 50.2 us -> none  [the longest x1 50.1 us: local(): value_rows = lax.all_gather(value_flat, spread, axis=0, tiled=False)]
    psum x1 -> x0, blocking collectives: 38.5 us -> none  [local(): grad_total = lax.psum(norm_part, ('ctx', 'dp', 'tp'))]
    all_to_all x0 -> x3, waiting for transfers between devices: none -> 30.5 us  [spread_copy(): return lax.all_to_all(stacked, axes, 0, 0, tiled=False)]
    all_to_all x0 -> x3, starting transfers between devices: none -> 15.3 us  [spread_copy(): return lax.all_to_all(stacked, axes, 0, 0, tiled=False)]
    unnamed x68 -> x54, local copies, waits for them, and re-layouts: 18.8 us -> 8.17 us
    broadcast_in_dim x0 -> x2, local copies, waits for them, and re-layouts: none -> 2.22 us  [spread_copy(): stacked = jnp.broadcast_to(array[None], (peers,) + array.shape)]
    another operation x1 -> x2, local copies, waits for them, and re-layouts: 0.09 us -> 2.07 us  [the longest x1 1.3 us: spread_copy(): stacked = jnp.broadcast_to(array[None], (peers,) + array.shape)]
  transfers between devices with their start and end apart: 5 -> 6, of which waited for: 2 -> 4; matrix products, arithmetic and copies ran while one was open for 19% -> 30% of each run, Pallas kernels for 0% -> 0%
where the time goes in v2:
time: 119 us; the launch traced here: 117 us
  waiting for transfers between devices  35.1 us (29%)
  starting transfers between devices  27.6 us (23%)
  local copies, waits for them, and re-layouts  23.6 us (20%)
  other arithmetic  19.4 us (16%)
  matrix products  9.94 us (8%)
  between operations  1.89 us (2%)
    all_to_all x3, waiting for transfers between devices, spread_copy(): return lax.all_to_all(stacked, axes, 0, 0, tiled=False)  30.5 us
    all_to_all x3, starting transfers between devices, spread_copy(): return lax.all_to_all(stacked, axes, 0, 0, tiled=False)  15.3 us
    unnamed x54, local copies, waits for them, and re-layouts  8.17 us
    ppermute x2, starting transfers between devices, shifted(): return lax.ppermute(array, axis, pairs)  6.81 us
    all_to_all x1, starting transfers between devices, local(): lax.all_to_all(feats.reshape(tok_rows, n_dp * n_ctx, piece_rows), spread,...  5.44 us
    ppermute x2, waiting for transfers between devices, shifted(): return lax.ppermute(array, axis, pairs)  4.52 us
    concatenate x2, local copies, waits for them, and re-layouts, rotate(): jnp.concatenate([-vectors[..., half:], vectors[..., :half]], axis=-1)  3.71 us
    sub x1, other arithmetic, adam_update(): new_param = param - LEARN_RATE * (step_size + DECAY_RATE * param)  3.47 us
  transfers between devices with their start and end apart: 6, of which 4 were waited for; matrix products, arithmetic and copies ran while one was open for 30% of the time, Pallas kernels for 0%

profile of v2, /device:TPU:0, one launch (start us, length us, event | category | flops | bytes accessed | tf_op | source)
XLA Modules:
  0.0 117.4 jit_solution(463668763667912196)
XLA Ops:
  0.6 0.8 copy.199
  1.8 0.6 copy-done.23
  3.3 0.7 fusion.46
  4.1 0.7 pad_maximum_fusion
  4.8 5.5 %collective-permute-start = (bf16[2,128,2,128]{3,1,2,0:T(8,128)(2,1)}, bf16[2,128,2,128]{3,1,2,0:T(8,128)(2,1)}, u32[]{:S(2)}, u32[]{:S(2)}) collective-permute-start(bf16[2,128,2,128]{3,1,2,0:T(8,128)(2,1)} %pad_maximum_fusion), channel_id=1, source_target_pairs={{0,8},{8,16},{16,24},{1,9},{9,17},{17,25},{2,10},{10,18},{18,26},{... | collective-permute-start | bytes 393224 | tf_op jit(solution)/shard_map/ppermute | solution.py:24
  10.3 1.3 %copy.232 = bf16[1,128,4096]{1,2,0:T(8,128)(2,1)} copy(bf16[1,128,4096]{2,1,0:T(8,128)(2,1)S(1)} %copy-done.11) | data formatting | bytes 2097152 | tf_op args[4]
  11.6 5.4 %all-to-all-start.1 = ((bf16[1,128,16,256]{1,3,0,2:T(8,128)(2,1)}), bf16[1,128,16,256]{1,3,0,2:T(8,128)(2,1)S(1)}, u32[]{:S(2)}, u32[]{:S(2)}) async-start(bf16[1,128,16,256]{1,3,0,2:T(8,128)(2,1)} %bitcast.56), calls=%async_computation.1 | async-start | bytes 2097152 | tf_op jit(solution)/shard_map/all_to_all | solution.py:204
  17.0 0.6 broadcast_compare_fusion
  17.7 0.7 copy.200
  18.5 1.1 convert_bitcast_fusion.1
  19.6 1.6 %copy.201 = f32[128,2,8,128]{0,3,2,1:T(8,128)S(1)} copy(f32[128,2,8,128]{3,2,1,0:T(8,128)} %get-tuple-element.54) | data formatting | bytes 2097152 | tf_op jit(solution)/shard_map/convert_element_type | solution.py:114
  21.2 1.7 %fusion.22 = (f32[128,2,8,64]{3,2,1,0:T(8,128)}, f32[128,2,8,64]{3,2,1,0:T(8,128)}) fusion(f32[128,16,128]{2,1,0:T(8,128)S(1)} %get-tuple-element.55), kind=kLoop, calls=%fused_computation.41 | loop fusion | flops 131072 | bytes 2097152 | tf_op jit(solution)/shard_map/concatenate | solution.py:65
  22.8 2.5 %copy.202 = f32[128,2,8,64]{0,3,2,1:T(8,128)} copy(f32[128,2,8,64]{3,2,1,0:T(8,128)} %get-tuple-element.52) | data formatting | bytes 1048576 | tf_op jit(solution)/shard_map/concatenate | solution.py:65
  25.3 1.2 %copy.203 = f32[128,2,8,64]{0,3,2,1:T(8,128)} copy(f32[128,2,8,64]{3,2,1,0:T(8,128)S(1)} %copy-done.3) | data formatting | bytes 1048576 | tf_op jit(solution)/shard_map/concatenate | solution.py:65
  26.5 1.1 fusion.41
  27.7 0.7 copy-done.21
  28.5 1.2 %fusion.24 = bf16[128,2,8,128]{0,3,2,1:T(8,128)(2,1)S(1)} fusion(f32[128,2,8,64]{0,3,2,1:T(8,128)} %copy.203, f32[128,2,8,64]{0,3,2,1:T(8,128)S(1)} %copy-done.5, f32[128,2,8,128]{0,3,2,1:T(8,128)S(1)} %copy.201, f32[128,128]{0,1:T(8,128)S(1)} %copy.204, f32[128,128]{0,1:T(8,128)} %copy.200), kind=kLoop, calls=%fused_computation.44 | loop fusion | flops 1310720 | bytes 2752512 | tf_op jit(solution)/shard_map/convert_element_type | solution.py:114
  30.1 0.7 copy-done.4
  30.8 1.2 %copy.228 = bf16[128,2,8,128]{0,3,2,1:T(8,128)(2,1)} copy(bf16[128,2,8,128]{3,2,1,0:T(8,128)(2,1)S(1)} %bitcast.183) | data formatting | bytes 1048576 | tf_op jit(solution)/shard_map/reshape;squeeze | solution.py:117
  32.0 1.1 fusion.54
  33.6 0.5 copy-done.20
  34.6 1.2 %fusion.3 = f32[2,8,128,128]{3,2,1,0:T(8,128)S(1)} fusion(f32[128,2,8,128]{3,0,2,1:T(8,128)S(1)} %convolution_bitcast_fusion.2, bf16[2,128,2,128]{3,1,2,0:T(8,128)(2,1)} %collective-permute-done, f32[2,8,128,128]{2,3,1,0:T(8,128)S(1)} %get-tuple-element.69, f32[2,8,128]{2,1,0:T(8,128)S(1)} %add.106, f32[2,8,128]{2,1,0:T(8,128)S(1)} %max.8, ...), kind=kOutput, calls=%fused_computation.8 | convolution fusion | flops 68419584 | bytes 3244032 | tf_op jit(solution)/shard_map/hgqk,khd->qhgd/dot_general | solution.py:157
  35.8 0.8 multiply_reduce_fusion
  36.7 1.9 %fusion.11 = bf16[2,8,128,128]{2,3,1,0:T(8,128)(2,1)S(1)} fusion(bf16[128,2,8,128]{0,3,2,1:T(8,128)(2,1)} %copy.228, f32[2,8,128]{2,1,0:T(8,128)S(1)} %copy.255, bf16[2,128,2,128]{3,1,2,0:T(8,128)(2,1)} %collective-permute-done, f32[2,8,128]{2,1,0:T(8,128)S(1)} %add.106, f32[2,8,128,128]{2,3,1,0:T(8,128)} %copy-done.1, f32[2,8,128]{2,1,0:T(8,128)S(1)} %max.8, ...), kind=kOutput, calls=%fused_computation.21 | convolution fusion | flops 68681728 | bytes 2203648 | tf_op jit(solution)/shard_map/qhgd,khd->hgqk/dot_general | solution.py:165
  39.3 0.6 copy-done.2
  40.3 1.3 %collective-permute-start.1 = (bf16[2,128,2,128]{3,1,2,0:T(8,128)(2,1)S(1)}, bf16[2,128,2,128]{3,1,2,0:T(8,128)(2,1)S(1)}, u32[]{:S(2)}, u32[]{:S(2)}) collective-permute-start(bf16[2,128,2,128]{3,1,2,0:T(8,128)(2,1)S(1)} %pad_maximum_fusion.1), channel_id=1, source_target_pairs={{8,0},{16,8},{24,16},{9,1},{17,9},{25,17},{10,2},{18,10},{26,18},{... | collective-permute-start | bytes 393224 | tf_op jit(solution)/shard_map/ppermute | solution.py:24
  42.7 4.5 %collective-permute-done.1 = bf16[2,128,2,128]{3,1,2,0:T(8,128)(2,1)S(1)} collective-permute-done((bf16[2,128,2,128]{3,1,2,0:T(8,128)(2,1)S(1)}, bf16[2,128,2,128]{3,1,2,0:T(8,128)(2,1)S(1)}, u32[]{:S(2)}, u32[]{:S(2)}) %collective-permute-start.1) | collective-permute-done | bytes 131104 | tf_op jit(solution)/shard_map/ppermute | solution.py:24
  48.0 1.2 broadcast_in_dim.37
  49.4 6.9 %all-to-all-start = ((bf16[16,128,256]{2,1,0:T(8,128)(2,1)}), bf16[16,128,256]{2,1,0:T(8,128)(2,1)S(1)}, u32[]{:S(2)}, u32[]{:S(2)}) async-start(bf16[16,128,256]{2,1,0:T(8,128)(2,1)} %broadcast_in_dim.37), calls=%async_computation | async-start | bytes 2097152 | tf_op jit(solution)/shard_map/all_to_all | solution.py:32
  56.6 0.7 copy-done.7
  57.3 1.2 %fusion.6 = f32[2,128,8,128]{3,1,2,0:T(8,128)S(1)} fusion(f32[2,128,8,128]{3,1,2,0:T(8,128)S(1)} %fusion.55, bf16[2,8,128,128]{2,3,1,0:T(8,128)(2,1)S(1)} %copy-done.7, bf16[2,128,2,128]{3,1,2,0:T(8,128)(2,1)} %collective-permute-done), kind=kOutput, calls=%fused_computation.12 | convolution fusion | flops 67633152 | bytes 2686976 | tf_op jit(solution)/shard_map/hgqk,khd->qhgd/dot_general | solution.py:170
  58.5 1.4 %copy.221 = f32[128,16,128]{2,1,0:T(8,128)} copy(f32[128,16,128]{0,2,1:T(8,128)S(1)} %bitcast.179) | data formatting | bytes 2097152 | tf_op jit(solution)/shard_map/reshape | solution.py:192
  60.4 1.3 %broadcast_multiply_fusion.1 = f32[128,16,128]{2,1,0:T(8,128)S(1)} fusion(f32[128,16,128]{2,1,0:T(8,128)} %copy.221, f32[128,128]{1,0:T(8,128)S(1)} %pad_maximum_fusion.3), kind=kLoop, calls=%fused_computation.58 | loop fusion | flops 262144 | bytes 2162688 | tf_op jit(solution)/shard_map/mul | solution.py:71
  61.7 1.7 %slice_bitcast_fusion = (f32[1,128,16,64]{3,2,1,0:T(8,128)}, f32[1,128,16,64]{3,2,1,0:T(8,128)}) fusion(f32[128,16,128]{2,1,0:T(8,128)S(1)} %broadcast_multiply_fusion.1), kind=kLoop, calls=%fused_computation.38 | loop fusion | flops 131072 | bytes 2097152 | tf_op jit(solution)/shard_map/concatenate | solution.py:72
  63.4 1.5 %copy.234 = bf16[1,128,16,256]{3,1,2,0:T(8,128)(2,1)S(1)} copy(bf16[1,128,16,256]{1,3,0,2:T(8,128)(2,1)} %copy-done) | data formatting | bytes 2097152 | tf_op jit(solution)/shard_map/all_to_all | solution.py:204
  64.9 13.9 %all-to-all-done = bf16[16,128,256]{2,1,0:T(8,128)(2,1)S(1)} async-done(((bf16[16,128,256]{2,1,0:T(8,128)(2,1)}), bf16[16,128,256]{2,1,0:T(8,128)(2,1)S(1)}, u32[]{:S(2)}, u32[]{:S(2)}) %all-to-all-start) | async-done | bytes 1048608 | tf_op jit(solution)/shard_map/all_to_all | solution.py:32
  78.8 1.8 %multiply_reduce_fusion.1 = (f32[]{:T(128)}, f32[256,256]{0,1:T(8,128)}) fusion(bf16[2048,256]{1,0:T(8,128)(2,1)S(1)} %bitcast.181, bf16[2048,256]{1,0:T(8,128)(2,1)S(1)} %bitcast.182), kind=kOutput, calls=%fused_computation.60 | convolution fusion | flops 268566528 | bytes 2359300 | tf_op jit(solution)/shard_map/dot_general | solution.py:208
  80.6 1.3 %broadcast_in_dim_broadcast_in_dim_broadcast_in_dim.3 = f32[32,8,128]{2,1,0:T(8,128)} broadcast(f32[]{:T(128)} %get-tuple-element.70), dimensions={} | broadcast | bytes 131076 | tf_op jit(solution)/shard_map/broadcast_in_dim;broadcast_in_dim;broadcast_in_dim | solution.py:31
  81.9 4.9 %all-to-all-start.3 = ((f32[32,8,128]{2,1,0:T(8,128)}), f32[32,8,128]{2,1,0:T(8,128)S(1)}, u32[]{:S(2)}, u32[]{:S(2)}) async-start(f32[32,8,128]{2,1,0:T(8,128)} %broadcast_in_dim_broadcast_in_dim_broadcast_in_dim.3), calls=%async_computation.3 | async-start | bytes 262144 | tf_op jit(solution)/shard_map/all_to_all | solution.py:32
  86.8 2.7 %fusion.25 = bf16[1,128,16,128]{3,2,1,0:T(8,128)(2,1)} fusion(f32[1,128,16,64]{3,2,1,0:T(8,128)} %get-tuple-element.51, f32[1,128,16,64]{3,2,1,0:T(8,128)} %get-tuple-element.50, f32[1,128,16,128]{3,2,1,0:T(8,128)S(1)} %copy.220, f32[128,128]{1,0:T(8,128)S(1)} %pad_maximum_fusion.2), kind=kLoop, calls=%fused_computation.46 | loop fusion | flops 1048576 | bytes 2686976 | tf_op jit(solution)/shard_map/convert_element_type | solution.py:192
  89.5 0.7 copy.238
  90.4 4.6 %all-to-all-done.3 = f32[32,8,128]{2,1,0:T(8,128)S(1)} async-done(((f32[32,8,128]{2,1,0:T(8,128)}), f32[32,8,128]{2,1,0:T(8,128)S(1)}, u32[]{:S(2)}, u32[]{:S(2)}) %all-to-all-start.3) | async-done | bytes 131104 | tf_op jit(solution)/shard_map/all_to_all | solution.py:32
  94.9 1.1 broadcast_in_dim.38
  96.0 3.5 %all-to-all-start.2 = ((f32[4,256,256]{2,1,0:T(8,128)}), f32[4,256,256]{2,1,0:T(8,128)S(1)}, u32[]{:S(2)}, u32[]{:S(2)}) async-start(f32[4,256,256]{2,1,0:T(8,128)} %broadcast_in_dim.38), calls=%async_computation.2 | async-start | bytes 2097152 | tf_op jit(solution)/shard_map/all_to_all | solution.py:32
  99.8 0.7 copy.237
  100.4 0.6 slice_reduce_fusion
  101.8 12.1 %all-to-all-done.2 = f32[4,256,256]{2,1,0:T(8,128)S(1)} async-done(((f32[4,256,256]{2,1,0:T(8,128)}), f32[4,256,256]{2,1,0:T(8,128)S(1)}, u32[]{:S(2)}, u32[]{:S(2)}) %all-to-all-start.2) | async-done | bytes 1048608 | tf_op jit(solution)/shard_map/all_to_all | solution.py:32
  114.0 3.5 %multiply_subtract_fusion = (f32[1024,256]{1,0:T(8,128)}, f32[1024,256]{1,0:T(8,128)}, f32[1024,256]{1,0:T(8,128)}) fusion(f32[1024,256]{1,0:T(8,128)S(1)} %copy-done.8, f32[4,256,256]{2,1,0:T(8,128)S(1)} %broadcast_multiply_fusion, f32[1024,256]{1,0:T(8,128)S(1)} %copy-done.9, f32[1024,256]{1,0:T(8,128)} %param.21), kind=kLoop, calls=%fused_computation.50 | loop fusion | flops 3932160 | bytes 7340032 | tf_op jit(solution)/shard_map/sub | solution.py:82
  (83 shorter events, 7.2 us)
Async XLA Ops:
  0.6 1.1 copy-start.19
  1.7 0.7 copy-start.23
  1.7 0.7 copy-start.24
  2.4 0.8 copy-start.16
  2.7 7.5 %copy-start.11 = (bf16[1,128,4096]{2,1,0:T(8,128)(2,1)S(1)}, bf16[1,128,4096]{2,1,0:T(8,128)(2,1)}, u32[]{:S(2)}) copy-start(bf16[1,128,4096]{2,1,0:T(8,128)(2,1)} %param.15) | copy-start | bytes 3145732
  4.8 27.3 %collective-permute-start = (bf16[2,128,2,128]{3,1,2,0:T(8,128)(2,1)}, bf16[2,128,2,128]{3,1,2,0:T(8,128)(2,1)}, u32[]{:S(2)}, u32[]{:S(2)}) collective-permute-start(bf16[2,128,2,128]{3,1,2,0:T(8,128)(2,1)} %pad_maximum_fusion), channel_id=1, source_target_pairs={{0,8},{8,16},{16,24},{1,9},{9,17},{17,25},{2,10},{10,18},{18,26},{... | collective-permute-start | bytes 393224 | tf_op jit(solution)/shard_map/ppermute | solution.py:24
  11.6 6.9 %copy-start.17 = (bf16[1,128,16,128]{3,2,1,0:T(8,128)(2,1)S(1)}, bf16[1,128,16,128]{3,2,1,0:T(8,128)(2,1)}, u32[]{:S(2)}) copy-start(bf16[1,128,16,128]{3,2,1,0:T(8,128)(2,1)} %param.11) | copy-start | bytes 1572868
  11.6 36.4 %all-to-all-start.1 = ((bf16[1,128,16,256]{1,3,0,2:T(8,128)(2,1)}), bf16[1,128,16,256]{1,3,0,2:T(8,128)(2,1)S(1)}, u32[]{:S(2)}, u32[]{:S(2)}) async-start(bf16[1,128,16,256]{1,3,0,2:T(8,128)(2,1)} %bitcast.56), calls=%async_computation.1 | async-start | bytes 2097152 | tf_op jit(solution)/shard_map/all_to_all | solution.py:204
  22.8 2.5 %copy-start.3 = (f32[128,2,8,64]{3,2,1,0:T(8,128)S(1)}, f32[128,2,8,64]{3,2,1,0:T(8,128)}, u32[]{:S(2)}) copy-start(f32[128,2,8,64]{3,2,1,0:T(8,128)} %get-tuple-element.53) | copy-start | bytes 1572868
  26.5 2.0 %copy-start.5 = (f32[128,2,8,64]{0,3,2,1:T(8,128)S(1)}, f32[128,2,8,64]{0,3,2,1:T(8,128)}, u32[]{:S(2)}) copy-start(f32[128,2,8,64]{0,3,2,1:T(8,128)} %copy.202) | copy-start | bytes 1572868
  27.6 2.1 %copy-start.14 = (bf16[128,2,128,1]{2,0,3,1:T(8,128)(2,1)}, bf16[128,2,128,1]{2,0,3,1:T(8,128)(2,1)S(1)}, u32[]{:S(2)}) copy-start(bf16[128,2,128,1]{2,0,3,1:T(8,128)(2,1)S(1)} %fusion.41) | copy-start | bytes 196612
  27.6 0.7 copy-start.21
  27.6 0.7 copy-start.22
  29.7 1.0 copy-start.4
  33.2 1.4 %copy-start.1 = (f32[2,8,128,128]{2,3,1,0:T(8,128)}, f32[2,8,128,128]{2,3,1,0:T(8,128)S(1)}, u32[]{:S(2)}) copy-start(f32[2,8,128,128]{2,3,1,0:T(8,128)S(1)} %get-tuple-element.69) | copy-start | bytes 3145732
  33.2 0.9 copy-start.20
  36.7 2.7 %copy-start.18 = (bf16[128,2,8,128]{0,3,2,1:T(8,128)(2,1)S(1)}, bf16[128,2,8,128]{0,3,2,1:T(8,128)(2,1)}, u32[]{:S(2)}) copy-start(bf16[128,2,8,128]{0,3,2,1:T(8,128)(2,1)} %copy.228) | copy-start | bytes 1572868
  38.5 0.8 copy-start.6
  38.5 1.4 %copy-start.2 = (f32[2,8,128,128]{2,3,1,0:T(8,128)S(1)}, f32[2,8,128,128]{2,3,1,0:T(8,128)}, u32[]{:S(2)}) copy-start(f32[2,8,128,128]{2,3,1,0:T(8,128)} %copy-done.1) | copy-start | bytes 3145732
  40.3 6.9 %collective-permute-start.1 = (bf16[2,128,2,128]{3,1,2,0:T(8,128)(2,1)S(1)}, bf16[2,128,2,128]{3,1,2,0:T(8,128)(2,1)S(1)}, u32[]{:S(2)}, u32[]{:S(2)}) collective-permute-start(bf16[2,128,2,128]{3,1,2,0:T(8,128)(2,1)S(1)} %pad_maximum_fusion.1), channel_id=1, source_target_pairs={{8,0},{16,8},{24,16},{9,1},{17,9},{25,17},{10,2},{18,10},{26,18},{... | collective-permute-start | bytes 393224 | tf_op jit(solution)/shard_map/ppermute | solution.py:24
  47.2 0.6 copy-start.12
  48.0 1.4 %copy-start = (bf16[1,128,16,256]{1,3,0,2:T(8,128)(2,1)}, bf16[1,128,16,256]{1,3,0,2:T(8,128)(2,1)S(1)}, u32[]{:S(2)}) copy-start(bf16[1,128,16,256]{1,3,0,2:T(8,128)(2,1)S(1)} %all-to-all-done.1) | copy-start | bytes 3145732
  49.2 7.1 %copy-start.15 = (bf16[128,2,128,1]{2,0,3,1:T(8,128)(2,1)S(1)}, bf16[128,2,128,1]{2,0,3,1:T(8,128)(2,1)}, u32[]{:S(2)}) copy-start(bf16[128,2,128,1]{2,0,3,1:T(8,128)(2,1)} %copy-done.14) | copy-start | bytes 196612
  49.4 29.4 %all-to-all-start = ((bf16[16,128,256]{2,1,0:T(8,128)(2,1)}), bf16[16,128,256]{2,1,0:T(8,128)(2,1)S(1)}, u32[]{:S(2)}, u32[]{:S(2)}) async-start(bf16[16,128,256]{2,1,0:T(8,128)(2,1)} %broadcast_in_dim.37), calls=%async_computation | async-start | bytes 2097152 | tf_op jit(solution)/shard_map/all_to_all | solution.py:32
  56.3 1.0 copy-start.7
  81.9 13.1 %all-to-all-start.3 = ((f32[32,8,128]{2,1,0:T(8,128)}), f32[32,8,128]{2,1,0:T(8,128)S(1)}, u32[]{:S(2)}, u32[]{:S(2)}) async-start(f32[32,8,128]{2,1,0:T(8,128)} %broadcast_in_dim_broadcast_in_dim_broadcast_in_dim.3), calls=%async_computation.3 | async-start | bytes 262144 | tf_op jit(solution)/shard_map/all_to_all | solution.py:32
  86.8 2.8 %copy-start.13 = (bf16[1,128,2,128]{3,1,2,0:T(8,128)(2,1)S(1)}, bf16[1,128,2,128]{3,1,2,0:T(8,128)(2,1)}, u32[]{:S(2)}) copy-start(bf16[1,128,2,128]{3,1,2,0:T(8,128)(2,1)} %copy-done.12) | copy-start | bytes 196612
  86.8 3.4 %copy-start.10 = (f32[256,256]{0,1:T(8,128)S(1)}, f32[256,256]{0,1:T(8,128)}, u32[]{:S(2)}) copy-start(f32[256,256]{0,1:T(8,128)} %get-tuple-element.71) | copy-start | bytes 786436
  96.0 17.9 %all-to-all-start.2 = ((f32[4,256,256]{2,1,0:T(8,128)}), f32[4,256,256]{2,1,0:T(8,128)S(1)}, u32[]{:S(2)}, u32[]{:S(2)}) async-start(f32[4,256,256]{2,1,0:T(8,128)} %broadcast_in_dim.38), calls=%async_computation.2 | async-start | bytes 2097152 | tf_op jit(solution)/shard_map/all_to_all | solution.py:32
  101.8 12.2 %copy-start.8 = (f32[1024,256]{1,0:T(8,128)S(1)}, f32[1024,256]{1,0:T(8,128)}, u32[]{:S(2)}) copy-start(f32[1024,256]{1,0:T(8,128)} %param.19) | copy-start | bytes 3145732
  101.8 12.2 %copy-start.9 = (f32[1024,256]{1,0:T(8,128)S(1)}, f32[1024,256]{1,0:T(8,128)}, u32[]{:S(2)}) copy-start(f32[1024,256]{1,0:T(8,128)} %param.20) | copy-start | bytes 3145732

commit v3 on v2

--- a/solution.py
+++ b/solution.py
@@ -30,6 +30,18 @@
         return lax.all_gather(array, axes, axis=0, tiled=False)
     stacked = jnp.broadcast_to(array[None], (peers,) + array.shape)
     return lax.all_to_all(stacked, axes, 0, 0, tiled=False)
+
+
+def ring_copy(array, axis):
+    peers = lax.axis_size(axis)
+    place = lax.axis_index(axis)
+    rows = array.shape[0]
+    out = jnp.zeros((peers * rows,) + array.shape[1:], array.dtype)
+    out = lax.dynamic_update_slice_in_dim(out, array, place * rows, 0)
+    for step in range(1, peers):
+        moved = lax.ppermute(array, axis, [(i, (i + step) % peers) for i in range(peers)])
+        out = lax.dynamic_update_slice_in_dim(out, moved, ((place - step) % peers) * rows, 0)
+    return out
 
 
 def spread_sum(value, axes):
@@ -211,10 +223,10 @@
         (((0,), (0,)), ((), ())),
         preferred_element_type=jnp.float32,
     )
+    weight_gradient = ring_copy(pieces, "ctx")
     norm_part = jnp.sum(pieces * pieces)
     everyone = ("ctx", "dp", "tp")
     grad_total = spread_sum(norm_part, everyone)
-    weight_gradient = spread_copy(pieces, "ctx").reshape(own_rows, pieces.shape[1])
     new_param, new_first, new_second = adam_update(
         param, first_moment_state, second_moment_state, weight_gradient, grad_total
     )

time: 119 us -> 105 us (0.88)
  waiting for transfers between devices: 35.1 us -> 21.9 us
  starting transfers between devices: 27.6 us -> 29.8 us
  other arithmetic: 19.4 us -> 17.3 us
    all_to_all x3 -> x2, waiting for transfers between devices: 30.5 us -> 16.3 us  [spread_copy(): return lax.all_to_all(stacked, axes, 0, 0, tiled=False)]
    ppermute x0 -> x3, starting transfers between devices: none -> 5.25 us  [ring_copy(): lax.ppermute(array, axis, [(i, (i + step) % peers) for i in range(peers)])]
    all_to_all x3 -> x2, starting transfers between devices: 15.3 us -> 12.3 us  [spread_copy(): return lax.all_to_all(stacked, axes, 0, 0, tiled=False)]
    unnamed x54 -> x60, local copies, waits for them, and re-layouts: 8.17 us -> 9.96 us
    ppermute x0 -> x3, waiting for transfers between devices: none -> 1.62 us  [ring_copy(): lax.ppermute(array, axis, [(i, (i + step) % peers) for i in range(peers)])]
    convert_element_type x1, other arithmetic: 2.72 us -> 1.18 us  [local(): unrotate(query_grad.reshape(tok_rows, head_count, head_dim), cosine, sine)]
  transfers between devices with their start and end apart: 6 -> 8, of which waited for: 4 -> 4; matrix products, arithmetic and copies ran while one was open for 30% -> 33% of each run, Pallas kernels for 0% -> 0%
where the time goes in v3:
time: 105 us; the launch traced here: 104 us
  starting transfers between devices  29.8 us (28%)
  local copies, waits for them, and re-layouts  24 us (23%)
  waiting for transfers between devices  21.9 us (21%)
  other arithmetic  17.3 us (16%)
  matrix products  9.24 us (9%)
  between operations  2.02 us (2%)
    all_to_all x2, waiting for transfers between devices, spread_copy(): return lax.all_to_all(stacked, axes, 0, 0, tiled=False)  16.3 us
    all_to_all x2, starting transfers between devices, spread_copy(): return lax.all_to_all(stacked, axes, 0, 0, tiled=False)  12.3 us
    unnamed x60, local copies, waits for them, and re-layouts  9.96 us
    ppermute x2, starting transfers between devices, shifted(): return lax.ppermute(array, axis, pairs)  6.8 us
    all_to_all x1, starting transfers between devices, local(): lax.all_to_all(feats.reshape(tok_rows, n_dp * n_ctx, piece_rows), spread,...  5.44 us
    ppermute x3, starting transfers between devices, ring_copy(): lax.ppermute(array, axis, [(i, (i + step) % peers) for i in range(peers)])  5.25 us
    ppermute x2, waiting for transfers between devices, shifted(): return lax.ppermute(array, axis, pairs)  4.02 us
    concatenate x2, local copies, waits for them, and re-layouts, rotate(): jnp.concatenate([-vectors[..., half:], vectors[..., :half]], axis=-1)  3.73 us
  transfers between devices with their start and end apart: 8, of which 4 were waited for; matrix products, arithmetic and copies ran while one was open for 33% of the time, Pallas kernels for 0%

profile of v3, /device:TPU:0, one launch (start us, length us, event | category | flops | bytes accessed | tf_op | source)
XLA Modules:
  0.0 104.3 jit_solution(7572633557373400127)
XLA Ops:
  0.7 0.8 copy.214
  1.8 0.6 copy-done.26
  3.3 0.7 fusion.45
  4.1 0.7 pad_maximum_fusion
  4.8 5.5 %collective-permute-start = (bf16[2,128,2,128]{3,1,2,0:T(8,128)(2,1)}, bf16[2,128,2,128]{3,1,2,0:T(8,128)(2,1)}, u32[]{:S(2)}, u32[]{:S(2)}) collective-permute-start(bf16[2,128,2,128]{3,1,2,0:T(8,128)(2,1)} %pad_maximum_fusion), channel_id=1, source_target_pairs={{0,8},{8,16},{16,24},{1,9},{9,17},{17,25},{2,10},{10,18},{18,26},{... | collective-permute-start | bytes 393224 | tf_op jit(solution)/shard_map/ppermute | solution.py:24
  10.3 1.3 %copy.247 = bf16[1,128,4096]{1,2,0:T(8,128)(2,1)} copy(bf16[1,128,4096]{2,1,0:T(8,128)(2,1)S(1)} %copy-done.11) | data formatting | bytes 2097152 | tf_op args[4]
  11.6 5.4 %all-to-all-start.1 = ((bf16[1,128,16,256]{1,3,0,2:T(8,128)(2,1)}), bf16[1,128,16,256]{1,3,0,2:T(8,128)(2,1)S(1)}, u32[]{:S(2)}, u32[]{:S(2)}) async-start(bf16[1,128,16,256]{1,3,0,2:T(8,128)(2,1)} %bitcast.56), calls=%async_computation.1 | async-start | bytes 2097152 | tf_op jit(solution)/shard_map/all_to_all | solution.py:216
  17.7 0.7 copy.215
  18.4 1.1 %convert_bitcast_fusion.1 = (f32[128,2,8,128]{3,2,1,0:T(8,128)}, f32[128,16,128]{2,1,0:T(8,128)S(1)}) fusion(bf16[1,128,16,128]{3,2,1,0:T(8,128)(2,1)S(1)} %copy-done.18), kind=kLoop, calls=%fused_computation.20 | loop fusion | flops 262144 | bytes 2621440 | tf_op jit(solution)/shard_map/convert_element_type | solution.py:126
  19.5 1.6 %copy.216 = f32[128,2,8,128]{0,3,2,1:T(8,128)S(1)} copy(f32[128,2,8,128]{3,2,1,0:T(8,128)} %get-tuple-element.54) | data formatting | bytes 2097152 | tf_op jit(solution)/shard_map/convert_element_type | solution.py:126
  21.1 1.7 %fusion.22 = (f32[128,2,8,64]{3,2,1,0:T(8,128)}, f32[128,2,8,64]{3,2,1,0:T(8,128)}) fusion(f32[128,16,128]{2,1,0:T(8,128)S(1)} %get-tuple-element.55), kind=kLoop, calls=%fused_computation.41 | loop fusion | flops 131072 | bytes 2097152 | tf_op jit(solution)/shard_map/concatenate | solution.py:77
  22.8 2.5 %copy.217 = f32[128,2,8,64]{0,3,2,1:T(8,128)} copy(f32[128,2,8,64]{3,2,1,0:T(8,128)} %get-tuple-element.52) | data formatting | bytes 1048576 | tf_op jit(solution)/shard_map/concatenate | solution.py:77
  25.3 1.2 %copy.218 = f32[128,2,8,64]{0,3,2,1:T(8,128)} copy(f32[128,2,8,64]{3,2,1,0:T(8,128)S(1)} %copy-done.4) | data formatting | bytes 1048576 | tf_op jit(solution)/shard_map/concatenate | solution.py:77
  26.5 1.1 %fusion.40 = bf16[128,2,128,1]{2,0,3,1:T(8,128)(2,1)S(1)} fusion(f32[128,2,64]{2,0,1:T(8,128)} %get-tuple-element.61, f32[128,2,64]{2,0,1:T(8,128)S(1)} %get-tuple-element.60, f32[128,128]{1,0:T(8,128)S(1)} %pad_maximum_fusion.3, f32[128,128]{1,0:T(8,128)S(1)} %pad_maximum_fusion.2, bf16[1,128,2,128]{3,2,1,0:T(2,128)(2,1)S(1)} %copy-done.17), kind=kLoop, calls=%fused_computation.83 | loop fusion | flops 196608 | bytes 393216 | tf_op jit(solution)/shard_map/convert_element_type | solution.py:128
  27.6 0.6 copy-done.24
  28.4 1.2 %fusion.24 = bf16[128,2,8,128]{0,3,2,1:T(8,128)(2,1)S(1)} fusion(f32[128,2,8,64]{0,3,2,1:T(8,128)} %copy.218, f32[128,2,8,64]{0,3,2,1:T(8,128)S(1)} %copy-done.8, f32[128,2,8,128]{0,3,2,1:T(8,128)S(1)} %copy.216, f32[128,128]{0,1:T(8,128)S(1)} %copy.219, f32[128,128]{0,1:T(8,128)} %copy.215), kind=kLoop, calls=%fused_computation.44 | loop fusion | flops 1310720 | bytes 2752512 | tf_op jit(solution)/shard_map/convert_element_type | solution.py:126
  30.0 0.7 copy-done.7
  30.7 1.2 %copy.243 = bf16[128,2,8,128]{0,3,2,1:T(8,128)(2,1)} copy(bf16[128,2,8,128]{3,2,1,0:T(8,128)(2,1)S(1)} %bitcast.176) | data formatting | bytes 1048576 | tf_op jit(solution)/shard_map/reshape;squeeze | solution.py:129
  31.9 1.1 %fusion.52 = (f32[2,8,128]{2,1,0:T(8,128)S(1)}, f32[2,8,128,128]{2,3,1,0:T(8,128)S(1)}) fusion(bf16[128,2,8,128]{0,3,2,1:T(8,128)(2,1)S(1)} %fusion.24, bf16[2,128,2,128]{3,1,2,0:T(8,128)(2,1)} %collective-permute-done, pred[128,128]{0,1:T(8,128)(4,1)S(1)} %get-tuple-element.62), kind=kOutput, calls=%fused_computation.111 | convolution fusion | flops 67893248 | bytes 1662976 | tf_op jit(solution)/shard_map/qhgd,khd->hgqk/dot_general | solution.py:148
  34.5 1.2 %fusion.3 = f32[2,8,128,128]{3,2,1,0:T(8,128)S(1)} fusion(f32[128,2,8,128]{3,0,2,1:T(8,128)S(1)} %convolution_bitcast_fusion.2, bf16[2,128,2,128]{3,1,2,0:T(8,128)(2,1)} %collective-permute-done, f32[2,8,128,128]{2,3,1,0:T(8,128)S(1)} %get-tuple-element.69, f32[2,8,128]{2,1,0:T(8,128)S(1)} %add.130, f32[2,8,128]{2,1,0:T(8,128)S(1)} %max.8, ...), kind=kOutput, calls=%fused_computation.8 | convolution fusion | flops 68419584 | bytes 3244032 | tf_op jit(solution)/shard_map/hgqk,khd->qhgd/dot_general | solution.py:169
  35.7 0.8 multiply_reduce_fusion
  36.5 1.9 %fusion.11 = bf16[2,8,128,128]{2,3,1,0:T(8,128)(2,1)S(1)} fusion(bf16[128,2,8,128]{0,3,2,1:T(8,128)(2,1)} %copy.243, f32[2,8,128]{2,1,0:T(8,128)S(1)} %copy.273, bf16[2,128,2,128]{3,1,2,0:T(8,128)(2,1)} %collective-permute-done, f32[2,8,128]{2,1,0:T(8,128)S(1)} %add.130, f32[2,8,128,128]{2,3,1,0:T(8,128)} %copy-done.2, f32[2,8,128]{2,1,0:T(8,128)S(1)} %max.8, ...), kind=kOutput, calls=%fused_computation.21 | convolution fusion | flops 68681728 | bytes 2203648 | tf_op jit(solution)/shard_map/qhgd,khd->hgqk/dot_general | solution.py:177
  39.2 0.6 copy-done.3
  40.2 1.3 %collective-permute-start.1 = (bf16[2,128,2,128]{3,1,2,0:T(8,128)(2,1)S(1)}, bf16[2,128,2,128]{3,1,2,0:T(8,128)(2,1)S(1)}, u32[]{:S(2)}, u32[]{:S(2)}) collective-permute-start(bf16[2,128,2,128]{3,1,2,0:T(8,128)(2,1)S(1)} %pad_maximum_fusion.1), channel_id=1, source_target_pairs={{8,0},{16,8},{24,16},{9,1},{17,9},{25,17},{10,2},{18,10},{26,18},{... | collective-permute-start | bytes 393224 | tf_op jit(solution)/shard_map/ppermute | solution.py:24
  43.1 4.0 %collective-permute-done.1 = bf16[2,128,2,128]{3,1,2,0:T(8,128)(2,1)S(1)} collective-permute-done((bf16[2,128,2,128]{3,1,2,0:T(8,128)(2,1)S(1)}, bf16[2,128,2,128]{3,1,2,0:T(8,128)(2,1)S(1)}, u32[]{:S(2)}, u32[]{:S(2)}) %collective-permute-start.1) | collective-permute-done | bytes 131104 | tf_op jit(solution)/shard_map/ppermute | solution.py:24
  47.9 1.2 %broadcast_in_dim.38 = bf16[16,128,256]{2,1,0:T(8,128)(2,1)} broadcast(bf16[128,256]{1,0:T(8,128)(2,1)S(1)} %copy.246), dimensions={1,2} | broadcast | bytes 1114112 | tf_op jit(solution)/shard_map/broadcast_in_dim | solution.py:31
  49.2 7.0 %all-to-all-start = ((bf16[16,128,256]{2,1,0:T(8,128)(2,1)}), bf16[16,128,256]{2,1,0:T(8,128)(2,1)S(1)}, u32[]{:S(2)}, u32[]{:S(2)}) async-start(bf16[16,128,256]{2,1,0:T(8,128)(2,1)} %broadcast_in_dim.38), calls=%async_computation | async-start | bytes 2097152 | tf_op jit(solution)/shard_map/all_to_all | solution.py:32
  56.3 0.8 copy-done.16
  57.4 0.7 copy-done.10
  58.1 1.2 %fusion.6 = f32[2,128,8,128]{3,1,2,0:T(8,128)S(1)} fusion(f32[2,128,8,128]{3,1,2,0:T(8,128)S(1)} %fusion.53, bf16[2,8,128,128]{2,3,1,0:T(8,128)(2,1)S(1)} %copy-done.10, bf16[2,128,2,128]{3,1,2,0:T(8,128)(2,1)} %collective-permute-done), kind=kOutput, calls=%fused_computation.12 | convolution fusion | flops 67633152 | bytes 2686976 | tf_op jit(solution)/shard_map/hgqk,khd->qhgd/dot_general | solution.py:182
  59.3 1.4 %copy.236 = f32[128,16,128]{2,1,0:T(8,128)} copy(f32[128,16,128]{0,2,1:T(8,128)S(1)} %bitcast.172) | data formatting | bytes 2097152 | tf_op jit(solution)/shard_map/reshape | solution.py:204
  61.2 1.3 %broadcast_multiply_fusion = f32[128,16,128]{2,1,0:T(8,128)S(1)} fusion(f32[128,16,128]{2,1,0:T(8,128)} %copy.236, f32[128,128]{1,0:T(8,128)S(1)} %pad_maximum_fusion.3), kind=kLoop, calls=%fused_computation.56 | loop fusion | flops 262144 | bytes 2162688 | tf_op jit(solution)/shard_map/mul | solution.py:83
  62.9 1.2 %fusion.25 = bf16[1,128,16,128]{3,2,1,0:T(8,128)(2,1)} fusion(f32[1,128,16,64]{3,2,1,0:T(8,128)S(1)} %get-tuple-element.51, f32[1,128,16,64]{3,2,1,0:T(8,128)S(1)} %get-tuple-element.50, f32[1,128,16,128]{3,2,1,0:T(8,128)S(1)} %copy.235, f32[128,128]{1,0:T(8,128)S(1)} %pad_maximum_fusion.2), kind=kLoop, calls=%fused_computation.46 | loop fusion | flops 1048576 | bytes 2686976 | tf_op jit(solution)/shard_map/convert_element_type | solution.py:204
  64.1 0.8 slice_bitcast_fusion.2
  65.4 13.4 %all-to-all-done = bf16[16,128,256]{2,1,0:T(8,128)(2,1)S(1)} async-done(((bf16[16,128,256]{2,1,0:T(8,128)(2,1)}), bf16[16,128,256]{2,1,0:T(8,128)(2,1)S(1)}, u32[]{:S(2)}, u32[]{:S(2)}) %all-to-all-start) | async-done | bytes 1048608 | tf_op jit(solution)/shard_map/all_to_all | solution.py:32
  78.8 1.1 %multiply_reduce_fusion.1 = (f32[]{:T(128)}, f32[256,256]{0,1:T(8,128)S(1)}) fusion(bf16[2048,256]{1,0:T(8,128)(2,1)S(1)} %bitcast.174, bf16[2048,256]{1,0:T(8,128)(2,1)S(1)} %bitcast.175), kind=kOutput, calls=%fused_computation.58 | convolution fusion | flops 268566528 | bytes 2359300 | tf_op jit(solution)/shard_map/dot_general | solution.py:220
  79.8 2.0 %collective-permute-start.3 = (f32[256,256]{0,1:T(8,128)S(1)}, f32[256,256]{0,1:T(8,128)S(1)}, u32[]{:S(2)}, u32[]{:S(2)}) collective-permute-start(f32[256,256]{0,1:T(8,128)S(1)} %get-tuple-element.71), channel_id=1, source_target_pairs={{0,16},{8,24},{16,0},{24,8},{1,17},{9,25},{17,1},{25,9},{2,18},{10... | collective-permute-start | bytes 786440 | tf_op jit(solution)/shard_map/ppermute | solution.py:42
  81.8 0.6 collective-permute-start.2
  82.4 1.3 %broadcast_in_dim_broadcast_in_dim_broadcast_in_dim.3 = f32[32,8,128]{2,1,0:T(8,128)} broadcast(f32[]{:T(128)} %get-tuple-element.70), dimensions={} | broadcast | bytes 131076 | tf_op jit(solution)/shard_map/broadcast_in_dim;broadcast_in_dim;broadcast_in_dim | solution.py:31
  83.7 5.2 %all-to-all-start.2 = ((f32[32,8,128]{2,1,0:T(8,128)}), f32[32,8,128]{2,1,0:T(8,128)S(1)}, u32[]{:S(2)}, u32[]{:S(2)}) async-start(f32[32,8,128]{2,1,0:T(8,128)} %broadcast_in_dim_broadcast_in_dim_broadcast_in_dim.3), calls=%async_computation.2 | async-start | bytes 262144 | tf_op jit(solution)/shard_map/all_to_all | solution.py:32
  89.1 0.7 copy-done.14
  89.8 0.7 copy.256
  90.5 0.7 copy.255
  91.3 2.7 %collective-permute-start.4 = (f32[256,256]{0,1:T(8,128)S(1)}, f32[256,256]{0,1:T(8,128)S(1)}, u32[]{:S(2)}, u32[]{:S(2)}) collective-permute-start(f32[256,256]{0,1:T(8,128)S(1)} %get-tuple-element.71), channel_id=1, source_target_pairs={{0,24},{8,0},{16,8},{24,16},{1,25},{9,1},{17,9},{25,17},{2,26},{10... | collective-permute-start | bytes 786440 | tf_op jit(solution)/shard_map/ppermute | solution.py:42
  94.1 2.9 %all-to-all-done.2 = f32[32,8,128]{2,1,0:T(8,128)S(1)} async-done(((f32[32,8,128]{2,1,0:T(8,128)}), f32[32,8,128]{2,1,0:T(8,128)S(1)}, u32[]{:S(2)}, u32[]{:S(2)}) %all-to-all-start.2) | async-done | bytes 131104 | tf_op jit(solution)/shard_map/all_to_all | solution.py:32
  97.1 0.6 slice_reduce_fusion
  98.8 1.6 %collective-permute-done.4 = f32[256,256]{0,1:T(8,128)S(1)} collective-permute-done((f32[256,256]{0,1:T(8,128)S(1)}, f32[256,256]{0,1:T(8,128)S(1)}, u32[]{:S(2)}, u32[]{:S(2)}) %collective-permute-start.4) | collective-permute-done | bytes 262176 | tf_op jit(solution)/shard_map/ppermute | solution.py:42
  100.6 3.7 %multiply_subtract_fusion = (f32[1024,256]{1,0:T(8,128)}, f32[1024,256]{1,0:T(8,128)}, f32[1024,256]{1,0:T(8,128)}) fusion(f32[1024,256]{1,0:T(8,128)S(1)} %copy-done.12, f32[1024,256]{1,0:T(8,128)S(1)} %constant_dynamic-update-slice_fusion, f32[]{:T(128)S(6)} %min_shard_map.3, f32[1024,256]{1,0:T(8,128)} %param.20, f32[1024,256]{1,0:T(8,128)} %param.21), kind=kLoop, calls=%fused_computation.48 | loop fusion | flops 4194304 | bytes 7340036 | tf_op jit(solution)/shard_map/sub | solution.py:94
  (99 shorter events, 9.9 us)
Async XLA Ops:
  0.6 1.1 %copy-start.22 = (bf16[1,128,2,128]{3,2,1,0:T(2,128)(2,1)S(1)}, bf16[1,128,2,128]{3,2,1,0:T(2,128)(2,1)}, u32[]{:S(2)}) copy-start(bf16[1,128,2,128]{3,2,1,0:T(2,128)(2,1)} %param.13) | copy-start | bytes 196612
  1.7 0.7 copy-start.26
  1.8 0.7 copy-start.27
  2.4 0.8 copy-start.17
  2.7 7.5 %copy-start.11 = (bf16[1,128,4096]{2,1,0:T(8,128)(2,1)S(1)}, bf16[1,128,4096]{2,1,0:T(8,128)(2,1)}, u32[]{:S(2)}) copy-start(bf16[1,128,4096]{2,1,0:T(8,128)(2,1)} %param.15) | copy-start | bytes 3145732
  4.8 27.1 %collective-permute-start = (bf16[2,128,2,128]{3,1,2,0:T(8,128)(2,1)}, bf16[2,128,2,128]{3,1,2,0:T(8,128)(2,1)}, u32[]{:S(2)}, u32[]{:S(2)}) collective-permute-start(bf16[2,128,2,128]{3,1,2,0:T(8,128)(2,1)} %pad_maximum_fusion), channel_id=1, source_target_pairs={{0,8},{8,16},{16,24},{1,9},{9,17},{17,25},{2,10},{10,18},{18,26},{... | collective-permute-start | bytes 393224 | tf_op jit(solution)/shard_map/ppermute | solution.py:24
  11.6 6.8 %copy-start.18 = (bf16[1,128,16,128]{3,2,1,0:T(8,128)(2,1)S(1)}, bf16[1,128,16,128]{3,2,1,0:T(8,128)(2,1)}, u32[]{:S(2)}) copy-start(bf16[1,128,16,128]{3,2,1,0:T(8,128)(2,1)} %param.11) | copy-start | bytes 1572868
  11.6 36.3 %all-to-all-start.1 = ((bf16[1,128,16,256]{1,3,0,2:T(8,128)(2,1)}), bf16[1,128,16,256]{1,3,0,2:T(8,128)(2,1)S(1)}, u32[]{:S(2)}, u32[]{:S(2)}) async-start(bf16[1,128,16,256]{1,3,0,2:T(8,128)(2,1)} %bitcast.56), calls=%async_computation.1 | async-start | bytes 2097152 | tf_op jit(solution)/shard_map/all_to_all | solution.py:216
  22.8 2.5 %copy-start.4 = (f32[128,2,8,64]{3,2,1,0:T(8,128)S(1)}, f32[128,2,8,64]{3,2,1,0:T(8,128)}, u32[]{:S(2)}) copy-start(f32[128,2,8,64]{3,2,1,0:T(8,128)} %get-tuple-element.53) | copy-start | bytes 1572868
  26.5 1.9 %copy-start.8 = (f32[128,2,8,64]{0,3,2,1:T(8,128)S(1)}, f32[128,2,8,64]{0,3,2,1:T(8,128)}, u32[]{:S(2)}) copy-start(f32[128,2,8,64]{0,3,2,1:T(8,128)} %copy.217) | copy-start | bytes 1572868
  27.6 2.0 %copy-start.15 = (bf16[128,2,128,1]{2,0,3,1:T(8,128)(2,1)}, bf16[128,2,128,1]{2,0,3,1:T(8,128)(2,1)S(1)}, u32[]{:S(2)}) copy-start(bf16[128,2,128,1]{2,0,3,1:T(8,128)(2,1)S(1)} %fusion.40) | copy-start | bytes 196612
  27.6 0.6 copy-start.24
  27.6 0.6 copy-start.25
  29.6 1.0 %copy-start.7 = (bf16[1,128,16,128]{3,2,1,0:T(8,128)(2,1)S(1)}, bf16[1,128,16,128]{3,2,1,0:T(8,128)(2,1)}, u32[]{:S(2)}) copy-start(bf16[1,128,16,128]{3,2,1,0:T(8,128)(2,1)} %param.14) | copy-start | bytes 1572868
  33.1 1.4 %copy-start.2 = (f32[2,8,128,128]{2,3,1,0:T(8,128)}, f32[2,8,128,128]{2,3,1,0:T(8,128)S(1)}, u32[]{:S(2)}) copy-start(f32[2,8,128,128]{2,3,1,0:T(8,128)S(1)} %get-tuple-element.69) | copy-start | bytes 3145732
  33.1 0.9 copy-start.23
  36.5 2.7 %copy-start.19 = (bf16[128,2,8,128]{0,3,2,1:T(8,128)(2,1)S(1)}, bf16[128,2,8,128]{0,3,2,1:T(8,128)(2,1)}, u32[]{:S(2)}) copy-start(bf16[128,2,8,128]{0,3,2,1:T(8,128)(2,1)} %copy.243) | copy-start | bytes 1572868
  38.4 0.8 copy-start.9
  38.4 1.4 %copy-start.3 = (f32[2,8,128,128]{2,3,1,0:T(8,128)S(1)}, f32[2,8,128,128]{2,3,1,0:T(8,128)}, u32[]{:S(2)}) copy-start(f32[2,8,128,128]{2,3,1,0:T(8,128)} %copy-done.2) | copy-start | bytes 3145732
  40.2 6.9 %collective-permute-start.1 = (bf16[2,128,2,128]{3,1,2,0:T(8,128)(2,1)S(1)}, bf16[2,128,2,128]{3,1,2,0:T(8,128)(2,1)S(1)}, u32[]{:S(2)}, u32[]{:S(2)}) collective-permute-start(bf16[2,128,2,128]{3,1,2,0:T(8,128)(2,1)S(1)} %pad_maximum_fusion.1), channel_id=1, source_target_pairs={{8,0},{16,8},{24,16},{9,1},{17,9},{25,17},{10,2},{18,10},{26,18},{... | collective-permute-start | bytes 393224 | tf_op jit(solution)/shard_map/ppermute | solution.py:24
  42.3 0.8 copy-start.5
  47.1 0.6 copy-start.13
  47.9 1.3 %copy-start = (bf16[1,128,16,256]{1,3,0,2:T(8,128)(2,1)}, bf16[1,128,16,256]{1,3,0,2:T(8,128)(2,1)S(1)}, u32[]{:S(2)}) copy-start(bf16[1,128,16,256]{1,3,0,2:T(8,128)(2,1)S(1)} %all-to-all-done.1) | copy-start | bytes 3145732
  49.1 7.2 %copy-start.6 = (bf16[2,8,128,128]{2,3,1,0:T(8,128)(2,1)S(1)}, bf16[2,8,128,128]{2,3,1,0:T(8,128)(2,1)}, u32[]{:S(2)}) copy-start(bf16[2,8,128,128]{2,3,1,0:T(8,128)(2,1)} %copy-done.5) | copy-start | bytes 1572868
  49.2 29.6 %all-to-all-start = ((bf16[16,128,256]{2,1,0:T(8,128)(2,1)}), bf16[16,128,256]{2,1,0:T(8,128)(2,1)S(1)}, u32[]{:S(2)}, u32[]{:S(2)}) async-start(bf16[16,128,256]{2,1,0:T(8,128)(2,1)} %broadcast_in_dim.38), calls=%async_computation | async-start | bytes 2097152 | tf_op jit(solution)/shard_map/all_to_all | solution.py:32
  56.2 0.8 copy-start.16
  57.1 1.0 copy-start.10
  62.9 2.0 %copy-start.1 = (bf16[1,128,16,256]{1,3,0,2:T(8,128)(2,1)S(1)}, bf16[1,128,16,256]{1,3,0,2:T(8,128)(2,1)}, u32[]{:S(2)}) copy-start(bf16[1,128,16,256]{1,3,0,2:T(8,128)(2,1)} %copy-done) | copy-start | bytes 3145732
  79.8 18.6 %collective-permute-start.3 = (f32[256,256]{0,1:T(8,128)S(1)}, f32[256,256]{0,1:T(8,128)S(1)}, u32[]{:S(2)}, u32[]{:S(2)}) collective-permute-start(f32[256,256]{0,1:T(8,128)S(1)} %get-tuple-element.71), channel_id=1, source_target_pairs={{0,16},{8,24},{16,0},{24,8},{1,17},{9,25},{17,1},{25,9},{2,18},{10... | collective-permute-start | bytes 786440 | tf_op jit(solution)/shard_map/ppermute | solution.py:42
  81.8 16.8 %collective-permute-start.2 = (f32[256,256]{0,1:T(8,128)S(1)}, f32[256,256]{0,1:T(8,128)S(1)}, u32[]{:S(2)}, u32[]{:S(2)}) collective-permute-start(f32[256,256]{0,1:T(8,128)S(1)} %get-tuple-element.71), channel_id=1, source_target_pairs={{0,8},{8,16},{16,24},{24,0},{1,9},{9,17},{17,25},{25,1},{2,10},{10... | collective-permute-start | bytes 786440 | tf_op jit(solution)/shard_map/ppermute | solution.py:42
  83.7 5.2 %copy-start.20 = (f32[1,128,2,64]{3,1,2,0:T(8,128)S(1)}, f32[1,128,2,64]{3,1,2,0:T(8,128)}, u32[]{:S(2)}) copy-start(f32[1,128,2,64]{3,1,2,0:T(8,128)} %get-tuple-element.56) | copy-start | bytes 196612
  83.7 5.3 %copy-start.21 = (f32[1,128,2,64]{3,1,2,0:T(8,128)S(1)}, f32[1,128,2,64]{3,1,2,0:T(8,128)}, u32[]{:S(2)}) copy-start(f32[1,128,2,64]{3,1,2,0:T(8,128)} %get-tuple-element.57) | copy-start | bytes 196612
  83.7 13.4 %all-to-all-start.2 = ((f32[32,8,128]{2,1,0:T(8,128)}), f32[32,8,128]{2,1,0:T(8,128)S(1)}, u32[]{:S(2)}, u32[]{:S(2)}) async-start(f32[32,8,128]{2,1,0:T(8,128)} %broadcast_in_dim_broadcast_in_dim_broadcast_in_dim.3), calls=%async_computation.2 | async-start | bytes 262144 | tf_op jit(solution)/shard_map/all_to_all | solution.py:32
  88.9 0.8 copy-start.14
  91.3 9.1 %collective-permute-start.4 = (f32[256,256]{0,1:T(8,128)S(1)}, f32[256,256]{0,1:T(8,128)S(1)}, u32[]{:S(2)}, u32[]{:S(2)}) collective-permute-start(f32[256,256]{0,1:T(8,128)S(1)} %get-tuple-element.71), channel_id=1, source_target_pairs={{0,24},{8,0},{16,8},{24,16},{1,25},{9,1},{17,9},{25,17},{2,26},{10... | collective-permute-start | bytes 786440 | tf_op jit(solution)/shard_map/ppermute | solution.py:42
  98.7 1.9 %copy-start.12 = (f32[1024,256]{1,0:T(8,128)S(1)}, f32[1024,256]{1,0:T(8,128)}, u32[]{:S(2)}) copy-start(f32[1024,256]{1,0:T(8,128)} %param.19) | copy-start | bytes 3145732

commit v4 on v3

--- a/solution.py
+++ b/solution.py
@@ -171,9 +171,18 @@
         ],
     )
     delta = jnp.einsum("qhgd,qhgd->hgq", grad_out.astype(jnp.float32), attn_out)[..., None]
+    value_terms = [
+        jnp.einsum("hgqk,qhgd->khd", probs_low, grad_out, preferred_element_type=jnp.float32)
+        for probs_low in low_list
+    ]
+    value_total = (
+        shifted(value_terms[reach].astype(jnp.bfloat16), "ctx", -1).astype(jnp.float32)
+        + value_terms[0]
+    )
+    grad_v = value_total.astype(jnp.bfloat16)
     query_terms = []
     key_terms = []
-    for pair_in, probs, probs_low, valid_in in zip(pairs, prob_list, low_list, masks):
+    for pair_in, probs, valid_in in zip(pairs, prob_list, masks):
         dprobs = jnp.einsum(
             "qhgd,khd->hgqk", grad_out, pair_in[1], preferred_element_type=jnp.float32
         )
@@ -188,24 +197,17 @@
             )
             * scale
         )
-        v_part = jnp.einsum(
-            "hgqk,qhgd->khd", probs_low, grad_out, preferred_element_type=jnp.float32
-        )
-        q_part, kv_part = (q_part, jnp.stack([k_part, v_part]))
         query_terms.append(q_part)
-        key_terms.append(kv_part)
+        key_terms.append(k_part)
     query_grad = reduce(jnp.add, query_terms)
-    key_total = key_terms[reach]
-    offset = 0
     key_total = (
-        shifted(key_total.astype(jnp.bfloat16), "ctx", -1).astype(key_total.dtype)
-        + key_terms[offset]
+        shifted(key_terms[reach].astype(jnp.bfloat16), "ctx", -1).astype(jnp.float32)
+        + key_terms[0]
     )
     grad_q = unrotate(query_grad.reshape(tok_rows, head_count, head_dim), cosine, sine).astype(
         jnp.bfloat16
     )
-    grad_k = unrotate(key_total[0], cosine, sine).astype(jnp.bfloat16)
-    grad_v = key_total[1].astype(jnp.bfloat16)
+    grad_k = unrotate(key_total, cosine, sine).astype(jnp.bfloat16)
     feats = features[0]
     width = feats.shape[1]
     value_flat = grad_v.reshape(tok_rows, kv_count * head_dim)

time: 105 us -> 106 us (level)
  matrix products: 9.24 us -> 13.4 us
  waiting for transfers between devices: 21.9 us -> 18.4 us
  starting transfers between devices: 29.8 us -> 32.9 us
  local copies, waits for them, and re-layouts: 24 us -> 21.6 us
    ppermute x2 -> x3, waiting for transfers between devices: 4.02 us -> 0.01 us  [shifted(): return lax.ppermute(array, axis, pairs)]
    unnamed x60 -> x48, local copies, waits for them, and re-layouts: 9.96 us -> 7.01 us
    all_to_all x2, starting transfers between devices: 12.3 us -> 14.1 us  [spread_copy(): return lax.all_to_all(stacked, axes, 0, 0, tiled=False)]
    dot_general x2, matrix products: 0.68 us -> 2.17 us  [local(): jnp.einsum('hgqk,qhgd->khd', probs_low, grad_out, preferred_element_type=...]
    dot_general x2, matrix products: 2.25 us -> 3.69 us  [local(): jnp.einsum('qhgd,khd->hgqk', grad_out, pair_in[1], preferred_element_type...]
    ppermute x2 -> x3, starting transfers between devices: 6.8 us -> 8.08 us  [shifted(): return lax.ppermute(array, axis, pairs)]
    dot_general x1, matrix products: 1.07 us -> 2.3 us  [local(): lax.dot_general(feat_cols.reshape(-1, piece_rows), value_rows.reshape(-1,...]
  transfers between devices with their start and end apart: 8 -> 9, of which waited for: 4 -> 3; matrix products, arithmetic and copies ran while one was open for 33% -> 35% of each run, Pallas kernels for 0% -> 0%
where the time goes in v4:
time: 106 us; the launch traced here: 105 us
  starting transfers between devices  32.9 us (31%)
  local copies, waits for them, and re-layouts  21.6 us (20%)
  waiting for transfers between devices  18.4 us (17%)
  other arithmetic  16.6 us (16%)
  matrix products  13.4 us (13%)
  between operations  1.94 us (2%)
    all_to_all x2, waiting for transfers between devices, spread_copy(): return lax.all_to_all(stacked, axes, 0, 0, tiled=False)  17.3 us
    all_to_all x2, starting transfers between devices, spread_copy(): return lax.all_to_all(stacked, axes, 0, 0, tiled=False)  14.1 us
    ppermute x3, starting transfers between devices, shifted(): return lax.ppermute(array, axis, pairs)  8.08 us
    unnamed x48, local copies, waits for them, and re-layouts  7.01 us
    all_to_all x1, starting transfers between devices, local(): lax.all_to_all(feats.reshape(tok_rows, n_dp * n_ctx, piece_rows), spread,...  5.45 us
    ppermute x3, starting transfers between devices, ring_copy(): lax.ppermute(array, axis, [(i, (i + step) % peers) for i in range(peers)])  5.24 us
    concatenate x2, local copies, waits for them, and re-layouts, rotate(): jnp.concatenate([-vectors[..., half:], vectors[..., :half]], axis=-1)  3.71 us
    sub x1, other arithmetic, adam_update(): new_param = param - LEARN_RATE * (step_size + DECAY_RATE * param)  3.71 us
  transfers between devices with their start and end apart: 9, of which 3 were waited for; matrix products, arithmetic and copies ran while one was open for 35% of the time, Pallas kernels for 0%

profile of v4, /device:TPU:0, one launch (start us, length us, event | category | flops | bytes accessed | tf_op | source)
XLA Modules:
  0.0 104.9 jit_solution(11620789951446367941)
XLA Ops:
  0.7 0.8 copy.214
  1.8 0.6 copy-done.20
  3.3 0.7 fusion.46
  4.1 0.7 pad_maximum_fusion
  4.8 5.5 %collective-permute-start = (bf16[2,128,2,128]{3,1,2,0:T(8,128)(2,1)}, bf16[2,128,2,128]{3,1,2,0:T(8,128)(2,1)}, u32[]{:S(2)}, u32[]{:S(2)}) collective-permute-start(bf16[2,128,2,128]{3,1,2,0:T(8,128)(2,1)} %pad_maximum_fusion), channel_id=1, source_target_pairs={{0,8},{8,16},{16,24},{1,9},{9,17},{17,25},{2,10},{10,18},{18,26},{... | collective-permute-start | bytes 393224 | tf_op jit(solution)/shard_map/ppermute | solution.py:24
  10.3 1.3 %copy.247 = bf16[1,128,4096]{1,2,0:T(8,128)(2,1)} copy(bf16[1,128,4096]{2,1,0:T(8,128)(2,1)S(1)} %copy-done.10) | data formatting | bytes 2097152 | tf_op args[4]
  11.6 5.4 %all-to-all-start.1 = ((bf16[1,128,16,256]{1,3,0,2:T(8,128)(2,1)}), bf16[1,128,16,256]{1,3,0,2:T(8,128)(2,1)S(1)}, u32[]{:S(2)}, u32[]{:S(2)}) async-start(bf16[1,128,16,256]{1,3,0,2:T(8,128)(2,1)} %bitcast.51), calls=%async_computation.1 | async-start | bytes 2097152 | tf_op jit(solution)/shard_map/all_to_all | solution.py:218
  17.6 0.7 copy.219
  18.4 0.7 copy.215
  19.1 1.1 %convert_bitcast_fusion.1 = (f32[128,2,8,128]{3,2,1,0:T(8,128)}, f32[128,16,128]{2,1,0:T(8,128)S(1)}) fusion(bf16[1,128,16,128]{3,2,1,0:T(8,128)(2,1)S(1)} %copy-done.13), kind=kLoop, calls=%fused_computation.20 | loop fusion | flops 262144 | bytes 2621440 | tf_op jit(solution)/shard_map/convert_element_type | solution.py:126
  20.2 1.6 %copy.216 = f32[128,2,8,128]{0,3,2,1:T(8,128)S(1)} copy(f32[128,2,8,128]{3,2,1,0:T(8,128)} %get-tuple-element.54) | data formatting | bytes 2097152 | tf_op jit(solution)/shard_map/convert_element_type | solution.py:126
  21.8 1.7 %fusion.22 = (f32[128,2,8,64]{3,2,1,0:T(8,128)}, f32[128,2,8,64]{3,2,1,0:T(8,128)}) fusion(f32[128,16,128]{2,1,0:T(8,128)S(1)} %get-tuple-element.55), kind=kLoop, calls=%fused_computation.41 | loop fusion | flops 131072 | bytes 2097152 | tf_op jit(solution)/shard_map/concatenate | solution.py:77
  23.5 2.5 %copy.217 = f32[128,2,8,64]{0,3,2,1:T(8,128)} copy(f32[128,2,8,64]{3,2,1,0:T(8,128)} %get-tuple-element.52) | data formatting | bytes 1048576 | tf_op jit(solution)/shard_map/concatenate | solution.py:77
  26.0 1.2 %copy.218 = f32[128,2,8,64]{0,3,2,1:T(8,128)} copy(f32[128,2,8,64]{3,2,1,0:T(8,128)S(1)} %copy-done.4) | data formatting | bytes 1048576 | tf_op jit(solution)/shard_map/concatenate | solution.py:77
  27.2 1.1 %fusion.41 = bf16[128,2,128,1]{2,0,3,1:T(8,128)(2,1)S(1)} fusion(f32[128,2,64]{2,0,1:T(8,128)} %get-tuple-element.61, f32[128,2,64]{2,0,1:T(8,128)S(1)} %get-tuple-element.60, f32[128,128]{1,0:T(8,128)S(1)} %pad_maximum_fusion.2, f32[128,128]{1,0:T(8,128)S(1)} %pad_maximum_fusion.1, bf16[1,128,2,128]{3,2,1,0:T(2,128)(2,1)S(1)} %copy-done.12), kind=kLoop, calls=%fused_computation.81 | loop fusion | flops 196608 | bytes 393216 | tf_op jit(solution)/shard_map/convert_element_type | solution.py:128
  28.3 0.7 copy-done.18
  29.1 1.2 %fusion.24 = bf16[128,2,8,128]{0,3,2,1:T(8,128)(2,1)S(1)} fusion(f32[128,2,8,64]{0,3,2,1:T(8,128)} %copy.218, f32[128,2,8,64]{0,3,2,1:T(8,128)S(1)} %copy-done.8, f32[128,2,8,128]{0,3,2,1:T(8,128)S(1)} %copy.216, f32[128,128]{0,1:T(8,128)} %copy.219, f32[128,128]{0,1:T(8,128)} %copy.215), kind=kLoop, calls=%fused_computation.44 | loop fusion | flops 1310720 | bytes 2752512 | tf_op jit(solution)/shard_map/convert_element_type | solution.py:126
  30.7 0.7 copy-done.5
  31.4 1.2 %copy.243 = bf16[128,2,8,128]{0,3,2,1:T(8,128)(2,1)} copy(bf16[128,2,8,128]{3,2,1,0:T(8,128)(2,1)S(1)} %bitcast.166) | data formatting | bytes 1048576 | tf_op jit(solution)/shard_map/reshape;squeeze | solution.py:129
  32.6 1.1 %fusion.56 = (f32[2,8,128]{2,1,0:T(8,128)S(1)}, f32[2,8,128,128]{2,3,1,0:T(8,128)S(1)}) fusion(bf16[128,2,8,128]{0,3,2,1:T(8,128)(2,1)S(1)} %fusion.24, bf16[2,128,2,128]{3,1,2,0:T(8,128)(2,1)} %collective-permute-done, pred[128,128]{0,1:T(8,128)(4,1)S(1)} %get-tuple-element.62), kind=kOutput, calls=%fused_computation.110 | convolution fusion | flops 67893248 | bytes 1662976 | tf_op jit(solution)/shard_map/qhgd,khd->hgqk/dot_general | solution.py:148
  34.2 1.0 copy-done.14
  35.2 1.0 fusion.18
  36.2 1.3 %collective-permute-start.2 = (bf16[128,2,128]{2,0,1:T(8,128)(2,1)}, bf16[128,2,128]{2,0,1:T(8,128)(2,1)}, u32[]{:S(2)}, u32[]{:S(2)}) collective-permute-start(bf16[128,2,128]{2,0,1:T(8,128)(2,1)} %fusion.18), channel_id=1, source_target_pairs={{8,0},{16,8},{24,16},{9,1},{17,9},{25,17},{10,2},{18,10},{26,18},{... | collective-permute-start | bytes 196616 | tf_op jit(solution)/shard_map/ppermute | solution.py:24
  37.9 1.2 %fusion.3 = f32[2,8,128,128]{3,2,1,0:T(8,128)S(1)} fusion(f32[128,2,8,128]{3,0,2,1:T(8,128)S(1)} %convolution_bitcast_fusion.2, bf16[2,128,2,128]{3,1,2,0:T(8,128)(2,1)} %collective-permute-done, f32[2,8,128,128]{2,3,1,0:T(8,128)S(1)} %get-tuple-element.69, f32[2,8,128]{2,1,0:T(8,128)S(1)} %add.132, f32[2,8,128]{2,1,0:T(8,128)S(1)} %max.8, ...), kind=kOutput, calls=%fused_computation.8 | convolution fusion | flops 68419584 | bytes 3244032 | tf_op jit(solution)/shard_map/hgqk,khd->qhgd/dot_general | solution.py:169
  39.2 0.8 multiply_reduce_fusion
  40.0 1.6 %fusion.12 = bf16[2,8,128,128]{2,3,1,0:T(8,128)(2,1)S(1)} fusion(bf16[128,2,8,128]{0,3,2,1:T(8,128)(2,1)} %copy.243, f32[2,8,128]{2,1,0:T(8,128)S(1)} %copy.273, bf16[128,2,128,1]{2,1,0,3:T(2,128)(2,1)} %bitcast.169, f32[2,8,128]{2,1,0:T(8,128)S(1)} %add.132, f32[2,8,128,128]{2,3,1,0:T(8,128)S(1)} %get-tuple-element.67, f32[2,8,128]{2,1,0:T(8,128)S(1)} %max.8, ...), kind=kOutput, calls=%fused_computation.22 | convolution fusion | flops 68681728 | bytes 2203648 | tf_op jit(solution)/shard_map/qhgd,khd->hgqk/dot_general | solution.py:186
  41.6 2.1 %fusion.11 = bf16[2,8,128,128]{2,3,1,0:T(8,128)(2,1)} fusion(bf16[128,2,8,128]{0,3,2,1:T(8,128)(2,1)S(1)} %copy-done.15, f32[2,8,128]{2,1,0:T(8,128)S(1)} %copy.273, bf16[2,128,2,128]{3,1,2,0:T(8,128)(2,1)} %collective-permute-done, f32[2,8,128]{2,1,0:T(8,128)S(1)} %add.132, f32[2,8,128,128]{2,3,1,0:T(8,128)S(1)} %copy-done.3, f32[2,8,128]{2,1,0:T(8,128)S(1)} %max.8, ...), kind=kOutput, calls=%fused_computation.21 | convolution fusion | flops 68681728 | bytes 2203648 | tf_op jit(solution)/shard_map/qhgd,khd->hgqk/dot_general | solution.py:186
  43.7 1.2 %add_convert_fusion = bf16[128,2,128]{2,0,1:T(8,128)(2,1)S(1)} fusion(bf16[128,2,128]{2,0,1:T(8,128)(2,1)} %collective-permute-done.2, bf16[128,2,8,128]{0,3,2,1:T(8,128)(2,1)S(1)} %copy-done.15, f32[2,8,128]{2,1,0:T(8,128)S(1)} %add.132, f32[2,8,128,128]{2,3,1,0:T(8,128)S(1)} %get-tuple-element.67, f32[2,8,128]{2,1,0:T(8,128)S(1)} %max.8, ...), kind=kOutput, calls=%fused_computation.75 | convolution fusion | flops 68255744 | bytes 1736704 | tf_op jit(solution)/shard_map/hgqk,qhgd->khd/dot_general | solution.py:175
  45.2 1.2 %broadcast_in_dim.80 = bf16[16,128,256]{2,1,0:T(8,128)(2,1)} broadcast(bf16[128,256]{1,0:T(8,128)(2,1)S(1)} %copy.246), dimensions={1,2} | broadcast | bytes 1114112 | tf_op jit(solution)/shard_map/broadcast_in_dim | solution.py:31
  46.5 8.9 %all-to-all-start = ((bf16[16,128,256]{2,1,0:T(8,128)(2,1)}), bf16[16,128,256]{2,1,0:T(8,128)(2,1)}, u32[]{:S(2)}, u32[]{:S(2)}) async-start(bf16[16,128,256]{2,1,0:T(8,128)(2,1)} %broadcast_in_dim.80), calls=%async_computation | async-start | bytes 2097152 | tf_op jit(solution)/shard_map/all_to_all | solution.py:32
  55.7 1.3 %collective-permute-start.1 = (bf16[128,2,128]{2,0,1:T(8,128)(2,1)S(1)}, bf16[128,2,128]{2,0,1:T(8,128)(2,1)S(1)}, u32[]{:S(2)}, u32[]{:S(2)}) collective-permute-start(bf16[128,2,128]{2,0,1:T(8,128)(2,1)S(1)} %fusion.19), channel_id=1, source_target_pairs={{8,0},{16,8},{24,16},{9,1},{17,9},{25,17},{10,2},{18,10},{26,18},{... | collective-permute-start | bytes 196616 | tf_op jit(solution)/shard_map/ppermute | solution.py:24
  57.3 1.2 %fusion.6 = f32[2,128,8,128]{3,1,2,0:T(8,128)S(1)} fusion(f32[2,128,8,128]{3,1,2,0:T(8,128)S(1)} %fusion.57, bf16[2,8,128,128]{2,3,1,0:T(8,128)(2,1)S(1)} %copy-done.9, bf16[2,128,2,128]{3,1,2,0:T(8,128)(2,1)} %collective-permute-done), kind=kOutput, calls=%fused_computation.12 | convolution fusion | flops 67633152 | bytes 2686976 | tf_op jit(solution)/shard_map/hgqk,khd->qhgd/dot_general | solution.py:191
  58.5 1.4 %copy.236 = f32[128,16,128]{2,1,0:T(8,128)} copy(f32[128,16,128]{0,2,1:T(8,128)S(1)} %bitcast.163) | data formatting | bytes 2097152 | tf_op jit(solution)/shard_map/reshape | solution.py:207
  60.4 1.3 %broadcast_multiply_fusion = f32[128,16,128]{2,1,0:T(8,128)S(1)} fusion(f32[128,16,128]{2,1,0:T(8,128)} %copy.236, f32[128,128]{1,0:T(8,128)S(1)} %pad_maximum_fusion.2), kind=kLoop, calls=%fused_computation.56 | loop fusion | flops 262144 | bytes 2162688 | tf_op jit(solution)/shard_map/mul | solution.py:83
  62.1 1.2 %fusion.25 = bf16[1,128,16,128]{3,2,1,0:T(8,128)(2,1)} fusion(f32[1,128,16,64]{3,2,1,0:T(8,128)S(1)} %get-tuple-element.51, f32[1,128,16,64]{3,2,1,0:T(8,128)S(1)} %get-tuple-element.50, f32[1,128,16,128]{3,2,1,0:T(8,128)S(1)} %copy.235, f32[128,128]{1,0:T(8,128)S(1)} %pad_maximum_fusion.1), kind=kLoop, calls=%fused_computation.46 | loop fusion | flops 1048576 | bytes 2686976 | tf_op jit(solution)/shard_map/convert_element_type | solution.py:207
  63.7 0.8 copy-done.1
  65.1 13.7 %all-to-all-done = bf16[16,128,256]{2,1,0:T(8,128)(2,1)} async-done(((bf16[16,128,256]{2,1,0:T(8,128)(2,1)}), bf16[16,128,256]{2,1,0:T(8,128)(2,1)}, u32[]{:S(2)}, u32[]{:S(2)}) %all-to-all-start) | async-done | bytes 1048608 | tf_op jit(solution)/shard_map/all_to_all | solution.py:32
  78.7 2.3 %multiply_reduce_fusion.1 = (f32[]{:T(128)}, f32[256,256]{0,1:T(8,128)S(1)}) fusion(bf16[2048,256]{1,0:T(8,128)(2,1)} %bitcast.49, bf16[2048,256]{1,0:T(8,128)(2,1)S(1)} %bitcast.165), kind=kOutput, calls=%fused_computation.57 | convolution fusion | flops 268566528 | bytes 2359300 | tf_op jit(solution)/shard_map/dot_general | solution.py:222
  81.0 2.0 %collective-permute-start.4 = (f32[256,256]{0,1:T(8,128)S(1)}, f32[256,256]{0,1:T(8,128)S(1)}, u32[]{:S(2)}, u32[]{:S(2)}) collective-permute-start(f32[256,256]{0,1:T(8,128)S(1)} %get-tuple-element.73), channel_id=1, source_target_pairs={{0,16},{8,24},{16,0},{24,8},{1,17},{9,25},{17,1},{25,9},{2,18},{10... | collective-permute-start | bytes 786440 | tf_op jit(solution)/shard_map/ppermute | solution.py:42
  83.5 1.3 %broadcast_in_dim_broadcast_in_dim_broadcast_in_dim.3 = f32[32,8,128]{2,1,0:T(8,128)} broadcast(f32[]{:T(128)} %get-tuple-element.72), dimensions={} | broadcast | bytes 131076 | tf_op jit(solution)/shard_map/broadcast_in_dim;broadcast_in_dim;broadcast_in_dim | solution.py:31
  84.8 5.3 %all-to-all-start.2 = ((f32[32,8,128]{2,1,0:T(8,128)}), f32[32,8,128]{2,1,0:T(8,128)S(1)}, u32[]{:S(2)}, u32[]{:S(2)}) async-start(f32[32,8,128]{2,1,0:T(8,128)} %broadcast_in_dim_broadcast_in_dim_broadcast_in_dim.3), calls=%async_computation.2 | async-start | bytes 262144 | tf_op jit(solution)/shard_map/all_to_all | solution.py:32
  90.2 0.7 copy.256
  90.9 0.7 copy.255
  91.7 2.7 %collective-permute-start.5 = (f32[256,256]{0,1:T(8,128)S(1)}, f32[256,256]{0,1:T(8,128)S(1)}, u32[]{:S(2)}, u32[]{:S(2)}) collective-permute-start(f32[256,256]{0,1:T(8,128)S(1)} %get-tuple-element.73), channel_id=1, source_target_pairs={{0,24},{8,0},{16,8},{24,16},{1,25},{9,1},{17,9},{25,17},{2,26},{10... | collective-permute-start | bytes 786440 | tf_op jit(solution)/shard_map/ppermute | solution.py:42
  94.6 3.7 %all-to-all-done.2 = f32[32,8,128]{2,1,0:T(8,128)S(1)} async-done(((f32[32,8,128]{2,1,0:T(8,128)}), f32[32,8,128]{2,1,0:T(8,128)S(1)}, u32[]{:S(2)}, u32[]{:S(2)}) %all-to-all-start.2) | async-done | bytes 131104 | tf_op jit(solution)/shard_map/all_to_all | solution.py:32
  98.3 0.6 slice_reduce_fusion
  100.0 1.0 collective-permute-done.5
  101.2 3.7 %multiply_subtract_fusion = (f32[1024,256]{1,0:T(8,128)}, f32[1024,256]{1,0:T(8,128)}, f32[1024,256]{1,0:T(8,128)}) fusion(f32[1024,256]{1,0:T(8,128)S(1)} %copy-done.11, f32[1024,256]{1,0:T(8,128)S(1)} %constant_dynamic-update-slice_fusion, f32[]{:T(128)S(6)} %min_shard_map.3, f32[1024,256]{1,0:T(8,128)} %param.20, f32[1024,256]{1,0:T(8,128)} %param.21), kind=kLoop, calls=%fused_computation.48 | loop fusion | flops 4194304 | bytes 7340036 | tf_op jit(solution)/shard_map/sub | solution.py:94
  (85 shorter events, 7.4 us)
Async XLA Ops:
  0.6 1.1 %copy-start.16 = (bf16[1,128,2,128]{3,2,1,0:T(2,128)(2,1)S(1)}, bf16[1,128,2,128]{3,2,1,0:T(2,128)(2,1)}, u32[]{:S(2)}) copy-start(bf16[1,128,2,128]{3,2,1,0:T(2,128)(2,1)} %param.13) | copy-start | bytes 196612
  1.7 0.7 copy-start.20
  1.8 0.7 copy-start.21
  2.4 0.8 copy-start.12
  2.7 7.5 %copy-start.10 = (bf16[1,128,4096]{2,1,0:T(8,128)(2,1)S(1)}, bf16[1,128,4096]{2,1,0:T(8,128)(2,1)}, u32[]{:S(2)}) copy-start(bf16[1,128,4096]{2,1,0:T(8,128)(2,1)} %param.15) | copy-start | bytes 3145732
  4.8 27.8 %collective-permute-start = (bf16[2,128,2,128]{3,1,2,0:T(8,128)(2,1)}, bf16[2,128,2,128]{3,1,2,0:T(8,128)(2,1)}, u32[]{:S(2)}, u32[]{:S(2)}) collective-permute-start(bf16[2,128,2,128]{3,1,2,0:T(8,128)(2,1)} %pad_maximum_fusion), channel_id=1, source_target_pairs={{0,8},{8,16},{16,24},{1,9},{9,17},{17,25},{2,10},{10,18},{18,26},{... | collective-permute-start | bytes 393224 | tf_op jit(solution)/shard_map/ppermute | solution.py:24
  11.6 7.5 %copy-start.13 = (bf16[1,128,16,128]{3,2,1,0:T(8,128)(2,1)S(1)}, bf16[1,128,16,128]{3,2,1,0:T(8,128)(2,1)}, u32[]{:S(2)}) copy-start(bf16[1,128,16,128]{3,2,1,0:T(8,128)(2,1)} %param.11) | copy-start | bytes 1572868
  11.6 33.6 %all-to-all-start.1 = ((bf16[1,128,16,256]{1,3,0,2:T(8,128)(2,1)}), bf16[1,128,16,256]{1,3,0,2:T(8,128)(2,1)S(1)}, u32[]{:S(2)}, u32[]{:S(2)}) async-start(bf16[1,128,16,256]{1,3,0,2:T(8,128)(2,1)} %bitcast.51), calls=%async_computation.1 | async-start | bytes 2097152 | tf_op jit(solution)/shard_map/all_to_all | solution.py:218
  23.5 2.5 %copy-start.4 = (f32[128,2,8,64]{3,2,1,0:T(8,128)S(1)}, f32[128,2,8,64]{3,2,1,0:T(8,128)}, u32[]{:S(2)}) copy-start(f32[128,2,8,64]{3,2,1,0:T(8,128)} %get-tuple-element.53) | copy-start | bytes 1572868
  27.2 1.9 %copy-start.8 = (f32[128,2,8,64]{0,3,2,1:T(8,128)S(1)}, f32[128,2,8,64]{0,3,2,1:T(8,128)}, u32[]{:S(2)}) copy-start(f32[128,2,8,64]{0,3,2,1:T(8,128)} %copy.217) | copy-start | bytes 1572868
  28.3 0.7 copy-start.18
  28.3 0.7 copy-start.19
  30.3 1.0 copy-start.5
  33.7 4.2 %copy-start.2 = (f32[2,8,128,128]{2,3,1,0:T(8,128)}, f32[2,8,128,128]{2,3,1,0:T(8,128)S(1)}, u32[]{:S(2)}) copy-start(f32[2,8,128,128]{2,3,1,0:T(8,128)S(1)} %get-tuple-element.69) | copy-start | bytes 3145732
  33.8 1.4 %copy-start.14 = (bf16[128,2,8,128]{0,3,2,1:T(8,128)(2,1)S(1)}, bf16[128,2,8,128]{0,3,2,1:T(8,128)(2,1)}, u32[]{:S(2)}) copy-start(bf16[128,2,8,128]{0,3,2,1:T(8,128)(2,1)} %copy.243) | copy-start | bytes 1572868
  35.2 2.3 %copy-start.17 = (bf16[1,128,2,128]{3,2,1,0:T(2,128)(2,1)S(1)}, bf16[1,128,2,128]{3,2,1,0:T(2,128)(2,1)}, u32[]{:S(2)}) copy-start(bf16[1,128,2,128]{3,2,1,0:T(2,128)(2,1)} %param.13) | copy-start | bytes 196612
  36.2 7.6 %collective-permute-start.2 = (bf16[128,2,128]{2,0,1:T(8,128)(2,1)}, bf16[128,2,128]{2,0,1:T(8,128)(2,1)}, u32[]{:S(2)}, u32[]{:S(2)}) collective-permute-start(bf16[128,2,128]{2,0,1:T(8,128)(2,1)} %fusion.18), channel_id=1, source_target_pairs={{8,0},{16,8},{24,16},{9,1},{17,9},{25,17},{10,2},{18,10},{26,18},{... | collective-permute-start | bytes 196616 | tf_op jit(solution)/shard_map/ppermute | solution.py:24
  40.0 1.6 %copy-start.3 = (f32[2,8,128,128]{2,3,1,0:T(8,128)S(1)}, f32[2,8,128,128]{2,3,1,0:T(8,128)}, u32[]{:S(2)}) copy-start(f32[2,8,128,128]{2,3,1,0:T(8,128)} %copy-done.2) | copy-start | bytes 3145732
  40.0 1.6 %copy-start.15 = (bf16[128,2,8,128]{0,3,2,1:T(8,128)(2,1)S(1)}, bf16[128,2,8,128]{0,3,2,1:T(8,128)(2,1)}, u32[]{:S(2)}) copy-start(bf16[128,2,8,128]{0,3,2,1:T(8,128)(2,1)} %copy.243) | copy-start | bytes 1572868
  41.6 15.4 %copy-start.6 = (bf16[2,8,128,128]{2,3,1,0:T(8,128)(2,1)}, bf16[2,8,128,128]{2,3,1,0:T(8,128)(2,1)S(1)}, u32[]{:S(2)}) copy-start(bf16[2,8,128,128]{2,3,1,0:T(8,128)(2,1)S(1)} %fusion.12) | copy-start | bytes 1572868
  45.2 1.3 %copy-start = (bf16[1,128,16,256]{1,3,0,2:T(8,128)(2,1)}, bf16[1,128,16,256]{1,3,0,2:T(8,128)(2,1)S(1)}, u32[]{:S(2)}) copy-start(bf16[1,128,16,256]{1,3,0,2:T(8,128)(2,1)S(1)} %all-to-all-done.1) | copy-start | bytes 3145732
  46.4 9.0 %copy-start.9 = (bf16[2,8,128,128]{2,3,1,0:T(8,128)(2,1)S(1)}, bf16[2,8,128,128]{2,3,1,0:T(8,128)(2,1)}, u32[]{:S(2)}) copy-start(bf16[2,8,128,128]{2,3,1,0:T(8,128)(2,1)} %fusion.11) | copy-start | bytes 1572868
  46.5 32.2 %all-to-all-start = ((bf16[16,128,256]{2,1,0:T(8,128)(2,1)}), bf16[16,128,256]{2,1,0:T(8,128)(2,1)}, u32[]{:S(2)}, u32[]{:S(2)}) async-start(bf16[16,128,256]{2,1,0:T(8,128)(2,1)} %broadcast_in_dim.80), calls=%async_computation | async-start | bytes 2097152 | tf_op jit(solution)/shard_map/all_to_all | solution.py:32
  55.7 7.6 %collective-permute-start.1 = (bf16[128,2,128]{2,0,1:T(8,128)(2,1)S(1)}, bf16[128,2,128]{2,0,1:T(8,128)(2,1)S(1)}, u32[]{:S(2)}, u32[]{:S(2)}) collective-permute-start(bf16[128,2,128]{2,0,1:T(8,128)(2,1)S(1)} %fusion.19), channel_id=1, source_target_pairs={{8,0},{16,8},{24,16},{9,1},{17,9},{25,17},{10,2},{18,10},{26,18},{... | collective-permute-start | bytes 196616 | tf_op jit(solution)/shard_map/ppermute | solution.py:24
  62.1 1.2 %copy-start.7 = (bf16[2,8,128,128]{2,3,1,0:T(8,128)(2,1)S(1)}, bf16[2,8,128,128]{2,3,1,0:T(8,128)(2,1)}, u32[]{:S(2)}) copy-start(bf16[2,8,128,128]{2,3,1,0:T(8,128)(2,1)} %copy-done.6) | copy-start | bytes 1572868
  63.3 1.2 %copy-start.1 = (bf16[1,128,16,256]{1,3,0,2:T(8,128)(2,1)S(1)}, bf16[1,128,16,256]{1,3,0,2:T(8,128)(2,1)}, u32[]{:S(2)}) copy-start(bf16[1,128,16,256]{1,3,0,2:T(8,128)(2,1)} %copy-done) | copy-start | bytes 3145732
  81.0 18.6 %collective-permute-start.4 = (f32[256,256]{0,1:T(8,128)S(1)}, f32[256,256]{0,1:T(8,128)S(1)}, u32[]{:S(2)}, u32[]{:S(2)}) collective-permute-start(f32[256,256]{0,1:T(8,128)S(1)} %get-tuple-element.73), channel_id=1, source_target_pairs={{0,16},{8,24},{16,0},{24,8},{1,17},{9,25},{17,1},{25,9},{2,18},{10... | collective-permute-start | bytes 786440 | tf_op jit(solution)/shard_map/ppermute | solution.py:42
  83.0 16.8 %collective-permute-start.3 = (f32[256,256]{0,1:T(8,128)S(1)}, f32[256,256]{0,1:T(8,128)S(1)}, u32[]{:S(2)}, u32[]{:S(2)}) collective-permute-start(f32[256,256]{0,1:T(8,128)S(1)} %get-tuple-element.73), channel_id=1, source_target_pairs={{0,8},{8,16},{16,24},{24,0},{1,9},{9,17},{17,25},{25,1},{2,10},{10... | collective-permute-start | bytes 786440 | tf_op jit(solution)/shard_map/ppermute | solution.py:42
  84.8 13.4 %all-to-all-start.2 = ((f32[32,8,128]{2,1,0:T(8,128)}), f32[32,8,128]{2,1,0:T(8,128)S(1)}, u32[]{:S(2)}, u32[]{:S(2)}) async-start(f32[32,8,128]{2,1,0:T(8,128)} %broadcast_in_dim_broadcast_in_dim_broadcast_in_dim.3), calls=%async_computation.2 | async-start | bytes 262144 | tf_op jit(solution)/shard_map/all_to_all | solution.py:32
  91.7 9.3 %collective-permute-start.5 = (f32[256,256]{0,1:T(8,128)S(1)}, f32[256,256]{0,1:T(8,128)S(1)}, u32[]{:S(2)}, u32[]{:S(2)}) collective-permute-start(f32[256,256]{0,1:T(8,128)S(1)} %get-tuple-element.73), channel_id=1, source_target_pairs={{0,24},{8,0},{16,8},{24,16},{1,25},{9,1},{17,9},{25,17},{2,26},{10... | collective-permute-start | bytes 786440 | tf_op jit(solution)/shard_map/ppermute | solution.py:42
  99.9 1.3 %copy-start.11 = (f32[1024,256]{1,0:T(8,128)S(1)}, f32[1024,256]{1,0:T(8,128)}, u32[]{:S(2)}) copy-start(f32[1024,256]{1,0:T(8,128)} %param.19) | copy-start | bytes 3145732

commit v5 on v4

--- a/solution.py
+++ b/solution.py
@@ -214,17 +214,17 @@
     own_rows = param.shape[0]
     n_dp = lax.axis_size("dp")
     piece_rows = own_rows // n_ctx
-    spread = ("dp", "ctx")
     feat_cols = lax.all_to_all(
-        feats.reshape(tok_rows, n_dp * n_ctx, piece_rows), spread, 1, 0, tiled=False
-    )
-    value_rows = spread_copy(value_flat, spread)
-    pieces = lax.dot_general(
-        feat_cols.reshape(-1, piece_rows),
-        value_rows.reshape(-1, kv_count * head_dim),
+        feats.reshape(tok_rows, n_dp, n_ctx, piece_rows), "ctx", 2, 0, tiled=False
+    )
+    value_rows = spread_copy(value_flat, "ctx")
+    partials = lax.dot_general(
+        feat_cols.reshape(n_ctx * tok_rows, n_dp * piece_rows),
+        value_rows.reshape(n_ctx * tok_rows, kv_count * head_dim),
         (((0,), (0,)), ((), ())),
         preferred_element_type=jnp.float32,
-    )
+    ).reshape(n_dp, piece_rows, kv_count * head_dim)
+    pieces = jnp.sum(lax.all_to_all(partials, "dp", 0, 0, tiled=False), axis=0)
     weight_gradient = ring_copy(pieces, "ctx")
     norm_part = jnp.sum(pieces * pieces)
     everyone = ("ctx", "dp", "tp")

time: 106 us -> 115 us (1.085)
  waiting for transfers between devices: 18.4 us -> 24.5 us
  other arithmetic: 16.6 us -> 19.5 us
    all_to_all x1 -> x2, waiting for transfers between devices: 0.01 us -> 16.1 us  [the longest x1 16.1 us: local(): pieces = jnp.sum(lax.all_to_all(partials, 'dp', 0, 0, tiled=False), axis=0)]
    all_to_all x2, waiting for transfers between devices: 17.3 us -> 6.63 us  [spread_copy(): return lax.all_to_all(stacked, axes, 0, 0, tiled=False)]
    all_to_all x1 -> x2, starting transfers between devices: 5.45 us -> 8.65 us  [the longest x1 5 us: local(): pieces = jnp.sum(lax.all_to_all(partials, 'dp', 0, 0, tiled=False), axis=0)]
    all_to_all x2, starting transfers between devices: 14.1 us -> 12.1 us  [spread_copy(): return lax.all_to_all(stacked, axes, 0, 0, tiled=False)]
    reduce_sum x0 -> x2, other arithmetic: none -> 1.99 us  [the longest x1 1.32 us: local(): pieces = jnp.sum(lax.all_to_all(partials, 'dp', 0, 0, tiled=False), axis=0)]
    dot_general x1, matrix products: 2.3 us -> 0.45 us  [local(): lax.dot_general(feat_cols.reshape(n_ctx * tok_rows, n_dp * piece_rows), v...]
    dot_general x2, matrix products: 0.6 us -> 2.07 us  [local(): jnp.einsum('hgqk,qhgd->khd', dscores, rotated_query_rows, preferred_eleme...]
    another operation x1 -> x2, local copies, waits for them, and re-layouts: 0.77 us -> 2.22 us  [the longest x1 1.45 us: local(): lax.all_to_all(feats.reshape(tok_rows, n_dp, n_ctx, piece_rows), 'ctx', 2...]
  transfers between devices with their start and end apart: 9 -> 10, of which waited for: 3 -> 4; matrix products, arithmetic and copies ran while one was open for 35% -> 36% of each run, Pallas kernels for 0% -> 0%
where the time goes in v5:
time: 115 us; the launch traced here: 114 us
  starting transfers between devices  33.3 us (29%)
  waiting for transfers between devices  24.5 us (21%)
  local copies, waits for them, and re-layouts  21.6 us (19%)
  other arithmetic  19.5 us (17%)
  matrix products  13.2 us (11%)
  between operations  1.99 us (2%)
    all_to_all x1, waiting for transfers between devices, local(): pieces = jnp.sum(lax.all_to_all(partials, 'dp', 0, 0, tiled=False), axis=0)  16.1 us
    all_to_all x2, starting transfers between devices, spread_copy(): return lax.all_to_all(stacked, axes, 0, 0, tiled=False)  12.1 us
    ppermute x3, starting transfers between devices, shifted(): return lax.ppermute(array, axis, pairs)  8.08 us
    all_to_all x2, waiting for transfers between devices, spread_copy(): return lax.all_to_all(stacked, axes, 0, 0, tiled=False)  6.63 us
    unnamed x57, local copies, waits for them, and re-layouts  6.13 us
    all_to_all x1, starting transfers between devices, local(): pieces = jnp.sum(lax.all_to_all(partials, 'dp', 0, 0, tiled=False), axis=0)  5 us
    ppermute x3, starting transfers between devices, ring_copy(): lax.ppermute(array, axis, [(i, (i + step) % peers) for i in range(peers)])  4.55 us
    concatenate x2, local copies, waits for them, and re-layouts, rotate(): jnp.concatenate([-vectors[..., half:], vectors[..., :half]], axis=-1)  3.72 us
  transfers between devices with their start and end apart: 10, of which 4 were waited for; matrix products, arithmetic and copies ran while one was open for 36% of the time, Pallas kernels for 0%

profile of v5, /device:TPU:0, one launch (start us, length us, event | category | flops | bytes accessed | tf_op | source)
XLA Modules:
  0.0 114.0 jit_solution(3784307507725175390)
XLA Ops:
  0.7 0.8 copy.209
  3.3 0.7 fusion.46
  4.8 5.5 %collective-permute-start = (bf16[2,128,2,128]{3,1,2,0:T(8,128)(2,1)}, bf16[2,128,2,128]{3,1,2,0:T(8,128)(2,1)}, u32[]{:S(2)}, u32[]{:S(2)}) collective-permute-start(bf16[2,128,2,128]{3,1,2,0:T(8,128)(2,1)} %pad_maximum_fusion), channel_id=1, source_target_pairs={{0,8},{8,16},{16,24},{1,9},{9,17},{17,25},{2,10},{10,18},{18,26},{... | collective-permute-start | bytes 393224 | tf_op jit(solution)/shard_map/ppermute | solution.py:24
  11.0 1.4 %copy.243 = bf16[1,128,4,4,256]{4,2,1,0,3:T(4,128)(2,1)} copy(bf16[1,128,4,4,256]{1,4,3,2,0:T(8,128)(2,1)S(1)} %bitcast.171) | data formatting | bytes 2097152 | tf_op jit(solution)/shard_map/broadcast_in_dim;reshape;squeeze | solution.py:217
  12.4 3.6 %all-to-all-start.1 = ((bf16[1,128,4,4,256]{4,2,1,0,3:T(4,128)(2,1)}), bf16[1,128,4,4,256]{4,2,1,0,3:T(4,128)(2,1)S(1)}, u32[]{:S(2)}, u32[]{:S(2)}) async-start(bf16[1,128,4,4,256]{4,2,1,0,3:T(4,128)(2,1)} %copy.243), calls=%async_computation.1 | async-start | bytes 2097152 | tf_op jit(solution)/shard_map/all_to_all | solution.py:217
  16.7 0.7 copy.210
  17.5 1.1 convert_bitcast_fusion.1
  18.6 1.6 %copy.211 = f32[128,2,8,128]{0,3,2,1:T(8,128)S(1)} copy(f32[128,2,8,128]{3,2,1,0:T(8,128)} %get-tuple-element.54) | data formatting | bytes 2097152 | tf_op jit(solution)/shard_map/convert_element_type | solution.py:126
  20.2 1.7 %fusion.22 = (f32[128,2,8,64]{3,2,1,0:T(8,128)}, f32[128,2,8,64]{3,2,1,0:T(8,128)}) fusion(f32[128,16,128]{2,1,0:T(8,128)S(1)} %get-tuple-element.55), kind=kLoop, calls=%fused_computation.41 | loop fusion | flops 131072 | bytes 2097152 | tf_op jit(solution)/shard_map/concatenate | solution.py:77
  21.8 2.5 %copy.212 = f32[128,2,8,64]{0,3,2,1:T(8,128)} copy(f32[128,2,8,64]{3,2,1,0:T(8,128)} %get-tuple-element.52) | data formatting | bytes 1048576 | tf_op jit(solution)/shard_map/concatenate | solution.py:77
  24.3 1.2 %copy.213 = f32[128,2,8,64]{0,3,2,1:T(8,128)} copy(f32[128,2,8,64]{3,2,1,0:T(8,128)S(1)} %copy-done.3) | data formatting | bytes 1048576 | tf_op jit(solution)/shard_map/concatenate | solution.py:77
  25.5 1.1 fusion.41
  27.5 1.2 %fusion.24 = bf16[128,2,8,128]{0,3,2,1:T(8,128)(2,1)S(1)} fusion(f32[128,2,8,64]{0,3,2,1:T(8,128)} %copy.213, f32[128,2,8,64]{0,3,2,1:T(8,128)S(1)} %copy-done.7, f32[128,2,8,128]{0,3,2,1:T(8,128)S(1)} %copy.211, f32[128,128]{0,1:T(8,128)S(1)} %copy.214, f32[128,128]{0,1:T(8,128)} %copy.210), kind=kLoop, calls=%fused_computation.44 | loop fusion | flops 1310720 | bytes 2752512 | tf_op jit(solution)/shard_map/convert_element_type | solution.py:126
  29.7 1.2 %copy.238 = bf16[128,2,8,128]{0,3,2,1:T(8,128)(2,1)} copy(bf16[128,2,8,128]{3,2,1,0:T(8,128)(2,1)S(1)} %bitcast.172) | data formatting | bytes 1048576 | tf_op jit(solution)/shard_map/reshape;squeeze | solution.py:129
  31.0 1.1 fusion.56
  32.5 1.0 copy-done.16
  33.5 1.0 fusion.18
  34.5 1.3 %collective-permute-start.2 = (bf16[128,2,128]{2,0,1:T(8,128)(2,1)}, bf16[128,2,128]{2,0,1:T(8,128)(2,1)}, u32[]{:S(2)}, u32[]{:S(2)}) collective-permute-start(bf16[128,2,128]{2,0,1:T(8,128)(2,1)} %fusion.18), channel_id=1, source_target_pairs={{8,0},{16,8},{24,16},{9,1},{17,9},{25,17},{10,2},{18,10},{26,18},{... | collective-permute-start | bytes 196616 | tf_op jit(solution)/shard_map/ppermute | solution.py:24
  36.3 1.2 %fusion.3 = f32[2,8,128,128]{3,2,1,0:T(8,128)S(1)} fusion(f32[128,2,8,128]{3,0,2,1:T(8,128)S(1)} %convolution_bitcast_fusion.2, bf16[2,128,2,128]{3,1,2,0:T(8,128)(2,1)} %collective-permute-done, f32[2,8,128,128]{2,3,1,0:T(8,128)S(1)} %get-tuple-element.69, f32[2,8,128]{2,1,0:T(8,128)S(1)} %add.132, f32[2,8,128]{2,1,0:T(8,128)S(1)} %max.8, ...), kind=kOutput, calls=%fused_computation.8 | convolution fusion | flops 68419584 | bytes 3244032 | tf_op jit(solution)/shard_map/hgqk,khd->qhgd/dot_general | solution.py:169
  37.5 0.8 multiply_reduce_fusion
  38.4 1.6 %fusion.12 = bf16[2,8,128,128]{2,3,1,0:T(8,128)(2,1)S(1)} fusion(bf16[128,2,8,128]{0,3,2,1:T(8,128)(2,1)} %copy.238, f32[2,8,128]{2,1,0:T(8,128)S(1)} %copy.269, bf16[128,2,128,1]{2,1,0,3:T(2,128)(2,1)S(1)} %bitcast.177, f32[2,8,128]{2,1,0:T(8,128)S(1)} %add.132, f32[2,8,128,128]{2,3,1,0:T(8,128)S(1)} %get-tuple-element.67, f32[2,8,128]{2,1,0:T(8,128)S(1)} %max.8, ...), kind=kOutput, calls=%fused_computation.22 | convolution fusion | flops 68681728 | bytes 2203648 | tf_op jit(solution)/shard_map/qhgd,khd->hgqk/dot_general | solution.py:186
  40.0 1.3 %fusion.11 = bf16[2,8,128,128]{2,3,1,0:T(8,128)(2,1)S(1)} fusion(bf16[128,2,8,128]{0,3,2,1:T(8,128)(2,1)S(1)} %copy-done.17, f32[2,8,128]{2,1,0:T(8,128)S(1)} %copy.269, bf16[2,128,2,128]{3,1,2,0:T(8,128)(2,1)} %collective-permute-done, f32[2,8,128]{2,1,0:T(8,128)S(1)} %add.132, f32[2,8,128,128]{2,3,1,0:T(8,128)S(1)} %copy-done.1, ...), kind=kOutput, calls=%fused_computation.21 | convolution fusion | flops 68681728 | bytes 2203648 | tf_op jit(solution)/shard_map/qhgd,khd->hgqk/dot_general | solution.py:186
  41.3 0.9 fusion.19
  42.2 1.3 %collective-permute-start.1 = (bf16[128,2,128]{2,0,1:T(8,128)(2,1)}, bf16[128,2,128]{2,0,1:T(8,128)(2,1)}, u32[]{:S(2)}, u32[]{:S(2)}) collective-permute-start(bf16[128,2,128]{2,0,1:T(8,128)(2,1)} %fusion.19), channel_id=1, source_target_pairs={{8,0},{16,8},{24,16},{9,1},{17,9},{25,17},{10,2},{18,10},{26,18},{... | collective-permute-start | bytes 196616 | tf_op jit(solution)/shard_map/ppermute | solution.py:24
  43.5 1.2 %add_convert_fusion = bf16[128,2,128]{2,0,1:T(8,128)(2,1)S(1)} fusion(bf16[128,2,128]{2,0,1:T(8,128)(2,1)} %collective-permute-done.2, bf16[128,2,8,128]{0,3,2,1:T(8,128)(2,1)S(1)} %copy-done.17, f32[2,8,128]{2,1,0:T(8,128)S(1)} %add.132, f32[2,8,128,128]{2,3,1,0:T(8,128)S(1)} %get-tuple-element.67, f32[2,8,128]{2,1,0:T(8,128)S(1)} %max.8, ...), kind=kOutput, calls=%fused_computation.75 | convolution fusion | flops 68255744 | bytes 1736704 | tf_op jit(solution)/shard_map/hgqk,qhgd->khd/dot_general | solution.py:175
  45.4 0.7 broadcast_in_dim.80
  46.2 8.1 %all-to-all-start = ((bf16[4,128,256]{2,1,0:T(8,128)(2,1)}), bf16[4,128,256]{2,1,0:T(8,128)(2,1)S(1)}, u32[]{:S(2)}, u32[]{:S(2)}) async-start(bf16[4,128,256]{2,1,0:T(8,128)(2,1)} %broadcast_in_dim.80), calls=%async_computation | async-start | bytes 524288 | tf_op jit(solution)/shard_map/all_to_all | solution.py:32
  54.3 1.3 %fusion.57 = f32[2,128,8,128]{3,1,2,0:T(8,128)} fusion(bf16[128,2,128,1]{2,0,3,1:T(8,128)(2,1)S(1)} %copy-done.13, bf16[2,8,128,128]{2,3,1,0:T(8,128)(2,1)S(1)} %fusion.12), kind=kOutput, calls=%fused_computation.111 | convolution fusion | flops 67108864 | bytes 1638400 | tf_op jit(solution)/shard_map/hgqk,khd->qhgd/dot_general | solution.py:191
  55.9 3.8 %all-to-all-done = bf16[4,128,256]{2,1,0:T(8,128)(2,1)S(1)} async-done(((bf16[4,128,256]{2,1,0:T(8,128)(2,1)}), bf16[4,128,256]{2,1,0:T(8,128)(2,1)S(1)}, u32[]{:S(2)}, u32[]{:S(2)}) %all-to-all-start) | async-done | bytes 262176 | tf_op jit(solution)/shard_map/all_to_all | solution.py:32
  60.1 1.1 copy.309
  61.2 5.0 %all-to-all-start.2 = ((f32[4,256,256]{1,2,0:T(8,128)}), f32[4,256,256]{1,2,0:T(8,128)}, u32[]{:S(2)}, u32[]{:S(2)}) async-start(f32[4,256,256]{1,2,0:T(8,128)} %bitcast.165), calls=%async_computation.2 | async-start | bytes 2097152 | tf_op jit(solution)/shard_map/all_to_all | solution.py:227
  66.2 1.2 %fusion.6 = f32[2,128,8,128]{3,1,2,0:T(8,128)S(1)} fusion(f32[2,128,8,128]{3,1,2,0:T(8,128)S(1)} %copy-done.2, bf16[2,8,128,128]{2,3,1,0:T(8,128)(2,1)S(1)} %copy-done.9, bf16[2,128,2,128]{3,1,2,0:T(8,128)(2,1)} %collective-permute-done), kind=kOutput, calls=%fused_computation.12 | convolution fusion | flops 67633152 | bytes 2686976 | tf_op jit(solution)/shard_map/hgqk,khd->qhgd/dot_general | solution.py:191
  67.4 1.4 %copy.231 = f32[128,16,128]{2,1,0:T(8,128)} copy(f32[128,16,128]{0,2,1:T(8,128)S(1)} %bitcast.166) | data formatting | bytes 2097152 | tf_op jit(solution)/shard_map/reshape | solution.py:207
  69.3 1.3 %broadcast_multiply_fusion = f32[128,16,128]{2,1,0:T(8,128)S(1)} fusion(f32[128,16,128]{2,1,0:T(8,128)} %copy.231, f32[128,128]{1,0:T(8,128)S(1)} %pad_maximum_fusion.2), kind=kLoop, calls=%fused_computation.56 | loop fusion | flops 262144 | bytes 2162688 | tf_op jit(solution)/shard_map/mul | solution.py:83
  71.0 1.2 %fusion.25 = bf16[1,128,16,128]{3,2,1,0:T(8,128)(2,1)} fusion(f32[1,128,16,64]{3,2,1,0:T(8,128)S(1)} %get-tuple-element.51, f32[1,128,16,64]{3,2,1,0:T(8,128)S(1)} %get-tuple-element.50, f32[1,128,16,128]{3,2,1,0:T(8,128)S(1)} %copy.230, f32[128,128]{1,0:T(8,128)S(1)} %pad_maximum_fusion.1), kind=kLoop, calls=%fused_computation.46 | loop fusion | flops 1048576 | bytes 2686976 | tf_op jit(solution)/shard_map/convert_element_type | solution.py:207
  72.2 1.1 fusion.39
  73.4 16.1 %all-to-all-done.2 = f32[4,256,256]{1,2,0:T(8,128)} async-done(((f32[4,256,256]{1,2,0:T(8,128)}), f32[4,256,256]{1,2,0:T(8,128)}, u32[]{:S(2)}, u32[]{:S(2)}) %all-to-all-start.2) | async-done | bytes 1048608 | tf_op jit(solution)/shard_map/all_to_all | solution.py:227
  89.5 1.3 %reduce_sum.71 = f32[256,256]{0,1:T(8,128)S(1)} reduce(f32[4,256,256]{1,2,0:T(8,128)} %all-to-all-done.2, f32[]{:T(128)} %constant.70.clone.1), dimensions={0}, to_apply=%region_8.9 | reduce | flops 196608 | bytes 1310724 | tf_op jit(solution)/shard_map/reduce_sum | solution.py:227
  91.5 1.6 %collective-permute-start.4 = (f32[256,256]{0,1:T(8,128)S(1)}, f32[256,256]{0,1:T(8,128)S(1)}, u32[]{:S(2)}, u32[]{:S(2)}) collective-permute-start(f32[256,256]{0,1:T(8,128)S(1)} %reduce_sum.71), channel_id=1, source_target_pairs={{0,16},{8,24},{16,0},{24,8},{1,17},{9,25},{17,1},{25,9},{2,18},{10... | collective-permute-start | bytes 786440 | tf_op jit(solution)/shard_map/ppermute | solution.py:42
  93.3 1.3 %broadcast_in_dim_broadcast_in_dim_broadcast_in_dim.3 = f32[32,8,128]{2,1,0:T(8,128)} broadcast(f32[]{:T(128)} %multiply_reduce_fusion.1), dimensions={} | broadcast | bytes 131076 | tf_op jit(solution)/shard_map/broadcast_in_dim;broadcast_in_dim;broadcast_in_dim | solution.py:31
  94.6 3.9 %all-to-all-start.3 = ((f32[32,8,128]{2,1,0:T(8,128)}), f32[32,8,128]{2,1,0:T(8,128)S(1)}, u32[]{:S(2)}, u32[]{:S(2)}) async-start(f32[32,8,128]{2,1,0:T(8,128)} %broadcast_in_dim_broadcast_in_dim_broadcast_in_dim.3), calls=%async_computation.3 | async-start | bytes 262144 | tf_op jit(solution)/shard_map/all_to_all | solution.py:32
  98.6 1.0 fusion.40
  99.6 0.7 copy.252
  100.3 0.7 copy.251
  101.1 2.7 %collective-permute-start.5 = (f32[256,256]{0,1:T(8,128)S(1)}, f32[256,256]{0,1:T(8,128)S(1)}, u32[]{:S(2)}, u32[]{:S(2)}) collective-permute-start(f32[256,256]{0,1:T(8,128)S(1)} %reduce_sum.71), channel_id=1, source_target_pairs={{0,24},{8,0},{16,8},{24,16},{1,25},{9,1},{17,9},{25,17},{2,26},{10... | collective-permute-start | bytes 786440 | tf_op jit(solution)/shard_map/ppermute | solution.py:42
  103.9 2.8 %all-to-all-done.3 = f32[32,8,128]{2,1,0:T(8,128)S(1)} async-done(((f32[32,8,128]{2,1,0:T(8,128)}), f32[32,8,128]{2,1,0:T(8,128)S(1)}, u32[]{:S(2)}, u32[]{:S(2)}) %all-to-all-start.3) | async-done | bytes 131104 | tf_op jit(solution)/shard_map/all_to_all | solution.py:32
  108.4 1.7 %collective-permute-done.5 = f32[256,256]{0,1:T(8,128)S(1)} collective-permute-done((f32[256,256]{0,1:T(8,128)S(1)}, f32[256,256]{0,1:T(8,128)S(1)}, u32[]{:S(2)}, u32[]{:S(2)}) %collective-permute-start.5) | collective-permute-done | bytes 262176 | tf_op jit(solution)/shard_map/ppermute | solution.py:42
  110.3 3.7 %multiply_subtract_fusion = (f32[1024,256]{1,0:T(8,128)}, f32[1024,256]{1,0:T(8,128)}, f32[1024,256]{1,0:T(8,128)}) fusion(f32[1024,256]{1,0:T(8,128)S(1)} %copy-done.11, f32[1024,256]{1,0:T(8,128)S(1)} %constant_dynamic-update-slice_fusion, f32[]{:T(128)S(6)} %min_shard_map.3, f32[1024,256]{1,0:T(8,128)} %param.20, f32[1024,256]{1,0:T(8,128)} %param.21), kind=kLoop, calls=%fused_computation.48 | loop fusion | flops 4194304 | bytes 7340036 | tf_op jit(solution)/shard_map/sub | solution.py:94
  (99 shorter events, 11.2 us)
Async XLA Ops:
  0.6 1.1 copy-start.20
  1.7 0.7 copy-start.24
  1.8 0.7 copy-start.25
  2.4 0.8 copy-start.14
  2.7 7.5 %copy-start.10 = (bf16[1,128,4096]{2,1,0:T(8,128)(2,1)S(1)}, bf16[1,128,4096]{2,1,0:T(8,128)(2,1)}, u32[]{:S(2)}) copy-start(bf16[1,128,4096]{2,1,0:T(8,128)(2,1)} %param.15) | copy-start | bytes 3145732
  4.8 26.2 %collective-permute-start = (bf16[2,128,2,128]{3,1,2,0:T(8,128)(2,1)}, bf16[2,128,2,128]{3,1,2,0:T(8,128)(2,1)}, u32[]{:S(2)}, u32[]{:S(2)}) collective-permute-start(bf16[2,128,2,128]{3,1,2,0:T(8,128)(2,1)} %pad_maximum_fusion), channel_id=1, source_target_pairs={{0,8},{8,16},{16,24},{1,9},{9,17},{17,25},{2,10},{10,18},{18,26},{... | collective-permute-start | bytes 393224 | tf_op jit(solution)/shard_map/ppermute | solution.py:24
  12.4 5.0 %copy-start.15 = (bf16[1,128,16,128]{3,2,1,0:T(8,128)(2,1)S(1)}, bf16[1,128,16,128]{3,2,1,0:T(8,128)(2,1)}, u32[]{:S(2)}) copy-start(bf16[1,128,16,128]{3,2,1,0:T(8,128)(2,1)} %param.11) | copy-start | bytes 1572868
  12.4 33.0 %all-to-all-start.1 = ((bf16[1,128,4,4,256]{4,2,1,0,3:T(4,128)(2,1)}), bf16[1,128,4,4,256]{4,2,1,0,3:T(4,128)(2,1)S(1)}, u32[]{:S(2)}, u32[]{:S(2)}) async-start(bf16[1,128,4,4,256]{4,2,1,0,3:T(4,128)(2,1)} %copy.243), calls=%async_computation.1 | async-start | bytes 2097152 | tf_op jit(solution)/shard_map/all_to_all | solution.py:217
  21.8 2.5 %copy-start.3 = (f32[128,2,8,64]{3,2,1,0:T(8,128)S(1)}, f32[128,2,8,64]{3,2,1,0:T(8,128)}, u32[]{:S(2)}) copy-start(f32[128,2,8,64]{3,2,1,0:T(8,128)} %get-tuple-element.53) | copy-start | bytes 1572868
  25.5 1.9 %copy-start.7 = (f32[128,2,8,64]{0,3,2,1:T(8,128)S(1)}, f32[128,2,8,64]{0,3,2,1:T(8,128)}, u32[]{:S(2)}) copy-start(f32[128,2,8,64]{0,3,2,1:T(8,128)} %copy.212) | copy-start | bytes 1572868
  26.6 2.1 %copy-start.12 = (bf16[128,2,128,1]{2,0,3,1:T(8,128)(2,1)}, bf16[128,2,128,1]{2,0,3,1:T(8,128)(2,1)S(1)}, u32[]{:S(2)}) copy-start(bf16[128,2,128,1]{2,0,3,1:T(8,128)(2,1)S(1)} %fusion.41) | copy-start | bytes 196612
  26.6 0.6 copy-start.22
  26.6 0.7 copy-start.23
  28.7 1.0 copy-start.4
  32.1 4.2 %copy-start = (f32[2,8,128,128]{2,3,1,0:T(8,128)}, f32[2,8,128,128]{2,3,1,0:T(8,128)S(1)}, u32[]{:S(2)}) copy-start(f32[2,8,128,128]{2,3,1,0:T(8,128)S(1)} %get-tuple-element.69) | copy-start | bytes 3145732
  32.1 1.4 %copy-start.16 = (bf16[128,2,8,128]{0,3,2,1:T(8,128)(2,1)S(1)}, bf16[128,2,8,128]{0,3,2,1:T(8,128)(2,1)}, u32[]{:S(2)}) copy-start(bf16[128,2,8,128]{0,3,2,1:T(8,128)(2,1)} %copy.238) | copy-start | bytes 1572868
  33.5 2.3 %copy-start.21 = (bf16[1,128,2,128]{3,2,1,0:T(2,128)(2,1)S(1)}, bf16[1,128,2,128]{3,2,1,0:T(2,128)(2,1)}, u32[]{:S(2)}) copy-start(bf16[1,128,2,128]{3,2,1,0:T(2,128)(2,1)} %param.13) | copy-start | bytes 196612
  34.5 9.0 %collective-permute-start.2 = (bf16[128,2,128]{2,0,1:T(8,128)(2,1)}, bf16[128,2,128]{2,0,1:T(8,128)(2,1)}, u32[]{:S(2)}, u32[]{:S(2)}) collective-permute-start(bf16[128,2,128]{2,0,1:T(8,128)(2,1)} %fusion.18), channel_id=1, source_target_pairs={{8,0},{16,8},{24,16},{9,1},{17,9},{25,17},{10,2},{18,10},{26,18},{... | collective-permute-start | bytes 196616 | tf_op jit(solution)/shard_map/ppermute | solution.py:24
  38.4 1.6 %copy-start.1 = (f32[2,8,128,128]{2,3,1,0:T(8,128)S(1)}, f32[2,8,128,128]{2,3,1,0:T(8,128)}, u32[]{:S(2)}) copy-start(f32[2,8,128,128]{2,3,1,0:T(8,128)} %copy-done) | copy-start | bytes 3145732
  38.4 1.6 %copy-start.17 = (bf16[128,2,8,128]{0,3,2,1:T(8,128)(2,1)S(1)}, bf16[128,2,8,128]{0,3,2,1:T(8,128)(2,1)}, u32[]{:S(2)}) copy-start(bf16[128,2,8,128]{0,3,2,1:T(8,128)(2,1)} %copy.238) | copy-start | bytes 1572868
  39.9 14.4 %copy-start.5 = (bf16[2,8,128,128]{2,3,1,0:T(8,128)(2,1)}, bf16[2,8,128,128]{2,3,1,0:T(8,128)(2,1)S(1)}, u32[]{:S(2)}) copy-start(bf16[2,8,128,128]{2,3,1,0:T(8,128)(2,1)S(1)} %fusion.12) | copy-start | bytes 1572868
  41.3 0.9 copy-start.8
  42.2 30.0 %collective-permute-start.1 = (bf16[128,2,128]{2,0,1:T(8,128)(2,1)}, bf16[128,2,128]{2,0,1:T(8,128)(2,1)}, u32[]{:S(2)}, u32[]{:S(2)}) collective-permute-start(bf16[128,2,128]{2,0,1:T(8,128)(2,1)} %fusion.19), channel_id=1, source_target_pairs={{8,0},{16,8},{24,16},{9,1},{17,9},{25,17},{10,2},{18,10},{26,18},{... | collective-permute-start | bytes 196616 | tf_op jit(solution)/shard_map/ppermute | solution.py:24
  44.7 0.6 copy-start.18
  46.2 8.2 %copy-start.13 = (bf16[128,2,128,1]{2,0,3,1:T(8,128)(2,1)S(1)}, bf16[128,2,128,1]{2,0,3,1:T(8,128)(2,1)}, u32[]{:S(2)}) copy-start(bf16[128,2,128,1]{2,0,3,1:T(8,128)(2,1)} %copy-done.12) | copy-start | bytes 196612
  46.2 13.5 %all-to-all-start = ((bf16[4,128,256]{2,1,0:T(8,128)(2,1)}), bf16[4,128,256]{2,1,0:T(8,128)(2,1)S(1)}, u32[]{:S(2)}, u32[]{:S(2)}) async-start(bf16[4,128,256]{2,1,0:T(8,128)(2,1)} %broadcast_in_dim.80), calls=%async_computation | async-start | bytes 524288 | tf_op jit(solution)/shard_map/all_to_all | solution.py:32
  61.2 5.0 %copy-start.2 = (f32[2,128,8,128]{3,1,2,0:T(8,128)S(1)}, f32[2,128,8,128]{3,1,2,0:T(8,128)}, u32[]{:S(2)}) copy-start(f32[2,128,8,128]{3,1,2,0:T(8,128)} %fusion.57) | copy-start | bytes 3145732
  61.2 5.0 %copy-start.9 = (bf16[2,8,128,128]{2,3,1,0:T(8,128)(2,1)S(1)}, bf16[2,8,128,128]{2,3,1,0:T(8,128)(2,1)}, u32[]{:S(2)}) copy-start(bf16[2,8,128,128]{2,3,1,0:T(8,128)(2,1)} %copy-done.8) | copy-start | bytes 1572868
  61.2 28.3 %all-to-all-start.2 = ((f32[4,256,256]{1,2,0:T(8,128)}), f32[4,256,256]{1,2,0:T(8,128)}, u32[]{:S(2)}, u32[]{:S(2)}) async-start(f32[4,256,256]{1,2,0:T(8,128)} %bitcast.165), calls=%async_computation.2 | async-start | bytes 2097152 | tf_op jit(solution)/shard_map/all_to_all | solution.py:227
  71.0 1.2 %copy-start.6 = (bf16[2,8,128,128]{2,3,1,0:T(8,128)(2,1)S(1)}, bf16[2,8,128,128]{2,3,1,0:T(8,128)(2,1)}, u32[]{:S(2)}) copy-start(bf16[2,8,128,128]{2,3,1,0:T(8,128)(2,1)} %copy-done.5) | copy-start | bytes 1572868
  91.5 16.6 %collective-permute-start.4 = (f32[256,256]{0,1:T(8,128)S(1)}, f32[256,256]{0,1:T(8,128)S(1)}, u32[]{:S(2)}, u32[]{:S(2)}) collective-permute-start(f32[256,256]{0,1:T(8,128)S(1)} %reduce_sum.71), channel_id=1, source_target_pairs={{0,16},{8,24},{16,0},{24,8},{1,17},{9,25},{17,1},{25,9},{2,18},{10... | collective-permute-start | bytes 786440 | tf_op jit(solution)/shard_map/ppermute | solution.py:42
  93.1 15.1 %collective-permute-start.3 = (f32[256,256]{0,1:T(8,128)S(1)}, f32[256,256]{0,1:T(8,128)S(1)}, u32[]{:S(2)}, u32[]{:S(2)}) collective-permute-start(f32[256,256]{0,1:T(8,128)S(1)} %reduce_sum.71), channel_id=1, source_target_pairs={{0,8},{8,16},{16,24},{24,0},{1,9},{9,17},{17,25},{25,1},{2,10},{10... | collective-permute-start | bytes 786440 | tf_op jit(solution)/shard_map/ppermute | solution.py:42
  94.6 12.1 %all-to-all-start.3 = ((f32[32,8,128]{2,1,0:T(8,128)}), f32[32,8,128]{2,1,0:T(8,128)S(1)}, u32[]{:S(2)}, u32[]{:S(2)}) async-start(f32[32,8,128]{2,1,0:T(8,128)} %broadcast_in_dim_broadcast_in_dim_broadcast_in_dim.3), calls=%async_computation.3 | async-start | bytes 262144 | tf_op jit(solution)/shard_map/all_to_all | solution.py:32
  98.6 1.0 copy-start.19
  101.1 9.1 %collective-permute-start.5 = (f32[256,256]{0,1:T(8,128)S(1)}, f32[256,256]{0,1:T(8,128)S(1)}, u32[]{:S(2)}, u32[]{:S(2)}) collective-permute-start(f32[256,256]{0,1:T(8,128)S(1)} %reduce_sum.71), channel_id=1, source_target_pairs={{0,24},{8,0},{16,8},{24,16},{1,25},{9,1},{17,9},{25,17},{2,26},{10... | collective-permute-start | bytes 786440 | tf_op jit(solution)/shard_map/ppermute | solution.py:42
  108.3 2.0 %copy-start.11 = (f32[1024,256]{1,0:T(8,128)S(1)}, f32[1024,256]{1,0:T(8,128)}, u32[]{:S(2)}) copy-start(f32[1024,256]{1,0:T(8,128)} %param.19) | copy-start | bytes 3145732

commit v6 on v4

--- a/solution.py
+++ b/solution.py
@@ -214,11 +214,15 @@
     own_rows = param.shape[0]
     n_dp = lax.axis_size("dp")
     piece_rows = own_rows // n_ctx
-    spread = ("dp", "ctx")
+    spread = ("ctx", "dp")
+    by_place = feats.reshape(tok_rows, n_dp, n_ctx, piece_rows).transpose(0, 2, 1, 3)
     feat_cols = lax.all_to_all(
-        feats.reshape(tok_rows, n_dp * n_ctx, piece_rows), spread, 1, 0, tiled=False
-    )
-    value_rows = spread_copy(value_flat, spread)
+        by_place.reshape(tok_rows, n_dp * n_ctx, piece_rows), spread, 1, 0, tiled=False
+    )
+    if n_dp * n_ctx <= 16:
+        value_rows = ring_copy(value_flat, spread)
+    else:
+        value_rows = spread_copy(value_flat, spread)
     pieces = lax.dot_general(
         feat_cols.reshape(-1, piece_rows),
         value_rows.reshape(-1, kv_count * head_dim),

time: 106 us -> 113 us (1.066)
  starting transfers between devices: 32.9 us -> 56.5 us
  waiting for transfers between devices: 18.4 us -> 6.53 us
  local copies, waits for them, and re-layouts: 21.6 us -> 18 us
    ppermute x3 -> x18, starting transfers between devices: 5.24 us -> 36.2 us  [ring_copy(): lax.ppermute(array, axis, [(i, (i + step) % peers) for i in range(peers)])]
    all_to_all x2 -> x1, waiting for transfers between devices: 17.3 us -> 3.7 us  [spread_copy(): return lax.all_to_all(stacked, axes, 0, 0, tiled=False)]
    all_to_all x2 -> x1, starting transfers between devices: 14.1 us -> 6.7 us  [spread_copy(): return lax.all_to_all(stacked, axes, 0, 0, tiled=False)]
    ppermute x3 -> x18, waiting for transfers between devices: 1.05 us -> 2.82 us  [ring_copy(): lax.ppermute(array, axis, [(i, (i + step) % peers) for i in range(peers)])]
    convert_element_type x1, other arithmetic: 1.16 us -> 2.79 us  [local(): unrotate(query_grad.reshape(tok_rows, head_count, head_dim), cosine, sine)]
    transpose x0 -> x1, local copies, waits for them, and re-layouts: none -> 1.32 us  [local(): feats.reshape(tok_rows, n_dp, n_ctx, piece_rows).transpose(0, 2, 1, 3)]
    broadcast_in_dim x2 -> x0, local copies, waits for them, and re-layouts: 1.3 us -> none  [spread_copy(): stacked = jnp.broadcast_to(array[None], (peers,) + array.shape)]
    concatenate x1, other arithmetic: 0.36 us -> 1.65 us  [unrotate(): turned = jnp.concatenate([scaled[..., half:], -scaled[..., :half]], axis=-1)]
  transfers between devices with their start and end apart: 9 -> 23, of which waited for: 3 -> 3; matrix products, arithmetic and copies ran while one was open for 35% -> 30% of each run, Pallas kernels for 0% -> 0%
where the time goes in v6:
time: 113 us; the launch traced here: 112 us
  starting transfers between devices  56.5 us (50%)
  local copies, waits for them, and re-layouts  18 us (16%)
  other arithmetic  16.2 us (14%)
  matrix products  12.4 us (11%)
  waiting for transfers between devices  6.53 us (6%)
  between operations  2.42 us (2%)
    ppermute x18, starting transfers between devices, ring_copy(): lax.ppermute(array, axis, [(i, (i + step) % peers) for i in range(peers)])  36.2 us
    ppermute x3, starting transfers between devices, shifted(): return lax.ppermute(array, axis, pairs)  8.09 us
    unnamed x44, local copies, waits for them, and re-layouts  6.94 us
    all_to_all x1, starting transfers between devices, spread_copy(): return lax.all_to_all(stacked, axes, 0, 0, tiled=False)  6.7 us
    all_to_all x1, starting transfers between devices, local(): lax.all_to_all(by_place.reshape(tok_rows, n_dp * n_ctx, piece_rows), spre...  5.49 us
    sub x1, other arithmetic, adam_update(): new_param = param - LEARN_RATE * (step_size + DECAY_RATE * param)  3.71 us
    all_to_all x1, waiting for transfers between devices, spread_copy(): return lax.all_to_all(stacked, axes, 0, 0, tiled=False)  3.7 us
    concatenate x2, local copies, waits for them, and re-layouts, rotate(): jnp.concatenate([-vectors[..., half:], vectors[..., :half]], axis=-1)  2.92 us
  transfers between devices with their start and end apart: 23, of which 3 were waited for; matrix products, arithmetic and copies ran while one was open for 30% of the time, Pallas kernels for 0%

profile of v6, /device:TPU:0, one launch (start us, length us, event | category | flops | bytes accessed | tf_op | source)
XLA Modules:
  0.0 112.1 jit_solution(16761842188983017948)
XLA Ops:
  3.6 0.7 fusion.46
  4.5 0.7 pad_maximum_fusion
  5.2 5.5 %collective-permute-start = (bf16[2,128,2,128]{3,1,2,0:T(8,128)(2,1)}, bf16[2,128,2,128]{3,1,2,0:T(8,128)(2,1)}, u32[]{:S(2)}, u32[]{:S(2)}) collective-permute-start(bf16[2,128,2,128]{3,1,2,0:T(8,128)(2,1)} %pad_maximum_fusion), channel_id=1, source_target_pairs={{0,8},{8,16},{16,24},{1,9},{9,17},{17,25},{2,10},{10,18},{18,26},{... | collective-permute-start | bytes 393224 | tf_op jit(solution)/shard_map/ppermute | solution.py:24
  11.4 1.3 %copy.243 = bf16[128,4,4,256]{3,0,2,1:T(8,128)(2,1)} copy(bf16[128,4,4,256]{0,3,1,2:T(8,128)(2,1)S(1)} %bitcast.167) | data formatting | bytes 2097152 | tf_op jit(solution)/shard_map/transpose | solution.py:218
  12.7 5.5 %all-to-all-start = ((bf16[1,128,16,256]{3,1,0,2:T(8,128)(2,1)}), bf16[1,128,16,256]{3,1,0,2:T(8,128)(2,1)}, u32[]{:S(2)}, u32[]{:S(2)}) async-start(bf16[1,128,16,256]{3,1,0,2:T(8,128)(2,1)} %bitcast.52), calls=%async_computation | async-start | bytes 2097152 | tf_op jit(solution)/shard_map/all_to_all | solution.py:219
  18.7 0.7 copy.211
  19.5 0.7 copy.215
  20.3 1.7 %fusion.22 = (f32[128,2,8,64]{3,2,1,0:T(8,128)}, f32[128,2,8,64]{3,2,1,0:T(8,128)}) fusion(f32[128,16,128]{2,1,0:T(8,128)S(1)} %get-tuple-element.55), kind=kLoop, calls=%fused_computation.41 | loop fusion | flops 131072 | bytes 2097152 | tf_op jit(solution)/shard_map/concatenate | solution.py:77
  22.0 1.7 %copy.213 = f32[128,2,8,64]{0,3,2,1:T(8,128)S(1)} copy(f32[128,2,8,64]{3,2,1,0:T(8,128)} %get-tuple-element.52) | data formatting | bytes 1048576 | tf_op jit(solution)/shard_map/concatenate | solution.py:77
  23.7 1.2 %copy.214 = f32[128,2,8,64]{0,3,2,1:T(8,128)} copy(f32[128,2,8,64]{3,2,1,0:T(8,128)S(1)} %copy-done.2) | data formatting | bytes 1048576 | tf_op jit(solution)/shard_map/concatenate | solution.py:77
  26.8 1.0 fusion.24
  28.5 1.1 copy-done.3
  29.6 1.2 %copy.239 = bf16[128,2,8,128]{0,3,2,1:T(8,128)(2,1)} copy(bf16[128,2,8,128]{3,2,1,0:T(8,128)(2,1)S(1)} %bitcast.168) | data formatting | bytes 1048576 | tf_op jit(solution)/shard_map/reshape;squeeze | solution.py:129
  30.8 1.1 %fusion.56 = (f32[2,8,128]{2,1,0:T(8,128)S(1)}, f32[2,8,128,128]{2,3,1,0:T(8,128)S(1)}) fusion(bf16[128,2,8,128]{0,3,2,1:T(8,128)(2,1)S(1)} %fusion.24, bf16[2,128,2,128]{3,1,2,0:T(8,128)(2,1)} %collective-permute-done, pred[128,128]{0,1:T(8,128)(4,1)S(1)} %get-tuple-element.62), kind=kOutput, calls=%fused_computation.126 | convolution fusion | flops 67893248 | bytes 1662976 | tf_op jit(solution)/shard_map/qhgd,khd->hgqk/dot_general | solution.py:148
  33.0 1.0 fusion.18
  34.0 1.3 %collective-permute-start.2 = (bf16[128,2,128]{2,0,1:T(8,128)(2,1)}, bf16[128,2,128]{2,0,1:T(8,128)(2,1)}, u32[]{:S(2)}, u32[]{:S(2)}) collective-permute-start(bf16[128,2,128]{2,0,1:T(8,128)(2,1)} %fusion.18), channel_id=1, source_target_pairs={{8,0},{16,8},{24,16},{9,1},{17,9},{25,17},{10,2},{18,10},{26,18},{... | collective-permute-start | bytes 196616 | tf_op jit(solution)/shard_map/ppermute | solution.py:24
  35.7 1.2 %fusion.3 = f32[2,8,128,128]{3,2,1,0:T(8,128)S(1)} fusion(f32[128,2,8,128]{3,0,2,1:T(8,128)S(1)} %convolution_bitcast_fusion.2, bf16[2,128,2,128]{3,1,2,0:T(8,128)(2,1)} %collective-permute-done, f32[2,8,128,128]{2,3,1,0:T(8,128)S(1)} %get-tuple-element.69, f32[2,8,128]{2,1,0:T(8,128)S(1)} %add.243, f32[2,8,128]{2,1,0:T(8,128)S(1)} %max.8, ...), kind=kOutput, calls=%fused_computation.8 | convolution fusion | flops 68419584 | bytes 3244032 | tf_op jit(solution)/shard_map/hgqk,khd->qhgd/dot_general | solution.py:169
  36.9 0.8 multiply_reduce_fusion
  37.8 1.5 %fusion.12 = bf16[2,8,128,128]{2,3,1,0:T(8,128)(2,1)S(1)} fusion(bf16[128,2,8,128]{0,3,2,1:T(8,128)(2,1)} %copy.239, f32[2,8,128]{2,1,0:T(8,128)S(1)} %copy.268, bf16[128,2,128,1]{2,1,0,3:T(2,128)(2,1)} %bitcast.186, f32[2,8,128]{2,1,0:T(8,128)S(1)} %add.243, f32[2,8,128,128]{2,3,1,0:T(8,128)S(1)} %get-tuple-element.67, f32[2,8,128]{2,1,0:T(8,128)S(1)} %max.8, ...), kind=kOutput, calls=%fused_computation.22 | convolution fusion | flops 68681728 | bytes 2203648 | tf_op jit(solution)/shard_map/qhgd,khd->hgqk/dot_general | solution.py:186
  39.3 1.2 %fusion.11 = bf16[2,8,128,128]{2,3,1,0:T(8,128)(2,1)S(1)} fusion(bf16[128,2,8,128]{0,3,2,1:T(8,128)(2,1)S(1)} %copy-done.10, f32[2,8,128]{2,1,0:T(8,128)S(1)} %copy.268, bf16[2,128,2,128]{3,1,2,0:T(8,128)(2,1)} %collective-permute-done, f32[2,8,128]{2,1,0:T(8,128)S(1)} %add.243, f32[2,8,128,128]{2,3,1,0:T(8,128)S(1)} %get-tuple-element.69, ...), kind=kOutput, calls=%fused_computation.21 | convolution fusion | flops 68681728 | bytes 2203648 | tf_op jit(solution)/shard_map/qhgd,khd->hgqk/dot_general | solution.py:186
  40.9 1.3 %collective-permute-start.1 = (bf16[128,2,128]{2,0,1:T(8,128)(2,1)S(1)}, bf16[128,2,128]{2,0,1:T(8,128)(2,1)S(1)}, u32[]{:S(2)}, u32[]{:S(2)}) collective-permute-start(bf16[128,2,128]{2,0,1:T(8,128)(2,1)S(1)} %fusion.19), channel_id=1, source_target_pairs={{8,0},{16,8},{24,16},{9,1},{17,9},{25,17},{10,2},{18,10},{26,18},{... | collective-permute-start | bytes 196616 | tf_op jit(solution)/shard_map/ppermute | solution.py:24
  42.5 1.2 %fusion.6 = f32[2,128,8,128]{3,1,2,0:T(8,128)S(1)} fusion(f32[2,128,8,128]{3,1,2,0:T(8,128)S(1)} %fusion.57, bf16[2,8,128,128]{2,3,1,0:T(8,128)(2,1)S(1)} %fusion.11, bf16[2,128,2,128]{3,1,2,0:T(8,128)(2,1)} %collective-permute-done), kind=kOutput, calls=%fused_computation.12 | convolution fusion | flops 67633152 | bytes 2686976 | tf_op jit(solution)/shard_map/hgqk,khd->qhgd/dot_general | solution.py:191
  44.3 1.7 %slice_bitcast_fusion = (f32[1,128,16,64]{3,2,1,0:T(8,128)}, f32[1,128,16,64]{3,2,1,0:T(8,128)}) fusion(f32[128,16,128]{2,1,0:T(8,128)S(1)} %broadcast_multiply_fusion), kind=kLoop, calls=%fused_computation.38 | loop fusion | flops 131072 | bytes 2097152 | tf_op jit(solution)/shard_map/concatenate | solution.py:84
  46.5 2.8 %fusion.25 = bf16[1,128,16,128]{3,2,1,0:T(8,128)(2,1)} fusion(f32[1,128,16,64]{3,2,1,0:T(8,128)} %get-tuple-element.51, f32[1,128,16,64]{3,2,1,0:T(8,128)} %get-tuple-element.50, f32[1,128,16,128]{3,2,1,0:T(8,128)S(1)} %copy.231, f32[128,128]{1,0:T(8,128)S(1)} %pad_maximum_fusion.1), kind=kLoop, calls=%fused_computation.46 | loop fusion | flops 1048576 | bytes 2686976 | tf_op jit(solution)/shard_map/convert_element_type | solution.py:207
  49.3 1.2 %add_convert_fusion = bf16[128,2,128]{2,0,1:T(8,128)(2,1)S(1)} fusion(bf16[128,2,128]{2,0,1:T(8,128)(2,1)} %collective-permute-done.2, bf16[128,2,8,128]{0,3,2,1:T(8,128)(2,1)S(1)} %copy-done.11, f32[2,8,128]{2,1,0:T(8,128)S(1)} %add.243, f32[2,8,128,128]{2,3,1,0:T(8,128)S(1)} %copy-done.1, f32[2,8,128]{2,1,0:T(8,128)S(1)} %max.8, ...), kind=kOutput, calls=%fused_computation.75 | convolution fusion | flops 68255744 | bytes 1736704 | tf_op jit(solution)/shard_map/hgqk,qhgd->khd/dot_general | solution.py:175
  50.7 1.9 %collective-permute-start.3 = (bf16[128,256]{0,1:T(8,128)(2,1)S(1)}, bf16[128,256]{0,1:T(8,128)(2,1)S(1)}, u32[]{:S(2)}, u32[]{:S(2)}) collective-permute-start(bf16[128,256]{0,1:T(8,128)(2,1)S(1)} %bitcast.170), channel_id=1, source_target_pairs={{0,2},{2,4},{4,6},{6,8},{8,10},{10,12},{12,14},{14,16},{16,18},{18... | collective-permute-start | bytes 196616 | tf_op jit(solution)/shard_map/ppermute | solution.py:42
  52.6 2.4 %collective-permute-start.4 = (bf16[128,256]{0,1:T(8,128)(2,1)S(1)}, bf16[128,256]{0,1:T(8,128)(2,1)S(1)}, u32[]{:S(2)}, u32[]{:S(2)}) collective-permute-start(bf16[128,256]{0,1:T(8,128)(2,1)S(1)} %bitcast.171), channel_id=1, source_target_pairs={{0,4},{2,6},{4,8},{6,10},{8,12},{10,14},{12,16},{14,18},{16,20},{1... | collective-permute-start | bytes 196616 | tf_op jit(solution)/shard_map/ppermute | solution.py:42
  55.0 4.2 %collective-permute-start.5 = (bf16[128,256]{0,1:T(8,128)(2,1)S(1)}, bf16[128,256]{0,1:T(8,128)(2,1)S(1)}, u32[]{:S(2)}, u32[]{:S(2)}) collective-permute-start(bf16[128,256]{0,1:T(8,128)(2,1)S(1)} %bitcast.172), channel_id=1, source_target_pairs={{0,6},{2,8},{4,10},{6,12},{8,14},{10,16},{12,18},{14,20},{16,22},{... | collective-permute-start | bytes 196616 | tf_op jit(solution)/shard_map/ppermute | solution.py:42
  59.1 2.9 %collective-permute-start.6 = (bf16[128,256]{0,1:T(8,128)(2,1)S(1)}, bf16[128,256]{0,1:T(8,128)(2,1)S(1)}, u32[]{:S(2)}, u32[]{:S(2)}) collective-permute-start(bf16[128,256]{0,1:T(8,128)(2,1)S(1)} %bitcast.173), channel_id=1, source_target_pairs={{0,8},{2,10},{4,12},{6,14},{8,16},{10,18},{12,20},{14,22},{16,24},... | collective-permute-start | bytes 196616 | tf_op jit(solution)/shard_map/ppermute | solution.py:42
  62.1 1.5 %collective-permute-start.7 = (bf16[128,256]{0,1:T(8,128)(2,1)S(1)}, bf16[128,256]{0,1:T(8,128)(2,1)S(1)}, u32[]{:S(2)}, u32[]{:S(2)}) collective-permute-start(bf16[128,256]{0,1:T(8,128)(2,1)S(1)} %bitcast.174), channel_id=1, source_target_pairs={{0,10},{2,12},{4,14},{6,16},{8,18},{10,20},{12,22},{14,24},{16,26}... | collective-permute-start | bytes 196616 | tf_op jit(solution)/shard_map/ppermute | solution.py:42
  64.4 4.7 %collective-permute-start.9 = (bf16[128,256]{0,1:T(8,128)(2,1)S(1)}, bf16[128,256]{0,1:T(8,128)(2,1)S(1)}, u32[]{:S(2)}, u32[]{:S(2)}) collective-permute-start(bf16[128,256]{0,1:T(8,128)(2,1)S(1)} %bitcast.177), channel_id=1, source_target_pairs={{0,14},{2,16},{4,18},{6,20},{8,22},{10,24},{12,26},{14,28},{16,30}... | collective-permute-start | bytes 196616 | tf_op jit(solution)/shard_map/ppermute | solution.py:42
  69.3 1.2 %collective-permute-start.11 = (bf16[128,256]{0,1:T(8,128)(2,1)S(1)}, bf16[128,256]{0,1:T(8,128)(2,1)S(1)}, u32[]{:S(2)}, u32[]{:S(2)}) collective-permute-start(bf16[128,256]{0,1:T(8,128)(2,1)S(1)} %bitcast.179), channel_id=1, source_target_pairs={{0,18},{2,20},{4,22},{6,24},{8,26},{10,28},{12,30},{14,0},{16,2},{... | collective-permute-start | bytes 196616 | tf_op jit(solution)/shard_map/ppermute | solution.py:42
  70.5 1.9 %collective-permute-start.12 = (bf16[128,256]{0,1:T(8,128)(2,1)S(1)}, bf16[128,256]{0,1:T(8,128)(2,1)S(1)}, u32[]{:S(2)}, u32[]{:S(2)}) collective-permute-start(bf16[128,256]{0,1:T(8,128)(2,1)S(1)} %bitcast.180), channel_id=1, source_target_pairs={{0,20},{2,22},{4,24},{6,26},{8,28},{10,30},{12,0},{14,2},{16,4},{1... | collective-permute-start | bytes 196616 | tf_op jit(solution)/shard_map/ppermute | solution.py:42
  72.4 3.9 %collective-permute-start.13 = (bf16[128,256]{0,1:T(8,128)(2,1)S(1)}, bf16[128,256]{0,1:T(8,128)(2,1)S(1)}, u32[]{:S(2)}, u32[]{:S(2)}) collective-permute-start(bf16[128,256]{0,1:T(8,128)(2,1)S(1)} %bitcast.181), channel_id=1, source_target_pairs={{0,22},{2,24},{4,26},{6,28},{8,30},{10,0},{12,2},{14,4},{16,6},{18... | collective-permute-start | bytes 196616 | tf_op jit(solution)/shard_map/ppermute | solution.py:42
  76.3 1.4 %collective-permute-start.14 = (bf16[128,256]{0,1:T(8,128)(2,1)S(1)}, bf16[128,256]{0,1:T(8,128)(2,1)S(1)}, u32[]{:S(2)}, u32[]{:S(2)}) collective-permute-start(bf16[128,256]{0,1:T(8,128)(2,1)S(1)} %bitcast.182), channel_id=1, source_target_pairs={{0,24},{2,26},{4,28},{6,30},{8,0},{10,2},{12,4},{14,6},{16,8},{18,... | collective-permute-start | bytes 196616 | tf_op jit(solution)/shard_map/ppermute | solution.py:42
  77.9 2.4 %collective-permute-start.16 = (bf16[128,256]{0,1:T(8,128)(2,1)S(1)}, bf16[128,256]{0,1:T(8,128)(2,1)S(1)}, u32[]{:S(2)}, u32[]{:S(2)}) collective-permute-start(bf16[128,256]{0,1:T(8,128)(2,1)S(1)} %bitcast.184), channel_id=1, source_target_pairs={{0,28},{2,30},{4,0},{6,2},{8,4},{10,6},{12,8},{14,10},{16,12},{18,... | collective-permute-start | bytes 196616 | tf_op jit(solution)/shard_map/ppermute | solution.py:42
  80.4 3.4 %collective-permute-start.17 = (bf16[128,256]{0,1:T(8,128)(2,1)S(1)}, bf16[128,256]{0,1:T(8,128)(2,1)S(1)}, u32[]{:S(2)}, u32[]{:S(2)}) collective-permute-start(bf16[128,256]{0,1:T(8,128)(2,1)S(1)} %bitcast.185), channel_id=1, source_target_pairs={{0,30},{2,0},{4,2},{6,4},{8,6},{10,8},{12,10},{14,12},{16,14},{18,... | collective-permute-start | bytes 196616 | tf_op jit(solution)/shard_map/ppermute | solution.py:42
  84.0 1.7 %collective-permute-done.17 = bf16[128,256]{0,1:T(8,128)(2,1)S(1)} collective-permute-done((bf16[128,256]{0,1:T(8,128)(2,1)S(1)}, bf16[128,256]{0,1:T(8,128)(2,1)S(1)}, u32[]{:S(2)}, u32[]{:S(2)}) %collective-permute-start.17) | collective-permute-done | bytes 65568 | tf_op jit(solution)/shard_map/ppermute | solution.py:42
  85.7 2.3 %multiply_reduce_fusion.1 = (f32[]{:T(128)}, f32[256,256]{0,1:T(8,128)S(1)}) fusion(bf16[2048,256]{0,1:T(8,128)(2,1)S(1)} %constant_dynamic-update-slice_fusion.4, bf16[2048,256]{1,0:T(8,128)(2,1)} %bitcast.55), kind=kOutput, calls=%fused_computation.57 | convolution fusion | flops 268566528 | bytes 2359300 | tf_op jit(solution)/shard_map/dot_general | solution.py:226
  88.0 1.0 collective-permute-start.18
  89.3 1.3 %broadcast_in_dim_broadcast_in_dim_broadcast_in_dim.3 = f32[32,8,128]{2,1,0:T(8,128)} broadcast(f32[]{:T(128)} %get-tuple-element.72), dimensions={} | broadcast | bytes 131076 | tf_op jit(solution)/shard_map/broadcast_in_dim;broadcast_in_dim;broadcast_in_dim | solution.py:31
  90.6 6.7 %all-to-all-start.1 = ((f32[32,8,128]{2,1,0:T(8,128)}), f32[32,8,128]{2,1,0:T(8,128)S(1)}, u32[]{:S(2)}, u32[]{:S(2)}) async-start(f32[32,8,128]{2,1,0:T(8,128)} %broadcast_in_dim_broadcast_in_dim_broadcast_in_dim.3), calls=%async_computation.1 | async-start | bytes 262144 | tf_op jit(solution)/shard_map/all_to_all | solution.py:32
  97.4 0.7 copy.251
  98.1 0.7 copy.250
  98.9 2.7 %collective-permute-start.20 = (f32[256,256]{0,1:T(8,128)S(1)}, f32[256,256]{0,1:T(8,128)S(1)}, u32[]{:S(2)}, u32[]{:S(2)}) collective-permute-start(f32[256,256]{0,1:T(8,128)S(1)} %get-tuple-element.73), channel_id=1, source_target_pairs={{0,24},{8,0},{16,8},{24,16},{1,25},{9,1},{17,9},{25,17},{2,26},{10... | collective-permute-start | bytes 786440 | tf_op jit(solution)/shard_map/ppermute | solution.py:42
  101.8 3.7 %all-to-all-done.1 = f32[32,8,128]{2,1,0:T(8,128)S(1)} async-done(((f32[32,8,128]{2,1,0:T(8,128)}), f32[32,8,128]{2,1,0:T(8,128)S(1)}, u32[]{:S(2)}, u32[]{:S(2)}) %all-to-all-start.1) | async-done | bytes 131104 | tf_op jit(solution)/shard_map/all_to_all | solution.py:32
  107.1 1.0 collective-permute-done.20
  108.4 3.7 %multiply_subtract_fusion = (f32[1024,256]{1,0:T(8,128)}, f32[1024,256]{1,0:T(8,128)}, f32[1024,256]{1,0:T(8,128)}) fusion(f32[1024,256]{1,0:T(8,128)S(1)} %copy-done.6, f32[1024,256]{1,0:T(8,128)S(1)} %constant_dynamic-update-slice_fusion, f32[]{:T(128)S(6)} %min_shard_map.3, f32[1024,256]{1,0:T(8,128)} %param.20, f32[1024,256]{1,0:T(8,128)} %param.21), kind=kLoop, calls=%fused_computation.48 | loop fusion | flops 4194304 | bytes 7340036 | tf_op jit(solution)/shard_map/sub | solution.py:94
  (124 shorter events, 12.9 us)
Async XLA Ops:
  0.6 0.7 copy-start.17
  1.7 0.7 copy-start.18
  1.7 0.7 copy-start.19
  2.7 0.8 copy-start.7
  2.8 7.9 %copy-start.5 = (bf16[1,128,4096]{2,1,0:T(8,128)(2,1)S(1)}, bf16[1,128,4096]{2,1,0:T(8,128)(2,1)}, u32[]{:S(2)}) copy-start(bf16[1,128,4096]{2,1,0:T(8,128)(2,1)} %param.15) | copy-start | bytes 3145732
  3.5 0.8 copy-start.13
  5.2 25.6 %collective-permute-start = (bf16[2,128,2,128]{3,1,2,0:T(8,128)(2,1)}, bf16[2,128,2,128]{3,1,2,0:T(8,128)(2,1)}, u32[]{:S(2)}, u32[]{:S(2)}) collective-permute-start(bf16[2,128,2,128]{3,1,2,0:T(8,128)(2,1)} %pad_maximum_fusion), channel_id=1, source_target_pairs={{0,8},{8,16},{16,24},{1,9},{9,17},{17,25},{2,10},{10,18},{18,26},{... | collective-permute-start | bytes 393224 | tf_op jit(solution)/shard_map/ppermute | solution.py:24
  12.7 7.5 %copy-start.8 = (bf16[1,128,16,128]{3,2,1,0:T(8,128)(2,1)S(1)}, bf16[1,128,16,128]{3,2,1,0:T(8,128)(2,1)}, u32[]{:S(2)}) copy-start(bf16[1,128,16,128]{3,2,1,0:T(8,128)(2,1)} %param.11) | copy-start | bytes 1572868
  12.7 73.1 %all-to-all-start = ((bf16[1,128,16,256]{3,1,0,2:T(8,128)(2,1)}), bf16[1,128,16,256]{3,1,0,2:T(8,128)(2,1)}, u32[]{:S(2)}, u32[]{:S(2)}) async-start(bf16[1,128,16,256]{3,1,0,2:T(8,128)(2,1)} %bitcast.52), calls=%async_computation | async-start | bytes 2097152 | tf_op jit(solution)/shard_map/all_to_all | solution.py:219
  22.0 1.7 %copy-start.2 = (f32[128,2,8,64]{3,2,1,0:T(8,128)S(1)}, f32[128,2,8,64]{3,2,1,0:T(8,128)}, u32[]{:S(2)}) copy-start(f32[128,2,8,64]{3,2,1,0:T(8,128)} %get-tuple-element.53) | copy-start | bytes 1572868
  24.9 0.9 copy-start.12
  25.4 1.4 %copy-start.4 = (f32[128,2,8,64]{0,3,2,1:T(8,128)S(1)}, f32[128,2,8,64]{0,3,2,1:T(8,128)}, u32[]{:S(2)}) copy-start(f32[128,2,8,64]{0,3,2,1:T(8,128)} %copy.214) | copy-start | bytes 1572868
  26.0 0.6 copy-start.15
  26.0 0.6 copy-start.16
  28.1 9.7 %copy-start = (f32[2,8,128,128]{2,3,1,0:T(8,128)}, f32[2,8,128,128]{2,3,1,0:T(8,128)S(1)}, u32[]{:S(2)}) copy-start(f32[2,8,128,128]{2,3,1,0:T(8,128)S(1)} %get-tuple-element.67) | copy-start | bytes 3145732
  28.1 1.4 %copy-start.3 = (bf16[1,128,16,128]{3,2,1,0:T(8,128)(2,1)S(1)}, bf16[1,128,16,128]{3,2,1,0:T(8,128)(2,1)}, u32[]{:S(2)}) copy-start(bf16[1,128,16,128]{3,2,1,0:T(8,128)(2,1)} %param.14) | copy-start | bytes 1572868
  31.9 1.0 copy-start.9
  33.0 2.3 %copy-start.14 = (bf16[1,128,2,128]{3,2,1,0:T(2,128)(2,1)S(1)}, bf16[1,128,2,128]{3,2,1,0:T(2,128)(2,1)}, u32[]{:S(2)}) copy-start(bf16[1,128,2,128]{3,2,1,0:T(2,128)(2,1)} %param.13) | copy-start | bytes 196612
  34.0 15.4 %collective-permute-start.2 = (bf16[128,2,128]{2,0,1:T(8,128)(2,1)}, bf16[128,2,128]{2,0,1:T(8,128)(2,1)}, u32[]{:S(2)}, u32[]{:S(2)}) collective-permute-start(bf16[128,2,128]{2,0,1:T(8,128)(2,1)} %fusion.18), channel_id=1, source_target_pairs={{8,0},{16,8},{24,16},{9,1},{17,9},{25,17},{10,2},{18,10},{26,18},{... | collective-permute-start | bytes 196616 | tf_op jit(solution)/shard_map/ppermute | solution.py:24
  37.8 1.5 %copy-start.10 = (bf16[128,2,8,128]{0,3,2,1:T(8,128)(2,1)S(1)}, bf16[128,2,8,128]{0,3,2,1:T(8,128)(2,1)}, u32[]{:S(2)}) copy-start(bf16[128,2,8,128]{0,3,2,1:T(8,128)(2,1)} %copy.239) | copy-start | bytes 1572868
  40.9 21.2 %collective-permute-start.1 = (bf16[128,2,128]{2,0,1:T(8,128)(2,1)S(1)}, bf16[128,2,128]{2,0,1:T(8,128)(2,1)S(1)}, u32[]{:S(2)}, u32[]{:S(2)}) collective-permute-start(bf16[128,2,128]{2,0,1:T(8,128)(2,1)S(1)} %fusion.19), channel_id=1, source_target_pairs={{8,0},{16,8},{24,16},{9,1},{17,9},{25,17},{10,2},{18,10},{26,18},{... | collective-permute-start | bytes 196616 | tf_op jit(solution)/shard_map/ppermute | solution.py:24
  46.5 2.8 %copy-start.1 = (f32[2,8,128,128]{2,3,1,0:T(8,128)S(1)}, f32[2,8,128,128]{2,3,1,0:T(8,128)}, u32[]{:S(2)}) copy-start(f32[2,8,128,128]{2,3,1,0:T(8,128)} %copy-done) | copy-start | bytes 3145732
  46.5 2.8 %copy-start.11 = (bf16[128,2,8,128]{0,3,2,1:T(8,128)(2,1)S(1)}, bf16[128,2,8,128]{0,3,2,1:T(8,128)(2,1)}, u32[]{:S(2)}) copy-start(bf16[128,2,8,128]{0,3,2,1:T(8,128)(2,1)} %copy.239) | copy-start | bytes 1572868
  50.7 13.4 %collective-permute-start.3 = (bf16[128,256]{0,1:T(8,128)(2,1)S(1)}, bf16[128,256]{0,1:T(8,128)(2,1)S(1)}, u32[]{:S(2)}, u32[]{:S(2)}) collective-permute-start(bf16[128,256]{0,1:T(8,128)(2,1)S(1)} %bitcast.170), channel_id=1, source_target_pairs={{0,2},{2,4},{4,6},{6,8},{8,10},{10,12},{12,14},{14,16},{16,18},{18... | collective-permute-start | bytes 196616 | tf_op jit(solution)/shard_map/ppermute | solution.py:42
  52.6 11.8 %collective-permute-start.4 = (bf16[128,256]{0,1:T(8,128)(2,1)S(1)}, bf16[128,256]{0,1:T(8,128)(2,1)S(1)}, u32[]{:S(2)}, u32[]{:S(2)}) collective-permute-start(bf16[128,256]{0,1:T(8,128)(2,1)S(1)} %bitcast.171), channel_id=1, source_target_pairs={{0,4},{2,6},{4,8},{6,10},{8,12},{10,14},{12,16},{14,18},{16,20},{1... | collective-permute-start | bytes 196616 | tf_op jit(solution)/shard_map/ppermute | solution.py:42
  55.0 14.2 %collective-permute-start.5 = (bf16[128,256]{0,1:T(8,128)(2,1)S(1)}, bf16[128,256]{0,1:T(8,128)(2,1)S(1)}, u32[]{:S(2)}, u32[]{:S(2)}) collective-permute-start(bf16[128,256]{0,1:T(8,128)(2,1)S(1)} %bitcast.172), channel_id=1, source_target_pairs={{0,6},{2,8},{4,10},{6,12},{8,14},{10,16},{12,18},{14,20},{16,22},{... | collective-permute-start | bytes 196616 | tf_op jit(solution)/shard_map/ppermute | solution.py:42
  59.1 10.1 %collective-permute-start.6 = (bf16[128,256]{0,1:T(8,128)(2,1)S(1)}, bf16[128,256]{0,1:T(8,128)(2,1)S(1)}, u32[]{:S(2)}, u32[]{:S(2)}) collective-permute-start(bf16[128,256]{0,1:T(8,128)(2,1)S(1)} %bitcast.173), channel_id=1, source_target_pairs={{0,8},{2,10},{4,12},{6,14},{8,16},{10,18},{12,20},{14,22},{16,24},... | collective-permute-start | bytes 196616 | tf_op jit(solution)/shard_map/ppermute | solution.py:42
  62.1 8.4 %collective-permute-start.7 = (bf16[128,256]{0,1:T(8,128)(2,1)S(1)}, bf16[128,256]{0,1:T(8,128)(2,1)S(1)}, u32[]{:S(2)}, u32[]{:S(2)}) collective-permute-start(bf16[128,256]{0,1:T(8,128)(2,1)S(1)} %bitcast.174), channel_id=1, source_target_pairs={{0,10},{2,12},{4,14},{6,16},{8,18},{10,20},{12,22},{14,24},{16,26}... | collective-permute-start | bytes 196616 | tf_op jit(solution)/shard_map/ppermute | solution.py:42
  64.1 8.3 %collective-permute-start.8 = (bf16[128,256]{0,1:T(8,128)(2,1)S(1)}, bf16[128,256]{0,1:T(8,128)(2,1)S(1)}, u32[]{:S(2)}, u32[]{:S(2)}) collective-permute-start(bf16[128,256]{0,1:T(8,128)(2,1)S(1)} %bitcast.176), channel_id=1, source_target_pairs={{0,12},{2,14},{4,16},{6,18},{8,20},{10,22},{12,24},{14,26},{16,28}... | collective-permute-start | bytes 196616 | tf_op jit(solution)/shard_map/ppermute | solution.py:42
  64.4 12.0 %collective-permute-start.9 = (bf16[128,256]{0,1:T(8,128)(2,1)S(1)}, bf16[128,256]{0,1:T(8,128)(2,1)S(1)}, u32[]{:S(2)}, u32[]{:S(2)}) collective-permute-start(bf16[128,256]{0,1:T(8,128)(2,1)S(1)} %bitcast.177), channel_id=1, source_target_pairs={{0,14},{2,16},{4,18},{6,20},{8,22},{10,24},{12,26},{14,28},{16,30}... | collective-permute-start | bytes 196616 | tf_op jit(solution)/shard_map/ppermute | solution.py:42
  69.2 8.6 %collective-permute-start.10 = (bf16[128,256]{0,1:T(8,128)(2,1)S(1)}, bf16[128,256]{0,1:T(8,128)(2,1)S(1)}, u32[]{:S(2)}, u32[]{:S(2)}) collective-permute-start(bf16[128,256]{0,1:T(8,128)(2,1)S(1)} %bitcast.178), channel_id=1, source_target_pairs={{0,16},{2,18},{4,20},{6,22},{8,24},{10,26},{12,28},{14,30},{16,0},... | collective-permute-start | bytes 196616 | tf_op jit(solution)/shard_map/ppermute | solution.py:42
  69.3 8.6 %collective-permute-start.11 = (bf16[128,256]{0,1:T(8,128)(2,1)S(1)}, bf16[128,256]{0,1:T(8,128)(2,1)S(1)}, u32[]{:S(2)}, u32[]{:S(2)}) collective-permute-start(bf16[128,256]{0,1:T(8,128)(2,1)S(1)} %bitcast.179), channel_id=1, source_target_pairs={{0,18},{2,20},{4,22},{6,24},{8,26},{10,28},{12,30},{14,0},{16,2},{... | collective-permute-start | bytes 196616 | tf_op jit(solution)/shard_map/ppermute | solution.py:42
  70.5 9.9 %collective-permute-start.12 = (bf16[128,256]{0,1:T(8,128)(2,1)S(1)}, bf16[128,256]{0,1:T(8,128)(2,1)S(1)}, u32[]{:S(2)}, u32[]{:S(2)}) collective-permute-start(bf16[128,256]{0,1:T(8,128)(2,1)S(1)} %bitcast.180), channel_id=1, source_target_pairs={{0,20},{2,22},{4,24},{6,26},{8,28},{10,30},{12,0},{14,2},{16,4},{1... | collective-permute-start | bytes 196616 | tf_op jit(solution)/shard_map/ppermute | solution.py:42
  72.4 11.5 %collective-permute-start.13 = (bf16[128,256]{0,1:T(8,128)(2,1)S(1)}, bf16[128,256]{0,1:T(8,128)(2,1)S(1)}, u32[]{:S(2)}, u32[]{:S(2)}) collective-permute-start(bf16[128,256]{0,1:T(8,128)(2,1)S(1)} %bitcast.181), channel_id=1, source_target_pairs={{0,22},{2,24},{4,26},{6,28},{8,30},{10,0},{12,2},{14,4},{16,6},{18... | collective-permute-start | bytes 196616 | tf_op jit(solution)/shard_map/ppermute | solution.py:42
  76.3 7.5 %collective-permute-start.14 = (bf16[128,256]{0,1:T(8,128)(2,1)S(1)}, bf16[128,256]{0,1:T(8,128)(2,1)S(1)}, u32[]{:S(2)}, u32[]{:S(2)}) collective-permute-start(bf16[128,256]{0,1:T(8,128)(2,1)S(1)} %bitcast.182), channel_id=1, source_target_pairs={{0,24},{2,26},{4,28},{6,30},{8,0},{10,2},{12,4},{14,6},{16,8},{18,... | collective-permute-start | bytes 196616 | tf_op jit(solution)/shard_map/ppermute | solution.py:42
  77.8 6.1 %collective-permute-start.15 = (bf16[128,256]{0,1:T(8,128)(2,1)S(1)}, bf16[128,256]{0,1:T(8,128)(2,1)S(1)}, u32[]{:S(2)}, u32[]{:S(2)}) collective-permute-start(bf16[128,256]{0,1:T(8,128)(2,1)S(1)} %bitcast.183), channel_id=1, source_target_pairs={{0,26},{2,28},{4,30},{6,0},{8,2},{10,4},{12,6},{14,8},{16,10},{18,... | collective-permute-start | bytes 196616 | tf_op jit(solution)/shard_map/ppermute | solution.py:42
  77.9 6.0 %collective-permute-start.16 = (bf16[128,256]{0,1:T(8,128)(2,1)S(1)}, bf16[128,256]{0,1:T(8,128)(2,1)S(1)}, u32[]{:S(2)}, u32[]{:S(2)}) collective-permute-start(bf16[128,256]{0,1:T(8,128)(2,1)S(1)} %bitcast.184), channel_id=1, source_target_pairs={{0,28},{2,30},{4,0},{6,2},{8,4},{10,6},{12,8},{14,10},{16,12},{18,... | collective-permute-start | bytes 196616 | tf_op jit(solution)/shard_map/ppermute | solution.py:42
  80.4 5.4 %collective-permute-start.17 = (bf16[128,256]{0,1:T(8,128)(2,1)S(1)}, bf16[128,256]{0,1:T(8,128)(2,1)S(1)}, u32[]{:S(2)}, u32[]{:S(2)}) collective-permute-start(bf16[128,256]{0,1:T(8,128)(2,1)S(1)} %bitcast.185), channel_id=1, source_target_pairs={{0,30},{2,0},{4,2},{6,4},{8,6},{10,8},{12,10},{14,12},{16,14},{18,... | collective-permute-start | bytes 196616 | tf_op jit(solution)/shard_map/ppermute | solution.py:42
  88.0 18.8 %collective-permute-start.18 = (f32[256,256]{0,1:T(8,128)S(1)}, f32[256,256]{0,1:T(8,128)S(1)}, u32[]{:S(2)}, u32[]{:S(2)}) collective-permute-start(f32[256,256]{0,1:T(8,128)S(1)} %get-tuple-element.73), channel_id=1, source_target_pairs={{0,8},{8,16},{16,24},{24,0},{1,9},{9,17},{17,25},{25,1},{2,10},{10... | collective-permute-start | bytes 786440 | tf_op jit(solution)/shard_map/ppermute | solution.py:42
  89.0 17.9 %collective-permute-start.19 = (f32[256,256]{0,1:T(8,128)S(1)}, f32[256,256]{0,1:T(8,128)S(1)}, u32[]{:S(2)}, u32[]{:S(2)}) collective-permute-start(f32[256,256]{0,1:T(8,128)S(1)} %get-tuple-element.73), channel_id=1, source_target_pairs={{0,16},{8,24},{16,0},{24,8},{1,17},{9,25},{17,1},{25,9},{2,18},{10... | collective-permute-start | bytes 786440 | tf_op jit(solution)/shard_map/ppermute | solution.py:42
  90.6 14.9 %all-to-all-start.1 = ((f32[32,8,128]{2,1,0:T(8,128)}), f32[32,8,128]{2,1,0:T(8,128)S(1)}, u32[]{:S(2)}, u32[]{:S(2)}) async-start(f32[32,8,128]{2,1,0:T(8,128)} %broadcast_in_dim_broadcast_in_dim_broadcast_in_dim.3), calls=%async_computation.1 | async-start | bytes 262144 | tf_op jit(solution)/shard_map/all_to_all | solution.py:32
  98.9 9.3 %collective-permute-start.20 = (f32[256,256]{0,1:T(8,128)S(1)}, f32[256,256]{0,1:T(8,128)S(1)}, u32[]{:S(2)}, u32[]{:S(2)}) collective-permute-start(f32[256,256]{0,1:T(8,128)S(1)} %get-tuple-element.73), channel_id=1, source_target_pairs={{0,24},{8,0},{16,8},{24,16},{1,25},{9,1},{17,9},{25,17},{2,26},{10... | collective-permute-start | bytes 786440 | tf_op jit(solution)/shard_map/ppermute | solution.py:42
  107.1 1.3 %copy-start.6 = (f32[1024,256]{1,0:T(8,128)S(1)}, f32[1024,256]{1,0:T(8,128)}, u32[]{:S(2)}) copy-start(f32[1024,256]{1,0:T(8,128)} %param.19) | copy-start | bytes 3145732

commit v7 on v3

--- a/solution.py
+++ b/solution.py
@@ -76,6 +76,17 @@
     half = vectors.shape[-1] // 2
     turned = jnp.concatenate([-vectors[..., half:], vectors[..., :half]], axis=-1)
     return vectors * cosine + turned * sine
+
+
+def rotate_low(vectors, cosine, sine):
+    half = vectors.shape[-1] // 2
+    eye = jnp.eye(half, dtype=jnp.bfloat16)
+    zero = jnp.zeros((half, half), jnp.bfloat16)
+    swap = jnp.concatenate(
+        [jnp.concatenate([zero, eye], axis=1), jnp.concatenate([-eye, zero], axis=1)], axis=0
+    )
+    turned = jnp.einsum("...d,de->...e", vectors, swap, preferred_element_type=jnp.float32)
+    return vectors.astype(jnp.float32) * cosine + turned * sine
 
 
 def unrotate(grads_in, cosine, sine):
@@ -123,9 +134,9 @@
     own_index = place * tok_rows + jnp.arange(tok_rows, dtype=jnp.int32)
     own_doc, position = doc_layout(lengths_row, own_index)
     cosine, sine = rope_tables(position, rope_num, rope_den, head_dim)
-    rotated_query_rows = rotate(queries[0].astype(jnp.float32), cosine, sine).astype(jnp.bfloat16)
+    rotated_query_rows = rotate_low(queries[0], cosine, sine).astype(jnp.bfloat16)
     rotated_query_rows = rotated_query_rows.reshape(tok_rows, kv_count, group_size, head_dim)
-    rotated_key_rows = rotate(keys[0].astype(jnp.float32), cosine, sine).astype(jnp.bfloat16)
+    rotated_key_rows = rotate_low(keys[0], cosine, sine).astype(jnp.bfloat16)
     grad_out = output_cotangent[0].reshape(tok_rows, kv_count, group_size, head_dim)
     kv_pair = jnp.stack([rotated_key_rows, values[0]])
     pairs = [kv_pair]

time: 105 us -> 99.8 us (0.950)
  other arithmetic: 17.3 us -> 8.01 us
  waiting for transfers between devices: 21.9 us -> 31.1 us
  local copies, waits for them, and re-layouts: 24 us -> 18.3 us
  matrix products: 9.24 us -> 10.7 us
  starting transfers between devices: 29.8 us -> 28.7 us
    concatenate x4 -> x0, local copies, waits for them, and re-layouts: 4.55 us -> none  [the longest x2 3.73 us: rotate(): jnp.concatenate([-vectors[..., half:], vectors[..., :half]], axis=-1)]
    convert_element_type x5 -> x1, other arithmetic: 3.5 us -> 0.01 us  [rotate_low(): eye = jnp.eye(half, dtype=jnp.bfloat16)]
    all_to_all x1, waiting for transfers between devices: 0.01 us -> 3.46 us  [local(): lax.all_to_all(feats.reshape(tok_rows, n_dp * n_ctx, piece_rows), spread,...]
    all_to_all x2, waiting for transfers between devices: 16.3 us -> 19.4 us  [spread_copy(): return lax.all_to_all(stacked, axes, 0, 0, tiled=False)]
    concatenate x2 -> x0, other arithmetic: 2.35 us -> none  [rotate(): jnp.concatenate([-vectors[..., half:], vectors[..., :half]], axis=-1)]
    reshape x2 -> x0, local copies, waits for them, and re-layouts: 1.88 us -> none  [local(): query_grad.reshape(tok_rows, head_count, head_dim)]
    ppermute x2, waiting for transfers between devices: 4.02 us -> 5.75 us  [shifted(): return lax.ppermute(array, axis, pairs)]
    convert_element_type x1 -> x0, local copies, waits for them, and re-layouts: 1.58 us -> none  [local(): queries[0].astype(jnp.float32)]
  transfers between devices with their start and end apart: 8 -> 8, of which waited for: 4 -> 5; matrix products, arithmetic and copies ran while one was open for 33% -> 21% of each run, Pallas kernels for 0% -> 0%
where the time goes in v7:
time: 99.8 us; the launch traced here: 98.7 us
  waiting for transfers between devices  31.1 us (31%)
  starting transfers between devices  28.7 us (29%)
  local copies, waits for them, and re-layouts  18.3 us (18%)
  matrix products  10.7 us (11%)
  other arithmetic  8.01 us (8%)
  between operations  1.93 us (2%)
    all_to_all x2, waiting for transfers between devices, spread_copy(): return lax.all_to_all(stacked, axes, 0, 0, tiled=False)  19.4 us
    unnamed x39, local copies, waits for them, and re-layouts  11.5 us
    all_to_all x2, starting transfers between devices, spread_copy(): return lax.all_to_all(stacked, axes, 0, 0, tiled=False)  11.2 us
    ppermute x2, starting transfers between devices, shifted(): return lax.ppermute(array, axis, pairs)  6.81 us
    ppermute x2, waiting for transfers between devices, shifted(): return lax.ppermute(array, axis, pairs)  5.75 us
    all_to_all x1, starting transfers between devices, local(): lax.all_to_all(feats.reshape(tok_rows, n_dp * n_ctx, piece_rows), spread,...  5.45 us
    ppermute x3, starting transfers between devices, ring_copy(): lax.ppermute(array, axis, [(i, (i + step) % peers) for i in range(peers)])  5.25 us
    sub x1, other arithmetic, adam_update(): new_param = param - LEARN_RATE * (step_size + DECAY_RATE * param)  3.71 us
  transfers between devices with their start and end apart: 8, of which 5 were waited for; matrix products, arithmetic and copies ran while one was open for 21% of the time, Pallas kernels for 0%

profile of v7, /device:TPU:0, one launch (start us, length us, event | category | flops | bytes accessed | tf_op | source)
XLA Modules:
  0.0 98.7 jit_solution(864553586378624362)
XLA Ops:
  0.7 0.8 copy.188
  1.8 0.7 convert_divide_fusion
  2.7 1.0 copy.187
  3.7 1.0 copy.194
  4.9 5.5 %collective-permute-start = (bf16[2,128,2,128]{1,3,2,0:T(8,128)(2,1)S(1)}, bf16[2,128,2,128]{1,3,2,0:T(8,128)(2,1)}, u32[]{:S(2)}, u32[]{:S(2)}) collective-permute-start(bf16[2,128,2,128]{1,3,2,0:T(8,128)(2,1)S(1)} %pad_maximum_fusion), channel_id=1, source_target_pairs={{0,8},{8,16},{16,24},{1,9},{9,17},{17,25},{2,10},{10,18},{18,26},{... | collective-permute-start | bytes 393224 | tf_op jit(solution)/shard_map/ppermute | solution.py:24
  10.5 1.3 %copy.214 = bf16[1,128,4096]{1,2,0:T(8,128)(2,1)} copy(bf16[1,128,4096]{2,1,0:T(8,128)(2,1)S(1)} %copy-done.5) | data formatting | bytes 2097152 | tf_op args[4]
  11.8 5.4 %all-to-all-start.1 = ((bf16[1,128,16,256]{1,3,0,2:T(8,128)(2,1)}), bf16[1,128,16,256]{1,3,0,2:T(8,128)(2,1)S(1)}, u32[]{:S(2)}, u32[]{:S(2)}) async-start(bf16[1,128,16,256]{1,3,0,2:T(8,128)(2,1)} %bitcast.61), calls=%async_computation.1 | async-start | bytes 2097152 | tf_op jit(solution)/shard_map/all_to_all | solution.py:227
  17.2 0.5 copy.190
  18.7 0.7 copy-done.2
  19.3 1.2 %copy.212 = bf16[128,2,8,128]{0,3,2,1:T(8,128)(2,1)} copy(bf16[128,2,8,128]{3,2,1,0:T(8,128)(2,1)S(1)} %bitcast.201) | data formatting | bytes 1048576 | tf_op jit(solution)/shard_map/reshape;squeeze | solution.py:140
  20.6 1.2 %fusion.70 = (f32[2,8,128]{2,1,0:T(8,128)S(1)}, f32[2,8,128,128]{2,3,1,0:T(8,128)S(1)}) fusion(bf16[128,2,8,128]{0,3,2,1:T(8,128)(2,1)S(1)} %bitcast.196, bf16[2,128,2,128]{1,3,2,0:T(8,128)(2,1)} %collective-permute-done, pred[128,128]{0,1:T(8,128)(4,1)S(1)} %get-tuple-element.54), kind=kOutput, calls=%fused_computation.122 | convolution fusion | flops 67893248 | bytes 1662976 | tf_op jit(solution)/shard_map/qhgd,khd->hgqk/dot_general | solution.py:159
  22.2 0.5 copy-done.15
  22.7 0.4 convolution_bitcast_fusion.2
  23.2 1.3 %fusion.5 = f32[2,8,128,128]{3,2,1,0:T(8,128)S(1)} fusion(f32[128,2,8,128]{3,0,2,1:T(8,128)S(1)} %convolution_bitcast_fusion.2, bf16[2,128,2,128]{1,3,2,0:T(8,128)(2,1)} %collective-permute-done, f32[2,8,128,128]{2,3,1,0:T(8,128)S(1)} %get-tuple-element.61, f32[2,8,128]{2,1,0:T(8,128)S(1)} %add.129, f32[2,8,128]{2,1,0:T(8,128)S(1)} %max.8, ...), kind=kOutput, calls=%fused_computation.11 | convolution fusion | flops 68419584 | bytes 3244032 | tf_op jit(solution)/shard_map/hgqk,khd->qhgd/dot_general | solution.py:180
  24.4 0.8 multiply_reduce_fusion
  25.3 1.9 %fusion.13 = bf16[2,8,128,128]{2,3,1,0:T(8,128)(2,1)S(1)} fusion(bf16[128,2,8,128]{0,3,2,1:T(8,128)(2,1)} %copy.212, f32[2,8,128]{2,1,0:T(8,128)S(1)} %copy.243, bf16[2,128,2,128]{1,3,2,0:T(8,128)(2,1)} %collective-permute-done, f32[2,8,128]{2,1,0:T(8,128)S(1)} %add.129, f32[2,8,128,128]{2,3,1,0:T(8,128)} %copy-done, f32[2,8,128]{2,1,0:T(8,128)S(1)} %max.8, ...), kind=kOutput, calls=%fused_computation.22 | convolution fusion | flops 68681728 | bytes 2203648 | tf_op jit(solution)/shard_map/qhgd,khd->hgqk/dot_general | solution.py:188
  27.5 0.5 copy-done.3
  28.0 0.6 copy-done.1
  28.6 0.4 fusion.24
  29.0 1.3 %collective-permute-start.1 = (bf16[2,128,2,128]{1,3,2,0:T(8,128)(2,1)S(1)}, bf16[2,128,2,128]{1,3,2,0:T(8,128)(2,1)S(1)}, u32[]{:S(2)}, u32[]{:S(2)}) collective-permute-start(bf16[2,128,2,128]{1,3,2,0:T(8,128)(2,1)S(1)} %pad_maximum_fusion.1), channel_id=1, source_target_pairs={{8,0},{16,8},{24,16},{9,1},{17,9},{25,17},{10,2},{18,10},{26,18},{... | collective-permute-start | bytes 393224 | tf_op jit(solution)/shard_map/ppermute | solution.py:24
  30.3 0.4 convolution_bitcast_fusion.6
  30.7 0.4 fusion.14
  31.4 5.7 %collective-permute-done.1 = bf16[2,128,2,128]{1,3,2,0:T(8,128)(2,1)S(1)} collective-permute-done((bf16[2,128,2,128]{1,3,2,0:T(8,128)(2,1)S(1)}, bf16[2,128,2,128]{1,3,2,0:T(8,128)(2,1)S(1)}, u32[]{:S(2)}, u32[]{:S(2)}) %collective-permute-start.1) | collective-permute-done | bytes 131104 | tf_op jit(solution)/shard_map/ppermute | solution.py:24
  37.3 0.5 copy-done.9
  37.8 3.5 %all-to-all-done.1 = bf16[1,128,16,256]{1,3,0,2:T(8,128)(2,1)S(1)} async-done(((bf16[1,128,16,256]{1,3,0,2:T(8,128)(2,1)}), bf16[1,128,16,256]{1,3,0,2:T(8,128)(2,1)S(1)}, u32[]{:S(2)}, u32[]{:S(2)}) %all-to-all-start.1) | async-done | bytes 1048608 | tf_op jit(solution)/shard_map/all_to_all | solution.py:227
  41.3 1.1 %broadcast_in_dim.38 = bf16[16,128,256]{2,1,0:T(8,128)(2,1)} broadcast(bf16[128,256]{1,0:T(8,128)(2,1)S(1)} %copy.213), dimensions={1,2} | broadcast | bytes 1114112 | tf_op jit(solution)/shard_map/broadcast_in_dim | solution.py:31
  42.4 5.9 %all-to-all-start = ((bf16[16,128,256]{2,1,0:T(8,128)(2,1)}), bf16[16,128,256]{2,1,0:T(8,128)(2,1)S(1)}, u32[]{:S(2)}, u32[]{:S(2)}) async-start(bf16[16,128,256]{2,1,0:T(8,128)(2,1)} %broadcast_in_dim.38), calls=%async_computation | async-start | bytes 2097152 | tf_op jit(solution)/shard_map/all_to_all | solution.py:32
  48.6 0.7 copy-done.4
  49.4 1.1 %fusion.8 = f32[2,128,8,128]{3,1,2,0:T(8,128)S(1)} fusion(f32[2,128,8,128]{3,1,2,0:T(8,128)S(1)} %fusion.41, bf16[2,8,128,128]{2,3,1,0:T(8,128)(2,1)S(1)} %copy-done.4, bf16[2,128,2,128]{1,3,2,0:T(8,128)(2,1)} %collective-permute-done), kind=kOutput, calls=%fused_computation.15 | convolution fusion | flops 67633152 | bytes 2686976 | tf_op jit(solution)/shard_map/hgqk,khd->qhgd/dot_general | solution.py:193
  50.8 0.7 copy-done.8
  51.6 1.2 %copy.222 = bf16[1,128,16,128]{3,2,1,0:T(8,128)(2,1)} copy(bf16[1,128,16,128]{1,3,2,0:T(8,128)(2,1)S(1)} %fusion.27) | data formatting | bytes 1048576
  52.8 0.7 slice_bitcast_fusion.1
  53.5 0.5 copy.216
  54.0 17.5 %all-to-all-done = bf16[16,128,256]{2,1,0:T(8,128)(2,1)S(1)} async-done(((bf16[16,128,256]{2,1,0:T(8,128)(2,1)}), bf16[16,128,256]{2,1,0:T(8,128)(2,1)S(1)}, u32[]{:S(2)}, u32[]{:S(2)}) %all-to-all-start) | async-done | bytes 1048608 | tf_op jit(solution)/shard_map/all_to_all | solution.py:32
  71.5 1.8 %multiply_reduce_fusion.1 = (f32[]{:T(128)}, f32[256,256]{0,1:T(8,128)}) fusion(bf16[2048,256]{1,0:T(8,128)(2,1)S(1)} %bitcast.199, bf16[2048,256]{1,0:T(8,128)(2,1)S(1)} %bitcast.200), kind=kOutput, calls=%fused_computation.60 | convolution fusion | flops 268566528 | bytes 2359300 | tf_op jit(solution)/shard_map/dot_general | solution.py:231
  73.3 0.6 collective-permute-start.2
  73.9 2.0 %collective-permute-start.3 = (f32[256,256]{0,1:T(8,128)}, f32[256,256]{0,1:T(8,128)S(1)}, u32[]{:S(2)}, u32[]{:S(2)}) collective-permute-start(f32[256,256]{0,1:T(8,128)} %get-tuple-element.63), channel_id=1, source_target_pairs={{0,16},{8,24},{16,0},{24,8},{1,17},{9,25},{17,1},{25,9},{2,18},{10... | collective-permute-start | bytes 786440 | tf_op jit(solution)/shard_map/ppermute | solution.py:42
  75.8 1.3 %broadcast_in_dim_broadcast_in_dim_broadcast_in_dim.3 = f32[32,8,128]{2,1,0:T(8,128)} broadcast(f32[]{:T(128)} %get-tuple-element.62), dimensions={} | broadcast | bytes 131076 | tf_op jit(solution)/shard_map/broadcast_in_dim;broadcast_in_dim;broadcast_in_dim | solution.py:31
  77.1 5.3 %all-to-all-start.2 = ((f32[32,8,128]{2,1,0:T(8,128)}), f32[32,8,128]{2,1,0:T(8,128)S(1)}, u32[]{:S(2)}, u32[]{:S(2)}) async-start(f32[32,8,128]{2,1,0:T(8,128)} %broadcast_in_dim_broadcast_in_dim_broadcast_in_dim.3), calls=%async_computation.2 | async-start | bytes 262144 | tf_op jit(solution)/shard_map/all_to_all | solution.py:32
  82.5 0.8 copy-done.10
  83.3 0.8 copy.224
  84.0 0.8 copy.223
  84.8 1.1 %copy.217 = f32[256,256]{1,0:T(8,128)S(1)} copy(f32[256,256]{0,1:T(8,128)} %get-tuple-element.63) | data formatting | bytes 524288 | tf_op jit(solution)/shard_map/dot_general | solution.py:231
  85.9 2.7 %collective-permute-start.4 = (f32[256,256]{0,1:T(8,128)}, f32[256,256]{0,1:T(8,128)S(1)}, u32[]{:S(2)}, u32[]{:S(2)}) collective-permute-start(f32[256,256]{0,1:T(8,128)} %get-tuple-element.63), channel_id=1, source_target_pairs={{0,24},{8,0},{16,8},{24,16},{1,25},{9,1},{17,9},{25,17},{2,26},{10... | collective-permute-start | bytes 786440 | tf_op jit(solution)/shard_map/ppermute | solution.py:42
  88.7 1.9 %all-to-all-done.2 = f32[32,8,128]{2,1,0:T(8,128)S(1)} async-done(((f32[32,8,128]{2,1,0:T(8,128)}), f32[32,8,128]{2,1,0:T(8,128)S(1)}, u32[]{:S(2)}, u32[]{:S(2)}) %all-to-all-start.2) | async-done | bytes 131104 | tf_op jit(solution)/shard_map/all_to_all | solution.py:32
  90.6 0.6 slice_reduce_fusion
  92.3 2.6 %collective-permute-done.4 = f32[256,256]{0,1:T(8,128)S(1)} collective-permute-done((f32[256,256]{0,1:T(8,128)}, f32[256,256]{0,1:T(8,128)S(1)}, u32[]{:S(2)}, u32[]{:S(2)}) %collective-permute-start.4) | collective-permute-done | bytes 262176 | tf_op jit(solution)/shard_map/ppermute | solution.py:42
  95.0 3.7 %multiply_subtract_fusion = (f32[1024,256]{1,0:T(8,128)}, f32[1024,256]{1,0:T(8,128)}, f32[1024,256]{1,0:T(8,128)}) fusion(f32[1024,256]{1,0:T(8,128)S(1)} %copy-done.6, f32[1024,256]{1,0:T(8,128)S(1)} %constant_dynamic-update-slice_fusion, f32[]{:T(128)S(6)} %min_shard_map.3, f32[1024,256]{1,0:T(8,128)} %param.20, f32[1024,256]{1,0:T(8,128)} %param.21), kind=kLoop, calls=%fused_computation.47 | loop fusion | flops 4194304 | bytes 7340036 | tf_op jit(solution)/shard_map/sub | solution.py:105
  (67 shorter events, 4.2 us)
Async XLA Ops:
  0.6 9.8 %copy-start.5 = (bf16[1,128,4096]{2,1,0:T(8,128)(2,1)S(1)}, bf16[1,128,4096]{2,1,0:T(8,128)(2,1)}, u32[]{:S(2)}) copy-start(bf16[1,128,4096]{2,1,0:T(8,128)(2,1)} %param.15) | copy-start | bytes 3145732
  2.7 15.0 %copy-start.7 = (f32[128,128]{0,1:T(8,128)}, f32[128,128]{0,1:T(8,128)S(1)}, u32[]{:S(2)}) copy-start(f32[128,128]{0,1:T(8,128)S(1)} %pad_maximum_fusion.2) | copy-start | bytes 196612
  4.9 15.6 %collective-permute-start = (bf16[2,128,2,128]{1,3,2,0:T(8,128)(2,1)S(1)}, bf16[2,128,2,128]{1,3,2,0:T(8,128)(2,1)}, u32[]{:S(2)}, u32[]{:S(2)}) collective-permute-start(bf16[2,128,2,128]{1,3,2,0:T(8,128)(2,1)S(1)} %pad_maximum_fusion), channel_id=1, source_target_pairs={{0,8},{8,16},{16,24},{1,9},{9,17},{17,25},{2,10},{10,18},{18,26},{... | collective-permute-start | bytes 393224 | tf_op jit(solution)/shard_map/ppermute | solution.py:24
  11.8 5.5 %copy-start.11 = (bf16[1,128,16,128]{3,2,1,0:T(8,128)(2,1)S(1)}, bf16[1,128,16,128]{3,2,1,0:T(8,128)(2,1)}, u32[]{:S(2)}) copy-start(bf16[1,128,16,128]{3,2,1,0:T(8,128)(2,1)} %param.11) | copy-start | bytes 1572868
  11.8 29.5 %all-to-all-start.1 = ((bf16[1,128,16,256]{1,3,0,2:T(8,128)(2,1)}), bf16[1,128,16,256]{1,3,0,2:T(8,128)(2,1)S(1)}, u32[]{:S(2)}, u32[]{:S(2)}) async-start(bf16[1,128,16,256]{1,3,0,2:T(8,128)(2,1)} %bitcast.61), calls=%async_computation.1 | async-start | bytes 2097152 | tf_op jit(solution)/shard_map/all_to_all | solution.py:227
  18.3 1.0 %copy-start.2 = (bf16[1,128,16,128]{3,2,1,0:T(8,128)(2,1)S(1)}, bf16[1,128,16,128]{3,2,1,0:T(8,128)(2,1)}, u32[]{:S(2)}) copy-start(bf16[1,128,16,128]{3,2,1,0:T(8,128)(2,1)} %param.14) | copy-start | bytes 1572868
  21.8 1.4 %copy-start = (f32[2,8,128,128]{2,3,1,0:T(8,128)}, f32[2,8,128,128]{2,3,1,0:T(8,128)S(1)}, u32[]{:S(2)}) copy-start(f32[2,8,128,128]{2,3,1,0:T(8,128)S(1)} %get-tuple-element.61) | copy-start | bytes 3145732
  21.8 0.9 copy-start.15
  25.2 2.7 %copy-start.12 = (bf16[128,2,8,128]{0,3,2,1:T(8,128)(2,1)S(1)}, bf16[128,2,8,128]{0,3,2,1:T(8,128)(2,1)}, u32[]{:S(2)}) copy-start(bf16[128,2,8,128]{0,3,2,1:T(8,128)(2,1)} %copy.212) | copy-start | bytes 1572868
  27.2 0.8 copy-start.3
  27.2 1.4 %copy-start.1 = (f32[2,8,128,128]{2,3,1,0:T(8,128)S(1)}, f32[2,8,128,128]{2,3,1,0:T(8,128)}, u32[]{:S(2)}) copy-start(f32[2,8,128,128]{2,3,1,0:T(8,128)} %copy-done) | copy-start | bytes 3145732
  29.0 8.2 %collective-permute-start.1 = (bf16[2,128,2,128]{1,3,2,0:T(8,128)(2,1)S(1)}, bf16[2,128,2,128]{1,3,2,0:T(8,128)(2,1)S(1)}, u32[]{:S(2)}, u32[]{:S(2)}) collective-permute-start(bf16[2,128,2,128]{1,3,2,0:T(8,128)(2,1)S(1)} %pad_maximum_fusion.1), channel_id=1, source_target_pairs={{8,0},{16,8},{24,16},{9,1},{17,9},{25,17},{10,2},{18,10},{26,18},{... | collective-permute-start | bytes 393224 | tf_op jit(solution)/shard_map/ppermute | solution.py:24
  37.2 0.6 copy-start.9
  42.4 29.2 %all-to-all-start = ((bf16[16,128,256]{2,1,0:T(8,128)(2,1)}), bf16[16,128,256]{2,1,0:T(8,128)(2,1)S(1)}, u32[]{:S(2)}, u32[]{:S(2)}) async-start(bf16[16,128,256]{2,1,0:T(8,128)(2,1)} %broadcast_in_dim.38), calls=%async_computation | async-start | bytes 2097152 | tf_op jit(solution)/shard_map/all_to_all | solution.py:32
  48.3 1.0 %copy-start.4 = (bf16[2,8,128,128]{2,3,1,0:T(8,128)(2,1)S(1)}, bf16[2,8,128,128]{2,3,1,0:T(8,128)(2,1)}, u32[]{:S(2)}) copy-start(bf16[2,8,128,128]{2,3,1,0:T(8,128)(2,1)} %copy-done.3) | copy-start | bytes 1572868
  50.6 0.8 copy-start.8
  73.3 18.6 %collective-permute-start.2 = (f32[256,256]{0,1:T(8,128)}, f32[256,256]{0,1:T(8,128)S(1)}, u32[]{:S(2)}, u32[]{:S(2)}) collective-permute-start(f32[256,256]{0,1:T(8,128)} %get-tuple-element.63), channel_id=1, source_target_pairs={{0,8},{8,16},{16,24},{24,0},{1,9},{9,17},{17,25},{25,1},{2,10},{10... | collective-permute-start | bytes 786440 | tf_op jit(solution)/shard_map/ppermute | solution.py:42
  73.9 18.2 %collective-permute-start.3 = (f32[256,256]{0,1:T(8,128)}, f32[256,256]{0,1:T(8,128)S(1)}, u32[]{:S(2)}, u32[]{:S(2)}) collective-permute-start(f32[256,256]{0,1:T(8,128)} %get-tuple-element.63), channel_id=1, source_target_pairs={{0,16},{8,24},{16,0},{24,8},{1,17},{9,25},{17,1},{25,9},{2,18},{10... | collective-permute-start | bytes 786440 | tf_op jit(solution)/shard_map/ppermute | solution.py:42
  77.1 5.3 %copy-start.13 = (f32[1,128,2,64]{1,3,2,0:T(8,128)S(1)}, f32[1,128,2,64]{1,3,2,0:T(8,128)}, u32[]{:S(2)}) copy-start(f32[1,128,2,64]{1,3,2,0:T(8,128)} %get-tuple-element.52) | copy-start | bytes 196612
  77.1 5.3 %copy-start.14 = (f32[1,128,2,64]{1,3,2,0:T(8,128)S(1)}, f32[1,128,2,64]{1,3,2,0:T(8,128)}, u32[]{:S(2)}) copy-start(f32[1,128,2,64]{1,3,2,0:T(8,128)} %get-tuple-element.53) | copy-start | bytes 196612
  77.1 13.4 %all-to-all-start.2 = ((f32[32,8,128]{2,1,0:T(8,128)}), f32[32,8,128]{2,1,0:T(8,128)S(1)}, u32[]{:S(2)}, u32[]{:S(2)}) async-start(f32[32,8,128]{2,1,0:T(8,128)} %broadcast_in_dim_broadcast_in_dim_broadcast_in_dim.3), calls=%async_computation.2 | async-start | bytes 262144 | tf_op jit(solution)/shard_map/all_to_all | solution.py:32
  82.4 0.8 copy-start.10
  85.9 9.0 %collective-permute-start.4 = (f32[256,256]{0,1:T(8,128)}, f32[256,256]{0,1:T(8,128)S(1)}, u32[]{:S(2)}, u32[]{:S(2)}) collective-permute-start(f32[256,256]{0,1:T(8,128)} %get-tuple-element.63), channel_id=1, source_target_pairs={{0,24},{8,0},{16,8},{24,16},{1,25},{9,1},{17,9},{25,17},{2,26},{10... | collective-permute-start | bytes 786440 | tf_op jit(solution)/shard_map/ppermute | solution.py:42
  92.2 2.8 %copy-start.6 = (f32[1024,256]{1,0:T(8,128)S(1)}, f32[1024,256]{1,0:T(8,128)}, u32[]{:S(2)}) copy-start(f32[1024,256]{1,0:T(8,128)} %param.19) | copy-start | bytes 3145732

commit v8 on v7

--- a/solution.py
+++ b/solution.py
@@ -5,6 +5,7 @@
 import jax.numpy as jnp
 from jax import lax
 from jax.sharding import PartitionSpec as P
+
 
 ROPE_BASE = 500000.0
 NEG_FILL = -1e30
@@ -72,12 +73,6 @@
     return (cosine[:, None, :], sine[:, None, :])
 
 
-def rotate(vectors, cosine, sine):
-    half = vectors.shape[-1] // 2
-    turned = jnp.concatenate([-vectors[..., half:], vectors[..., :half]], axis=-1)
-    return vectors * cosine + turned * sine
-
-
 def rotate_low(vectors, cosine, sine):
     half = vectors.shape[-1] // 2
     eye = jnp.eye(half, dtype=jnp.bfloat16)
@@ -106,7 +101,7 @@
     return (new_param, new_first, new_second)
 
 
-def local(
+def local_body(
     queries,
     keys,
     values,
@@ -218,7 +213,6 @@
     grad_k = unrotate(key_total[0], cosine, sine).astype(jnp.bfloat16)
     grad_v = key_total[1].astype(jnp.bfloat16)
     feats = features[0]
-    width = feats.shape[1]
     value_flat = grad_v.reshape(tok_rows, kv_count * head_dim)
     own_rows = param.shape[0]
     n_dp = lax.axis_size("dp")
@@ -259,7 +253,7 @@
         P("dp", "tp"),
     )
     return jax.shard_map(
-        local,
+        local_body,
         mesh=mesh,
         in_specs=placed,
         out_specs=(

time: 99.8 us -> 99.8 us (level)
  no operation moved by 1% of the time
where the time goes in v8:
time: 99.8 us; the launch traced here: 98.7 us
  waiting for transfers between devices  31.1 us (31%)
  starting transfers between devices  28.7 us (29%)
  local copies, waits for them, and re-layouts  18.3 us (18%)
  matrix products  10.7 us (11%)
  other arithmetic  8.01 us (8%)
  between operations  1.93 us (2%)
    all_to_all x2, waiting for transfers between devices, spread_copy(): return lax.all_to_all(stacked, axes, 0, 0, tiled=False)  19.4 us
    unnamed x39, local copies, waits for them, and re-layouts  11.5 us
    all_to_all x2, starting transfers between devices, spread_copy(): return lax.all_to_all(stacked, axes, 0, 0, tiled=False)  11.2 us
    ppermute x2, starting transfers between devices, shifted(): return lax.ppermute(array, axis, pairs)  6.81 us
    ppermute x2, waiting for transfers between devices, shifted(): return lax.ppermute(array, axis, pairs)  5.75 us
    all_to_all x1, starting transfers between devices, local_body(): lax.all_to_all(feats.reshape(tok_rows, n_dp * n_ctx, piece_rows), spread,...  5.45 us
    ppermute x3, starting transfers between devices, ring_copy(): lax.ppermute(array, axis, [(i, (i + step) % peers) for i in range(peers)])  5.25 us
    sub x1, other arithmetic, adam_update(): new_param = param - LEARN_RATE * (step_size + DECAY_RATE * param)  3.71 us
  transfers between devices with their start and end apart: 8, of which 5 were waited for; matrix products, arithmetic and copies ran while one was open for 21% of the time, Pallas kernels for 0%

profile of v8, /device:TPU:0, one launch (start us, length us, event | category | flops | bytes accessed | tf_op | source)
XLA Modules:
  0.0 98.7 jit_solution(864553586378624362)
XLA Ops:
  0.7 0.8 copy.188
  1.8 0.7 convert_divide_fusion
  2.7 1.0 copy.187
  3.7 1.0 copy.194
  4.9 5.5 %collective-permute-start = (bf16[2,128,2,128]{1,3,2,0:T(8,128)(2,1)S(1)}, bf16[2,128,2,128]{1,3,2,0:T(8,128)(2,1)}, u32[]{:S(2)}, u32[]{:S(2)}) collective-permute-start(bf16[2,128,2,128]{1,3,2,0:T(8,128)(2,1)S(1)} %pad_maximum_fusion), channel_id=1, source_target_pairs={{0,8},{8,16},{16,24},{1,9},{9,17},{17,25},{2,10},{10,18},{18,26},{... | collective-permute-start | bytes 393224 | tf_op jit(solution)/shard_map/ppermute | solution.py:25
  10.5 1.3 %copy.214 = bf16[1,128,4096]{1,2,0:T(8,128)(2,1)} copy(bf16[1,128,4096]{2,1,0:T(8,128)(2,1)S(1)} %copy-done.5) | data formatting | bytes 2097152 | tf_op args[4]
  11.8 5.4 %all-to-all-start.1 = ((bf16[1,128,16,256]{1,3,0,2:T(8,128)(2,1)}), bf16[1,128,16,256]{1,3,0,2:T(8,128)(2,1)S(1)}, u32[]{:S(2)}, u32[]{:S(2)}) async-start(bf16[1,128,16,256]{1,3,0,2:T(8,128)(2,1)} %bitcast.61), calls=%async_computation.1 | async-start | bytes 2097152 | tf_op jit(solution)/shard_map/all_to_all | solution.py:221
  17.2 0.5 copy.190
  18.7 0.7 copy-done.2
  19.3 1.2 %copy.212 = bf16[128,2,8,128]{0,3,2,1:T(8,128)(2,1)} copy(bf16[128,2,8,128]{3,2,1,0:T(8,128)(2,1)S(1)} %bitcast.201) | data formatting | bytes 1048576 | tf_op jit(solution)/shard_map/reshape;squeeze | solution.py:135
  20.6 1.2 %fusion.70 = (f32[2,8,128]{2,1,0:T(8,128)S(1)}, f32[2,8,128,128]{2,3,1,0:T(8,128)S(1)}) fusion(bf16[128,2,8,128]{0,3,2,1:T(8,128)(2,1)S(1)} %bitcast.196, bf16[2,128,2,128]{1,3,2,0:T(8,128)(2,1)} %collective-permute-done, pred[128,128]{0,1:T(8,128)(4,1)S(1)} %get-tuple-element.54), kind=kOutput, calls=%fused_computation.122 | convolution fusion | flops 67893248 | bytes 1662976 | tf_op jit(solution)/shard_map/qhgd,khd->hgqk/dot_general | solution.py:154
  22.2 0.5 copy-done.15
  22.7 0.4 convolution_bitcast_fusion.2
  23.2 1.3 %fusion.5 = f32[2,8,128,128]{3,2,1,0:T(8,128)S(1)} fusion(f32[128,2,8,128]{3,0,2,1:T(8,128)S(1)} %convolution_bitcast_fusion.2, bf16[2,128,2,128]{1,3,2,0:T(8,128)(2,1)} %collective-permute-done, f32[2,8,128,128]{2,3,1,0:T(8,128)S(1)} %get-tuple-element.61, f32[2,8,128]{2,1,0:T(8,128)S(1)} %add.129, f32[2,8,128]{2,1,0:T(8,128)S(1)} %max.8, ...), kind=kOutput, calls=%fused_computation.11 | convolution fusion | flops 68419584 | bytes 3244032 | tf_op jit(solution)/shard_map/hgqk,khd->qhgd/dot_general | solution.py:175
  24.4 0.8 multiply_reduce_fusion
  25.3 1.9 %fusion.13 = bf16[2,8,128,128]{2,3,1,0:T(8,128)(2,1)S(1)} fusion(bf16[128,2,8,128]{0,3,2,1:T(8,128)(2,1)} %copy.212, f32[2,8,128]{2,1,0:T(8,128)S(1)} %copy.243, bf16[2,128,2,128]{1,3,2,0:T(8,128)(2,1)} %collective-permute-done, f32[2,8,128]{2,1,0:T(8,128)S(1)} %add.129, f32[2,8,128,128]{2,3,1,0:T(8,128)} %copy-done, f32[2,8,128]{2,1,0:T(8,128)S(1)} %max.8, ...), kind=kOutput, calls=%fused_computation.22 | convolution fusion | flops 68681728 | bytes 2203648 | tf_op jit(solution)/shard_map/qhgd,khd->hgqk/dot_general | solution.py:183
  27.5 0.5 copy-done.3
  28.0 0.6 copy-done.1
  28.6 0.4 fusion.24
  29.0 1.3 %collective-permute-start.1 = (bf16[2,128,2,128]{1,3,2,0:T(8,128)(2,1)S(1)}, bf16[2,128,2,128]{1,3,2,0:T(8,128)(2,1)S(1)}, u32[]{:S(2)}, u32[]{:S(2)}) collective-permute-start(bf16[2,128,2,128]{1,3,2,0:T(8,128)(2,1)S(1)} %pad_maximum_fusion.1), channel_id=1, source_target_pairs={{8,0},{16,8},{24,16},{9,1},{17,9},{25,17},{10,2},{18,10},{26,18},{... | collective-permute-start | bytes 393224 | tf_op jit(solution)/shard_map/ppermute | solution.py:25
  30.3 0.4 convolution_bitcast_fusion.6
  30.7 0.4 fusion.14
  31.4 5.7 %collective-permute-done.1 = bf16[2,128,2,128]{1,3,2,0:T(8,128)(2,1)S(1)} collective-permute-done((bf16[2,128,2,128]{1,3,2,0:T(8,128)(2,1)S(1)}, bf16[2,128,2,128]{1,3,2,0:T(8,128)(2,1)S(1)}, u32[]{:S(2)}, u32[]{:S(2)}) %collective-permute-start.1) | collective-permute-done | bytes 131104 | tf_op jit(solution)/shard_map/ppermute | solution.py:25
  37.3 0.5 copy-done.9
  37.8 3.5 %all-to-all-done.1 = bf16[1,128,16,256]{1,3,0,2:T(8,128)(2,1)S(1)} async-done(((bf16[1,128,16,256]{1,3,0,2:T(8,128)(2,1)}), bf16[1,128,16,256]{1,3,0,2:T(8,128)(2,1)S(1)}, u32[]{:S(2)}, u32[]{:S(2)}) %all-to-all-start.1) | async-done | bytes 1048608 | tf_op jit(solution)/shard_map/all_to_all | solution.py:221
  41.3 1.1 %broadcast_in_dim.38 = bf16[16,128,256]{2,1,0:T(8,128)(2,1)} broadcast(bf16[128,256]{1,0:T(8,128)(2,1)S(1)} %copy.213), dimensions={1,2} | broadcast | bytes 1114112 | tf_op jit(solution)/shard_map/broadcast_in_dim | solution.py:32
  42.4 5.9 %all-to-all-start = ((bf16[16,128,256]{2,1,0:T(8,128)(2,1)}), bf16[16,128,256]{2,1,0:T(8,128)(2,1)S(1)}, u32[]{:S(2)}, u32[]{:S(2)}) async-start(bf16[16,128,256]{2,1,0:T(8,128)(2,1)} %broadcast_in_dim.38), calls=%async_computation | async-start | bytes 2097152 | tf_op jit(solution)/shard_map/all_to_all | solution.py:33
  48.6 0.7 copy-done.4
  49.4 1.1 %fusion.8 = f32[2,128,8,128]{3,1,2,0:T(8,128)S(1)} fusion(f32[2,128,8,128]{3,1,2,0:T(8,128)S(1)} %fusion.41, bf16[2,8,128,128]{2,3,1,0:T(8,128)(2,1)S(1)} %copy-done.4, bf16[2,128,2,128]{1,3,2,0:T(8,128)(2,1)} %collective-permute-done), kind=kOutput, calls=%fused_computation.15 | convolution fusion | flops 67633152 | bytes 2686976 | tf_op jit(solution)/shard_map/hgqk,khd->qhgd/dot_general | solution.py:188
  50.8 0.7 copy-done.8
  51.6 1.2 %copy.222 = bf16[1,128,16,128]{3,2,1,0:T(8,128)(2,1)} copy(bf16[1,128,16,128]{1,3,2,0:T(8,128)(2,1)S(1)} %fusion.27) | data formatting | bytes 1048576
  52.8 0.7 slice_bitcast_fusion.1
  53.5 0.5 copy.216
  54.0 17.5 %all-to-all-done = bf16[16,128,256]{2,1,0:T(8,128)(2,1)S(1)} async-done(((bf16[16,128,256]{2,1,0:T(8,128)(2,1)}), bf16[16,128,256]{2,1,0:T(8,128)(2,1)S(1)}, u32[]{:S(2)}, u32[]{:S(2)}) %all-to-all-start) | async-done | bytes 1048608 | tf_op jit(solution)/shard_map/all_to_all | solution.py:33
  71.5 1.8 %multiply_reduce_fusion.1 = (f32[]{:T(128)}, f32[256,256]{0,1:T(8,128)}) fusion(bf16[2048,256]{1,0:T(8,128)(2,1)S(1)} %bitcast.199, bf16[2048,256]{1,0:T(8,128)(2,1)S(1)} %bitcast.200), kind=kOutput, calls=%fused_computation.60 | convolution fusion | flops 268566528 | bytes 2359300 | tf_op jit(solution)/shard_map/dot_general | solution.py:225
  73.3 0.6 collective-permute-start.2
  73.9 2.0 %collective-permute-start.3 = (f32[256,256]{0,1:T(8,128)}, f32[256,256]{0,1:T(8,128)S(1)}, u32[]{:S(2)}, u32[]{:S(2)}) collective-permute-start(f32[256,256]{0,1:T(8,128)} %get-tuple-element.63), channel_id=1, source_target_pairs={{0,16},{8,24},{16,0},{24,8},{1,17},{9,25},{17,1},{25,9},{2,18},{10... | collective-permute-start | bytes 786440 | tf_op jit(solution)/shard_map/ppermute | solution.py:43
  75.8 1.3 %broadcast_in_dim_broadcast_in_dim_broadcast_in_dim.3 = f32[32,8,128]{2,1,0:T(8,128)} broadcast(f32[]{:T(128)} %get-tuple-element.62), dimensions={} | broadcast | bytes 131076 | tf_op jit(solution)/shard_map/broadcast_in_dim;broadcast_in_dim;broadcast_in_dim | solution.py:32
  77.1 5.3 %all-to-all-start.2 = ((f32[32,8,128]{2,1,0:T(8,128)}), f32[32,8,128]{2,1,0:T(8,128)S(1)}, u32[]{:S(2)}, u32[]{:S(2)}) async-start(f32[32,8,128]{2,1,0:T(8,128)} %broadcast_in_dim_broadcast_in_dim_broadcast_in_dim.3), calls=%async_computation.2 | async-start | bytes 262144 | tf_op jit(solution)/shard_map/all_to_all | solution.py:33
  82.5 0.8 copy-done.10
  83.3 0.8 copy.224
  84.0 0.8 copy.223
  84.8 1.1 %copy.217 = f32[256,256]{1,0:T(8,128)S(1)} copy(f32[256,256]{0,1:T(8,128)} %get-tuple-element.63) | data formatting | bytes 524288 | tf_op jit(solution)/shard_map/dot_general | solution.py:225
  85.9 2.7 %collective-permute-start.4 = (f32[256,256]{0,1:T(8,128)}, f32[256,256]{0,1:T(8,128)S(1)}, u32[]{:S(2)}, u32[]{:S(2)}) collective-permute-start(f32[256,256]{0,1:T(8,128)} %get-tuple-element.63), channel_id=1, source_target_pairs={{0,24},{8,0},{16,8},{24,16},{1,25},{9,1},{17,9},{25,17},{2,26},{10... | collective-permute-start | bytes 786440 | tf_op jit(solution)/shard_map/ppermute | solution.py:43
  88.7 1.9 %all-to-all-done.2 = f32[32,8,128]{2,1,0:T(8,128)S(1)} async-done(((f32[32,8,128]{2,1,0:T(8,128)}), f32[32,8,128]{2,1,0:T(8,128)S(1)}, u32[]{:S(2)}, u32[]{:S(2)}) %all-to-all-start.2) | async-done | bytes 131104 | tf_op jit(solution)/shard_map/all_to_all | solution.py:33
  90.6 0.6 slice_reduce_fusion
  92.3 2.6 %collective-permute-done.4 = f32[256,256]{0,1:T(8,128)S(1)} collective-permute-done((f32[256,256]{0,1:T(8,128)}, f32[256,256]{0,1:T(8,128)S(1)}, u32[]{:S(2)}, u32[]{:S(2)}) %collective-permute-start.4) | collective-permute-done | bytes 262176 | tf_op jit(solution)/shard_map/ppermute | solution.py:43
  95.0 3.7 %multiply_subtract_fusion = (f32[1024,256]{1,0:T(8,128)}, f32[1024,256]{1,0:T(8,128)}, f32[1024,256]{1,0:T(8,128)}) fusion(f32[1024,256]{1,0:T(8,128)S(1)} %copy-done.6, f32[1024,256]{1,0:T(8,128)S(1)} %constant_dynamic-update-slice_fusion, f32[]{:T(128)S(6)} %min_shard_map.3, f32[1024,256]{1,0:T(8,128)} %param.20, f32[1024,256]{1,0:T(8,128)} %param.21), kind=kLoop, calls=%fused_computation.47 | loop fusion | flops 4194304 | bytes 7340036 | tf_op jit(solution)/shard_map/sub | solution.py:100
  (67 shorter events, 4.2 us)
Async XLA Ops:
  0.6 9.8 %copy-start.5 = (bf16[1,128,4096]{2,1,0:T(8,128)(2,1)S(1)}, bf16[1,128,4096]{2,1,0:T(8,128)(2,1)}, u32[]{:S(2)}) copy-start(bf16[1,128,4096]{2,1,0:T(8,128)(2,1)} %param.15) | copy-start | bytes 3145732
  2.7 15.0 %copy-start.7 = (f32[128,128]{0,1:T(8,128)}, f32[128,128]{0,1:T(8,128)S(1)}, u32[]{:S(2)}) copy-start(f32[128,128]{0,1:T(8,128)S(1)} %pad_maximum_fusion.2) | copy-start | bytes 196612
  4.9 15.6 %collective-permute-start = (bf16[2,128,2,128]{1,3,2,0:T(8,128)(2,1)S(1)}, bf16[2,128,2,128]{1,3,2,0:T(8,128)(2,1)}, u32[]{:S(2)}, u32[]{:S(2)}) collective-permute-start(bf16[2,128,2,128]{1,3,2,0:T(8,128)(2,1)S(1)} %pad_maximum_fusion), channel_id=1, source_target_pairs={{0,8},{8,16},{16,24},{1,9},{9,17},{17,25},{2,10},{10,18},{18,26},{... | collective-permute-start | bytes 393224 | tf_op jit(solution)/shard_map/ppermute | solution.py:25
  11.8 5.5 %copy-start.11 = (bf16[1,128,16,128]{3,2,1,0:T(8,128)(2,1)S(1)}, bf16[1,128,16,128]{3,2,1,0:T(8,128)(2,1)}, u32[]{:S(2)}) copy-start(bf16[1,128,16,128]{3,2,1,0:T(8,128)(2,1)} %param.11) | copy-start | bytes 1572868
  11.8 29.5 %all-to-all-start.1 = ((bf16[1,128,16,256]{1,3,0,2:T(8,128)(2,1)}), bf16[1,128,16,256]{1,3,0,2:T(8,128)(2,1)S(1)}, u32[]{:S(2)}, u32[]{:S(2)}) async-start(bf16[1,128,16,256]{1,3,0,2:T(8,128)(2,1)} %bitcast.61), calls=%async_computation.1 | async-start | bytes 2097152 | tf_op jit(solution)/shard_map/all_to_all | solution.py:221
  18.3 1.0 %copy-start.2 = (bf16[1,128,16,128]{3,2,1,0:T(8,128)(2,1)S(1)}, bf16[1,128,16,128]{3,2,1,0:T(8,128)(2,1)}, u32[]{:S(2)}) copy-start(bf16[1,128,16,128]{3,2,1,0:T(8,128)(2,1)} %param.14) | copy-start | bytes 1572868
  21.8 1.4 %copy-start = (f32[2,8,128,128]{2,3,1,0:T(8,128)}, f32[2,8,128,128]{2,3,1,0:T(8,128)S(1)}, u32[]{:S(2)}) copy-start(f32[2,8,128,128]{2,3,1,0:T(8,128)S(1)} %get-tuple-element.61) | copy-start | bytes 3145732
  21.8 0.9 copy-start.15
  25.2 2.7 %copy-start.12 = (bf16[128,2,8,128]{0,3,2,1:T(8,128)(2,1)S(1)}, bf16[128,2,8,128]{0,3,2,1:T(8,128)(2,1)}, u32[]{:S(2)}) copy-start(bf16[128,2,8,128]{0,3,2,1:T(8,128)(2,1)} %copy.212) | copy-start | bytes 1572868
  27.2 0.8 copy-start.3
  27.2 1.4 %copy-start.1 = (f32[2,8,128,128]{2,3,1,0:T(8,128)S(1)}, f32[2,8,128,128]{2,3,1,0:T(8,128)}, u32[]{:S(2)}) copy-start(f32[2,8,128,128]{2,3,1,0:T(8,128)} %copy-done) | copy-start | bytes 3145732
  29.0 8.2 %collective-permute-start.1 = (bf16[2,128,2,128]{1,3,2,0:T(8,128)(2,1)S(1)}, bf16[2,128,2,128]{1,3,2,0:T(8,128)(2,1)S(1)}, u32[]{:S(2)}, u32[]{:S(2)}) collective-permute-start(bf16[2,128,2,128]{1,3,2,0:T(8,128)(2,1)S(1)} %pad_maximum_fusion.1), channel_id=1, source_target_pairs={{8,0},{16,8},{24,16},{9,1},{17,9},{25,17},{10,2},{18,10},{26,18},{... | collective-permute-start | bytes 393224 | tf_op jit(solution)/shard_map/ppermute | solution.py:25
  37.2 0.6 copy-start.9
  42.4 29.2 %all-to-all-start = ((bf16[16,128,256]{2,1,0:T(8,128)(2,1)}), bf16[16,128,256]{2,1,0:T(8,128)(2,1)S(1)}, u32[]{:S(2)}, u32[]{:S(2)}) async-start(bf16[16,128,256]{2,1,0:T(8,128)(2,1)} %broadcast_in_dim.38), calls=%async_computation | async-start | bytes 2097152 | tf_op jit(solution)/shard_map/all_to_all | solution.py:33
  48.3 1.0 %copy-start.4 = (bf16[2,8,128,128]{2,3,1,0:T(8,128)(2,1)S(1)}, bf16[2,8,128,128]{2,3,1,0:T(8,128)(2,1)}, u32[]{:S(2)}) copy-start(bf16[2,8,128,128]{2,3,1,0:T(8,128)(2,1)} %copy-done.3) | copy-start | bytes 1572868
  50.6 0.8 copy-start.8
  73.3 18.6 %collective-permute-start.2 = (f32[256,256]{0,1:T(8,128)}, f32[256,256]{0,1:T(8,128)S(1)}, u32[]{:S(2)}, u32[]{:S(2)}) collective-permute-start(f32[256,256]{0,1:T(8,128)} %get-tuple-element.63), channel_id=1, source_target_pairs={{0,8},{8,16},{16,24},{24,0},{1,9},{9,17},{17,25},{25,1},{2,10},{10... | collective-permute-start | bytes 786440 | tf_op jit(solution)/shard_map/ppermute | solution.py:43
  73.9 18.2 %collective-permute-start.3 = (f32[256,256]{0,1:T(8,128)}, f32[256,256]{0,1:T(8,128)S(1)}, u32[]{:S(2)}, u32[]{:S(2)}) collective-permute-start(f32[256,256]{0,1:T(8,128)} %get-tuple-element.63), channel_id=1, source_target_pairs={{0,16},{8,24},{16,0},{24,8},{1,17},{9,25},{17,1},{25,9},{2,18},{10... | collective-permute-start | bytes 786440 | tf_op jit(solution)/shard_map/ppermute | solution.py:43
  77.1 5.3 %copy-start.13 = (f32[1,128,2,64]{1,3,2,0:T(8,128)S(1)}, f32[1,128,2,64]{1,3,2,0:T(8,128)}, u32[]{:S(2)}) copy-start(f32[1,128,2,64]{1,3,2,0:T(8,128)} %get-tuple-element.52) | copy-start | bytes 196612
  77.1 5.3 %copy-start.14 = (f32[1,128,2,64]{1,3,2,0:T(8,128)S(1)}, f32[1,128,2,64]{1,3,2,0:T(8,128)}, u32[]{:S(2)}) copy-start(f32[1,128,2,64]{1,3,2,0:T(8,128)} %get-tuple-element.53) | copy-start | bytes 196612
  77.1 13.4 %all-to-all-start.2 = ((f32[32,8,128]{2,1,0:T(8,128)}), f32[32,8,128]{2,1,0:T(8,128)S(1)}, u32[]{:S(2)}, u32[]{:S(2)}) async-start(f32[32,8,128]{2,1,0:T(8,128)} %broadcast_in_dim_broadcast_in_dim_broadcast_in_dim.3), calls=%async_computation.2 | async-start | bytes 262144 | tf_op jit(solution)/shard_map/all_to_all | solution.py:33
  82.4 0.8 copy-start.10
  85.9 9.0 %collective-permute-start.4 = (f32[256,256]{0,1:T(8,128)}, f32[256,256]{0,1:T(8,128)S(1)}, u32[]{:S(2)}, u32[]{:S(2)}) collective-permute-start(f32[256,256]{0,1:T(8,128)} %get-tuple-element.63), channel_id=1, source_target_pairs={{0,24},{8,0},{16,8},{24,16},{1,25},{9,1},{17,9},{25,17},{2,26},{10... | collective-permute-start | bytes 786440 | tf_op jit(solution)/shard_map/ppermute | solution.py:43
  92.2 2.8 %copy-start.6 = (f32[1024,256]{1,0:T(8,128)S(1)}, f32[1024,256]{1,0:T(8,128)}, u32[]{:S(2)}) copy-start(f32[1024,256]{1,0:T(8,128)} %param.19) | copy-start | bytes 3145732

commit v9 on v4

--- a/solution.py
+++ b/solution.py
@@ -5,6 +5,7 @@
 import jax.numpy as jnp
 from jax import lax
 from jax.sharding import PartitionSpec as P
+
 
 ROPE_BASE = 500000.0
 NEG_FILL = -1e30
@@ -44,6 +45,25 @@
     return out
 
 
+def doubling_copy(array, axis):
+    peers = lax.axis_size(axis)
+    if peers & (peers - 1):
+        return ring_copy(array, axis)
+    place = lax.axis_index(axis)
+    gathered = array
+    span = 1
+    while span < peers:
+        other = lax.ppermute(gathered, axis, [(i, i ^ span) for i in range(peers)])
+        low_half = (place & span) == 0
+        gathered = jnp.where(
+            low_half,
+            jnp.concatenate([gathered, other], axis=0),
+            jnp.concatenate([other, gathered], axis=0),
+        )
+        span *= 2
+    return gathered
+
+
 def spread_sum(value, axes):
     peers = lax.axis_size(axes)
     if peers > 64:
@@ -72,10 +92,15 @@
     return (cosine[:, None, :], sine[:, None, :])
 
 
-def rotate(vectors, cosine, sine):
+def rotate_low(vectors, cosine, sine):
     half = vectors.shape[-1] // 2
-    turned = jnp.concatenate([-vectors[..., half:], vectors[..., :half]], axis=-1)
-    return vectors * cosine + turned * sine
+    eye = jnp.eye(half, dtype=jnp.bfloat16)
+    zero = jnp.zeros((half, half), jnp.bfloat16)
+    swap = jnp.concatenate(
+        [jnp.concatenate([zero, eye], axis=1), jnp.concatenate([-eye, zero], axis=1)], axis=0
+    )
+    turned = jnp.einsum("...d,de->...e", vectors, swap, preferred_element_type=jnp.float32)
+    return vectors.astype(jnp.float32) * cosine + turned * sine
 
 
 def unrotate(grads_in, cosine, sine):
@@ -95,7 +120,7 @@
     return (new_param, new_first, new_second)
 
 
-def local(
+def local_body(
     queries,
     keys,
     values,
@@ -123,9 +148,9 @@
     own_index = place * tok_rows + jnp.arange(tok_rows, dtype=jnp.int32)
     own_doc, position = doc_layout(lengths_row, own_index)
     cosine, sine = rope_tables(position, rope_num, rope_den, head_dim)
-    rotated_query_rows = rotate(queries[0].astype(jnp.float32), cosine, sine).astype(jnp.bfloat16)
+    rotated_query_rows = rotate_low(queries[0], cosine, sine).astype(jnp.bfloat16)
     rotated_query_rows = rotated_query_rows.reshape(tok_rows, kv_count, group_size, head_dim)
-    rotated_key_rows = rotate(keys[0].astype(jnp.float32), cosine, sine).astype(jnp.bfloat16)
+    rotated_key_rows = rotate_low(keys[0], cosine, sine).astype(jnp.bfloat16)
     grad_out = output_cotangent[0].reshape(tok_rows, kv_count, group_size, head_dim)
     kv_pair = jnp.stack([rotated_key_rows, values[0]])
     pairs = [kv_pair]
@@ -209,7 +234,6 @@
     )
     grad_k = unrotate(key_total, cosine, sine).astype(jnp.bfloat16)
     feats = features[0]
-    width = feats.shape[1]
     value_flat = grad_v.reshape(tok_rows, kv_count * head_dim)
     own_rows = param.shape[0]
     n_dp = lax.axis_size("dp")
@@ -225,7 +249,7 @@
         (((0,), (0,)), ((), ())),
         preferred_element_type=jnp.float32,
     )
-    weight_gradient = ring_copy(pieces, "ctx")
+    weight_gradient = doubling_copy(pieces, "ctx")
     norm_part = jnp.sum(pieces * pieces)
     everyone = ("ctx", "dp", "tp")
     grad_total = spread_sum(norm_part, everyone)
@@ -250,7 +274,7 @@
         P("dp", "tp"),
     )
     return jax.shard_map(
-        local,
+        local_body,
         mesh=mesh,
         in_specs=placed,
         out_specs=(

time: 106 us -> 106 us (level)
  waiting for transfers between devices: 18.4 us -> 33.8 us
  local copies, waits for them, and re-layouts: 21.6 us -> 15.4 us
  other arithmetic: 16.6 us -> 11.5 us
  starting transfers between devices: 32.9 us -> 27.9 us
  matrix products: 13.4 us -> 14.5 us
    all_to_all x1, waiting for transfers between devices: 0.01 us -> 8.19 us  [local_body(): lax.all_to_all(feats.reshape(tok_rows, n_dp * n_ctx, piece_rows), spread,...]
    concatenate x4 -> x0, local copies, waits for them, and re-layouts: 5.17 us -> none  [the longest x2 3.71 us: rotate(): jnp.concatenate([-vectors[..., half:], vectors[..., :half]], axis=-1)]
    ppermute x3 -> x2, waiting for transfers between devices: 1.05 us -> 6.03 us  [doubling_copy(): other = lax.ppermute(gathered, axis, [(i, i ^ span) for i in range(peers)])]
    convert_element_type x6 -> x2, other arithmetic: 4.66 us -> 0.15 us  [the longest x1 0.14 us: local_body(): unrotate(query_grad.reshape(tok_rows, head_count, head_dim), cosine, sine)]
    ppermute x3, waiting for transfers between devices: 0.01 us -> 4.48 us  [shifted(): return lax.ppermute(array, axis, pairs)]
    ppermute x3 -> x2, starting transfers between devices: 5.24 us -> 2.43 us  [doubling_copy(): other = lax.ppermute(gathered, axis, [(i, i ^ span) for i in range(peers)])]
    unnamed x48 -> x45, local copies, waits for them, and re-layouts: 7.01 us -> 9.42 us
    concatenate x2 -> x0, other arithmetic: 2.36 us -> none  [rotate(): jnp.concatenate([-vectors[..., half:], vectors[..., :half]], axis=-1)]
  transfers between devices with their start and end apart: 9 -> 8, of which waited for: 3 -> 5; matrix products, arithmetic and copies ran while one was open for 35% -> 29% of each run, Pallas kernels for 0% -> 0%
where the time goes in v9:
time: 106 us; the launch traced here: 105 us
  waiting for transfers between devices  33.8 us (32%)
  starting transfers between devices  27.9 us (26%)
  local copies, waits for them, and re-layouts  15.4 us (15%)
  matrix products  14.5 us (14%)
  other arithmetic  11.5 us (11%)
  between operations  1.79 us (2%)
    all_to_all x2, waiting for transfers between devices, spread_copy(): return lax.all_to_all(stacked, axes, 0, 0, tiled=False)  15.1 us
    all_to_all x2, starting transfers between devices, spread_copy(): return lax.all_to_all(stacked, axes, 0, 0, tiled=False)  11.9 us
    unnamed x45, local copies, waits for them, and re-layouts  9.42 us
    all_to_all x1, waiting for transfers between devices, local_body(): lax.all_to_all(feats.reshape(tok_rows, n_dp * n_ctx, piece_rows), spread,...  8.19 us
    ppermute x3, starting transfers between devices, shifted(): return lax.ppermute(array, axis, pairs)  8.12 us
    ppermute x2, waiting for transfers between devices, doubling_copy(): other = lax.ppermute(gathered, axis, [(i, i ^ span) for i in range(peers)])  6.03 us
    all_to_all x1, starting transfers between devices, local_body(): lax.all_to_all(feats.reshape(tok_rows, n_dp * n_ctx, piece_rows), spread,...  5.44 us
    ppermute x3, waiting for transfers between devices, shifted(): return lax.ppermute(array, axis, pairs)  4.48 us
  transfers between devices with their start and end apart: 8, of which 5 were waited for; matrix products, arithmetic and copies ran while one was open for 29% of the time, Pallas kernels for 0%

profile of v9, /device:TPU:0, one launch (start us, length us, event | category | flops | bytes accessed | tf_op | source)
XLA Modules:
  0.0 105.0 jit_solution(17313234305650853673)
XLA Ops:
  0.7 0.8 copy.171
  1.8 0.7 convert_divide_fusion
  2.7 1.0 copy.170
  3.7 1.0 copy.177
  4.9 5.5 %collective-permute-start = (bf16[2,128,2,128]{1,3,2,0:T(8,128)(2,1)S(1)}, bf16[2,128,2,128]{1,3,2,0:T(8,128)(2,1)}, u32[]{:S(2)}, u32[]{:S(2)}) collective-permute-start(bf16[2,128,2,128]{1,3,2,0:T(8,128)(2,1)S(1)} %pad_maximum_fusion), channel_id=1, source_target_pairs={{0,8},{8,16},{16,24},{1,9},{9,17},{17,25},{2,10},{10,18},{18,26},{... | collective-permute-start | bytes 393224 | tf_op jit(solution)/shard_map/ppermute | solution.py:25
  10.4 1.3 %copy.198 = bf16[1,128,4096]{1,2,0:T(8,128)(2,1)} copy(bf16[1,128,4096]{2,1,0:T(8,128)(2,1)S(1)} %copy-done.4) | data formatting | bytes 2097152 | tf_op args[4]
  11.7 5.4 %all-to-all-start.1 = ((bf16[1,128,16,256]{1,3,0,2:T(8,128)(2,1)}), bf16[1,128,16,256]{1,3,0,2:T(8,128)(2,1)S(1)}, u32[]{:S(2)}, u32[]{:S(2)}) async-start(bf16[1,128,16,256]{1,3,0,2:T(8,128)(2,1)} %bitcast.56), calls=%async_computation.1 | async-start | bytes 2097152 | tf_op jit(solution)/shard_map/all_to_all | solution.py:242
  17.2 0.5 copy.173
  17.7 0.4 fusion.15
  18.3 0.4 fusion.74
  18.6 0.7 copy-done.1
  19.3 1.2 %copy.194 = bf16[128,2,8,128]{0,3,2,1:T(8,128)(2,1)} copy(bf16[128,2,8,128]{3,2,1,0:T(8,128)(2,1)S(1)} %bitcast.190) | data formatting | bytes 1048576 | tf_op jit(solution)/shard_map/reshape;squeeze | solution.py:154
  20.5 1.2 %fusion.75 = (f32[2,8,128]{2,1,0:T(8,128)S(1)}, f32[2,8,128,128]{2,3,1,0:T(8,128)S(1)}) fusion(bf16[128,2,8,128]{0,3,2,1:T(8,128)(2,1)S(1)} %bitcast.187, bf16[2,128,2,128]{1,3,2,0:T(8,128)(2,1)} %collective-permute-done, pred[128,128]{0,1:T(8,128)(4,1)S(1)} %get-tuple-element.54), kind=kOutput, calls=%fused_computation.120 | convolution fusion | flops 67893248 | bytes 1662976 | tf_op jit(solution)/shard_map/qhgd,khd->hgqk/dot_general | solution.py:173
  21.8 0.4 fusion.32
  22.2 1.0 copy-done.8
  23.2 0.3 fusion.24
  23.5 1.3 %collective-permute-start.2 = (bf16[128,2,128]{2,0,1:T(8,128)(2,1)S(1)}, bf16[128,2,128]{2,0,1:T(8,128)(2,1)S(1)}, u32[]{:S(2)}, u32[]{:S(2)}) collective-permute-start(bf16[128,2,128]{2,0,1:T(8,128)(2,1)S(1)} %fusion.24), channel_id=1, source_target_pairs={{8,0},{16,8},{24,16},{9,1},{17,9},{25,17},{10,2},{18,10},{26,18},{... | collective-permute-start | bytes 196616 | tf_op jit(solution)/shard_map/ppermute | solution.py:25
  24.8 0.4 convolution_bitcast_fusion.2
  25.3 2.2 %fusion.5 = f32[2,8,128,128]{3,2,1,0:T(8,128)} fusion(f32[128,2,8,128]{3,0,2,1:T(8,128)S(1)} %convolution_bitcast_fusion.2, bf16[2,128,2,128]{1,3,2,0:T(8,128)(2,1)} %collective-permute-done, f32[2,8,128,128]{2,3,1,0:T(8,128)S(1)} %get-tuple-element.61, f32[2,8,128]{2,1,0:T(8,128)S(1)} %add.107, f32[2,8,128]{2,1,0:T(8,128)S(1)} %max.8, ...), kind=kOutput, calls=%fused_computation.11 | convolution fusion | flops 68419584 | bytes 3244032 | tf_op jit(solution)/shard_map/hgqk,khd->qhgd/dot_general | solution.py:194
  27.5 4.5 %collective-permute-done.2 = bf16[128,2,128]{2,0,1:T(8,128)(2,1)S(1)} collective-permute-done((bf16[128,2,128]{2,0,1:T(8,128)(2,1)S(1)}, bf16[128,2,128]{2,0,1:T(8,128)(2,1)S(1)}, u32[]{:S(2)}, u32[]{:S(2)}) %collective-permute-start.2) | collective-permute-done | bytes 65568 | tf_op jit(solution)/shard_map/ppermute | solution.py:25
  32.0 0.3 add_convert_fusion
  32.5 0.5 copy-done.11
  33.1 8.2 %all-to-all-done.1 = bf16[1,128,16,256]{1,3,0,2:T(8,128)(2,1)S(1)} async-done(((bf16[1,128,16,256]{1,3,0,2:T(8,128)(2,1)}), bf16[1,128,16,256]{1,3,0,2:T(8,128)(2,1)S(1)}, u32[]{:S(2)}, u32[]{:S(2)}) %all-to-all-start.1) | async-done | bytes 1048608 | tf_op jit(solution)/shard_map/all_to_all | solution.py:242
  41.3 1.1 %broadcast_in_dim.76 = bf16[16,128,256]{2,1,0:T(8,128)(2,1)} broadcast(bf16[128,256]{1,0:T(8,128)(2,1)S(1)} %copy.197), dimensions={1,2} | broadcast | bytes 1114112 | tf_op jit(solution)/shard_map/broadcast_in_dim | solution.py:32
  42.3 6.0 %all-to-all-start = ((bf16[16,128,256]{2,1,0:T(8,128)(2,1)}), bf16[16,128,256]{2,1,0:T(8,128)(2,1)}, u32[]{:S(2)}, u32[]{:S(2)}) async-start(bf16[16,128,256]{2,1,0:T(8,128)(2,1)} %broadcast_in_dim.76), calls=%async_computation | async-start | bytes 2097152 | tf_op jit(solution)/shard_map/all_to_all | solution.py:33
  48.3 2.0 %multiply_reduce_fusion = f32[2,8,128]{1,0,2:T(2,128)S(1)} fusion(f32[2,8,128,128]{3,2,1,0:T(8,128)} %fusion.5, bf16[1,128,16,128]{3,2,1,0:T(8,128)(2,1)S(1)} %copy-done.1), kind=kLoop, calls=%fused_computation.48 | loop fusion | flops 784384 | bytes 1581056
  50.4 1.9 %fusion.13 = bf16[2,8,128,128]{2,3,1,0:T(8,128)(2,1)S(1)} fusion(bf16[128,2,8,128]{0,3,2,1:T(8,128)(2,1)} %copy.194, f32[2,8,128]{2,1,0:T(8,128)S(1)} %copy.223, bf16[2,128,2,128]{1,3,2,0:T(8,128)(2,1)} %collective-permute-done, f32[2,8,128]{2,1,0:T(8,128)S(1)} %add.107, f32[2,8,128,128]{2,3,1,0:T(8,128)} %copy-done, f32[2,8,128]{2,1,0:T(8,128)S(1)} %max.8, ...), kind=kOutput, calls=%fused_computation.22 | convolution fusion | flops 68681728 | bytes 2203648 | tf_op jit(solution)/shard_map/qhgd,khd->hgqk/dot_general | solution.py:211
  52.3 0.3 fusion.25
  52.6 1.3 %collective-permute-start.1 = (bf16[128,2,128]{0,2,1:T(8,128)(2,1)S(1)}, bf16[128,2,128]{0,2,1:T(8,128)(2,1)S(1)}, u32[]{:S(2)}, u32[]{:S(2)}) collective-permute-start(bf16[128,2,128]{0,2,1:T(8,128)(2,1)S(1)} %fusion.25), channel_id=1, source_target_pairs={{8,0},{16,8},{24,16},{9,1},{17,9},{25,17},{10,2},{18,10},{26,18},{... | collective-permute-start | bytes 196616 | tf_op jit(solution)/shard_map/ppermute | solution.py:25
  53.9 1.1 %fusion.14 = bf16[2,8,128,128]{2,3,1,0:T(8,128)(2,1)S(1)} fusion(bf16[128,2,8,128]{0,3,2,1:T(8,128)(2,1)S(1)} %copy-done.9, f32[2,8,128]{2,1,0:T(8,128)} %copy-done.18, bf16[128,2,128,1]{2,1,0,3:T(2,128)(2,1)S(1)} %bitcast.197, f32[2,8,128]{2,1,0:T(8,128)S(1)} %copy-done.17, f32[2,8,128,128]{2,3,1,0:T(8,128)S(1)} %get-tuple-element.59, ...), kind=kOutput, calls=%fused_computation.23 | convolution fusion | flops 68681728 | bytes 2203648 | tf_op jit(solution)/shard_map/qhgd,khd->hgqk/dot_general | solution.py:211
  55.3 1.1 %fusion.8 = f32[2,128,8,128]{3,1,2,0:T(8,128)S(1)} fusion(f32[2,128,8,128]{3,1,2,0:T(8,128)S(1)} %fusion.43, bf16[2,8,128,128]{2,3,1,0:T(8,128)(2,1)S(1)} %fusion.13, bf16[2,128,2,128]{1,3,2,0:T(8,128)(2,1)} %collective-permute-done), kind=kOutput, calls=%fused_computation.15 | convolution fusion | flops 67633152 | bytes 2686976 | tf_op jit(solution)/shard_map/hgqk,khd->qhgd/dot_general | solution.py:216
  56.6 1.1 %slice_bitcast_fusion = (f32[1,128,16,64]{1,3,2,0:T(8,128)}, f32[1,128,16,64]{1,3,2,0:T(8,128)}) fusion(f32[128,16,128]{0,2,1:T(8,128)S(1)} %bitcast_multiply_fusion), kind=kLoop, calls=%fused_computation.59 | loop fusion | flops 131072 | bytes 2097152 | tf_op jit(solution)/shard_map/concatenate | solution.py:109
  57.6 1.3 %copy.200 = bf16[1,128,16,256]{3,1,2,0:T(8,128)(2,1)} copy(bf16[1,128,16,256]{1,3,0,2:T(8,128)(2,1)S(1)} %all-to-all-done.1) | data formatting | bytes 2097152 | tf_op jit(solution)/shard_map/all_to_all | solution.py:242
  58.9 12.4 %all-to-all-done = bf16[16,128,256]{2,1,0:T(8,128)(2,1)} async-done(((bf16[16,128,256]{2,1,0:T(8,128)(2,1)}), bf16[16,128,256]{2,1,0:T(8,128)(2,1)}, u32[]{:S(2)}, u32[]{:S(2)}) %all-to-all-start) | async-done | bytes 1048608 | tf_op jit(solution)/shard_map/all_to_all | solution.py:33
  71.3 3.5 %multiply_reduce_fusion.1 = (f32[]{:T(128)}, f32[256,256]{1,0:T(8,128)}) fusion(bf16[2048,256]{1,0:T(8,128)(2,1)} %bitcast.54, bf16[2048,256]{1,0:T(8,128)(2,1)} %bitcast.191), kind=kOutput, calls=%fused_computation.62 | convolution fusion | flops 268566528 | bytes 2359300 | tf_op jit(solution)/shard_map/dot_general | solution.py:246
  74.8 0.7 collective-permute-start.3
  75.6 1.2 %copy.202 = bf16[1,128,16,128]{3,2,1,0:T(8,128)(2,1)} copy(bf16[1,128,16,128]{1,3,2,0:T(8,128)(2,1)S(1)} %fusion.27) | data formatting | bytes 1048576
  76.8 1.0 fusion.40
  77.8 1.3 %broadcast_in_dim_broadcast_in_dim_broadcast_in_dim.3 = f32[32,8,128]{2,1,0:T(8,128)} broadcast(f32[]{:T(128)} %get-tuple-element.64), dimensions={} | broadcast | bytes 131076 | tf_op jit(solution)/shard_map/broadcast_in_dim;broadcast_in_dim;broadcast_in_dim | solution.py:32
  79.1 5.9 %all-to-all-start.2 = ((f32[32,8,128]{2,1,0:T(8,128)}), f32[32,8,128]{2,1,0:T(8,128)}, u32[]{:S(2)}, u32[]{:S(2)}) async-start(f32[32,8,128]{2,1,0:T(8,128)} %broadcast_in_dim_broadcast_in_dim_broadcast_in_dim.3), calls=%async_computation.2 | async-start | bytes 262144 | tf_op jit(solution)/shard_map/all_to_all | solution.py:33
  85.0 1.3 %maximum_select_fusion.1 = f32[512,256]{1,0:T(8,128)S(1)} fusion(f32[256,256]{1,0:T(8,128)} %collective-permute-done.3, f32[256,256]{1,0:T(8,128)} %get-tuple-element.65, pred[]{:T(512)S(6)} %eq.43), kind=kLoop, calls=%fused_computation.60 | loop fusion | flops 393216 | bytes 1048577 | tf_op jit(solution)/shard_map/jit(_where)/select_n | solution.py:58
  86.4 1.8 %collective-permute-start.4 = (f32[512,256]{1,0:T(8,128)S(1)}, f32[512,256]{1,0:T(8,128)S(1)}, u32[]{:S(2)}, u32[]{:S(2)}) collective-permute-start(f32[512,256]{1,0:T(8,128)S(1)} %maximum_select_fusion.1), channel_id=1, source_target_pairs={{0,16},{8,24},{16,0},{24,8},{1,17},{9,25},{17,1},{25,9},{2,18},{10... | collective-permute-start | bytes 1572872 | tf_op jit(solution)/shard_map/ppermute | solution.py:56
  88.2 1.5 %copy.204 = bf16[1,128,2,128]{3,2,1,0:T(2,128)(2,1)} copy(bf16[1,128,2,128]{3,1,2,0:T(8,128)(2,1)} %bitcast.194) | data formatting | bytes 131072
  89.8 0.8 copy.203
  90.5 2.7 %all-to-all-done.2 = f32[32,8,128]{2,1,0:T(8,128)} async-done(((f32[32,8,128]{2,1,0:T(8,128)}), f32[32,8,128]{2,1,0:T(8,128)}, u32[]{:S(2)}, u32[]{:S(2)}) %all-to-all-start.2) | async-done | bytes 131104 | tf_op jit(solution)/shard_map/all_to_all | solution.py:33
  93.3 1.5 %slice_reduce_fusion = f32[]{:T(128)} fusion(f32[32,8,128]{2,1,0:T(8,128)} %all-to-all-done.2), kind=kLoop, calls=%fused_computation.102 | loop fusion | flops 31 | bytes 132 | tf_op jit(solution)/shard_map/reduce_sum | solution.py:71
  95.5 6.0 %collective-permute-done.4 = f32[512,256]{1,0:T(8,128)S(1)} collective-permute-done((f32[512,256]{1,0:T(8,128)S(1)}, f32[512,256]{1,0:T(8,128)S(1)}, u32[]{:S(2)}, u32[]{:S(2)}) %collective-permute-start.4) | collective-permute-done | bytes 524320 | tf_op jit(solution)/shard_map/ppermute | solution.py:56
  101.5 3.4 %multiply_subtract_fusion = (f32[1024,256]{1,0:T(8,128)}, f32[1024,256]{1,0:T(8,128)}, f32[1024,256]{1,0:T(8,128)}) fusion(f32[1024,256]{1,0:T(8,128)S(1)} %copy-done.5, f32[]{:T(128)S(6)} %min_shard_map.3, f32[512,256]{1,0:T(8,128)S(1)} %maximum_select_fusion.1, f32[512,256]{1,0:T(8,128)S(1)} %collective-permute-done.4, pred[]{:T(512)S(6)} %eq.42, ...), kind=kLoop, calls=%fused_computation.49 | loop fusion | flops 4980736 | bytes 7340037 | tf_op jit(solution)/shard_map/sub | solution.py:119
  (62 shorter events, 1.9 us)
Async XLA Ops:
  0.6 9.8 %copy-start.4 = (bf16[1,128,4096]{2,1,0:T(8,128)(2,1)S(1)}, bf16[1,128,4096]{2,1,0:T(8,128)(2,1)}, u32[]{:S(2)}) copy-start(bf16[1,128,4096]{2,1,0:T(8,128)(2,1)} %param.15) | copy-start | bytes 3145732
  4.9 15.6 %collective-permute-start = (bf16[2,128,2,128]{1,3,2,0:T(8,128)(2,1)S(1)}, bf16[2,128,2,128]{1,3,2,0:T(8,128)(2,1)}, u32[]{:S(2)}, u32[]{:S(2)}) collective-permute-start(bf16[2,128,2,128]{1,3,2,0:T(8,128)(2,1)S(1)} %pad_maximum_fusion), channel_id=1, source_target_pairs={{0,8},{8,16},{16,24},{1,9},{9,17},{17,25},{2,10},{10,18},{18,26},{... | collective-permute-start | bytes 393224 | tf_op jit(solution)/shard_map/ppermute | solution.py:25
  11.7 5.5 %copy-start.7 = (bf16[1,128,16,128]{3,2,1,0:T(8,128)(2,1)S(1)}, bf16[1,128,16,128]{3,2,1,0:T(8,128)(2,1)}, u32[]{:S(2)}) copy-start(bf16[1,128,16,128]{3,2,1,0:T(8,128)(2,1)} %param.11) | copy-start | bytes 1572868
  11.7 29.5 %all-to-all-start.1 = ((bf16[1,128,16,256]{1,3,0,2:T(8,128)(2,1)}), bf16[1,128,16,256]{1,3,0,2:T(8,128)(2,1)S(1)}, u32[]{:S(2)}, u32[]{:S(2)}) async-start(bf16[1,128,16,256]{1,3,0,2:T(8,128)(2,1)} %bitcast.56), calls=%async_computation.1 | async-start | bytes 2097152 | tf_op jit(solution)/shard_map/all_to_all | solution.py:242
  18.2 1.0 copy-start.1
  21.7 3.5 %copy-start = (f32[2,8,128,128]{2,3,1,0:T(8,128)}, f32[2,8,128,128]{2,3,1,0:T(8,128)S(1)}, u32[]{:S(2)}) copy-start(f32[2,8,128,128]{2,3,1,0:T(8,128)S(1)} %get-tuple-element.61) | copy-start | bytes 3145732
  21.7 28.6 %copy-start.14 = (f32[2,8,128]{2,1,0:T(8,128)}, f32[2,8,128]{2,1,0:T(8,128)S(1)}, u32[]{:S(2)}) copy-start(f32[2,8,128]{2,1,0:T(8,128)S(1)} %max.8) | copy-start | bytes 24580
  21.8 1.4 %copy-start.8 = (bf16[128,2,8,128]{0,3,2,1:T(8,128)(2,1)S(1)}, bf16[128,2,8,128]{0,3,2,1:T(8,128)(2,1)}, u32[]{:S(2)}) copy-start(bf16[128,2,8,128]{0,3,2,1:T(8,128)(2,1)} %copy.194) | copy-start | bytes 1572868
  23.2 27.2 %copy-start.16 = (f32[2,8,128]{2,1,0:T(8,128)}, f32[2,8,128]{2,1,0:T(8,128)S(1)}, u32[]{:S(2)}) copy-start(f32[2,8,128]{2,1,0:T(8,128)S(1)} %add.107) | copy-start | bytes 24580
  23.2 1.7 %copy-start.12 = (bf16[1,128,2,128]{3,2,1,0:T(2,128)(2,1)S(1)}, bf16[1,128,2,128]{3,2,1,0:T(2,128)(2,1)}, u32[]{:S(2)}) copy-start(bf16[1,128,2,128]{3,2,1,0:T(2,128)(2,1)} %param.13) | copy-start | bytes 196612
  23.5 8.5 %collective-permute-start.2 = (bf16[128,2,128]{2,0,1:T(8,128)(2,1)S(1)}, bf16[128,2,128]{2,0,1:T(8,128)(2,1)S(1)}, u32[]{:S(2)}, u32[]{:S(2)}) collective-permute-start(bf16[128,2,128]{2,0,1:T(8,128)(2,1)S(1)} %fusion.24), channel_id=1, source_target_pairs={{8,0},{16,8},{24,16},{9,1},{17,9},{25,17},{10,2},{18,10},{26,18},{... | collective-permute-start | bytes 196616 | tf_op jit(solution)/shard_map/ppermute | solution.py:25
  32.3 0.6 copy-start.11
  42.3 29.0 %all-to-all-start = ((bf16[16,128,256]{2,1,0:T(8,128)(2,1)}), bf16[16,128,256]{2,1,0:T(8,128)(2,1)}, u32[]{:S(2)}, u32[]{:S(2)}) async-start(bf16[16,128,256]{2,1,0:T(8,128)(2,1)} %broadcast_in_dim.76), calls=%async_computation | async-start | bytes 2097152 | tf_op jit(solution)/shard_map/all_to_all | solution.py:33
  50.4 1.9 %copy-start.18 = (f32[2,8,128]{2,1,0:T(8,128)}, f32[2,8,128]{2,1,0:T(8,128)S(1)}, u32[]{:S(2)}) copy-start(f32[2,8,128]{2,1,0:T(8,128)S(1)} %copy.223) | copy-start | bytes 24580
  52.2 1.7 %copy-start.9 = (bf16[128,2,8,128]{0,3,2,1:T(8,128)(2,1)S(1)}, bf16[128,2,8,128]{0,3,2,1:T(8,128)(2,1)}, u32[]{:S(2)}) copy-start(bf16[128,2,8,128]{0,3,2,1:T(8,128)(2,1)} %copy.194) | copy-start | bytes 1572868
  52.3 1.7 %copy-start.13 = (bf16[1,128,2,128]{3,2,1,0:T(2,128)(2,1)S(1)}, bf16[1,128,2,128]{3,2,1,0:T(2,128)(2,1)}, u32[]{:S(2)}) copy-start(bf16[1,128,2,128]{3,2,1,0:T(2,128)(2,1)} %param.13) | copy-start | bytes 196612
  52.3 1.6 %copy-start.15 = (f32[2,8,128]{2,1,0:T(8,128)S(1)}, f32[2,8,128]{2,1,0:T(8,128)}, u32[]{:S(2)}) copy-start(f32[2,8,128]{2,1,0:T(8,128)} %copy-done.14) | copy-start | bytes 24580
  52.3 1.6 %copy-start.17 = (f32[2,8,128]{2,1,0:T(8,128)S(1)}, f32[2,8,128]{2,1,0:T(8,128)}, u32[]{:S(2)}) copy-start(f32[2,8,128]{2,1,0:T(8,128)} %copy-done.16) | copy-start | bytes 24580
  52.6 24.2 %collective-permute-start.1 = (bf16[128,2,128]{0,2,1:T(8,128)(2,1)S(1)}, bf16[128,2,128]{0,2,1:T(8,128)(2,1)S(1)}, u32[]{:S(2)}, u32[]{:S(2)}) collective-permute-start(bf16[128,2,128]{0,2,1:T(8,128)(2,1)S(1)} %fusion.25), channel_id=1, source_target_pairs={{8,0},{16,8},{24,16},{9,1},{17,9},{25,17},{10,2},{18,10},{26,18},{... | collective-permute-start | bytes 196616 | tf_op jit(solution)/shard_map/ppermute | solution.py:25
  71.3 4.1 %copy-start.2 = (f32[1,128,16,64]{1,3,2,0:T(8,128)S(1)}, f32[1,128,16,64]{1,3,2,0:T(8,128)}, u32[]{:S(2)}) copy-start(f32[1,128,16,64]{1,3,2,0:T(8,128)} %get-tuple-element.50) | copy-start | bytes 1572868
  71.3 4.1 %copy-start.3 = (f32[1,128,16,64]{1,3,2,0:T(8,128)S(1)}, f32[1,128,16,64]{1,3,2,0:T(8,128)}, u32[]{:S(2)}) copy-start(f32[1,128,16,64]{1,3,2,0:T(8,128)} %get-tuple-element.51) | copy-start | bytes 1572868
  74.8 10.3 %collective-permute-start.3 = (f32[256,256]{1,0:T(8,128)}, f32[256,256]{1,0:T(8,128)}, u32[]{:S(2)}, u32[]{:S(2)}) collective-permute-start(f32[256,256]{1,0:T(8,128)} %get-tuple-element.65), channel_id=1, source_target_pairs={{0,8},{8,0},{16,24},{24,16},{1,9},{9,1},{17,25},{25,17},{2,10},{10... | collective-permute-start | bytes 786440 | tf_op jit(solution)/shard_map/ppermute | solution.py:56
  79.1 9.1 %copy-start.10 = (f32[128,2,128]{0,2,1:T(8,128)S(1)}, f32[128,2,128]{0,2,1:T(8,128)}, u32[]{:S(2)}) copy-start(f32[128,2,128]{0,2,1:T(8,128)} %get-tuple-element.62) | copy-start | bytes 393220
  79.1 22.4 %copy-start.6 = (f32[1024,256]{1,0:T(8,128)S(1)}, f32[1024,256]{1,0:T(8,128)}, u32[]{:S(2)}) copy-start(f32[1024,256]{1,0:T(8,128)} %param.20) | copy-start | bytes 3145732
  79.1 14.2 %all-to-all-start.2 = ((f32[32,8,128]{2,1,0:T(8,128)}), f32[32,8,128]{2,1,0:T(8,128)}, u32[]{:S(2)}, u32[]{:S(2)}) async-start(f32[32,8,128]{2,1,0:T(8,128)} %broadcast_in_dim_broadcast_in_dim_broadcast_in_dim.3), calls=%async_computation.2 | async-start | bytes 262144 | tf_op jit(solution)/shard_map/all_to_all | solution.py:33
  85.0 16.5 %copy-start.5 = (f32[1024,256]{1,0:T(8,128)S(1)}, f32[1024,256]{1,0:T(8,128)}, u32[]{:S(2)}) copy-start(f32[1024,256]{1,0:T(8,128)} %param.19) | copy-start | bytes 3145732
  86.4 15.1 %collective-permute-start.4 = (f32[512,256]{1,0:T(8,128)S(1)}, f32[512,256]{1,0:T(8,128)S(1)}, u32[]{:S(2)}, u32[]{:S(2)}) collective-permute-start(f32[512,256]{1,0:T(8,128)S(1)} %maximum_select_fusion.1), channel_id=1, source_target_pairs={{0,16},{8,24},{16,0},{24,8},{1,17},{9,25},{17,1},{25,9},{2,18},{10... | collective-permute-start | bytes 1572872 | tf_op jit(solution)/shard_map/ppermute | solution.py:56

commit v10 on v9

--- a/solution.py
+++ b/solution.py
@@ -45,30 +45,11 @@
     return out
 
 
-def doubling_copy(array, axis):
-    peers = lax.axis_size(axis)
-    if peers & (peers - 1):
-        return ring_copy(array, axis)
-    place = lax.axis_index(axis)
-    gathered = array
-    span = 1
-    while span < peers:
-        other = lax.ppermute(gathered, axis, [(i, i ^ span) for i in range(peers)])
-        low_half = (place & span) == 0
-        gathered = jnp.where(
-            low_half,
-            jnp.concatenate([gathered, other], axis=0),
-            jnp.concatenate([other, gathered], axis=0),
-        )
-        span *= 2
-    return gathered
-
-
 def spread_sum(value, axes):
     peers = lax.axis_size(axes)
     if peers > 64:
         return lax.psum(value, axes)
-    return jnp.sum(spread_copy(jnp.full((8, 128), value), axes)[:, 0, 0])
+    return jnp.sum(spread_copy(jnp.full((1, 128), value), axes)[:, 0, 0])
 
 
 def doc_layout(lengths_row, token_index):
@@ -249,7 +230,7 @@
         (((0,), (0,)), ((), ())),
         preferred_element_type=jnp.float32,
     )
-    weight_gradient = doubling_copy(pieces, "ctx")
+    weight_gradient = ring_copy(pieces, "ctx")
     norm_part = jnp.sum(pieces * pieces)
     everyone = ("ctx", "dp", "tp")
     grad_total = spread_sum(norm_part, everyone)

time: 106 us -> 98.8 us (0.932)
  other arithmetic: 11.5 us -> 7.33 us
  matrix products: 14.5 us -> 11.5 us
    all_to_all x2, waiting for transfers between devices: 15.1 us -> 21.3 us  [spread_copy(): return lax.all_to_all(stacked, axes, 0, 0, tiled=False)]
    ppermute x2 -> x3, waiting for transfers between devices: 6.03 us -> 0.01 us  [ring_copy(): lax.ppermute(array, axis, [(i, (i + step) % peers) for i in range(peers)])]
    all_to_all x1, waiting for transfers between devices: 8.19 us -> 4.95 us  [local_body(): lax.all_to_all(feats.reshape(tok_rows, n_dp * n_ctx, piece_rows), spread,...]
    ppermute x2 -> x3, starting transfers between devices: 2.43 us -> 4.95 us  [ring_copy(): lax.ppermute(array, axis, [(i, (i + step) % peers) for i in range(peers)])]
    dot_general x1, matrix products: 3.45 us -> 1.08 us  [local_body(): lax.dot_general(feat_cols.reshape(-1, piece_rows), value_rows.reshape(-1,...]
    all_to_all x2, starting transfers between devices: 11.9 us -> 9.65 us  [spread_copy(): return lax.all_to_all(stacked, axes, 0, 0, tiled=False)]
    ppermute x3, waiting for transfers between devices: 4.48 us -> 6.48 us  [shifted(): return lax.ppermute(array, axis, pairs)]
    dot_general x2, matrix products: 0.69 us -> 2.13 us  [local_body(): jnp.einsum('hgqk,qhgd->khd', probs_low, grad_out, preferred_element_type=...]
  transfers between devices with their start and end apart: 8 -> 9, of which waited for: 5 -> 5; matrix products, arithmetic and copies ran while one was open for 29% -> 22% of each run, Pallas kernels for 0% -> 0%
where the time goes in v10:
time: 98.8 us; the launch traced here: 97.9 us
  waiting for transfers between devices  32.8 us (33%)
  starting transfers between devices  28.3 us (29%)
  local copies, waits for them, and re-layouts  16.1 us (16%)
  matrix products  11.5 us (12%)
  other arithmetic  7.33 us (7%)
  between operations  1.89 us (2%)
    all_to_all x2, waiting for transfers between devices, spread_copy(): return lax.all_to_all(stacked, axes, 0, 0, tiled=False)  21.3 us
    all_to_all x2, starting transfers between devices, spread_copy(): return lax.all_to_all(stacked, axes, 0, 0, tiled=False)  9.65 us
    unnamed x33, local copies, waits for them, and re-layouts  9.15 us
    ppermute x3, starting transfers between devices, shifted(): return lax.ppermute(array, axis, pairs)  8.24 us
    ppermute x3, waiting for transfers between devices, shifted(): return lax.ppermute(array, axis, pairs)  6.48 us
    all_to_all x1, starting transfers between devices, local_body(): lax.all_to_all(feats.reshape(tok_rows, n_dp * n_ctx, piece_rows), spread,...  5.44 us
    all_to_all x1, waiting for transfers between devices, local_body(): lax.all_to_all(feats.reshape(tok_rows, n_dp * n_ctx, piece_rows), spread,...  4.95 us
    ppermute x3, starting transfers between devices, ring_copy(): lax.ppermute(array, axis, [(i, (i + step) % peers) for i in range(peers)])  4.95 us
  transfers between devices with their start and end apart: 9, of which 5 were waited for; matrix products, arithmetic and copies ran while one was open for 22% of the time, Pallas kernels for 0%

profile of v10, /device:TPU:0, one launch (start us, length us, event | category | flops | bytes accessed | tf_op | source)
XLA Modules:
  0.0 97.9 jit_solution(9988926909694587491)
XLA Ops:
  0.7 0.8 copy.191
  1.8 0.7 convert_divide_fusion
  2.7 1.0 copy.190
  3.7 1.0 copy.197
  4.9 5.5 %collective-permute-start = (bf16[2,128,2,128]{1,3,2,0:T(8,128)(2,1)S(1)}, bf16[2,128,2,128]{1,3,2,0:T(8,128)(2,1)}, u32[]{:S(2)}, u32[]{:S(2)}) collective-permute-start(bf16[2,128,2,128]{1,3,2,0:T(8,128)(2,1)S(1)} %pad_maximum_fusion), channel_id=1, source_target_pairs={{0,8},{8,16},{16,24},{1,9},{9,17},{17,25},{2,10},{10,18},{18,26},{... | collective-permute-start | bytes 393224 | tf_op jit(solution)/shard_map/ppermute | solution.py:25
  10.4 1.3 %copy.218 = bf16[1,128,4096]{1,2,0:T(8,128)(2,1)} copy(bf16[1,128,4096]{2,1,0:T(8,128)(2,1)S(1)} %copy-done.5) | data formatting | bytes 2097152 | tf_op args[4]
  11.7 5.4 %all-to-all-start.1 = ((bf16[1,128,16,256]{1,3,0,2:T(8,128)(2,1)}), bf16[1,128,16,256]{1,3,0,2:T(8,128)(2,1)S(1)}, u32[]{:S(2)}, u32[]{:S(2)}) async-start(bf16[1,128,16,256]{1,3,0,2:T(8,128)(2,1)} %bitcast.56), calls=%async_computation.1 | async-start | bytes 2097152 | tf_op jit(solution)/shard_map/all_to_all | solution.py:223
  17.2 0.5 copy.193
  17.7 0.4 fusion.15
  18.3 0.4 fusion.73
  18.7 0.6 copy-done.3
  19.3 1.2 %copy.214 = bf16[128,2,8,128]{0,3,2,1:T(8,128)(2,1)} copy(bf16[128,2,8,128]{3,2,1,0:T(8,128)(2,1)S(1)} %bitcast.192) | data formatting | bytes 1048576 | tf_op jit(solution)/shard_map/reshape;squeeze | solution.py:135
  20.5 1.2 %fusion.74 = (f32[2,8,128]{2,1,0:T(8,128)S(1)}, f32[2,8,128,128]{2,3,1,0:T(8,128)S(1)}) fusion(bf16[128,2,8,128]{0,3,2,1:T(8,128)(2,1)S(1)} %bitcast.187, bf16[2,128,2,128]{1,3,2,0:T(8,128)(2,1)} %collective-permute-done, pred[128,128]{0,1:T(8,128)(4,1)S(1)} %get-tuple-element.54), kind=kOutput, calls=%fused_computation.121 | convolution fusion | flops 67893248 | bytes 1662976 | tf_op jit(solution)/shard_map/qhgd,khd->hgqk/dot_general | solution.py:154
  21.8 0.4 fusion.31
  22.2 0.5 copy-done.11
  22.7 0.4 convolution_bitcast_fusion.2
  23.1 1.2 %fusion.5 = f32[2,8,128,128]{3,2,1,0:T(8,128)S(1)} fusion(f32[128,2,8,128]{3,0,2,1:T(8,128)S(1)} %convolution_bitcast_fusion.2, bf16[2,128,2,128]{1,3,2,0:T(8,128)(2,1)} %collective-permute-done, f32[2,8,128,128]{2,3,1,0:T(8,128)S(1)} %get-tuple-element.61, f32[2,8,128]{2,1,0:T(8,128)S(1)} %add.131, f32[2,8,128]{2,1,0:T(8,128)S(1)} %max.8, ...), kind=kOutput, calls=%fused_computation.11 | convolution fusion | flops 68419584 | bytes 3244032 | tf_op jit(solution)/shard_map/hgqk,khd->qhgd/dot_general | solution.py:175
  24.4 0.8 multiply_reduce_fusion
  25.2 1.8 %fusion.24 = bf16[128,2,128]{2,0,1:T(8,128)(2,1)S(1)} fusion(bf16[128,2,8,128]{0,3,2,1:T(8,128)(2,1)} %copy.214, f32[2,8,128,128]{2,3,1,0:T(8,128)} %copy-done.1, f32[2,8,128]{2,1,0:T(8,128)S(1)} %add.131, f32[2,8,128]{2,1,0:T(8,128)S(1)} %max.8, pred[128,128]{0,1:T(8,128)(4,1)S(1)} %get-tuple-element.54), kind=kOutput, calls=%fused_computation.39 | convolution fusion | flops 68190208 | bytes 1671168 | tf_op jit(solution)/shard_map/hgqk,qhgd->khd/dot_general | solution.py:181
  27.0 1.4 %collective-permute-start.2 = (bf16[128,2,128]{2,0,1:T(8,128)(2,1)S(1)}, bf16[128,2,128]{2,0,1:T(8,128)(2,1)S(1)}, u32[]{:S(2)}, u32[]{:S(2)}) collective-permute-start(bf16[128,2,128]{2,0,1:T(8,128)(2,1)S(1)} %fusion.24), channel_id=1, source_target_pairs={{8,0},{16,8},{24,16},{9,1},{17,9},{25,17},{10,2},{18,10},{26,18},{... | collective-permute-start | bytes 196616 | tf_op jit(solution)/shard_map/ppermute | solution.py:25
  28.5 0.4 fusion.14
  28.9 2.1 %fusion.13 = bf16[2,8,128,128]{2,3,1,0:T(8,128)(2,1)} fusion(bf16[128,2,8,128]{0,3,2,1:T(8,128)(2,1)S(1)} %copy-done.8, f32[2,8,128]{2,1,0:T(8,128)S(1)} %copy.247, bf16[2,128,2,128]{1,3,2,0:T(8,128)(2,1)} %collective-permute-done, f32[2,8,128]{2,1,0:T(8,128)S(1)} %add.131, f32[2,8,128,128]{2,3,1,0:T(8,128)S(1)} %copy-done.2, f32[2,8,128]{2,1,0:T(8,128)S(1)} %max.8, ...), kind=kOutput, calls=%fused_computation.22 | convolution fusion | flops 68681728 | bytes 2203648 | tf_op jit(solution)/shard_map/qhgd,khd->hgqk/dot_general | solution.py:192
  30.9 4.3 %collective-permute-done.2 = bf16[128,2,128]{2,0,1:T(8,128)(2,1)S(1)} collective-permute-done((bf16[128,2,128]{2,0,1:T(8,128)(2,1)S(1)}, bf16[128,2,128]{2,0,1:T(8,128)(2,1)S(1)}, u32[]{:S(2)}, u32[]{:S(2)}) %collective-permute-start.2) | collective-permute-done | bytes 65568 | tf_op jit(solution)/shard_map/ppermute | solution.py:25
  35.2 0.3 add_convert_fusion
  35.7 0.5 copy-done.9
  36.3 4.9 %all-to-all-done.1 = bf16[1,128,16,256]{1,3,0,2:T(8,128)(2,1)S(1)} async-done(((bf16[1,128,16,256]{1,3,0,2:T(8,128)(2,1)}), bf16[1,128,16,256]{1,3,0,2:T(8,128)(2,1)S(1)}, u32[]{:S(2)}, u32[]{:S(2)}) %all-to-all-start.1) | async-done | bytes 1048608 | tf_op jit(solution)/shard_map/all_to_all | solution.py:223
  41.3 1.2 %broadcast_in_dim.80 = bf16[16,128,256]{2,1,0:T(8,128)(2,1)} broadcast(bf16[128,256]{1,0:T(8,128)(2,1)S(1)} %copy.217), dimensions={1,2} | broadcast | bytes 1114112 | tf_op jit(solution)/shard_map/broadcast_in_dim | solution.py:32
  42.6 6.0 %all-to-all-start = ((bf16[16,128,256]{2,1,0:T(8,128)(2,1)}), bf16[16,128,256]{2,1,0:T(8,128)(2,1)S(1)}, u32[]{:S(2)}, u32[]{:S(2)}) async-start(bf16[16,128,256]{2,1,0:T(8,128)(2,1)} %broadcast_in_dim.80), calls=%async_computation | async-start | bytes 2097152 | tf_op jit(solution)/shard_map/all_to_all | solution.py:33
  48.6 0.3 fusion.25
  49.0 1.3 %collective-permute-start.1 = (bf16[128,2,128]{0,2,1:T(8,128)(2,1)S(1)}, bf16[128,2,128]{0,2,1:T(8,128)(2,1)S(1)}, u32[]{:S(2)}, u32[]{:S(2)}) collective-permute-start(bf16[128,2,128]{0,2,1:T(8,128)(2,1)S(1)} %fusion.25), channel_id=1, source_target_pairs={{8,0},{16,8},{24,16},{9,1},{17,9},{25,17},{10,2},{18,10},{26,18},{... | collective-permute-start | bytes 196616 | tf_op jit(solution)/shard_map/ppermute | solution.py:25
  50.5 1.1 %fusion.8 = f32[2,128,8,128]{3,1,2,0:T(8,128)S(1)} fusion(f32[2,128,8,128]{3,1,2,0:T(8,128)S(1)} %fusion.42, bf16[2,8,128,128]{2,3,1,0:T(8,128)(2,1)S(1)} %copy-done.4, bf16[2,128,2,128]{1,3,2,0:T(8,128)(2,1)} %collective-permute-done), kind=kOutput, calls=%fused_computation.15 | convolution fusion | flops 67633152 | bytes 2686976 | tf_op jit(solution)/shard_map/hgqk,khd->qhgd/dot_general | solution.py:197
  52.1 1.2 %copy.226 = bf16[1,128,16,128]{3,2,1,0:T(8,128)(2,1)} copy(bf16[1,128,16,128]{1,3,2,0:T(8,128)(2,1)S(1)} %fusion.27) | data formatting | bytes 1048576
  53.2 2.2 %collective-permute-done.1 = bf16[128,2,128]{0,2,1:T(8,128)(2,1)S(1)} collective-permute-done((bf16[128,2,128]{0,2,1:T(8,128)(2,1)S(1)}, bf16[128,2,128]{0,2,1:T(8,128)(2,1)S(1)}, u32[]{:S(2)}, u32[]{:S(2)}) %collective-permute-start.1) | collective-permute-done | bytes 65568 | tf_op jit(solution)/shard_map/ppermute | solution.py:25
  55.4 0.3 fusion.39
  55.8 1.5 %copy.220 = bf16[1,128,16,256]{3,1,2,0:T(8,128)(2,1)S(1)} copy(bf16[1,128,16,256]{1,3,0,2:T(8,128)(2,1)} %copy-done) | data formatting | bytes 2097152 | tf_op jit(solution)/shard_map/all_to_all | solution.py:223
  57.3 14.3 %all-to-all-done = bf16[16,128,256]{2,1,0:T(8,128)(2,1)S(1)} async-done(((bf16[16,128,256]{2,1,0:T(8,128)(2,1)}), bf16[16,128,256]{2,1,0:T(8,128)(2,1)S(1)}, u32[]{:S(2)}, u32[]{:S(2)}) %all-to-all-start) | async-done | bytes 1048608 | tf_op jit(solution)/shard_map/all_to_all | solution.py:33
  71.6 1.1 %multiply_reduce_fusion.1 = (f32[]{:T(128)}, f32[256,256]{0,1:T(8,128)S(1)}) fusion(bf16[2048,256]{1,0:T(8,128)(2,1)S(1)} %bitcast.190, bf16[2048,256]{1,0:T(8,128)(2,1)S(1)} %bitcast.191), kind=kOutput, calls=%fused_computation.59 | convolution fusion | flops 268566528 | bytes 2359300 | tf_op jit(solution)/shard_map/dot_general | solution.py:227
  72.7 0.6 collective-permute-start.3
  73.2 2.0 %collective-permute-start.4 = (f32[256,256]{0,1:T(8,128)S(1)}, f32[256,256]{0,1:T(8,128)S(1)}, u32[]{:S(2)}, u32[]{:S(2)}) collective-permute-start(f32[256,256]{0,1:T(8,128)S(1)} %get-tuple-element.65), channel_id=1, source_target_pairs={{0,16},{8,24},{16,0},{24,8},{1,17},{9,25},{17,1},{25,9},{2,18},{10... | collective-permute-start | bytes 786440 | tf_op jit(solution)/shard_map/ppermute | solution.py:43
  75.2 0.8 copy.227
  76.1 0.7 copy.228
  76.9 2.4 %collective-permute-start.5 = (f32[256,256]{0,1:T(8,128)S(1)}, f32[256,256]{0,1:T(8,128)S(1)}, u32[]{:S(2)}, u32[]{:S(2)}) collective-permute-start(f32[256,256]{0,1:T(8,128)S(1)} %get-tuple-element.65), channel_id=1, source_target_pairs={{0,24},{8,0},{16,8},{24,16},{1,25},{9,1},{17,9},{25,17},{2,26},{10... | collective-permute-start | bytes 786440 | tf_op jit(solution)/shard_map/ppermute | solution.py:43
  79.3 1.3 %broadcast_in_dim_broadcast_in_dim_broadcast_in_dim.3 = f32[32,1,128]{2,1,0:T(1,128)} broadcast(f32[]{:T(128)} %get-tuple-element.64), dimensions={} | broadcast | bytes 16388 | tf_op jit(solution)/shard_map/broadcast_in_dim;broadcast_in_dim;broadcast_in_dim | solution.py:32
  80.6 3.6 %all-to-all-start.2 = ((f32[32,1,128]{2,1,0:T(1,128)}), f32[32,1,128]{2,1,0:T(1,128)S(1)}, u32[]{:S(2)}, u32[]{:S(2)}) async-start(f32[32,1,128]{2,1,0:T(1,128)} %broadcast_in_dim_broadcast_in_dim_broadcast_in_dim.3), calls=%async_computation.2 | async-start | bytes 32768 | tf_op jit(solution)/shard_map/all_to_all | solution.py:33
  84.3 7.0 %all-to-all-done.2 = f32[32,1,128]{2,1,0:T(1,128)S(1)} async-done(((f32[32,1,128]{2,1,0:T(1,128)}), f32[32,1,128]{2,1,0:T(1,128)S(1)}, u32[]{:S(2)}, u32[]{:S(2)}) %all-to-all-start.2) | async-done | bytes 16416 | tf_op jit(solution)/shard_map/all_to_all | solution.py:33
  91.3 0.6 slice_reduce_fusion
  93.2 1.0 copy-done.6
  94.1 3.7 %multiply_subtract_fusion = (f32[1024,256]{1,0:T(8,128)}, f32[1024,256]{1,0:T(8,128)}, f32[1024,256]{1,0:T(8,128)}) fusion(f32[1024,256]{1,0:T(8,128)S(1)} %copy-done.6, f32[1024,256]{1,0:T(8,128)S(1)} %constant_dynamic-update-slice_fusion, f32[]{:T(128)S(6)} %min_shard_map.3, f32[1024,256]{1,0:T(8,128)} %param.20, f32[1024,256]{1,0:T(8,128)} %param.21), kind=kLoop, calls=%fused_computation.47 | loop fusion | flops 4194304 | bytes 7340036 | tf_op jit(solution)/shard_map/sub | solution.py:100
  (60 shorter events, 2.8 us)
Async XLA Ops:
  0.6 9.8 %copy-start.5 = (bf16[1,128,4096]{2,1,0:T(8,128)(2,1)S(1)}, bf16[1,128,4096]{2,1,0:T(8,128)(2,1)}, u32[]{:S(2)}) copy-start(bf16[1,128,4096]{2,1,0:T(8,128)(2,1)} %param.15) | copy-start | bytes 3145732
  4.9 15.6 %collective-permute-start = (bf16[2,128,2,128]{1,3,2,0:T(8,128)(2,1)S(1)}, bf16[2,128,2,128]{1,3,2,0:T(8,128)(2,1)}, u32[]{:S(2)}, u32[]{:S(2)}) collective-permute-start(bf16[2,128,2,128]{1,3,2,0:T(8,128)(2,1)S(1)} %pad_maximum_fusion), channel_id=1, source_target_pairs={{0,8},{8,16},{16,24},{1,9},{9,17},{17,25},{2,10},{10,18},{18,26},{... | collective-permute-start | bytes 393224 | tf_op jit(solution)/shard_map/ppermute | solution.py:25
  11.7 5.5 %copy-start.7 = (bf16[1,128,16,128]{3,2,1,0:T(8,128)(2,1)S(1)}, bf16[1,128,16,128]{3,2,1,0:T(8,128)(2,1)}, u32[]{:S(2)}) copy-start(bf16[1,128,16,128]{3,2,1,0:T(8,128)(2,1)} %param.11) | copy-start | bytes 1572868
  11.7 29.5 %all-to-all-start.1 = ((bf16[1,128,16,256]{1,3,0,2:T(8,128)(2,1)}), bf16[1,128,16,256]{1,3,0,2:T(8,128)(2,1)S(1)}, u32[]{:S(2)}, u32[]{:S(2)}) async-start(bf16[1,128,16,256]{1,3,0,2:T(8,128)(2,1)} %bitcast.56), calls=%async_computation.1 | async-start | bytes 2097152 | tf_op jit(solution)/shard_map/all_to_all | solution.py:223
  18.2 1.0 %copy-start.3 = (bf16[1,128,16,128]{3,2,1,0:T(8,128)(2,1)S(1)}, bf16[1,128,16,128]{3,2,1,0:T(8,128)(2,1)}, u32[]{:S(2)}) copy-start(bf16[1,128,16,128]{3,2,1,0:T(8,128)(2,1)} %param.14) | copy-start | bytes 1572868
  21.7 1.4 %copy-start.1 = (f32[2,8,128,128]{2,3,1,0:T(8,128)}, f32[2,8,128,128]{2,3,1,0:T(8,128)S(1)}, u32[]{:S(2)}) copy-start(f32[2,8,128,128]{2,3,1,0:T(8,128)S(1)} %get-tuple-element.61) | copy-start | bytes 3145732
  21.7 0.9 copy-start.11
  25.2 3.2 %copy-start.8 = (bf16[128,2,8,128]{0,3,2,1:T(8,128)(2,1)S(1)}, bf16[128,2,8,128]{0,3,2,1:T(8,128)(2,1)}, u32[]{:S(2)}) copy-start(bf16[128,2,8,128]{0,3,2,1:T(8,128)(2,1)} %copy.214) | copy-start | bytes 1572868
  25.2 3.2 %copy-start.12 = (bf16[1,128,2,128]{3,2,1,0:T(2,128)(2,1)S(1)}, bf16[1,128,2,128]{3,2,1,0:T(2,128)(2,1)}, u32[]{:S(2)}) copy-start(bf16[1,128,2,128]{3,2,1,0:T(2,128)(2,1)} %param.13) | copy-start | bytes 196612
  27.0 1.9 %copy-start.2 = (f32[2,8,128,128]{2,3,1,0:T(8,128)S(1)}, f32[2,8,128,128]{2,3,1,0:T(8,128)}, u32[]{:S(2)}) copy-start(f32[2,8,128,128]{2,3,1,0:T(8,128)} %copy-done.1) | copy-start | bytes 3145732
  27.0 8.2 %collective-permute-start.2 = (bf16[128,2,128]{2,0,1:T(8,128)(2,1)S(1)}, bf16[128,2,128]{2,0,1:T(8,128)(2,1)S(1)}, u32[]{:S(2)}, u32[]{:S(2)}) collective-permute-start(bf16[128,2,128]{2,0,1:T(8,128)(2,1)S(1)} %fusion.24), channel_id=1, source_target_pairs={{8,0},{16,8},{24,16},{9,1},{17,9},{25,17},{10,2},{18,10},{26,18},{... | collective-permute-start | bytes 196616 | tf_op jit(solution)/shard_map/ppermute | solution.py:25
  35.6 0.6 copy-start.9
  41.3 1.3 %copy-start = (bf16[1,128,16,256]{1,3,0,2:T(8,128)(2,1)}, bf16[1,128,16,256]{1,3,0,2:T(8,128)(2,1)S(1)}, u32[]{:S(2)}) copy-start(bf16[1,128,16,256]{1,3,0,2:T(8,128)(2,1)S(1)} %all-to-all-done.1) | copy-start | bytes 3145732
  42.5 6.2 %copy-start.4 = (bf16[2,8,128,128]{2,3,1,0:T(8,128)(2,1)S(1)}, bf16[2,8,128,128]{2,3,1,0:T(8,128)(2,1)}, u32[]{:S(2)}) copy-start(bf16[2,8,128,128]{2,3,1,0:T(8,128)(2,1)} %fusion.13) | copy-start | bytes 1572868
  42.6 29.0 %all-to-all-start = ((bf16[16,128,256]{2,1,0:T(8,128)(2,1)}), bf16[16,128,256]{2,1,0:T(8,128)(2,1)S(1)}, u32[]{:S(2)}, u32[]{:S(2)}) async-start(bf16[16,128,256]{2,1,0:T(8,128)(2,1)} %broadcast_in_dim.80), calls=%async_computation | async-start | bytes 2097152 | tf_op jit(solution)/shard_map/all_to_all | solution.py:33
  49.0 6.5 %collective-permute-start.1 = (bf16[128,2,128]{0,2,1:T(8,128)(2,1)S(1)}, bf16[128,2,128]{0,2,1:T(8,128)(2,1)S(1)}, u32[]{:S(2)}, u32[]{:S(2)}) collective-permute-start(bf16[128,2,128]{0,2,1:T(8,128)(2,1)S(1)} %fusion.25), channel_id=1, source_target_pairs={{8,0},{16,8},{24,16},{9,1},{17,9},{25,17},{10,2},{18,10},{26,18},{... | collective-permute-start | bytes 196616 | tf_op jit(solution)/shard_map/ppermute | solution.py:25
  72.7 20.0 %collective-permute-start.3 = (f32[256,256]{0,1:T(8,128)S(1)}, f32[256,256]{0,1:T(8,128)S(1)}, u32[]{:S(2)}, u32[]{:S(2)}) collective-permute-start(f32[256,256]{0,1:T(8,128)S(1)} %get-tuple-element.65), channel_id=1, source_target_pairs={{0,8},{8,16},{16,24},{24,0},{1,9},{9,17},{17,25},{25,1},{2,10},{10... | collective-permute-start | bytes 786440 | tf_op jit(solution)/shard_map/ppermute | solution.py:43
  73.2 19.5 %collective-permute-start.4 = (f32[256,256]{0,1:T(8,128)S(1)}, f32[256,256]{0,1:T(8,128)S(1)}, u32[]{:S(2)}, u32[]{:S(2)}) collective-permute-start(f32[256,256]{0,1:T(8,128)S(1)} %get-tuple-element.65), channel_id=1, source_target_pairs={{0,16},{8,24},{16,0},{24,8},{1,17},{9,25},{17,1},{25,9},{2,18},{10... | collective-permute-start | bytes 786440 | tf_op jit(solution)/shard_map/ppermute | solution.py:43
  75.2 0.8 copy-start.10
  76.9 16.1 %collective-permute-start.5 = (f32[256,256]{0,1:T(8,128)S(1)}, f32[256,256]{0,1:T(8,128)S(1)}, u32[]{:S(2)}, u32[]{:S(2)}) collective-permute-start(f32[256,256]{0,1:T(8,128)S(1)} %get-tuple-element.65), channel_id=1, source_target_pairs={{0,24},{8,0},{16,8},{24,16},{1,25},{9,1},{17,9},{25,17},{2,26},{10... | collective-permute-start | bytes 786440 | tf_op jit(solution)/shard_map/ppermute | solution.py:43
  80.6 10.7 %all-to-all-start.2 = ((f32[32,1,128]{2,1,0:T(1,128)}), f32[32,1,128]{2,1,0:T(1,128)S(1)}, u32[]{:S(2)}, u32[]{:S(2)}) async-start(f32[32,1,128]{2,1,0:T(1,128)} %broadcast_in_dim_broadcast_in_dim_broadcast_in_dim.3), calls=%async_computation.2 | async-start | bytes 32768 | tf_op jit(solution)/shard_map/all_to_all | solution.py:33
  92.9 1.2 %copy-start.6 = (f32[1024,256]{1,0:T(8,128)S(1)}, f32[1024,256]{1,0:T(8,128)}, u32[]{:S(2)}) copy-start(f32[1024,256]{1,0:T(8,128)} %param.19) | copy-start | bytes 3145732

commit v11 on v10

--- a/solution.py
+++ b/solution.py
@@ -49,7 +49,7 @@
     peers = lax.axis_size(axes)
     if peers > 64:
         return lax.psum(value, axes)
-    return jnp.sum(spread_copy(jnp.full((1, 128), value), axes)[:, 0, 0])
+    return jnp.sum(spread_copy(jnp.full((8, 128), value), axes)[:, 0, 0])
 
 
 def doc_layout(lengths_row, token_index):
@@ -223,13 +223,28 @@
     feat_cols = lax.all_to_all(
         feats.reshape(tok_rows, n_dp * n_ctx, piece_rows), spread, 1, 0, tiled=False
     )
-    value_rows = spread_copy(value_flat, spread)
-    pieces = lax.dot_general(
-        feat_cols.reshape(-1, piece_rows),
-        value_rows.reshape(-1, kv_count * head_dim),
-        (((0,), (0,)), ((), ())),
-        preferred_element_type=jnp.float32,
-    )
+    if n_dp * n_ctx * 2 * value_flat.size * 2 > (4 << 20):
+        value_rows = spread_copy(value_flat, spread)
+        pieces = lax.dot_general(
+            feat_cols.reshape(-1, piece_rows),
+            value_rows.reshape(-1, kv_count * head_dim),
+            (((0,), (0,)), ((), ())),
+            preferred_element_type=jnp.float32,
+        )
+    else:
+        own_and_back = jnp.stack(
+            [value_terms[0].astype(jnp.bfloat16), value_terms[reach].astype(jnp.bfloat16)]
+        ).reshape(2, tok_rows, kv_count * head_dim)
+        value_rows = spread_copy(own_and_back, spread)
+        by_block = feat_cols.reshape(n_dp, n_ctx, tok_rows, piece_rows)
+        earlier = jnp.roll(by_block, 1, axis=1)
+        feat_pairs = jnp.stack([by_block, earlier], axis=2)
+        pieces = lax.dot_general(
+            feat_pairs.reshape(-1, piece_rows),
+            value_rows.reshape(-1, kv_count * head_dim),
+            (((0,), (0,)), ((), ())),
+            preferred_element_type=jnp.float32,
+        )
     weight_gradient = ring_copy(pieces, "ctx")
     norm_part = jnp.sum(pieces * pieces)
     everyone = ("ctx", "dp", "tp")

time: 98.8 us -> 129 us (1.31)
  waiting for transfers between devices: 32.8 us -> 50.8 us
  starting transfers between devices: 28.3 us -> 33.1 us
  matrix products: 11.5 us -> 14.6 us
  local copies, waits for them, and re-layouts: 16.1 us -> 18.9 us
  other arithmetic: 7.33 us -> 8.89 us
    all_to_all x2, waiting for transfers between devices: 21.3 us -> 29.9 us  [spread_copy(): return lax.all_to_all(stacked, axes, 0, 0, tiled=False)]
    all_to_all x2, starting transfers between devices: 9.65 us -> 15 us  [spread_copy(): return lax.all_to_all(stacked, axes, 0, 0, tiled=False)]
    ppermute x3, waiting for transfers between devices: 0.01 us -> 5.03 us  [ring_copy(): lax.ppermute(array, axis, [(i, (i + step) % peers) for i in range(peers)])]
    all_to_all x1, waiting for transfers between devices: 4.95 us -> 9.92 us  [local_body(): lax.all_to_all(feats.reshape(tok_rows, n_dp * n_ctx, piece_rows), spread,...]
    dynamic_update_slice x3, local copies, waits for them, and re-layouts: 0.07 us -> 2.91 us  [ring_copy(): lax.dynamic_update_slice_in_dim(out, moved, (place - step) % peers * rows...]
    dot_general x1, matrix products: 1.08 us -> 3.69 us  [local_body(): lax.dot_general(feat_pairs.reshape(-1, piece_rows), value_rows.reshape(-1...]
    all_to_all x1 -> x0, local copies, waits for them, and re-layouts: 1.49 us -> none  [local_body(): lax.all_to_all(feats.reshape(tok_rows, n_dp * n_ctx, piece_rows), spread,...]
    unnamed x33 -> x35, local copies, waits for them, and re-layouts: 9.15 us -> 8.51 us
  transfers between devices with their start and end apart: 9 -> 9, of which waited for: 5 -> 7; matrix products, arithmetic and copies ran while one was open for 22% -> 20% of each run, Pallas kernels for 0% -> 0%
where the time goes in v11:
time: 129 us; the launch traced here: 128 us
  waiting for transfers between devices  50.8 us (39%)
  starting transfers between devices  33.1 us (26%)
  local copies, waits for them, and re-layouts  18.9 us (15%)
  matrix products  14.6 us (11%)
  other arithmetic  8.89 us (7%)
  between operations  1.88 us (1%)
    all_to_all x2, waiting for transfers between devices, spread_copy(): return lax.all_to_all(stacked, axes, 0, 0, tiled=False)  29.9 us
    all_to_all x2, starting transfers between devices, spread_copy(): return lax.all_to_all(stacked, axes, 0, 0, tiled=False)  15 us
    all_to_all x1, waiting for transfers between devices, local_body(): lax.all_to_all(feats.reshape(tok_rows, n_dp * n_ctx, piece_rows), spread,...  9.92 us
    unnamed x35, local copies, waits for them, and re-layouts  8.51 us
    ppermute x3, starting transfers between devices, shifted(): return lax.ppermute(array, axis, pairs)  8.1 us
    ppermute x3, waiting for transfers between devices, shifted(): return lax.ppermute(array, axis, pairs)  5.98 us
    all_to_all x1, starting transfers between devices, local_body(): lax.all_to_all(feats.reshape(tok_rows, n_dp * n_ctx, piece_rows), spread,...  5.3 us
    ppermute x3, waiting for transfers between devices, ring_copy(): lax.ppermute(array, axis, [(i, (i + step) % peers) for i in range(peers)])  5.03 us
  transfers between devices with their start and end apart: 9, of which 7 were waited for; matrix products, arithmetic and copies ran while one was open for 20% of the time, Pallas kernels for 0%

profile of v11, /device:TPU:0, one launch (start us, length us, event | category | flops | bytes accessed | tf_op | source)
XLA Modules:
  0.0 128.2 jit_solution(5385982641401434428)
XLA Ops:
  0.7 0.7 copy.165
  1.7 0.7 convert_divide_fusion
  2.6 1.0 copy.164
  3.6 1.0 copy.171
  4.8 5.5 %collective-permute-start = (bf16[2,128,2,128]{1,3,2,0:T(8,128)(2,1)S(1)}, bf16[2,128,2,128]{1,3,2,0:T(8,128)(2,1)}, u32[]{:S(2)}, u32[]{:S(2)}) collective-permute-start(bf16[2,128,2,128]{1,3,2,0:T(8,128)(2,1)S(1)} %pad_maximum_fusion.1), channel_id=1, source_target_pairs={{0,8},{8,16},{16,24},{1,9},{9,17},{17,25},{2,10},{10,18},{18,26},{... | collective-permute-start | bytes 393224 | tf_op jit(solution)/shard_map/ppermute | solution.py:25
  10.3 1.6 %copy.190 = bf16[1,128,4096]{1,2,0:T(8,128)(2,1)S(1)} copy(bf16[1,128,4096]{2,1,0:T(8,128)(2,1)} %param.15) | data formatting | bytes 2097152 | tf_op args[4]
  12.0 1.3 %copy.191 = bf16[1,128,16,256]{3,1,0,2:T(8,128)(2,1)} copy(bf16[1,128,16,256]{1,3,2,0:T(8,128)(2,1)S(1)} %bitcast.197) | data formatting | bytes 2097152 | tf_op jit(solution)/shard_map/broadcast_in_dim;reshape;squeeze | solution.py:223
  13.3 5.3 %all-to-all-start = ((bf16[1,128,16,256]{3,1,0,2:T(8,128)(2,1)}), bf16[1,128,16,256]{3,1,0,2:T(8,128)(2,1)S(1)}, u32[]{:S(2)}, u32[]{:S(2)}) async-start(bf16[1,128,16,256]{3,1,0,2:T(8,128)(2,1)} %copy.191), calls=%async_computation | async-start | bytes 2097152 | tf_op jit(solution)/shard_map/all_to_all | solution.py:223
  18.6 0.5 copy.167
  20.0 1.2 copy.187
  21.3 1.3 fusion.73
  23.0 0.4 fusion.23
  23.5 1.3 collective-permute-start.2
  24.8 5.2 %collective-permute-done.2 = bf16[128,2,128]{0,2,1:T(8,128)(2,1)S(1)} collective-permute-done((bf16[128,2,128]{0,2,1:T(8,128)(2,1)S(1)}, bf16[128,2,128]{0,2,1:T(8,128)(2,1)S(1)}, u32[]{:S(2)}, u32[]{:S(2)}) %collective-permute-start.2) | collective-permute-done | bytes 65568 | tf_op jit(solution)/shard_map/ppermute | solution.py:25
  30.0 1.0 fusion.70
  31.1 0.7 maximum_bitcast_fusion.1
  31.7 1.0 copy.192
  32.8 9.9 %all-to-all-done = bf16[1,128,16,256]{3,1,0,2:T(8,128)(2,1)S(1)} async-done(((bf16[1,128,16,256]{3,1,0,2:T(8,128)(2,1)}), bf16[1,128,16,256]{3,1,0,2:T(8,128)(2,1)S(1)}, u32[]{:S(2)}, u32[]{:S(2)}) %all-to-all-start) | async-done | bytes 1048608 | tf_op jit(solution)/shard_map/all_to_all | solution.py:223
  42.7 1.5 %broadcast_in_dim.80 = bf16[16,2,128,256]{3,2,1,0:T(8,128)(2,1)} broadcast(bf16[2,128,256]{2,1,0:T(8,128)(2,1)S(1)} %copy.192), dimensions={1,2,3} | broadcast | bytes 2228224 | tf_op jit(solution)/shard_map/broadcast_in_dim | solution.py:32
  44.2 6.1 %all-to-all-start.1 = ((bf16[16,2,128,256]{3,2,1,0:T(8,128)(2,1)}), bf16[16,2,128,256]{3,2,1,0:T(8,128)(2,1)}, u32[]{:S(2)}, u32[]{:S(2)}) async-start(bf16[16,2,128,256]{3,2,1,0:T(8,128)(2,1)} %broadcast_in_dim.80), calls=%async_computation.1 | async-start | bytes 4194304 | tf_op jit(solution)/shard_map/all_to_all | solution.py:33
  50.4 0.4 convolution_bitcast_fusion.2
  50.8 0.8 copy-done.1
  51.6 1.2 fusion.5
  52.9 0.8 multiply_reduce_fusion
  53.8 1.9 %fusion.13 = bf16[2,8,128,128]{2,3,1,0:T(8,128)(2,1)S(1)} fusion(bf16[128,2,8,128]{0,3,2,1:T(8,128)(2,1)} %copy.187, f32[2,8,128]{2,1,0:T(8,128)S(1)} %copy.215, bf16[2,128,2,128]{1,3,2,0:T(8,128)(2,1)} %collective-permute-done, f32[2,8,128]{2,1,0:T(8,128)S(1)} %add.131, f32[2,8,128,128]{2,3,1,0:T(8,128)} %copy-done, f32[2,8,128]{2,1,0:T(8,128)S(1)} %max.8, ...), kind=kOutput, calls=%fused_computation.23 | convolution fusion | flops 68681728 | bytes 2203648 | tf_op jit(solution)/shard_map/qhgd,khd->hgqk/dot_general | solution.py:192
  56.0 1.3 %collective-permute-start.1 = (bf16[128,2,128]{0,2,1:T(8,128)(2,1)S(1)}, bf16[128,2,128]{0,2,1:T(8,128)(2,1)S(1)}, u32[]{:S(2)}, u32[]{:S(2)}) collective-permute-start(bf16[128,2,128]{0,2,1:T(8,128)(2,1)S(1)} %fusion.24), channel_id=1, source_target_pairs={{8,0},{16,8},{24,16},{9,1},{17,9},{25,17},{10,2},{18,10},{26,18},{... | collective-permute-start | bytes 196616 | tf_op jit(solution)/shard_map/ppermute | solution.py:25
  57.3 1.1 fusion.14
  58.7 1.1 fusion.8
  60.2 1.2 copy.194
  61.4 0.7 collective-permute-done.1
  62.1 1.0 fusion.38
  63.5 28.8 %all-to-all-done.1 = bf16[16,2,128,256]{3,2,1,0:T(8,128)(2,1)} async-done(((bf16[16,2,128,256]{3,2,1,0:T(8,128)(2,1)}), bf16[16,2,128,256]{3,2,1,0:T(8,128)(2,1)}, u32[]{:S(2)}, u32[]{:S(2)}) %all-to-all-start.1) | async-done | bytes 2097184 | tf_op jit(solution)/shard_map/all_to_all | solution.py:33
  92.4 3.7 %multiply_reduce_fusion.1 = (f32[]{:T(128)}, f32[1024,256]{1,0:T(8,128)S(1)}, f32[256,256]{1,0:T(8,128)}) fusion(f32[1024,256]{1,0:T(8,128)S(1)} %broadcast_in_dim.78, s32[]{:T(128)S(6)} %select_n.49, bf16[4096,256]{1,0:T(8,128)(2,1)S(1)} %bitcast.198, bf16[4096,256]{1,0:T(8,128)(2,1)} %bitcast.67), kind=kOutput, calls=%fused_computation.59 | convolution fusion | flops 537001984 | bytes 4718600 | tf_op jit(solution)/shard_map/dot_general | solution.py:242
  96.1 1.5 %broadcast_in_dim_broadcast_in_dim_broadcast_in_dim.3 = f32[32,8,128]{2,1,0:T(8,128)} broadcast(f32[]{:T(128)} %get-tuple-element.52), dimensions={} | broadcast | bytes 131076 | tf_op jit(solution)/shard_map/broadcast_in_dim;broadcast_in_dim;broadcast_in_dim | solution.py:32
  97.5 8.9 %all-to-all-start.2 = ((f32[32,8,128]{2,1,0:T(8,128)}), f32[32,8,128]{2,1,0:T(8,128)}, u32[]{:S(2)}, u32[]{:S(2)}) async-start(f32[32,8,128]{2,1,0:T(8,128)} %broadcast_in_dim_broadcast_in_dim_broadcast_in_dim.3), calls=%async_computation.2 | async-start | bytes 262144 | tf_op jit(solution)/shard_map/all_to_all | solution.py:33
  106.5 1.7 %collective-permute-start.3 = (f32[256,256]{1,0:T(8,128)}, f32[256,256]{1,0:T(8,128)}, u32[]{:S(2)}, u32[]{:S(2)}) collective-permute-start(f32[256,256]{1,0:T(8,128)} %get-tuple-element.68), channel_id=1, source_target_pairs={{0,8},{8,16},{16,24},{24,0},{1,9},{9,17},{17,25},{25,1},{2,10},{10... | collective-permute-start | bytes 786440 | tf_op jit(solution)/shard_map/ppermute | solution.py:43
  108.2 1.5 %collective-permute-start.4 = (f32[256,256]{1,0:T(8,128)}, f32[256,256]{1,0:T(8,128)}, u32[]{:S(2)}, u32[]{:S(2)}) collective-permute-start(f32[256,256]{1,0:T(8,128)} %get-tuple-element.68), channel_id=1, source_target_pairs={{0,16},{8,24},{16,0},{24,8},{1,17},{9,25},{17,1},{25,9},{2,18},{10... | collective-permute-start | bytes 786440 | tf_op jit(solution)/shard_map/ppermute | solution.py:43
  109.7 0.8 copy.195
  110.5 1.6 %copy.196 = bf16[1,128,2,128]{3,2,1,0:T(2,128)(2,1)} copy(bf16[1,128,2,128]{1,3,2,0:T(8,128)(2,1)} %get-tuple-element.55) | data formatting | bytes 131072
  112.1 1.5 %collective-permute-start.5 = (f32[256,256]{1,0:T(8,128)}, f32[256,256]{1,0:T(8,128)}, u32[]{:S(2)}, u32[]{:S(2)}) collective-permute-start(f32[256,256]{1,0:T(8,128)} %get-tuple-element.68), channel_id=1, source_target_pairs={{0,24},{8,0},{16,8},{24,16},{1,25},{9,1},{17,9},{25,17},{2,26},{10... | collective-permute-start | bytes 786440 | tf_op jit(solution)/shard_map/ppermute | solution.py:43
  113.5 1.0 all-to-all-done.2
  114.6 1.5 %slice_reduce_fusion = f32[]{:T(128)} fusion(f32[32,8,128]{2,1,0:T(8,128)} %all-to-all-done.2), kind=kLoop, calls=%fused_computation.101 | loop fusion | flops 31 | bytes 132 | tf_op jit(solution)/shard_map/reduce_sum | solution.py:52
  116.8 1.0 collective-permute-done.3
  117.9 1.0 constant_dynamic-update-slice_fusion.2
  118.8 4.0 %collective-permute-done.4 = f32[256,256]{1,0:T(8,128)} collective-permute-done((f32[256,256]{1,0:T(8,128)}, f32[256,256]{1,0:T(8,128)}, u32[]{:S(2)}, u32[]{:S(2)}) %collective-permute-start.4) | collective-permute-done | bytes 262176 | tf_op jit(solution)/shard_map/ppermute | solution.py:43
  122.8 1.0 constant_dynamic-update-slice_fusion.1
  123.8 1.0 constant_dynamic-update-slice_fusion
  124.8 3.4 %multiply_subtract_fusion = (f32[1024,256]{1,0:T(8,128)}, f32[1024,256]{1,0:T(8,128)}, f32[1024,256]{1,0:T(8,128)}) fusion(f32[1024,256]{1,0:T(8,128)S(1)} %copy-done.3, f32[1024,256]{1,0:T(8,128)S(1)} %constant_dynamic-update-slice_fusion, f32[]{:T(128)S(6)} %min_shard_map.3, f32[1024,256]{1,0:T(8,128)S(1)} %copy-done.4, f32[1024,256]{1,0:T(8,128)} %param.21), kind=kLoop, calls=%fused_computation.47 | loop fusion | flops 4194304 | bytes 7340036 | tf_op jit(solution)/shard_map/sub | solution.py:100
  (61 shorter events, 3.7 us)
Async XLA Ops:
  4.8 16.5 %collective-permute-start = (bf16[2,128,2,128]{1,3,2,0:T(8,128)(2,1)S(1)}, bf16[2,128,2,128]{1,3,2,0:T(8,128)(2,1)}, u32[]{:S(2)}, u32[]{:S(2)}) collective-permute-start(bf16[2,128,2,128]{1,3,2,0:T(8,128)(2,1)S(1)} %pad_maximum_fusion.1), channel_id=1, source_target_pairs={{0,8},{8,16},{16,24},{1,9},{9,17},{17,25},{2,10},{10,18},{18,26},{... | collective-permute-start | bytes 393224 | tf_op jit(solution)/shard_map/ppermute | solution.py:25
  12.0 6.7 %copy-start.5 = (bf16[1,128,16,128]{3,2,1,0:T(8,128)(2,1)S(1)}, bf16[1,128,16,128]{3,2,1,0:T(8,128)(2,1)}, u32[]{:S(2)}) copy-start(bf16[1,128,16,128]{3,2,1,0:T(8,128)(2,1)} %param.11) | copy-start | bytes 1572868
  13.3 29.4 %all-to-all-start = ((bf16[1,128,16,256]{3,1,0,2:T(8,128)(2,1)}), bf16[1,128,16,256]{3,1,0,2:T(8,128)(2,1)S(1)}, u32[]{:S(2)}, u32[]{:S(2)}) async-start(bf16[1,128,16,256]{3,1,0,2:T(8,128)(2,1)} %copy.191), calls=%async_computation | async-start | bytes 2097152 | tf_op jit(solution)/shard_map/all_to_all | solution.py:223
  18.6 1.4 %copy-start.2 = (bf16[1,128,16,128]{3,2,1,0:T(8,128)(2,1)S(1)}, bf16[1,128,16,128]{3,2,1,0:T(8,128)(2,1)}, u32[]{:S(2)}) copy-start(bf16[1,128,16,128]{3,2,1,0:T(8,128)(2,1)} %param.14) | copy-start | bytes 1572868
  21.3 1.7 %copy-start.6 = (bf16[128,2,8,128]{0,3,2,1:T(8,128)(2,1)S(1)}, bf16[128,2,8,128]{0,3,2,1:T(8,128)(2,1)}, u32[]{:S(2)}) copy-start(bf16[128,2,8,128]{0,3,2,1:T(8,128)(2,1)} %copy.187) | copy-start | bytes 1572868
  22.5 1.0 copy-start
  22.6 31.2 %copy-start.11 = (f32[2,8,128]{2,1,0:T(8,128)}, f32[2,8,128]{2,1,0:T(8,128)S(1)}, u32[]{:S(2)}) copy-start(f32[2,8,128]{2,1,0:T(8,128)S(1)} %max.8) | copy-start | bytes 24580
  23.0 30.7 %copy-start.12 = (f32[2,8,128]{2,1,0:T(8,128)}, f32[2,8,128]{2,1,0:T(8,128)S(1)}, u32[]{:S(2)}) copy-start(f32[2,8,128]{2,1,0:T(8,128)S(1)} %add.131) | copy-start | bytes 24580
  23.5 6.5 %collective-permute-start.2 = (bf16[128,2,128]{0,2,1:T(8,128)(2,1)S(1)}, bf16[128,2,128]{0,2,1:T(8,128)(2,1)S(1)}, u32[]{:S(2)}, u32[]{:S(2)}) collective-permute-start(bf16[128,2,128]{0,2,1:T(8,128)(2,1)S(1)} %bitcast.204), channel_id=1, source_target_pairs={{8,0},{16,8},{24,16},{9,1},{17,9},{25,17},{10,2},{18,10},{26,18},{... | collective-permute-start | bytes 196616 | tf_op jit(solution)/shard_map/ppermute | solution.py:25
  44.2 6.2 %copy-start.9 = (bf16[1,128,2,128]{3,2,1,0:T(2,128)(2,1)S(1)}, bf16[1,128,2,128]{3,2,1,0:T(2,128)(2,1)}, u32[]{:S(2)}) copy-start(bf16[1,128,2,128]{3,2,1,0:T(2,128)(2,1)} %param.13) | copy-start | bytes 196612
  44.2 48.1 %all-to-all-start.1 = ((bf16[16,2,128,256]{3,2,1,0:T(8,128)(2,1)}), bf16[16,2,128,256]{3,2,1,0:T(8,128)(2,1)}, u32[]{:S(2)}, u32[]{:S(2)}) async-start(bf16[16,2,128,256]{3,2,1,0:T(8,128)(2,1)} %broadcast_in_dim.80), calls=%async_computation.1 | async-start | bytes 4194304 | tf_op jit(solution)/shard_map/all_to_all | solution.py:33
  50.4 1.2 copy-start.1
  53.7 1.9 %copy-start.13 = (f32[2,8,128]{2,1,0:T(8,128)}, f32[2,8,128]{2,1,0:T(8,128)S(1)}, u32[]{:S(2)}) copy-start(f32[2,8,128]{2,1,0:T(8,128)S(1)} %copy.215) | copy-start | bytes 24580
  53.7 3.6 %copy-start.7 = (bf16[128,2,8,128]{0,3,2,1:T(8,128)(2,1)S(1)}, bf16[128,2,8,128]{0,3,2,1:T(8,128)(2,1)}, u32[]{:S(2)}) copy-start(bf16[128,2,8,128]{0,3,2,1:T(8,128)(2,1)} %copy.187) | copy-start | bytes 1572868
  53.7 3.5 %copy-start.10 = (bf16[1,128,2,128]{3,2,1,0:T(2,128)(2,1)S(1)}, bf16[1,128,2,128]{3,2,1,0:T(2,128)(2,1)}, u32[]{:S(2)}) copy-start(bf16[1,128,2,128]{3,2,1,0:T(2,128)(2,1)} %param.13) | copy-start | bytes 196612
  56.0 6.2 %collective-permute-start.1 = (bf16[128,2,128]{0,2,1:T(8,128)(2,1)S(1)}, bf16[128,2,128]{0,2,1:T(8,128)(2,1)S(1)}, u32[]{:S(2)}, u32[]{:S(2)}) collective-permute-start(bf16[128,2,128]{0,2,1:T(8,128)(2,1)S(1)} %fusion.24), channel_id=1, source_target_pairs={{8,0},{16,8},{24,16},{9,1},{17,9},{25,17},{10,2},{18,10},{26,18},{... | collective-permute-start | bytes 196616 | tf_op jit(solution)/shard_map/ppermute | solution.py:25
  92.4 14.1 %copy-start.8 = (f32[128,2,128]{0,2,1:T(8,128)S(1)}, f32[128,2,128]{0,2,1:T(8,128)}, u32[]{:S(2)}) copy-start(f32[128,2,128]{0,2,1:T(8,128)} %get-tuple-element.66) | copy-start | bytes 393220
  96.1 28.7 %copy-start.3 = (f32[1024,256]{1,0:T(8,128)S(1)}, f32[1024,256]{1,0:T(8,128)}, u32[]{:S(2)}) copy-start(f32[1024,256]{1,0:T(8,128)} %param.19) | copy-start | bytes 3145732
  96.1 28.7 %copy-start.4 = (f32[1024,256]{1,0:T(8,128)S(1)}, f32[1024,256]{1,0:T(8,128)}, u32[]{:S(2)}) copy-start(f32[1024,256]{1,0:T(8,128)} %param.20) | copy-start | bytes 3145732
  97.5 17.1 %all-to-all-start.2 = ((f32[32,8,128]{2,1,0:T(8,128)}), f32[32,8,128]{2,1,0:T(8,128)}, u32[]{:S(2)}, u32[]{:S(2)}) async-start(f32[32,8,128]{2,1,0:T(8,128)} %broadcast_in_dim_broadcast_in_dim_broadcast_in_dim.3), calls=%async_computation.2 | async-start | bytes 262144 | tf_op jit(solution)/shard_map/all_to_all | solution.py:33
  106.5 11.4 %collective-permute-start.3 = (f32[256,256]{1,0:T(8,128)}, f32[256,256]{1,0:T(8,128)}, u32[]{:S(2)}, u32[]{:S(2)}) collective-permute-start(f32[256,256]{1,0:T(8,128)} %get-tuple-element.68), channel_id=1, source_target_pairs={{0,8},{8,16},{16,24},{24,0},{1,9},{9,17},{17,25},{25,1},{2,10},{10... | collective-permute-start | bytes 786440 | tf_op jit(solution)/shard_map/ppermute | solution.py:43
  108.2 14.6 %collective-permute-start.4 = (f32[256,256]{1,0:T(8,128)}, f32[256,256]{1,0:T(8,128)}, u32[]{:S(2)}, u32[]{:S(2)}) collective-permute-start(f32[256,256]{1,0:T(8,128)} %get-tuple-element.68), channel_id=1, source_target_pairs={{0,16},{8,24},{16,0},{24,8},{1,17},{9,25},{17,1},{25,9},{2,18},{10... | collective-permute-start | bytes 786440 | tf_op jit(solution)/shard_map/ppermute | solution.py:43
  112.1 11.7 %collective-permute-start.5 = (f32[256,256]{1,0:T(8,128)}, f32[256,256]{1,0:T(8,128)}, u32[]{:S(2)}, u32[]{:S(2)}) collective-permute-start(f32[256,256]{1,0:T(8,128)} %get-tuple-element.68), channel_id=1, source_target_pairs={{0,24},{8,0},{16,8},{24,16},{1,25},{9,1},{17,9},{25,17},{2,26},{10... | collective-permute-start | bytes 786440 | tf_op jit(solution)/shard_map/ppermute | solution.py:43

commit v12 on v10

--- a/solution.py
+++ b/solution.py
@@ -49,7 +49,7 @@
     peers = lax.axis_size(axes)
     if peers > 64:
         return lax.psum(value, axes)
-    return jnp.sum(spread_copy(jnp.full((1, 128), value), axes)[:, 0, 0])
+    return jnp.sum(spread_copy(jnp.full((8, 128), value), axes)[:, 0, 0])
 
 
 def doc_layout(lengths_row, token_index):
@@ -220,9 +220,22 @@
     n_dp = lax.axis_size("dp")
     piece_rows = own_rows // n_ctx
     spread = ("dp", "ctx")
-    feat_cols = lax.all_to_all(
-        feats.reshape(tok_rows, n_dp * n_ctx, piece_rows), spread, 1, 0, tiled=False
-    )
+    n_tp = lax.axis_size("tp")
+    core = lax.axis_index("tp")
+    split_cols = n_tp == 2 and piece_rows % 2 == 0
+    if split_cols:
+        halves = feats.reshape(tok_rows, n_dp * n_ctx, 2, piece_rows // 2)
+        mine = lax.dynamic_index_in_dim(halves, core, axis=2, keepdims=False)
+    else:
+        mine = feats.reshape(tok_rows, n_dp * n_ctx, piece_rows)
+    feat_cols = lax.all_to_all(mine, spread, 1, 0, tiled=False)
+    if split_cols:
+        other = lax.ppermute(feat_cols, "tp", [(0, 1), (1, 0)])
+        feat_cols = jnp.where(
+            core == 0,
+            jnp.concatenate([feat_cols, other], axis=-1),
+            jnp.concatenate([other, feat_cols], axis=-1),
+        )
     value_rows = spread_copy(value_flat, spread)
     pieces = lax.dot_general(
         feat_cols.reshape(-1, piece_rows),

time: 98.8 us -> 98.3 us (level)
  waiting for transfers between devices: 32.8 us -> 27.6 us
  starting transfers between devices: 28.3 us -> 30.2 us
  matrix products: 11.5 us -> 12.6 us
    ppermute x3, waiting for transfers between devices: 0.01 us -> 5.02 us  [ring_copy(): lax.ppermute(array, axis, [(i, (i + step) % peers) for i in range(peers)])]
    all_to_all x1, waiting for transfers between devices: 4.95 us -> 0.01 us  [local_body(): feat_cols = lax.all_to_all(mine, spread, 1, 0, tiled=False)]
    all_to_all x2, waiting for transfers between devices: 21.3 us -> 17.6 us  [spread_copy(): return lax.all_to_all(stacked, axes, 0, 0, tiled=False)]
    all_to_all x2, starting transfers between devices: 9.65 us -> 11.9 us  [spread_copy(): return lax.all_to_all(stacked, axes, 0, 0, tiled=False)]
    dot_general x1, matrix products: 1.08 us -> 3.33 us  [local_body(): lax.dot_general(feat_cols.reshape(-1, piece_rows), value_rows.reshape(-1,...]
    dynamic_update_slice x3, local copies, waits for them, and re-layouts: 0.07 us -> 1.96 us  [ring_copy(): lax.dynamic_update_slice_in_dim(out, moved, (place - step) % peers * rows...]
    ppermute x3, waiting for transfers between devices: 6.48 us -> 4.98 us  [shifted(): return lax.ppermute(array, axis, pairs)]
    all_to_all x1 -> x0, local copies, waits for them, and re-layouts: 1.49 us -> none  [local_body(): lax.all_to_all(feats.reshape(tok_rows, n_dp * n_ctx, piece_rows), spread,...]
  transfers between devices with their start and end apart: 9 -> 10, of which waited for: 5 -> 6; matrix products, arithmetic and copies ran while one was open for 22% -> 23% of each run, Pallas kernels for 0% -> 0%
where the time goes in v12:
time: 98.3 us; the launch traced here: 97.2 us
  starting transfers between devices  30.2 us (31%)
  waiting for transfers between devices  27.6 us (28%)
  local copies, waits for them, and re-layouts  17 us (17%)
  matrix products  12.6 us (13%)
  other arithmetic  7.94 us (8%)
  between operations  1.93 us (2%)
    all_to_all x2, waiting for transfers between devices, spread_copy(): return lax.all_to_all(stacked, axes, 0, 0, tiled=False)  17.6 us
    all_to_all x2, starting transfers between devices, spread_copy(): return lax.all_to_all(stacked, axes, 0, 0, tiled=False)  11.9 us
    unnamed x41, local copies, waits for them, and re-layouts  8.35 us
    ppermute x3, starting transfers between devices, shifted(): return lax.ppermute(array, axis, pairs)  8.11 us
    all_to_all x1, starting transfers between devices, local_body(): feat_cols = lax.all_to_all(mine, spread, 1, 0, tiled=False)  5.37 us
    ppermute x3, waiting for transfers between devices, ring_copy(): lax.ppermute(array, axis, [(i, (i + step) % peers) for i in range(peers)])  5.02 us
    ppermute x3, waiting for transfers between devices, shifted(): return lax.ppermute(array, axis, pairs)  4.98 us
    ppermute x3, starting transfers between devices, ring_copy(): lax.ppermute(array, axis, [(i, (i + step) % peers) for i in range(peers)])  4.67 us
  transfers between devices with their start and end apart: 10, of which 6 were waited for; matrix products, arithmetic and copies ran while one was open for 23% of the time, Pallas kernels for 0%

profile of v12, /device:TPU:0, one launch (start us, length us, event | category | flops | bytes accessed | tf_op | source)
XLA Modules:
  0.0 97.2 jit_solution(11106840388618759303)
XLA Ops:
  0.7 0.8 copy.136
  1.8 0.7 convert_divide_fusion
  2.7 1.0 copy.135
  3.7 1.0 copy.142
  4.9 5.5 %collective-permute-start = (bf16[2,128,2,128]{1,3,2,0:T(8,128)(2,1)S(1)}, bf16[2,128,2,128]{1,3,2,0:T(8,128)(2,1)}, u32[]{:S(2)}, u32[]{:S(2)}) collective-permute-start(bf16[2,128,2,128]{1,3,2,0:T(8,128)(2,1)S(1)} %pad_maximum_fusion), channel_id=1, source_target_pairs={{0,8},{8,16},{16,24},{1,9},{9,17},{17,25},{2,10},{10,18},{18,26},{... | collective-permute-start | bytes 393224 | tf_op jit(solution)/shard_map/ppermute | solution.py:25
  10.4 0.8 reshape_squeeze.7
  11.2 1.1 %constant_dynamic-slice_fusion = bf16[128,16,1,128]{3,2,1,0:T(2,128)(2,1)S(1)} fusion(bf16[128,16,2,128]{3,2,1,0:T(2,128)(2,1)S(1)} %reshape_squeeze.7, s32[]{:T(128)S(6)} %select_n.62), kind=kLoop, calls=%fused_computation.114 | loop fusion | bytes 1048580 | tf_op jit(solution)/shard_map/jit(dynamic_index_in_dim)/dynamic_slice | solution.py:228
  12.3 1.9 %copy.215 = bf16[128,16,1,128]{0,3,1,2:T(8,128)(2,1)} copy(bf16[128,16,1,128]{3,2,1,0:T(2,128)(2,1)S(1)} %constant_dynamic-slice_fusion) | data formatting | bytes 1048576
  14.2 5.4 %all-to-all-start = ((bf16[1,128,16,128]{1,3,0,2:T(8,128)(2,1)}), bf16[1,128,16,128]{1,3,0,2:T(8,128)(2,1)}, u32[]{:S(2)}, u32[]{:S(2)}) async-start(bf16[1,128,16,128]{1,3,0,2:T(8,128)(2,1)} %bitcast.53), calls=%async_computation | async-start | bytes 1048576 | tf_op jit(solution)/shard_map/all_to_all | solution.py:231
  19.6 0.5 copy.138
  20.1 0.4 fusion.15
  20.6 0.4 fusion.80
  21.1 0.4 copy-done
  21.5 1.2 %copy.159 = bf16[128,2,8,128]{0,3,2,1:T(8,128)(2,1)} copy(bf16[128,2,8,128]{3,2,1,0:T(8,128)(2,1)S(1)} %bitcast.186) | data formatting | bytes 1048576 | tf_op jit(solution)/shard_map/reshape;squeeze | solution.py:135
  22.7 1.2 %fusion.81 = (f32[2,8,128]{2,1,0:T(8,128)S(1)}, f32[2,8,128,128]{2,3,1,0:T(8,128)S(1)}) fusion(bf16[128,2,8,128]{0,3,2,1:T(8,128)(2,1)S(1)} %bitcast.183, bf16[2,128,2,128]{1,3,2,0:T(8,128)(2,1)} %collective-permute-done, pred[128,128]{0,1:T(8,128)(4,1)S(1)} %get-tuple-element.50), kind=kOutput, calls=%fused_computation.130 | convolution fusion | flops 67893248 | bytes 1662976 | tf_op jit(solution)/shard_map/qhgd,khd->hgqk/dot_general | solution.py:154
  24.0 0.4 fusion.37
  24.4 0.4 copy-done.9
  24.8 0.4 convolution_bitcast_fusion.2
  25.2 1.3 %fusion.5 = f32[2,8,128,128]{3,2,1,0:T(8,128)S(1)} fusion(f32[128,2,8,128]{3,0,2,1:T(8,128)S(1)} %convolution_bitcast_fusion.2, bf16[2,128,2,128]{1,3,2,0:T(8,128)(2,1)} %collective-permute-done, f32[2,8,128,128]{2,3,1,0:T(8,128)S(1)} %get-tuple-element.57, f32[2,8,128]{2,1,0:T(8,128)S(1)} %add.135, f32[2,8,128]{2,1,0:T(8,128)S(1)} %max.8, ...), kind=kOutput, calls=%fused_computation.11 | convolution fusion | flops 68419584 | bytes 3244032 | tf_op jit(solution)/shard_map/hgqk,khd->qhgd/dot_general | solution.py:175
  26.5 0.8 multiply_reduce_fusion
  27.3 1.5 %fusion.24 = bf16[128,2,128]{2,0,1:T(8,128)(2,1)S(1)} fusion(bf16[128,2,8,128]{0,3,2,1:T(8,128)(2,1)} %copy.159, f32[2,8,128,128]{2,3,1,0:T(8,128)S(1)} %get-tuple-element.57, f32[2,8,128]{2,1,0:T(8,128)S(1)} %add.135, f32[2,8,128]{2,1,0:T(8,128)S(1)} %max.8, pred[128,128]{0,1:T(8,128)(4,1)S(1)} %get-tuple-element.50), kind=kOutput, calls=%fused_computation.39 | convolution fusion | flops 68190208 | bytes 1671168 | tf_op jit(solution)/shard_map/hgqk,qhgd->khd/dot_general | solution.py:181
  28.8 1.3 %collective-permute-start.2 = (bf16[128,2,128]{2,0,1:T(8,128)(2,1)S(1)}, bf16[128,2,128]{2,0,1:T(8,128)(2,1)S(1)}, u32[]{:S(2)}, u32[]{:S(2)}) collective-permute-start(bf16[128,2,128]{2,0,1:T(8,128)(2,1)S(1)} %fusion.24), channel_id=1, source_target_pairs={{8,0},{16,8},{24,16},{9,1},{17,9},{25,17},{10,2},{18,10},{26,18},{... | collective-permute-start | bytes 196616 | tf_op jit(solution)/shard_map/ppermute | solution.py:25
  30.1 1.3 %fusion.13 = bf16[2,8,128,128]{2,3,1,0:T(8,128)(2,1)S(1)} fusion(bf16[128,2,8,128]{0,3,2,1:T(8,128)(2,1)S(1)} %copy-done.5, f32[2,8,128]{2,1,0:T(8,128)S(1)} %copy.186, bf16[2,128,2,128]{1,3,2,0:T(8,128)(2,1)} %collective-permute-done, f32[2,8,128]{2,1,0:T(8,128)S(1)} %add.135, f32[2,8,128,128]{2,3,1,0:T(8,128)S(1)} %get-tuple-element.57, ...), kind=kOutput, calls=%fused_computation.22 | convolution fusion | flops 68681728 | bytes 2203648 | tf_op jit(solution)/shard_map/qhgd,khd->hgqk/dot_general | solution.py:192
  31.4 3.6 %collective-permute-done.2 = bf16[128,2,128]{2,0,1:T(8,128)(2,1)S(1)} collective-permute-done((bf16[128,2,128]{2,0,1:T(8,128)(2,1)S(1)}, bf16[128,2,128]{2,0,1:T(8,128)(2,1)S(1)}, u32[]{:S(2)}, u32[]{:S(2)}) %collective-permute-start.2) | collective-permute-done | bytes 65568 | tf_op jit(solution)/shard_map/ppermute | solution.py:25
  35.5 0.5 copy-done.7
  36.1 1.1 %broadcast_in_dim.84 = bf16[16,128,256]{2,1,0:T(8,128)(2,1)} broadcast(bf16[128,256]{1,0:T(8,128)(2,1)S(1)} %copy.163), dimensions={1,2} | broadcast | bytes 1114112 | tf_op jit(solution)/shard_map/broadcast_in_dim | solution.py:32
  37.2 6.9 %all-to-all-start.1 = ((bf16[16,128,256]{2,1,0:T(8,128)(2,1)}), bf16[16,128,256]{2,1,0:T(8,128)(2,1)}, u32[]{:S(2)}, u32[]{:S(2)}) async-start(bf16[16,128,256]{2,1,0:T(8,128)(2,1)} %broadcast_in_dim.84), calls=%async_computation.1 | async-start | bytes 2097152 | tf_op jit(solution)/shard_map/all_to_all | solution.py:33
  44.4 1.3 %collective-permute-start.1 = (bf16[128,2,128]{0,2,1:T(8,128)(2,1)S(1)}, bf16[128,2,128]{0,2,1:T(8,128)(2,1)S(1)}, u32[]{:S(2)}, u32[]{:S(2)}) collective-permute-start(bf16[128,2,128]{0,2,1:T(8,128)(2,1)S(1)} %fusion.25), channel_id=1, source_target_pairs={{8,0},{16,8},{24,16},{9,1},{17,9},{25,17},{10,2},{18,10},{26,18},{... | collective-permute-start | bytes 196616 | tf_op jit(solution)/shard_map/ppermute | solution.py:25
  45.8 0.4 fusion.14
  46.5 1.1 %fusion.8 = f32[2,128,8,128]{3,1,2,0:T(8,128)S(1)} fusion(f32[2,128,8,128]{3,1,2,0:T(8,128)S(1)} %fusion.48, bf16[2,8,128,128]{2,3,1,0:T(8,128)(2,1)S(1)} %fusion.13, bf16[2,128,2,128]{1,3,2,0:T(8,128)(2,1)} %collective-permute-done), kind=kOutput, calls=%fused_computation.15 | convolution fusion | flops 67633152 | bytes 2686976 | tf_op jit(solution)/shard_map/hgqk,khd->qhgd/dot_general | solution.py:197
  48.1 1.2 %copy.165 = bf16[1,128,16,128]{3,2,1,0:T(8,128)(2,1)} copy(bf16[1,128,16,128]{1,3,2,0:T(8,128)(2,1)S(1)} %fusion.27) | data formatting | bytes 1048576
  49.2 1.4 %collective-permute-done.1 = bf16[128,2,128]{0,2,1:T(8,128)(2,1)S(1)} collective-permute-done((bf16[128,2,128]{0,2,1:T(8,128)(2,1)S(1)}, bf16[128,2,128]{0,2,1:T(8,128)(2,1)S(1)}, u32[]{:S(2)}, u32[]{:S(2)}) %collective-permute-start.1) | collective-permute-done | bytes 65568 | tf_op jit(solution)/shard_map/ppermute | solution.py:25
  51.0 15.6 %all-to-all-done.1 = bf16[16,128,256]{2,1,0:T(8,128)(2,1)} async-done(((bf16[16,128,256]{2,1,0:T(8,128)(2,1)}), bf16[16,128,256]{2,1,0:T(8,128)(2,1)}, u32[]{:S(2)}, u32[]{:S(2)}) %all-to-all-start.1) | async-done | bytes 1048608 | tf_op jit(solution)/shard_map/all_to_all | solution.py:33
  66.7 3.3 %multiply_reduce_fusion.1 = (f32[]{:T(128)}, f32[1024,256]{1,0:T(8,128)S(1)}, f32[256,256]{1,0:T(8,128)}) fusion(f32[1024,256]{1,0:T(8,128)S(1)} %broadcast_in_dim.81, s32[]{:T(128)S(6)} %select_n.64, bf16[16,128,256]{2,1,0:T(8,128)(2,1)} %all-to-all-done.1, bf16[16,128,128]{1,2,0:T(8,128)(2,1)S(1)} %collective-permute-done.3, ...), kind=kOutput, calls=%fused_computation.66 | convolution fusion | flops 273285120 | bytes 2621449 | tf_op jit(solution)/shard_map/dot_general | solution.py:240
  70.0 1.3 %broadcast_in_dim_broadcast_in_dim_broadcast_in_dim.3 = f32[32,8,128]{2,1,0:T(8,128)} broadcast(f32[]{:T(128)} %get-tuple-element.46), dimensions={} | broadcast | bytes 131076 | tf_op jit(solution)/shard_map/broadcast_in_dim;broadcast_in_dim;broadcast_in_dim | solution.py:32
  71.4 5.0 %all-to-all-start.2 = ((f32[32,8,128]{2,1,0:T(8,128)}), f32[32,8,128]{2,1,0:T(8,128)}, u32[]{:S(2)}, u32[]{:S(2)}) async-start(f32[32,8,128]{2,1,0:T(8,128)} %broadcast_in_dim_broadcast_in_dim_broadcast_in_dim.3), calls=%async_computation.2 | async-start | bytes 262144 | tf_op jit(solution)/shard_map/all_to_all | solution.py:33
  76.4 1.7 %collective-permute-start.4 = (f32[256,256]{1,0:T(8,128)}, f32[256,256]{1,0:T(8,128)}, u32[]{:S(2)}, u32[]{:S(2)}) collective-permute-start(f32[256,256]{1,0:T(8,128)} %get-tuple-element.60), channel_id=1, source_target_pairs={{0,8},{8,16},{16,24},{24,0},{1,9},{9,17},{17,25},{25,1},{2,10},{10... | collective-permute-start | bytes 786440 | tf_op jit(solution)/shard_map/ppermute | solution.py:43
  78.2 1.5 %collective-permute-start.5 = (f32[256,256]{1,0:T(8,128)}, f32[256,256]{1,0:T(8,128)}, u32[]{:S(2)}, u32[]{:S(2)}) collective-permute-start(f32[256,256]{1,0:T(8,128)} %get-tuple-element.60), channel_id=1, source_target_pairs={{0,16},{8,24},{16,0},{24,8},{1,17},{9,25},{17,1},{25,9},{2,18},{10... | collective-permute-start | bytes 786440 | tf_op jit(solution)/shard_map/ppermute | solution.py:43
  79.7 0.8 copy.166
  80.5 0.7 copy.167
  81.2 1.5 %collective-permute-start.6 = (f32[256,256]{1,0:T(8,128)}, f32[256,256]{1,0:T(8,128)S(1)}, u32[]{:S(2)}, u32[]{:S(2)}) collective-permute-start(f32[256,256]{1,0:T(8,128)} %get-tuple-element.60), channel_id=1, source_target_pairs={{0,24},{8,0},{16,8},{24,16},{1,25},{9,1},{17,9},{25,17},{2,26},{10... | collective-permute-start | bytes 786440 | tf_op jit(solution)/shard_map/ppermute | solution.py:43
  82.6 1.9 %all-to-all-done.2 = f32[32,8,128]{2,1,0:T(8,128)} async-done(((f32[32,8,128]{2,1,0:T(8,128)}), f32[32,8,128]{2,1,0:T(8,128)}, u32[]{:S(2)}, u32[]{:S(2)}) %all-to-all-start.2) | async-done | bytes 131104 | tf_op jit(solution)/shard_map/all_to_all | solution.py:33
  84.6 1.5 %slice_reduce_fusion = f32[]{:T(128)} fusion(f32[32,8,128]{2,1,0:T(8,128)} %all-to-all-done.2), kind=kLoop, calls=%fused_computation.106 | loop fusion | flops 31 | bytes 132 | tf_op jit(solution)/shard_map/reduce_sum | solution.py:52
  86.8 1.0 %collective-permute-done.4 = f32[256,256]{1,0:T(8,128)} collective-permute-done((f32[256,256]{1,0:T(8,128)}, f32[256,256]{1,0:T(8,128)}, u32[]{:S(2)}, u32[]{:S(2)}) %collective-permute-start.4) | collective-permute-done | bytes 262176 | tf_op jit(solution)/shard_map/ppermute | solution.py:43
  87.8 1.0 constant_dynamic-update-slice_fusion.2
  88.8 4.0 %collective-permute-done.5 = f32[256,256]{1,0:T(8,128)} collective-permute-done((f32[256,256]{1,0:T(8,128)}, f32[256,256]{1,0:T(8,128)}, u32[]{:S(2)}, u32[]{:S(2)}) %collective-permute-start.5) | collective-permute-done | bytes 262176 | tf_op jit(solution)/shard_map/ppermute | solution.py:43
  92.8 1.0 constant_dynamic-update-slice_fusion.1
  93.8 3.4 %multiply_subtract_fusion = (f32[1024,256]{1,0:T(8,128)}, f32[1024,256]{1,0:T(8,128)}, f32[1024,256]{1,0:T(8,128)}) fusion(f32[1024,256]{1,0:T(8,128)S(1)} %copy-done.2, f32[1024,256]{1,0:T(8,128)S(1)} %constant_dynamic-update-slice_fusion, f32[]{:T(128)S(6)} %min_shard_map.3, f32[1024,256]{1,0:T(8,128)S(1)} %copy-done.3, f32[1024,256]{1,0:T(8,128)} %param.21), kind=kLoop, calls=%fused_computation.53 | loop fusion | flops 4194304 | bytes 7340036 | tf_op jit(solution)/shard_map/sub | solution.py:100
  (66 shorter events, 3.1 us)
Async XLA Ops:
  0.6 9.8 %copy-start.1 = (bf16[1,128,4096]{2,1,0:T(8,128)(2,1)S(1)}, bf16[1,128,4096]{2,1,0:T(8,128)(2,1)}, u32[]{:S(2)}) copy-start(bf16[1,128,4096]{2,1,0:T(8,128)(2,1)} %param.15) | copy-start | bytes 3145732
  4.9 17.8 %collective-permute-start = (bf16[2,128,2,128]{1,3,2,0:T(8,128)(2,1)S(1)}, bf16[2,128,2,128]{1,3,2,0:T(8,128)(2,1)}, u32[]{:S(2)}, u32[]{:S(2)}) collective-permute-start(bf16[2,128,2,128]{1,3,2,0:T(8,128)(2,1)S(1)} %pad_maximum_fusion), channel_id=1, source_target_pairs={{0,8},{8,16},{16,24},{1,9},{9,17},{17,25},{2,10},{10,18},{18,26},{... | collective-permute-start | bytes 393224 | tf_op jit(solution)/shard_map/ppermute | solution.py:25
  12.3 7.3 %copy-start.4 = (bf16[1,128,16,128]{3,2,1,0:T(8,128)(2,1)S(1)}, bf16[1,128,16,128]{3,2,1,0:T(8,128)(2,1)}, u32[]{:S(2)}) copy-start(bf16[1,128,16,128]{3,2,1,0:T(8,128)(2,1)} %param.11) | copy-start | bytes 1572868
  14.2 21.9 %all-to-all-start = ((bf16[1,128,16,128]{1,3,0,2:T(8,128)(2,1)}), bf16[1,128,16,128]{1,3,0,2:T(8,128)(2,1)}, u32[]{:S(2)}, u32[]{:S(2)}) async-start(bf16[1,128,16,128]{1,3,0,2:T(8,128)(2,1)} %bitcast.53), calls=%async_computation | async-start | bytes 1048576 | tf_op jit(solution)/shard_map/all_to_all | solution.py:231
  20.5 1.0 %copy-start = (bf16[1,128,16,128]{3,2,1,0:T(8,128)(2,1)S(1)}, bf16[1,128,16,128]{3,2,1,0:T(8,128)(2,1)}, u32[]{:S(2)}) copy-start(bf16[1,128,16,128]{3,2,1,0:T(8,128)(2,1)} %param.14) | copy-start | bytes 1572868
  23.9 11.0 %copy-start.11 = (f32[2,8,128]{2,1,0:T(8,128)}, f32[2,8,128]{2,1,0:T(8,128)S(1)}, u32[]{:S(2)}) copy-start(f32[2,8,128]{2,1,0:T(8,128)S(1)} %max.8) | copy-start | bytes 24580
  24.0 0.8 copy-start.9
  24.4 10.6 %copy-start.13 = (f32[2,8,128]{2,1,0:T(8,128)}, f32[2,8,128]{2,1,0:T(8,128)S(1)}, u32[]{:S(2)}) copy-start(f32[2,8,128]{2,1,0:T(8,128)S(1)} %add.135) | copy-start | bytes 24580
  27.3 2.8 %copy-start.15 = (f32[2,8,128]{2,1,0:T(8,128)}, f32[2,8,128]{2,1,0:T(8,128)S(1)}, u32[]{:S(2)}) copy-start(f32[2,8,128]{2,1,0:T(8,128)S(1)} %copy.186) | copy-start | bytes 24580
  27.3 2.8 %copy-start.5 = (bf16[128,2,8,128]{0,3,2,1:T(8,128)(2,1)S(1)}, bf16[128,2,8,128]{0,3,2,1:T(8,128)(2,1)}, u32[]{:S(2)}) copy-start(bf16[128,2,8,128]{0,3,2,1:T(8,128)(2,1)} %copy.159) | copy-start | bytes 1572868
  28.8 6.2 %collective-permute-start.2 = (bf16[128,2,128]{2,0,1:T(8,128)(2,1)S(1)}, bf16[128,2,128]{2,0,1:T(8,128)(2,1)S(1)}, u32[]{:S(2)}, u32[]{:S(2)}) collective-permute-start(bf16[128,2,128]{2,0,1:T(8,128)(2,1)S(1)} %fusion.24), channel_id=1, source_target_pairs={{8,0},{16,8},{24,16},{9,1},{17,9},{25,17},{10,2},{18,10},{26,18},{... | collective-permute-start | bytes 196616 | tf_op jit(solution)/shard_map/ppermute | solution.py:25
  35.3 0.6 copy-start.7
  37.2 29.5 %all-to-all-start.1 = ((bf16[16,128,256]{2,1,0:T(8,128)(2,1)}), bf16[16,128,256]{2,1,0:T(8,128)(2,1)}, u32[]{:S(2)}, u32[]{:S(2)}) async-start(bf16[16,128,256]{2,1,0:T(8,128)(2,1)} %broadcast_in_dim.84), calls=%async_computation.1 | async-start | bytes 2097152 | tf_op jit(solution)/shard_map/all_to_all | solution.py:33
  44.1 1.7 %copy-start.6 = (bf16[128,2,8,128]{0,3,2,1:T(8,128)(2,1)S(1)}, bf16[128,2,8,128]{0,3,2,1:T(8,128)(2,1)}, u32[]{:S(2)}) copy-start(bf16[128,2,8,128]{0,3,2,1:T(8,128)(2,1)} %copy.159) | copy-start | bytes 1572868
  44.1 1.7 %copy-start.10 = (bf16[1,128,2,128]{3,2,1,0:T(2,128)(2,1)S(1)}, bf16[1,128,2,128]{3,2,1,0:T(2,128)(2,1)}, u32[]{:S(2)}) copy-start(bf16[1,128,2,128]{3,2,1,0:T(2,128)(2,1)} %param.13) | copy-start | bytes 196612
  44.1 1.7 %copy-start.12 = (f32[2,8,128]{2,1,0:T(8,128)S(1)}, f32[2,8,128]{2,1,0:T(8,128)}, u32[]{:S(2)}) copy-start(f32[2,8,128]{2,1,0:T(8,128)} %copy-done.11) | copy-start | bytes 24580
  44.1 1.7 %copy-start.14 = (f32[2,8,128]{2,1,0:T(8,128)S(1)}, f32[2,8,128]{2,1,0:T(8,128)}, u32[]{:S(2)}) copy-start(f32[2,8,128]{2,1,0:T(8,128)} %copy-done.13) | copy-start | bytes 24580
  44.1 1.7 %copy-start.16 = (f32[2,8,128]{2,1,0:T(8,128)S(1)}, f32[2,8,128]{2,1,0:T(8,128)}, u32[]{:S(2)}) copy-start(f32[2,8,128]{2,1,0:T(8,128)} %copy-done.15) | copy-start | bytes 24580
  44.4 6.2 %collective-permute-start.1 = (bf16[128,2,128]{0,2,1:T(8,128)(2,1)S(1)}, bf16[128,2,128]{0,2,1:T(8,128)(2,1)S(1)}, u32[]{:S(2)}, u32[]{:S(2)}) collective-permute-start(bf16[128,2,128]{0,2,1:T(8,128)(2,1)S(1)} %fusion.25), channel_id=1, source_target_pairs={{8,0},{16,8},{24,16},{9,1},{17,9},{25,17},{10,2},{18,10},{26,18},{... | collective-permute-start | bytes 196616 | tf_op jit(solution)/shard_map/ppermute | solution.py:25
  47.8 3.2 %collective-permute-start.3 = (bf16[16,128,128]{1,2,0:T(8,128)(2,1)}, bf16[16,128,128]{1,2,0:T(8,128)(2,1)S(1)}, u32[]{:S(2)}, u32[]{:S(2)}) collective-permute-start(bf16[16,128,128]{1,2,0:T(8,128)(2,1)} %bitcast.56), channel_id=1, source_target_pairs={{0,1},{1,0},{2,3},{3,2},{4,5},{5,4},{6,7},{7,6},{8,9},{9,8},{10,11... | collective-permute-start | bytes 1572872 | tf_op jit(solution)/shard_map/ppermute | solution.py:233
  70.0 10.4 %copy-start.8 = (bf16[128,2,128]{2,0,1:T(8,128)(2,1)S(1)}, bf16[128,2,128]{2,0,1:T(8,128)(2,1)}, u32[]{:S(2)}) copy-start(bf16[128,2,128]{2,0,1:T(8,128)(2,1)} %copy-done.7) | copy-start | bytes 196612
  71.4 13.2 %all-to-all-start.2 = ((f32[32,8,128]{2,1,0:T(8,128)}), f32[32,8,128]{2,1,0:T(8,128)}, u32[]{:S(2)}, u32[]{:S(2)}) async-start(f32[32,8,128]{2,1,0:T(8,128)} %broadcast_in_dim_broadcast_in_dim_broadcast_in_dim.3), calls=%async_computation.2 | async-start | bytes 262144 | tf_op jit(solution)/shard_map/all_to_all | solution.py:33
  76.4 11.4 %collective-permute-start.4 = (f32[256,256]{1,0:T(8,128)}, f32[256,256]{1,0:T(8,128)}, u32[]{:S(2)}, u32[]{:S(2)}) collective-permute-start(f32[256,256]{1,0:T(8,128)} %get-tuple-element.60), channel_id=1, source_target_pairs={{0,8},{8,16},{16,24},{24,0},{1,9},{9,17},{17,25},{25,1},{2,10},{10... | collective-permute-start | bytes 786440 | tf_op jit(solution)/shard_map/ppermute | solution.py:43
  78.2 14.6 %collective-permute-start.5 = (f32[256,256]{1,0:T(8,128)}, f32[256,256]{1,0:T(8,128)}, u32[]{:S(2)}, u32[]{:S(2)}) collective-permute-start(f32[256,256]{1,0:T(8,128)} %get-tuple-element.60), channel_id=1, source_target_pairs={{0,16},{8,24},{16,0},{24,8},{1,17},{9,25},{17,1},{25,9},{2,18},{10... | collective-permute-start | bytes 786440 | tf_op jit(solution)/shard_map/ppermute | solution.py:43
  79.7 14.2 %copy-start.2 = (f32[1024,256]{1,0:T(8,128)S(1)}, f32[1024,256]{1,0:T(8,128)}, u32[]{:S(2)}) copy-start(f32[1024,256]{1,0:T(8,128)} %param.19) | copy-start | bytes 3145732
  79.7 14.2 %copy-start.3 = (f32[1024,256]{1,0:T(8,128)S(1)}, f32[1024,256]{1,0:T(8,128)}, u32[]{:S(2)}) copy-start(f32[1024,256]{1,0:T(8,128)} %param.20) | copy-start | bytes 3145732
  81.2 12.6 %collective-permute-start.6 = (f32[256,256]{1,0:T(8,128)}, f32[256,256]{1,0:T(8,128)S(1)}, u32[]{:S(2)}, u32[]{:S(2)}) collective-permute-start(f32[256,256]{1,0:T(8,128)} %get-tuple-element.60), channel_id=1, source_target_pairs={{0,24},{8,0},{16,8},{24,16},{1,25},{9,1},{17,9},{25,17},{2,26},{10... | collective-permute-start | bytes 786440 | tf_op jit(solution)/shard_map/ppermute | solution.py:43

commit v13 on v10

--- a/solution.py
+++ b/solution.py
@@ -49,7 +49,7 @@
     peers = lax.axis_size(axes)
     if peers > 64:
         return lax.psum(value, axes)
-    return jnp.sum(spread_copy(jnp.full((1, 128), value), axes)[:, 0, 0])
+    return jnp.sum(spread_copy(jnp.full((8, 128), value), axes)[:, 0, 0])
 
 
 def doc_layout(lengths_row, token_index):
@@ -219,9 +219,10 @@
     own_rows = param.shape[0]
     n_dp = lax.axis_size("dp")
     piece_rows = own_rows // n_ctx
-    spread = ("dp", "ctx")
+    spread = ("ctx", "dp")
+    by_place = feats.reshape(tok_rows, n_dp, n_ctx, piece_rows).transpose(0, 2, 1, 3)
     feat_cols = lax.all_to_all(
-        feats.reshape(tok_rows, n_dp * n_ctx, piece_rows), spread, 1, 0, tiled=False
+        by_place.reshape(tok_rows, n_dp * n_ctx, piece_rows), spread, 1, 0, tiled=False
     )
     value_rows = spread_copy(value_flat, spread)
     pieces = lax.dot_general(

time: 98.8 us -> 99.3 us (level)
  starting transfers between devices: 28.3 us -> 24.3 us
  waiting for transfers between devices: 32.8 us -> 35.9 us
  matrix products: 11.5 us -> 12.5 us
    all_to_all x1, waiting for transfers between devices: 4.95 us -> 9.98 us  [local_body(): lax.all_to_all(by_place.reshape(tok_rows, n_dp * n_ctx, piece_rows), spre...]
    all_to_all x2, starting transfers between devices: 9.65 us -> 6.68 us  [spread_copy(): return lax.all_to_all(stacked, axes, 0, 0, tiled=False)]
    ppermute x3, waiting for transfers between devices: 6.48 us -> 4.48 us  [shifted(): return lax.ppermute(array, axis, pairs)]
    all_to_all x1 -> x0, local copies, waits for them, and re-layouts: 1.49 us -> none  [local_body(): lax.all_to_all(feats.reshape(tok_rows, n_dp * n_ctx, piece_rows), spread,...]
    transpose x0 -> x1, local copies, waits for them, and re-layouts: none -> 1.31 us  [local_body(): feats.reshape(tok_rows, n_dp, n_ctx, piece_rows).transpose(0, 2, 1, 3)]
    ppermute x3, starting transfers between devices: 4.95 us -> 3.85 us  [ring_copy(): lax.ppermute(array, axis, [(i, (i + step) % peers) for i in range(peers)])]
    dot_general x2, matrix products: 0.6 us -> 1.64 us  [local_body(): jnp.einsum('hgqk,qhgd->khd', dscores, rotated_query_rows, preferred_eleme...]
    unnamed x33 -> x31, local copies, waits for them, and re-layouts: 9.15 us -> 8.77 us
  transfers between devices with their start and end apart: 9 -> 9, of which waited for: 5 -> 6; matrix products, arithmetic and copies ran while one was open for 22% -> 24% of each run, Pallas kernels for 0% -> 0%
where the time goes in v13:
time: 99.3 us; the launch traced here: 98.2 us
  waiting for transfers between devices  35.9 us (36%)
  starting transfers between devices  24.3 us (24%)
  local copies, waits for them, and re-layouts  15.5 us (16%)
  matrix products  12.5 us (13%)
  other arithmetic  8.12 us (8%)
  between operations  1.88 us (2%)
    all_to_all x2, waiting for transfers between devices, spread_copy(): return lax.all_to_all(stacked, axes, 0, 0, tiled=False)  20.8 us
    all_to_all x1, waiting for transfers between devices, local_body(): lax.all_to_all(by_place.reshape(tok_rows, n_dp * n_ctx, piece_rows), spre...  9.98 us
    unnamed x31, local copies, waits for them, and re-layouts  8.77 us
    ppermute x3, starting transfers between devices, shifted(): return lax.ppermute(array, axis, pairs)  8.36 us
    all_to_all x2, starting transfers between devices, spread_copy(): return lax.all_to_all(stacked, axes, 0, 0, tiled=False)  6.68 us
    all_to_all x1, starting transfers between devices, local_body(): lax.all_to_all(by_place.reshape(tok_rows, n_dp * n_ctx, piece_rows), spre...  5.46 us
    ppermute x3, waiting for transfers between devices, shifted(): return lax.ppermute(array, axis, pairs)  4.48 us
    ppermute x3, starting transfers between devices, ring_copy(): lax.ppermute(array, axis, [(i, (i + step) % peers) for i in range(peers)])  3.85 us
  transfers between devices with their start and end apart: 9, of which 6 were waited for; matrix products, arithmetic and copies ran while one was open for 24% of the time, Pallas kernels for 0%

profile of v13, /device:TPU:0, one launch (start us, length us, event | category | flops | bytes accessed | tf_op | source)
XLA Modules:
  0.0 98.2 jit_solution(14463700913036185047)
XLA Ops:
  0.7 0.8 copy.191
  1.8 0.7 convert_divide_fusion
  2.7 1.0 copy.190
  3.7 1.0 copy.197
  4.9 5.5 %collective-permute-start = (bf16[2,128,2,128]{1,3,2,0:T(8,128)(2,1)S(1)}, bf16[2,128,2,128]{1,3,2,0:T(8,128)(2,1)}, u32[]{:S(2)}, u32[]{:S(2)}) collective-permute-start(bf16[2,128,2,128]{1,3,2,0:T(8,128)(2,1)S(1)} %pad_maximum_fusion), channel_id=1, source_target_pairs={{0,8},{8,16},{16,24},{1,9},{9,17},{17,25},{2,10},{10,18},{18,26},{... | collective-permute-start | bytes 393224 | tf_op jit(solution)/shard_map/ppermute | solution.py:25
  10.4 0.7 copy.218
  11.1 1.3 %copy.219 = bf16[128,4,4,256]{3,0,2,1:T(8,128)(2,1)} copy(bf16[128,4,4,256]{0,3,1,2:T(8,128)(2,1)S(1)} %bitcast.195) | data formatting | bytes 2097152 | tf_op jit(solution)/shard_map/transpose | solution.py:223
  12.4 5.5 %all-to-all-start.1 = ((bf16[1,128,16,256]{3,1,0,2:T(8,128)(2,1)}), bf16[1,128,16,256]{3,1,0,2:T(8,128)(2,1)S(1)}, u32[]{:S(2)}, u32[]{:S(2)}) async-start(bf16[1,128,16,256]{3,1,0,2:T(8,128)(2,1)} %bitcast.58), calls=%async_computation.1 | async-start | bytes 2097152 | tf_op jit(solution)/shard_map/all_to_all | solution.py:224
  17.9 0.5 copy.193
  18.4 0.4 fusion.15
  18.9 0.4 fusion.73
  19.4 0.6 copy-done.2
  20.0 1.2 %copy.214 = bf16[128,2,8,128]{0,3,2,1:T(8,128)(2,1)} copy(bf16[128,2,8,128]{3,2,1,0:T(8,128)(2,1)S(1)} %bitcast.196) | data formatting | bytes 1048576 | tf_op jit(solution)/shard_map/reshape;squeeze | solution.py:135
  21.2 1.2 %fusion.74 = (f32[2,8,128]{2,1,0:T(8,128)S(1)}, f32[2,8,128,128]{2,3,1,0:T(8,128)S(1)}) fusion(bf16[128,2,8,128]{0,3,2,1:T(8,128)(2,1)S(1)} %bitcast.190, bf16[2,128,2,128]{1,3,2,0:T(8,128)(2,1)} %collective-permute-done, pred[128,128]{0,1:T(8,128)(4,1)S(1)} %get-tuple-element.54), kind=kOutput, calls=%fused_computation.121 | convolution fusion | flops 67893248 | bytes 1662976 | tf_op jit(solution)/shard_map/qhgd,khd->hgqk/dot_general | solution.py:154
  22.4 0.4 fusion.31
  22.8 0.5 copy-done.10
  23.4 0.4 convolution_bitcast_fusion.2
  23.8 1.2 %fusion.5 = f32[2,8,128,128]{3,2,1,0:T(8,128)S(1)} fusion(f32[128,2,8,128]{3,0,2,1:T(8,128)S(1)} %convolution_bitcast_fusion.2, bf16[2,128,2,128]{1,3,2,0:T(8,128)(2,1)} %collective-permute-done, f32[2,8,128,128]{2,3,1,0:T(8,128)S(1)} %get-tuple-element.61, f32[2,8,128]{2,1,0:T(8,128)S(1)} %add.131, f32[2,8,128]{2,1,0:T(8,128)S(1)} %max.8, ...), kind=kOutput, calls=%fused_computation.11 | convolution fusion | flops 68419584 | bytes 3244032 | tf_op jit(solution)/shard_map/hgqk,khd->qhgd/dot_general | solution.py:175
  25.0 0.8 multiply_reduce_fusion
  25.9 1.8 %fusion.24 = bf16[128,2,128]{2,0,1:T(8,128)(2,1)S(1)} fusion(bf16[128,2,8,128]{0,3,2,1:T(8,128)(2,1)} %copy.214, f32[2,8,128,128]{2,3,1,0:T(8,128)} %copy-done, f32[2,8,128]{2,1,0:T(8,128)S(1)} %add.131, f32[2,8,128]{2,1,0:T(8,128)S(1)} %max.8, pred[128,128]{0,1:T(8,128)(4,1)S(1)} %get-tuple-element.54), kind=kOutput, calls=%fused_computation.39 | convolution fusion | flops 68190208 | bytes 1671168 | tf_op jit(solution)/shard_map/hgqk,qhgd->khd/dot_general | solution.py:181
  27.7 1.4 %collective-permute-start.2 = (bf16[128,2,128]{2,0,1:T(8,128)(2,1)S(1)}, bf16[128,2,128]{2,0,1:T(8,128)(2,1)S(1)}, u32[]{:S(2)}, u32[]{:S(2)}) collective-permute-start(bf16[128,2,128]{2,0,1:T(8,128)(2,1)S(1)} %fusion.24), channel_id=1, source_target_pairs={{8,0},{16,8},{24,16},{9,1},{17,9},{25,17},{10,2},{18,10},{26,18},{... | collective-permute-start | bytes 196616 | tf_op jit(solution)/shard_map/ppermute | solution.py:25
  29.1 0.4 fusion.14
  29.5 2.1 %fusion.13 = bf16[2,8,128,128]{2,3,1,0:T(8,128)(2,1)} fusion(bf16[128,2,8,128]{0,3,2,1:T(8,128)(2,1)S(1)} %copy-done.7, f32[2,8,128]{2,1,0:T(8,128)S(1)} %copy.247, bf16[2,128,2,128]{1,3,2,0:T(8,128)(2,1)} %collective-permute-done, f32[2,8,128]{2,1,0:T(8,128)S(1)} %add.131, f32[2,8,128,128]{2,3,1,0:T(8,128)S(1)} %copy-done.1, f32[2,8,128]{2,1,0:T(8,128)S(1)} %max.8, ...), kind=kOutput, calls=%fused_computation.22 | convolution fusion | flops 68681728 | bytes 2203648 | tf_op jit(solution)/shard_map/qhgd,khd->hgqk/dot_general | solution.py:192
  31.6 2.4 %collective-permute-done.2 = bf16[128,2,128]{2,0,1:T(8,128)(2,1)S(1)} collective-permute-done((bf16[128,2,128]{2,0,1:T(8,128)(2,1)S(1)}, bf16[128,2,128]{2,0,1:T(8,128)(2,1)S(1)}, u32[]{:S(2)}, u32[]{:S(2)}) %collective-permute-start.2) | collective-permute-done | bytes 65568 | tf_op jit(solution)/shard_map/ppermute | solution.py:25
  34.0 0.3 add_convert_fusion
  34.5 0.5 copy-done.8
  35.1 10.0 %all-to-all-done.1 = bf16[1,128,16,256]{3,1,0,2:T(8,128)(2,1)S(1)} async-done(((bf16[1,128,16,256]{3,1,0,2:T(8,128)(2,1)}), bf16[1,128,16,256]{3,1,0,2:T(8,128)(2,1)S(1)}, u32[]{:S(2)}, u32[]{:S(2)}) %all-to-all-start.1) | async-done | bytes 1048608 | tf_op jit(solution)/shard_map/all_to_all | solution.py:224
  45.1 1.1 %broadcast_in_dim.80 = bf16[16,128,256]{2,1,0:T(8,128)(2,1)} broadcast(bf16[128,256]{1,0:T(8,128)(2,1)S(1)} %copy.217), dimensions={1,2} | broadcast | bytes 1114112 | tf_op jit(solution)/shard_map/broadcast_in_dim | solution.py:32
  46.1 3.7 %all-to-all-start = ((bf16[16,128,256]{2,1,0:T(8,128)(2,1)}), bf16[16,128,256]{2,1,0:T(8,128)(2,1)S(1)}, u32[]{:S(2)}, u32[]{:S(2)}) async-start(bf16[16,128,256]{2,1,0:T(8,128)(2,1)} %broadcast_in_dim.80), calls=%async_computation | async-start | bytes 2097152 | tf_op jit(solution)/shard_map/all_to_all | solution.py:33
  49.8 1.3 %fusion.25 = bf16[128,2,128]{0,2,1:T(8,128)(2,1)S(1)} fusion(bf16[128,2,8,128]{0,3,2,1:T(8,128)(2,1)S(1)} %bitcast.191, bf16[2,8,128,128]{2,3,1,0:T(8,128)(2,1)} %fusion.13), kind=kOutput, calls=%fused_computation.40 | convolution fusion | flops 67174400 | bytes 1114112 | tf_op jit(solution)/shard_map/hgqk,qhgd->khd/dot_general | solution.py:201
  51.2 1.4 %collective-permute-start.1 = (bf16[128,2,128]{0,2,1:T(8,128)(2,1)S(1)}, bf16[128,2,128]{0,2,1:T(8,128)(2,1)S(1)}, u32[]{:S(2)}, u32[]{:S(2)}) collective-permute-start(bf16[128,2,128]{0,2,1:T(8,128)(2,1)S(1)} %fusion.25), channel_id=1, source_target_pairs={{8,0},{16,8},{24,16},{9,1},{17,9},{25,17},{10,2},{18,10},{26,18},{... | collective-permute-start | bytes 196616 | tf_op jit(solution)/shard_map/ppermute | solution.py:25
  52.9 1.1 %fusion.8 = f32[2,128,8,128]{3,1,2,0:T(8,128)S(1)} fusion(f32[2,128,8,128]{3,1,2,0:T(8,128)S(1)} %fusion.42, bf16[2,8,128,128]{2,3,1,0:T(8,128)(2,1)S(1)} %copy-done.3, bf16[2,128,2,128]{1,3,2,0:T(8,128)(2,1)} %collective-permute-done), kind=kOutput, calls=%fused_computation.15 | convolution fusion | flops 67633152 | bytes 2686976 | tf_op jit(solution)/shard_map/hgqk,khd->qhgd/dot_general | solution.py:197
  54.2 0.9 fusion.27
  55.2 2.2 %copy.226 = bf16[1,128,16,128]{3,2,1,0:T(8,128)(2,1)} copy(bf16[1,128,16,128]{1,3,2,0:T(8,128)(2,1)} %fusion.27) | data formatting | bytes 1048576
  57.4 2.1 %collective-permute-done.1 = bf16[128,2,128]{0,2,1:T(8,128)(2,1)S(1)} collective-permute-done((bf16[128,2,128]{0,2,1:T(8,128)(2,1)S(1)}, bf16[128,2,128]{0,2,1:T(8,128)(2,1)S(1)}, u32[]{:S(2)}, u32[]{:S(2)}) %collective-permute-start.1) | collective-permute-done | bytes 65568 | tf_op jit(solution)/shard_map/ppermute | solution.py:25
  59.5 0.3 fusion.39
  59.8 16.7 %all-to-all-done = bf16[16,128,256]{2,1,0:T(8,128)(2,1)S(1)} async-done(((bf16[16,128,256]{2,1,0:T(8,128)(2,1)}), bf16[16,128,256]{2,1,0:T(8,128)(2,1)S(1)}, u32[]{:S(2)}, u32[]{:S(2)}) %all-to-all-start) | async-done | bytes 1048608 | tf_op jit(solution)/shard_map/all_to_all | solution.py:33
  76.6 1.1 %multiply_reduce_fusion.1 = (f32[]{:T(128)}, f32[256,256]{0,1:T(8,128)S(1)}) fusion(bf16[2048,256]{1,0:T(8,128)(2,1)S(1)} %bitcast.194, bf16[2048,256]{1,0:T(8,128)(2,1)S(1)} %bitcast.193), kind=kOutput, calls=%fused_computation.59 | convolution fusion | flops 268566528 | bytes 2359300 | tf_op jit(solution)/shard_map/dot_general | solution.py:228
  77.7 1.1 %collective-permute-start.4 = (f32[256,256]{0,1:T(8,128)S(1)}, f32[256,256]{0,1:T(8,128)S(1)}, u32[]{:S(2)}, u32[]{:S(2)}) collective-permute-start(f32[256,256]{0,1:T(8,128)S(1)} %get-tuple-element.65), channel_id=1, source_target_pairs={{0,16},{8,24},{16,0},{24,8},{1,17},{9,25},{17,1},{25,9},{2,18},{10... | collective-permute-start | bytes 786440 | tf_op jit(solution)/shard_map/ppermute | solution.py:43
  78.8 1.3 %broadcast_in_dim_broadcast_in_dim_broadcast_in_dim.3 = f32[32,8,128]{2,1,0:T(8,128)} broadcast(f32[]{:T(128)} %get-tuple-element.64), dimensions={} | broadcast | bytes 131076 | tf_op jit(solution)/shard_map/broadcast_in_dim;broadcast_in_dim;broadcast_in_dim | solution.py:32
  80.1 3.0 %all-to-all-start.2 = ((f32[32,8,128]{2,1,0:T(8,128)}), f32[32,8,128]{2,1,0:T(8,128)S(1)}, u32[]{:S(2)}, u32[]{:S(2)}) async-start(f32[32,8,128]{2,1,0:T(8,128)} %broadcast_in_dim_broadcast_in_dim_broadcast_in_dim.3), calls=%async_computation.2 | async-start | bytes 262144 | tf_op jit(solution)/shard_map/all_to_all | solution.py:33
  83.2 0.8 copy.227
  84.0 0.7 copy.228
  84.8 2.7 %collective-permute-start.5 = (f32[256,256]{0,1:T(8,128)S(1)}, f32[256,256]{0,1:T(8,128)S(1)}, u32[]{:S(2)}, u32[]{:S(2)}) collective-permute-start(f32[256,256]{0,1:T(8,128)S(1)} %get-tuple-element.65), channel_id=1, source_target_pairs={{0,24},{8,0},{16,8},{24,16},{1,25},{9,1},{17,9},{25,17},{2,26},{10... | collective-permute-start | bytes 786440 | tf_op jit(solution)/shard_map/ppermute | solution.py:43
  87.7 4.0 %all-to-all-done.2 = f32[32,8,128]{2,1,0:T(8,128)S(1)} async-done(((f32[32,8,128]{2,1,0:T(8,128)}), f32[32,8,128]{2,1,0:T(8,128)S(1)}, u32[]{:S(2)}, u32[]{:S(2)}) %all-to-all-start.2) | async-done | bytes 131104 | tf_op jit(solution)/shard_map/all_to_all | solution.py:33
  91.7 0.6 slice_reduce_fusion
  93.4 0.7 collective-permute-done.5
  94.5 3.7 %multiply_subtract_fusion = (f32[1024,256]{1,0:T(8,128)}, f32[1024,256]{1,0:T(8,128)}, f32[1024,256]{1,0:T(8,128)}) fusion(f32[1024,256]{1,0:T(8,128)S(1)} %copy-done.5, f32[1024,256]{1,0:T(8,128)S(1)} %constant_dynamic-update-slice_fusion, f32[]{:T(128)S(6)} %min_shard_map.3, f32[1024,256]{1,0:T(8,128)} %param.20, f32[1024,256]{1,0:T(8,128)} %param.21), kind=kLoop, calls=%fused_computation.47 | loop fusion | flops 4194304 | bytes 7340036 | tf_op jit(solution)/shard_map/sub | solution.py:100
  (58 shorter events, 2.9 us)
Async XLA Ops:
  0.6 9.8 %copy-start.4 = (bf16[1,128,4096]{2,1,0:T(8,128)(2,1)S(1)}, bf16[1,128,4096]{2,1,0:T(8,128)(2,1)}, u32[]{:S(2)}) copy-start(bf16[1,128,4096]{2,1,0:T(8,128)(2,1)} %param.15) | copy-start | bytes 3145732
  4.9 16.3 %collective-permute-start = (bf16[2,128,2,128]{1,3,2,0:T(8,128)(2,1)S(1)}, bf16[2,128,2,128]{1,3,2,0:T(8,128)(2,1)}, u32[]{:S(2)}, u32[]{:S(2)}) collective-permute-start(bf16[2,128,2,128]{1,3,2,0:T(8,128)(2,1)S(1)} %pad_maximum_fusion), channel_id=1, source_target_pairs={{0,8},{8,16},{16,24},{1,9},{9,17},{17,25},{2,10},{10,18},{18,26},{... | collective-permute-start | bytes 393224 | tf_op jit(solution)/shard_map/ppermute | solution.py:25
  12.4 5.5 %copy-start.6 = (bf16[1,128,16,128]{3,2,1,0:T(8,128)(2,1)S(1)}, bf16[1,128,16,128]{3,2,1,0:T(8,128)(2,1)}, u32[]{:S(2)}) copy-start(bf16[1,128,16,128]{3,2,1,0:T(8,128)(2,1)} %param.11) | copy-start | bytes 1572868
  12.4 32.7 %all-to-all-start.1 = ((bf16[1,128,16,256]{3,1,0,2:T(8,128)(2,1)}), bf16[1,128,16,256]{3,1,0,2:T(8,128)(2,1)S(1)}, u32[]{:S(2)}, u32[]{:S(2)}) async-start(bf16[1,128,16,256]{3,1,0,2:T(8,128)(2,1)} %bitcast.58), calls=%async_computation.1 | async-start | bytes 2097152 | tf_op jit(solution)/shard_map/all_to_all | solution.py:224
  18.9 1.0 %copy-start.2 = (bf16[1,128,16,128]{3,2,1,0:T(8,128)(2,1)S(1)}, bf16[1,128,16,128]{3,2,1,0:T(8,128)(2,1)}, u32[]{:S(2)}) copy-start(bf16[1,128,16,128]{3,2,1,0:T(8,128)(2,1)} %param.14) | copy-start | bytes 1572868
  22.4 1.4 %copy-start = (f32[2,8,128,128]{2,3,1,0:T(8,128)}, f32[2,8,128,128]{2,3,1,0:T(8,128)S(1)}, u32[]{:S(2)}) copy-start(f32[2,8,128,128]{2,3,1,0:T(8,128)S(1)} %get-tuple-element.61) | copy-start | bytes 3145732
  22.4 0.9 copy-start.10
  25.9 3.2 %copy-start.7 = (bf16[128,2,8,128]{0,3,2,1:T(8,128)(2,1)S(1)}, bf16[128,2,8,128]{0,3,2,1:T(8,128)(2,1)}, u32[]{:S(2)}) copy-start(bf16[128,2,8,128]{0,3,2,1:T(8,128)(2,1)} %copy.214) | copy-start | bytes 1572868
  25.9 3.2 %copy-start.11 = (bf16[1,128,2,128]{3,2,1,0:T(2,128)(2,1)S(1)}, bf16[1,128,2,128]{3,2,1,0:T(2,128)(2,1)}, u32[]{:S(2)}) copy-start(bf16[1,128,2,128]{3,2,1,0:T(2,128)(2,1)} %param.13) | copy-start | bytes 196612
  27.7 1.9 %copy-start.1 = (f32[2,8,128,128]{2,3,1,0:T(8,128)S(1)}, f32[2,8,128,128]{2,3,1,0:T(8,128)}, u32[]{:S(2)}) copy-start(f32[2,8,128,128]{2,3,1,0:T(8,128)} %copy-done) | copy-start | bytes 3145732
  27.7 6.3 %collective-permute-start.2 = (bf16[128,2,128]{2,0,1:T(8,128)(2,1)S(1)}, bf16[128,2,128]{2,0,1:T(8,128)(2,1)S(1)}, u32[]{:S(2)}, u32[]{:S(2)}) collective-permute-start(bf16[128,2,128]{2,0,1:T(8,128)(2,1)S(1)} %fusion.24), channel_id=1, source_target_pairs={{8,0},{16,8},{24,16},{9,1},{17,9},{25,17},{10,2},{18,10},{26,18},{... | collective-permute-start | bytes 196616 | tf_op jit(solution)/shard_map/ppermute | solution.py:25
  34.3 0.6 copy-start.8
  46.1 30.5 %all-to-all-start = ((bf16[16,128,256]{2,1,0:T(8,128)(2,1)}), bf16[16,128,256]{2,1,0:T(8,128)(2,1)S(1)}, u32[]{:S(2)}, u32[]{:S(2)}) async-start(bf16[16,128,256]{2,1,0:T(8,128)(2,1)} %broadcast_in_dim.80), calls=%async_computation | async-start | bytes 2097152 | tf_op jit(solution)/shard_map/all_to_all | solution.py:33
  51.1 1.7 %copy-start.3 = (bf16[2,8,128,128]{2,3,1,0:T(8,128)(2,1)S(1)}, bf16[2,8,128,128]{2,3,1,0:T(8,128)(2,1)}, u32[]{:S(2)}) copy-start(bf16[2,8,128,128]{2,3,1,0:T(8,128)(2,1)} %fusion.13) | copy-start | bytes 1572868
  51.2 8.4 %collective-permute-start.1 = (bf16[128,2,128]{0,2,1:T(8,128)(2,1)S(1)}, bf16[128,2,128]{0,2,1:T(8,128)(2,1)S(1)}, u32[]{:S(2)}, u32[]{:S(2)}) collective-permute-start(bf16[128,2,128]{0,2,1:T(8,128)(2,1)S(1)} %fusion.25), channel_id=1, source_target_pairs={{8,0},{16,8},{24,16},{9,1},{17,9},{25,17},{10,2},{18,10},{26,18},{... | collective-permute-start | bytes 196616 | tf_op jit(solution)/shard_map/ppermute | solution.py:25
  77.7 15.3 %collective-permute-start.3 = (f32[256,256]{0,1:T(8,128)S(1)}, f32[256,256]{0,1:T(8,128)S(1)}, u32[]{:S(2)}, u32[]{:S(2)}) collective-permute-start(f32[256,256]{0,1:T(8,128)S(1)} %get-tuple-element.65), channel_id=1, source_target_pairs={{0,8},{8,16},{16,24},{24,0},{1,9},{9,17},{17,25},{25,1},{2,10},{10... | collective-permute-start | bytes 786440 | tf_op jit(solution)/shard_map/ppermute | solution.py:43
  77.7 15.5 %collective-permute-start.4 = (f32[256,256]{0,1:T(8,128)S(1)}, f32[256,256]{0,1:T(8,128)S(1)}, u32[]{:S(2)}, u32[]{:S(2)}) collective-permute-start(f32[256,256]{0,1:T(8,128)S(1)} %get-tuple-element.65), channel_id=1, source_target_pairs={{0,16},{8,24},{16,0},{24,8},{1,17},{9,25},{17,1},{25,9},{2,18},{10... | collective-permute-start | bytes 786440 | tf_op jit(solution)/shard_map/ppermute | solution.py:43
  80.1 11.6 %all-to-all-start.2 = ((f32[32,8,128]{2,1,0:T(8,128)}), f32[32,8,128]{2,1,0:T(8,128)S(1)}, u32[]{:S(2)}, u32[]{:S(2)}) async-start(f32[32,8,128]{2,1,0:T(8,128)} %broadcast_in_dim_broadcast_in_dim_broadcast_in_dim.3), calls=%async_computation.2 | async-start | bytes 262144 | tf_op jit(solution)/shard_map/all_to_all | solution.py:33
  83.2 0.8 copy-start.9
  84.8 9.2 %collective-permute-start.5 = (f32[256,256]{0,1:T(8,128)S(1)}, f32[256,256]{0,1:T(8,128)S(1)}, u32[]{:S(2)}, u32[]{:S(2)}) collective-permute-start(f32[256,256]{0,1:T(8,128)S(1)} %get-tuple-element.65), channel_id=1, source_target_pairs={{0,24},{8,0},{16,8},{24,16},{1,25},{9,1},{17,9},{25,17},{2,26},{10... | collective-permute-start | bytes 786440 | tf_op jit(solution)/shard_map/ppermute | solution.py:43
  93.3 1.2 %copy-start.5 = (f32[1024,256]{1,0:T(8,128)S(1)}, f32[1024,256]{1,0:T(8,128)}, u32[]{:S(2)}) copy-start(f32[1024,256]{1,0:T(8,128)} %param.19) | copy-start | bytes 3145732
